TPU v7x, 128 devices: a whole 4x4x4 slice. The times are simulated.
128 devices in a mesh: shot: 8 (over x, y_hi), space: 16 (over y_lo, z, core).
Axes of the slice: x: 4, y: 4 (y_hi: 2, y_lo: 2; y = y_hi * 2 + y_lo), z: 4, core: 2. Of those that a mesh axis runs over, the one named last changes fastest.
Arguments:
- residual: bfloat16 [8, 4096, 1536], P('shot', 'space'), may hold values from -6 to 6
- record_tile: int32 [8, 4096, 1], P('shot', 'space'), may hold values from 0 to 15; in each aligned block of 256 rows (0 to 255, 256 to 511, ..., all dimensions but the last counted through in order) at most 48 rows name the same one
- record_cell: int32 [8, 4096], P('shot', 'space'), may hold values from 0 to 1023
- time_filter: bfloat16 [6, 1536], replicated, may hold values from -0.15625 to 0.15625
- offsets: int32 [8], P('shot'), may hold values from 0 to 16
- velocity: float32 [8, 64, 256, 256], P('shot', None, 'space'), may hold values from 0.05 to 0.19
- adjoint_prev: float32 [8, 64, 256, 256], P('shot', None, 'space'), may hold values from -6 to 6
- adjoint_now: float32 [8, 64, 256, 256], P('shot', None, 'space'), may hold values from -6 to 6
- forward_accel: bfloat16 [8, 6, 64, 256, 256], P('shot', None, None, 'space'), may hold values from -6 to 6
Outputs:
- gradient: float32 [80, 256, 256], P('shot', 'space')
- adjoint_last: float32 [8, 64, 256, 256], P('shot', None, 'space')
Inputs may be any that keep to these rules, and one draw needn't show every extreme that they name: `record_tile`: among the 256 records of one device, at most 48 name the same tile.
All inputs are finite; a program needn't handle non-finite values.
Results may differ from a plain program's by a relative error of at most 0.0003.
Values sent between devices are 32-bit elements; how exact they have to be, the bound alone decides.
No kernel may reach another device: no remote copies, remote signals or barrier semaphores. Data moves between devices by JAX's collectives and lax.ppermute only.
A program may use at most 64 MiB of HBM per device.

v0:
```python
import jax
import jax.numpy as jnp
from jax import lax
from jax.sharding import PartitionSpec as P

STENCIL = (-205.0 / 72.0, 8.0 / 5.0, -1.0 / 5.0, 8.0 / 315.0, -1.0 / 560.0)


def extended(shard, sides, width):
    for axis, dim in sides:
        devices, length = (lax.axis_size(axis), shard.shape[dim])
        up = [(i, (i + 1) % devices) for i in range(devices - 1)]
        down = [(j, i) for i, j in up]
        last = lax.slice_in_dim(shard, length - width, length, axis=dim)
        leading = lax.slice_in_dim(shard, 0, width, axis=dim)
        before = lax.ppermute(last, axis, up)
        after = lax.ppermute(leading, axis, down)
        shard = jnp.concatenate([before, shard, after], axis=dim)
    return shard


def laplace(padded):
    span_y = padded.shape[0] - 8
    span_x = padded.shape[1] - 8
    span_z = padded.shape[2] - 8

    def window(shift_y, shift_x, shift_z):
        return padded[
            4 + shift_y : 4 + shift_y + span_y,
            4 + shift_x : 4 + shift_x + span_x,
            4 + shift_z : 4 + shift_z + span_z,
        ]

    summed = 3.0 * STENCIL[0] * window(0, 0, 0)
    for reach in range(1, 5):
        beside_all = (
            window(reach, 0, 0)
            + window(-reach, 0, 0)
            + window(0, reach, 0)
            + window(0, -reach, 0)
            + window(0, 0, reach)
            + window(0, 0, -reach)
        )
        summed = summed + STENCIL[reach] * beside_all
    return summed


def pad_sides(field):
    return jnp.pad(field, ((4, 4), (0, 0), (4, 4)))


def local(
    residual,
    record_tile,
    record_cell,
    time_filter,
    offsets,
    velocity,
    adjoint_prev,
    adjoint_now,
    forward_accel,
):
    tiles_count = lax.axis_size("space")
    record_count = residual.shape[1]
    cells_y = velocity.shape[1]
    cells_x = velocity.shape[2]
    step_count = forward_accel.shape[1]
    slot_count = record_count * 3 // 16
    surface = cells_y * cells_x
    block_rows = (cells_y + cells_y // 4) // lax.axis_size("shot")
    trace_rows = residual[0]
    tile_ids = record_tile[0, :, 0]
    cell_ids = record_cell[0]
    one_hot = (tile_ids[:, None] == jnp.arange(tiles_count, dtype=jnp.int32)[None, :]).astype(
        jnp.int32
    )
    order_rank = jnp.sum((jnp.cumsum(one_hot, axis=0) - 1) * one_hot, axis=1)
    slot_index = tile_ids * slot_count + order_rank
    cell_buffer = (
        jnp.full((tiles_count * slot_count,), surface, jnp.int32).at[slot_index].set(cell_ids)
    )
    cell_buffer = cell_buffer.reshape(tiles_count, slot_count)
    filtered = jnp.dot(trace_rows, time_filter.T, preferred_element_type=jnp.float32)
    value_buffer = (
        jnp.zeros((tiles_count * slot_count, step_count), jnp.float32).at[slot_index].set(filtered)
    )
    value_buffer = value_buffer.reshape(tiles_count, slot_count, step_count)
    values, arrived_cells = (
        lax.all_to_all(value_buffer, "space", split_axis=0, concat_axis=0, tiled=True),
        lax.all_to_all(cell_buffer, "space", split_axis=0, concat_axis=0, tiled=True),
    )
    source = jax.ops.segment_sum(
        values.reshape(-1, step_count), arrived_cells.reshape(-1), num_segments=surface + 1
    )[:surface]
    source = source.T.reshape(step_count, cells_y, cells_x)
    shift_rows = offsets[0]
    speed_sq = velocity[0]
    previous = adjoint_prev[0]
    current = adjoint_now[0]
    forward = forward_accel[0]
    imaging = jnp.zeros_like(current)
    for moment in range(step_count):
        rimmed = extended(current, (("space", 1),), 4)
        advanced = 2.0 * current - previous + speed_sq * laplace(pad_sides(rimmed))
        advanced = advanced.at[:, :, 0].add(source[moment])
        imaging = imaging + forward[moment] * advanced
        previous, current = (current, advanced)
    row_index = jnp.arange(lax.axis_size("shot") * block_rows, dtype=jnp.int32) - shift_rows
    inside = (row_index >= 0) & (row_index < cells_y)
    chosen = jnp.take(imaging, jnp.clip(row_index, 0, cells_y - 1), axis=0)
    gradient = lax.psum_scatter(
        jnp.where(inside[:, None, None], chosen, 0.0), "shot", scatter_dimension=0, tiled=True
    )
    return (gradient, current[None])


def solution(mesh):
    in_specs = (
        P("shot", "space", None),
        P("shot", "space", None),
        P("shot", "space"),
        P(),
        P("shot"),
        P("shot", None, "space", None),
        P("shot", None, "space", None),
        P("shot", None, "space", None),
        P("shot", None, None, "space", None),
    )
    out_specs = (P("shot", "space", None), P("shot", None, "space", None))
    return jax.shard_map(local, mesh=mesh, in_specs=in_specs, out_specs=out_specs, check_vma=False)
```

profile of v0, /device:TPU:97, one launch (start us, length us, event | category | flops | bytes accessed | tf_op | source)
XLA Modules:
  0.0 313.9 jit_solution(16388737999919964273)
XLA Ops:
  7.2 0.8 fusion.196
  8.7 0.8 fusion.195
  10.2 1.6 scatter_custom_fusion
  12.4 5.8 %all-to-all-start = ((s32[16,1,48]{2,1,0:T(1,128)}), s32[16,1,48]{2,1,0:T(1,128)S(1)}, u32[]{:S(2)}, u32[]{:S(2)}) async-start(s32[16,1,48]{2,1,0:T(1,128)} %all_to_all.9), calls=%async_computation | async-start | bytes 16384 | tf_op jit(solution)/shard_map/all_to_all | solution.py:90
  18.3 1.1 fusion.188
  19.3 1.2 scatter_custom_fusion.1
  20.8 0.7 reshape.372
  22.0 5.7 %all-to-all-start.1 = ((f32[16,1,288]{2,1,0:T(1,128)}), f32[16,1,288]{2,1,0:T(1,128)S(1)}, u32[]{:S(2)}, u32[]{:S(2)}) async-start(f32[16,1,288]{2,1,0:T(1,128)} %reshape.372), calls=%async_computation.1 | async-start | bytes 49152 | tf_op jit(solution)/shard_map/all_to_all | solution.py:89
  27.7 1.3 fusion.205
  29.0 3.4 %collective-permute-start = (f32[64,4,256]{2,1,0:T(4,128)S(1)}, f32[64,4,256]{2,1,0:T(4,128)S(1)}, u32[]{:S(2)}, u32[]{:S(2)}) collective-permute-start(f32[64,4,256]{2,1,0:T(4,128)S(1)} %get-tuple-element.87), channel_id=1, source_target_pairs={{0,1},{1,2},{2,3},{3,4},{4,5},{5,6},{6,7},{7,8},{8,9},{9,10},{10,1... | collective-permute-start | bytes 786440 | tf_op jit(solution)/shard_map/ppermute | solution.py:16
  32.4 1.9 collective-permute-start.1
  37.1 6.6 %scatter_custom_fusion.2 = f32[1025,6]{1,0:T(8,128)S(1)} fusion(s32[768]{0:T(1024)S(1)} %reshape.349, f32[768,6]{1,0:T(8,128)S(1)} %bitcast.88, f32[]{:T(128)} %constant.167.clone.1), kind=kCustom, calls=%fused_computation.345 | custom fusion | flops 4608 | bytes 24604 | tf_op jit(solution)/shard_map/scatter-add | solution.py:92
  43.8 2.4 fusion.206
  46.2 0.7 copy-done.4
  46.9 2.2 select_maximum_fusion.10
  49.2 12.3 %fusion.146 = f32[64,16,256]{2,1,0:T(8,128)} fusion(f32[64,16,256]{2,1,0:T(8,128)} %bitcast.78, f32[64,4,256]{2,1,0:T(4,128)} %copy-done.4, f32[64,4,256]{2,1,0:T(4,128)} %collective-permute-done.1, f32[72,24,264]{2,1,0:T(8,128)S(1)} %select_maximum_fusion.10, f32[1,64,16,256]{3,2,1,0:T(8,128)} %param.26, f32[1,64,16,256]{3,2,1,0:T(8,128)} %param.27), kind=kLoop, calls=%fused_computation.239 | loop fusion | flops 10747904 | bytes 21495808 | tf_op jit(solution)/shard_map/add | solution.py:104
  61.5 1.3 slice_add_fusion.41
  62.7 2.4 scatter-add.29
  65.1 1.3 fusion.204
  66.4 5.9 %collective-permute-start.2 = (f32[64,4,256]{2,1,0:T(4,128)S(1)}, f32[64,4,256]{2,1,0:T(4,128)S(1)}, u32[]{:S(2)}, u32[]{:S(2)}) collective-permute-start(f32[64,4,256]{2,1,0:T(4,128)S(1)} %get-tuple-element.85), channel_id=1, source_target_pairs={{0,1},{1,2},{2,3},{3,4},{4,5},{5,6},{6,7},{7,8},{8,9},{9,10},{10,1... | collective-permute-start | bytes 786440 | tf_op jit(solution)/shard_map/ppermute | solution.py:16
  72.3 2.1 collective-permute-start.3
  74.4 1.2 collective-permute-done.2
  75.6 6.5 %collective-permute-done.3 = f32[64,4,256]{2,1,0:T(4,128)S(1)} collective-permute-done((f32[64,4,256]{2,1,0:T(4,128)S(1)}, f32[64,4,256]{2,1,0:T(4,128)S(1)}, u32[]{:S(2)}, u32[]{:S(2)}) %collective-permute-start.3) | collective-permute-done | bytes 262176 | tf_op jit(solution)/shard_map/ppermute | solution.py:17
  82.8 2.4 select_maximum_fusion.8
  85.3 11.2 %fusion.119 = f32[64,16,256]{2,1,0:T(8,128)} fusion(f32[64,16,256]{2,1,0:T(8,128)} %scatter-add.29, f32[64,4,256]{2,1,0:T(4,128)} %copy-done.8, f32[64,4,256]{2,1,0:T(4,128)} %copy-done.12, f32[72,24,264]{2,1,0:T(8,128)S(1)} %select_maximum_fusion.8, f32[1,64,16,256]{3,2,1,0:T(8,128)} %param.26, f32[1,64,16,256]{3,2,1,0:T(8,128)} %param.28), kind=kLoop, calls=%fused_computation.212 | loop fusion | flops 10747904 | bytes 21495808 | tf_op jit(solution)/shard_map/add | solution.py:104
  96.5 1.3 slice_add_fusion.40
  97.8 2.4 scatter-add.30
  100.2 1.3 fusion.203
  101.5 1.9 collective-permute-start.4
  103.4 2.4 collective-permute-start.5
  105.8 0.9 collective-permute-done.4
  106.7 6.5 %collective-permute-done.5 = f32[64,4,256]{2,1,0:T(4,128)S(1)} collective-permute-done((f32[64,4,256]{2,1,0:T(4,128)S(1)}, f32[64,4,256]{2,1,0:T(4,128)S(1)}, u32[]{:S(2)}, u32[]{:S(2)}) %collective-permute-start.5) | collective-permute-done | bytes 262176 | tf_op jit(solution)/shard_map/ppermute | solution.py:17
  113.9 2.4 select_maximum_fusion.6
  116.4 11.9 %fusion.92 = f32[64,16,256]{2,1,0:T(8,128)} fusion(f32[64,16,256]{2,1,0:T(8,128)} %scatter-add.30, f32[64,4,256]{2,1,0:T(4,128)} %copy-done.9, f32[64,4,256]{2,1,0:T(4,128)} %copy-done.13, f32[72,24,264]{2,1,0:T(8,128)S(1)} %select_maximum_fusion.6, f32[1,64,16,256]{3,2,1,0:T(8,128)} %param.26, f32[64,16,256]{2,1,0:T(8,128)} %scatter-add.29), kind=kLoop, calls=%fused_computation.185 | loop fusion | flops 10747904 | bytes 21495808 | tf_op jit(solution)/shard_map/add | solution.py:104
  128.3 1.3 slice_add_fusion.39
  129.5 2.4 scatter-add.31
  132.0 1.3 fusion.202
  133.2 1.9 collective-permute-start.6
  135.2 2.6 collective-permute-start.7
  138.5 6.5 %collective-permute-done.7 = f32[64,4,256]{2,1,0:T(4,128)S(1)} collective-permute-done((f32[64,4,256]{2,1,0:T(4,128)S(1)}, f32[64,4,256]{2,1,0:T(4,128)S(1)}, u32[]{:S(2)}, u32[]{:S(2)}) %collective-permute-start.7) | collective-permute-done | bytes 262176 | tf_op jit(solution)/shard_map/ppermute | solution.py:17
  145.7 2.4 select_maximum_fusion.4
  148.1 11.7 %fusion.65 = f32[64,16,256]{2,1,0:T(8,128)} fusion(f32[64,16,256]{2,1,0:T(8,128)} %scatter-add.31, f32[64,4,256]{2,1,0:T(4,128)} %copy-done.10, f32[64,4,256]{2,1,0:T(4,128)} %copy-done.14, f32[72,24,264]{2,1,0:T(8,128)S(1)} %select_maximum_fusion.4, f32[1,64,16,256]{3,2,1,0:T(8,128)} %param.26, f32[64,16,256]{2,1,0:T(8,128)} %scatter-add.30), kind=kLoop, calls=%fused_computation.158 | loop fusion | flops 10747904 | bytes 21495808 | tf_op jit(solution)/shard_map/add | solution.py:104
  159.9 1.3 slice_add_fusion.38
  161.1 2.4 scatter-add.34
  163.5 1.3 fusion.201
  164.8 1.9 collective-permute-start.8
  166.8 2.4 collective-permute-start.9
  170.1 6.5 %collective-permute-done.9 = f32[64,4,256]{2,1,0:T(4,128)S(1)} collective-permute-done((f32[64,4,256]{2,1,0:T(4,128)S(1)}, f32[64,4,256]{2,1,0:T(4,128)S(1)}, u32[]{:S(2)}, u32[]{:S(2)}) %collective-permute-start.9) | collective-permute-done | bytes 262176 | tf_op jit(solution)/shard_map/ppermute | solution.py:17
  177.3 2.4 select_maximum_fusion.2
  179.7 11.2 %fusion.38 = f32[64,16,256]{2,1,0:T(8,128)} fusion(f32[64,16,256]{2,1,0:T(8,128)} %scatter-add.34, f32[64,4,256]{2,1,0:T(4,128)} %copy-done.7, f32[64,4,256]{2,1,0:T(4,128)} %copy-done.11, f32[72,24,264]{2,1,0:T(8,128)S(1)} %select_maximum_fusion.2, f32[1,64,16,256]{3,2,1,0:T(8,128)} %param.26, f32[64,16,256]{2,1,0:T(8,128)} %scatter-add.31), kind=kLoop, calls=%fused_computation.131 | loop fusion | flops 10747904 | bytes 21495808 | tf_op jit(solution)/shard_map/add | solution.py:104
  190.9 1.3 slice_add_fusion.37
  192.2 2.4 scatter-add.42
  194.6 1.3 fusion.200
  195.9 1.9 collective-permute-start.10
  197.8 2.7 collective-permute-start.11
  201.1 6.5 %collective-permute-done.11 = f32[64,4,256]{2,1,0:T(4,128)S(1)} collective-permute-done((f32[64,4,256]{2,1,0:T(4,128)S(1)}, f32[64,4,256]{2,1,0:T(4,128)S(1)}, u32[]{:S(2)}, u32[]{:S(2)}) %collective-permute-start.11) | collective-permute-done | bytes 262176 | tf_op jit(solution)/shard_map/ppermute | solution.py:17
  208.4 2.4 select_maximum_fusion
  210.8 11.1 %fusion.11 = f32[64,16,256]{2,1,0:T(8,128)} fusion(f32[64,16,256]{2,1,0:T(8,128)} %scatter-add.42, f32[64,4,256]{2,1,0:T(4,128)} %copy-done.5, f32[64,4,256]{2,1,0:T(4,128)} %copy-done.6, f32[72,24,264]{2,1,0:T(8,128)S(1)} %select_maximum_fusion, f32[1,64,16,256]{3,2,1,0:T(8,128)} %param.26, f32[64,16,256]{2,1,0:T(8,128)} %scatter-add.34), kind=kLoop, calls=%fused_computation.104 | loop fusion | flops 10747904 | bytes 21495808 | tf_op jit(solution)/shard_map/add | solution.py:104
  222.0 1.4 slice_add_fusion.36
  223.4 2.4 scatter-add.43
  225.8 5.0 %fusion.183 = f32[64,16,256]{2,1,0:T(8,128)} fusion(f32[64,16,256]{2,1,0:T(8,128)} %scatter-add.43, f32[64,16,256]{2,1,0:T(8,128)} %scatter-add.42, f32[64,16,256]{2,1,0:T(8,128)} %scatter-add.34, f32[64,16,256]{2,1,0:T(8,128)} %scatter-add.31, f32[64,16,256]{2,1,0:T(8,128)S(1)} %copy-done.2, f32[64,16,256]{2,1,0:T(8,128)S(1)} %copy-done.1, ...), kind=kLoop, calls=%fused_computation.325 | loop fusion | flops 4456448 | bytes 10485760 | tf_op jit(solution)/shard_map/add | solution.py:106
  230.8 1.9 gather_fusion
  232.7 1.3 select_select_fusion
  234.0 73.1 %reduce-scatter.2.cloned.1.call-done = f32[10,16,256]{2,1,0:T(8,128)} async-done(((f32[80,16,256]{2,1,0:T(8,128)}), f32[10,16,256]{2,1,0:T(8,128)}) %reduce-scatter.2.cloned.1.call-update) | async-done | bytes 163856 | tf_op jit(solution)/shard_map/reduce_scatter | solution.py:111
  (56 shorter events, 10.8 us)
Async XLA Ops:
  7.2 11.1 %copy-start = (bf16[1,256,1536]{2,1,0:T(8,128)(2,1)S(1)}, bf16[1,256,1536]{2,1,0:T(8,128)(2,1)}, u32[]{:S(2)}) copy-start(bf16[1,256,1536]{2,1,0:T(8,128)(2,1)} %param.21) | copy-start | bytes 2359300
  12.4 9.6 %all-to-all-start = ((s32[16,1,48]{2,1,0:T(1,128)}), s32[16,1,48]{2,1,0:T(1,128)S(1)}, u32[]{:S(2)}, u32[]{:S(2)}) async-start(s32[16,1,48]{2,1,0:T(1,128)} %all_to_all.9), calls=%async_computation | async-start | bytes 16384 | tf_op jit(solution)/shard_map/all_to_all | solution.py:90
  22.0 13.6 %all-to-all-start.1 = ((f32[16,1,288]{2,1,0:T(1,128)}), f32[16,1,288]{2,1,0:T(1,128)S(1)}, u32[]{:S(2)}, u32[]{:S(2)}) async-start(f32[16,1,288]{2,1,0:T(1,128)} %reshape.372), calls=%async_computation.1 | async-start | bytes 49152 | tf_op jit(solution)/shard_map/all_to_all | solution.py:89
  27.7 279.4 %reduce-scatter.2.cloned.1.call-start = ((), (), s32[]{:S(2)}) async-start(), calls=%async_computation.3 | async-start | bytes 1474560 | tf_op jit(solution)/shard_map/reduce_scatter | solution.py:111
  29.0 17.2 %collective-permute-start = (f32[64,4,256]{2,1,0:T(4,128)S(1)}, f32[64,4,256]{2,1,0:T(4,128)S(1)}, u32[]{:S(2)}, u32[]{:S(2)}) collective-permute-start(f32[64,4,256]{2,1,0:T(4,128)S(1)} %get-tuple-element.87), channel_id=1, source_target_pairs={{0,1},{1,2},{2,3},{3,4},{4,5},{5,6},{6,7},{7,8},{8,9},{9,10},{10,1... | collective-permute-start | bytes 786440 | tf_op jit(solution)/shard_map/ppermute | solution.py:16
  32.4 14.5 %collective-permute-start.1 = (f32[64,4,256]{2,1,0:T(4,128)S(1)}, f32[64,4,256]{2,1,0:T(4,128)}, u32[]{:S(2)}, u32[]{:S(2)}) collective-permute-start(f32[64,4,256]{2,1,0:T(4,128)S(1)} %get-tuple-element.86), channel_id=1, source_target_pairs={{1,0},{2,1},{3,2},{4,3},{5,4},{6,5},{7,6},{8,7},{9,8},{10,9},{11,1... | collective-permute-start | bytes 786440 | tf_op jit(solution)/shard_map/ppermute | solution.py:17
  43.8 3.1 copy-start.3
  46.2 0.7 copy-start.4
  66.4 9.2 %collective-permute-start.2 = (f32[64,4,256]{2,1,0:T(4,128)S(1)}, f32[64,4,256]{2,1,0:T(4,128)S(1)}, u32[]{:S(2)}, u32[]{:S(2)}) collective-permute-start(f32[64,4,256]{2,1,0:T(4,128)S(1)} %get-tuple-element.85), channel_id=1, source_target_pairs={{0,1},{1,2},{2,3},{3,4},{4,5},{5,6},{6,7},{7,8},{8,9},{9,10},{10,1... | collective-permute-start | bytes 786440 | tf_op jit(solution)/shard_map/ppermute | solution.py:16
  72.3 9.8 %collective-permute-start.3 = (f32[64,4,256]{2,1,0:T(4,128)S(1)}, f32[64,4,256]{2,1,0:T(4,128)S(1)}, u32[]{:S(2)}, u32[]{:S(2)}) collective-permute-start(f32[64,4,256]{2,1,0:T(4,128)S(1)} %get-tuple-element.84), channel_id=1, source_target_pairs={{1,0},{2,1},{3,2},{4,3},{5,4},{6,5},{7,6},{8,7},{9,8},{10,9},{11,1... | collective-permute-start | bytes 786440 | tf_op jit(solution)/shard_map/ppermute | solution.py:17
  75.6 6.5 %copy-start.8 = (f32[64,4,256]{2,1,0:T(4,128)}, f32[64,4,256]{2,1,0:T(4,128)S(1)}, u32[]{:S(2)}) copy-start(f32[64,4,256]{2,1,0:T(4,128)S(1)} %collective-permute-done.2) | copy-start | bytes 786436
  82.1 0.7 copy-start.12
  101.5 5.2 %collective-permute-start.4 = (f32[64,4,256]{2,1,0:T(4,128)S(1)}, f32[64,4,256]{2,1,0:T(4,128)S(1)}, u32[]{:S(2)}, u32[]{:S(2)}) collective-permute-start(f32[64,4,256]{2,1,0:T(4,128)S(1)} %get-tuple-element.83), channel_id=1, source_target_pairs={{0,1},{1,2},{2,3},{3,4},{4,5},{5,6},{6,7},{7,8},{8,9},{9,10},{10,1... | collective-permute-start | bytes 786440 | tf_op jit(solution)/shard_map/ppermute | solution.py:16
  103.4 9.8 %collective-permute-start.5 = (f32[64,4,256]{2,1,0:T(4,128)S(1)}, f32[64,4,256]{2,1,0:T(4,128)S(1)}, u32[]{:S(2)}, u32[]{:S(2)}) collective-permute-start(f32[64,4,256]{2,1,0:T(4,128)S(1)} %get-tuple-element.82), channel_id=1, source_target_pairs={{1,0},{2,1},{3,2},{4,3},{5,4},{6,5},{7,6},{8,7},{9,8},{10,9},{11,1... | collective-permute-start | bytes 786440 | tf_op jit(solution)/shard_map/ppermute | solution.py:17
  106.7 6.5 %copy-start.9 = (f32[64,4,256]{2,1,0:T(4,128)}, f32[64,4,256]{2,1,0:T(4,128)S(1)}, u32[]{:S(2)}) copy-start(f32[64,4,256]{2,1,0:T(4,128)S(1)} %collective-permute-done.4) | copy-start | bytes 786436
  113.2 0.7 copy-start.13
  133.2 5.2 %collective-permute-start.6 = (f32[64,4,256]{2,1,0:T(4,128)S(1)}, f32[64,4,256]{2,1,0:T(4,128)S(1)}, u32[]{:S(2)}, u32[]{:S(2)}) collective-permute-start(f32[64,4,256]{2,1,0:T(4,128)S(1)} %get-tuple-element.81), channel_id=1, source_target_pairs={{0,1},{1,2},{2,3},{3,4},{4,5},{5,6},{6,7},{7,8},{8,9},{9,10},{10,1... | collective-permute-start | bytes 786440 | tf_op jit(solution)/shard_map/ppermute | solution.py:16
  135.2 9.8 %collective-permute-start.7 = (f32[64,4,256]{2,1,0:T(4,128)S(1)}, f32[64,4,256]{2,1,0:T(4,128)S(1)}, u32[]{:S(2)}, u32[]{:S(2)}) collective-permute-start(f32[64,4,256]{2,1,0:T(4,128)S(1)} %get-tuple-element.80), channel_id=1, source_target_pairs={{1,0},{2,1},{3,2},{4,3},{5,4},{6,5},{7,6},{8,7},{9,8},{10,9},{11,1... | collective-permute-start | bytes 786440 | tf_op jit(solution)/shard_map/ppermute | solution.py:17
  138.5 6.5 %copy-start.10 = (f32[64,4,256]{2,1,0:T(4,128)}, f32[64,4,256]{2,1,0:T(4,128)S(1)}, u32[]{:S(2)}) copy-start(f32[64,4,256]{2,1,0:T(4,128)S(1)} %collective-permute-done.6) | copy-start | bytes 786436
  145.0 0.7 copy-start.14
  164.8 5.2 %collective-permute-start.8 = (f32[64,4,256]{2,1,0:T(4,128)S(1)}, f32[64,4,256]{2,1,0:T(4,128)S(1)}, u32[]{:S(2)}, u32[]{:S(2)}) collective-permute-start(f32[64,4,256]{2,1,0:T(4,128)S(1)} %get-tuple-element.79), channel_id=1, source_target_pairs={{0,1},{1,2},{2,3},{3,4},{4,5},{5,6},{6,7},{7,8},{8,9},{9,10},{10,1... | collective-permute-start | bytes 786440 | tf_op jit(solution)/shard_map/ppermute | solution.py:16
  166.8 9.8 %collective-permute-start.9 = (f32[64,4,256]{2,1,0:T(4,128)S(1)}, f32[64,4,256]{2,1,0:T(4,128)S(1)}, u32[]{:S(2)}, u32[]{:S(2)}) collective-permute-start(f32[64,4,256]{2,1,0:T(4,128)S(1)} %get-tuple-element.78), channel_id=1, source_target_pairs={{1,0},{2,1},{3,2},{4,3},{5,4},{6,5},{7,6},{8,7},{9,8},{10,9},{11,1... | collective-permute-start | bytes 786440 | tf_op jit(solution)/shard_map/ppermute | solution.py:17
  170.1 6.5 %copy-start.7 = (f32[64,4,256]{2,1,0:T(4,128)}, f32[64,4,256]{2,1,0:T(4,128)S(1)}, u32[]{:S(2)}) copy-start(f32[64,4,256]{2,1,0:T(4,128)S(1)} %collective-permute-done.8) | copy-start | bytes 786436
  176.6 0.7 copy-start.11
  195.9 5.2 %collective-permute-start.10 = (f32[64,4,256]{2,1,0:T(4,128)S(1)}, f32[64,4,256]{2,1,0:T(4,128)S(1)}, u32[]{:S(2)}, u32[]{:S(2)}) collective-permute-start(f32[64,4,256]{2,1,0:T(4,128)S(1)} %get-tuple-element.77), channel_id=1, source_target_pairs={{0,1},{1,2},{2,3},{3,4},{4,5},{5,6},{6,7},{7,8},{8,9},{9,10},{10,1... | collective-permute-start | bytes 786440 | tf_op jit(solution)/shard_map/ppermute | solution.py:16
  197.8 9.8 %collective-permute-start.11 = (f32[64,4,256]{2,1,0:T(4,128)S(1)}, f32[64,4,256]{2,1,0:T(4,128)S(1)}, u32[]{:S(2)}, u32[]{:S(2)}) collective-permute-start(f32[64,4,256]{2,1,0:T(4,128)S(1)} %get-tuple-element.76), channel_id=1, source_target_pairs={{1,0},{2,1},{3,2},{4,3},{5,4},{6,5},{7,6},{8,7},{9,8},{10,9},{11,1... | collective-permute-start | bytes 786440 | tf_op jit(solution)/shard_map/ppermute | solution.py:17
  201.1 6.5 %copy-start.5 = (f32[64,4,256]{2,1,0:T(4,128)}, f32[64,4,256]{2,1,0:T(4,128)S(1)}, u32[]{:S(2)}) copy-start(f32[64,4,256]{2,1,0:T(4,128)S(1)} %collective-permute-done.10) | copy-start | bytes 786436
  207.7 0.7 copy-start.6
  221.9 3.8 %copy-start.1 = (f32[64,16,256]{2,1,0:T(8,128)S(1)}, f32[64,16,256]{2,1,0:T(8,128)}, u32[]{:S(2)}) copy-start(f32[64,16,256]{2,1,0:T(8,128)} %scatter-add.29) | copy-start | bytes 3145732
  221.9 3.8 %copy-start.2 = (f32[64,16,256]{2,1,0:T(8,128)S(1)}, f32[64,16,256]{2,1,0:T(8,128)}, u32[]{:S(2)}) copy-start(f32[64,16,256]{2,1,0:T(8,128)} %scatter-add.30) | copy-start | bytes 3145732
Sparse Core Ops, SparseCore 0:
  234.1 72.8 reduce-scatter.1
where the time goes:
time: 318 us; the launch traced here: 314 us
  waiting for transfers between devices  110 us (35%)
  other arithmetic  109 us (34%)
  starting transfers between devices  42.6 us (13%)
  local copies, waits for them, and re-layouts  36.7 us (12%)
  between operations  15 us (5%)
    reduce_scatter x1, waiting for transfers between devices, local(): lax.psum_scatter(jnp.where(inside[:, None, None], chosen, 0.0), 'shot', s...  73.1 us
    add x6, other arithmetic, local(): advanced = 2.0 * current - previous + speed_sq * laplace(pad_sides(rimmed))  69.4 us
    ppermute x6, waiting for transfers between devices, extended(): after = lax.ppermute(leading, axis, down)  32.5 us
    ppermute x6, starting transfers between devices, extended(): before = lax.ppermute(last, axis, up)  17 us
    scatter-add x6, local copies, waits for them, and re-layouts, local(): advanced = advanced.at[:, :, 0].add(source[moment])  14.4 us
    concatenate x6, other arithmetic, extended(): shard = jnp.concatenate([before, shard, after], axis=dim)  14.4 us
    ppermute x6, starting transfers between devices, extended(): after = lax.ppermute(leading, axis, down)  14.1 us
    add x6, other arithmetic, local(): advanced = advanced.at[:, :, 0].add(source[moment])  7.76 us
  transfers between devices with their start and end apart: 15, of which 12 were waited for; matrix products, arithmetic and copies ran while one was open for 5% of the time, Pallas kernels for 0%

commit v1 on v0

--- a/solution.py
+++ b/solution.py
@@ -102,15 +102,18 @@
     for moment in range(step_count):
         rimmed = extended(current, (("space", 1),), 4)
         advanced = 2.0 * current - previous + speed_sq * laplace(pad_sides(rimmed))
-        advanced = advanced.at[:, :, 0].add(source[moment])
+        depth = lax.broadcasted_iota(jnp.int32, advanced.shape, 2)
+        advanced = jnp.where(depth == 0, advanced + source[moment][:, :, None], advanced)
         imaging = imaging + forward[moment] * advanced
         previous, current = (current, advanced)
     row_index = jnp.arange(lax.axis_size("shot") * block_rows, dtype=jnp.int32) - shift_rows
     inside = (row_index >= 0) & (row_index < cells_y)
     chosen = jnp.take(imaging, jnp.clip(row_index, 0, cells_y - 1), axis=0)
-    gradient = lax.psum_scatter(
-        jnp.where(inside[:, None, None], chosen, 0.0), "shot", scatter_dimension=0, tiled=True
-    )
+    placed = jnp.where(inside[:, None, None], chosen, 0.0)
+    shots = lax.axis_size("shot")
+    placed = placed.reshape((shots, block_rows) + placed.shape[1:])
+    arrived = lax.all_to_all(placed, "shot", split_axis=0, concat_axis=0, tiled=True)
+    gradient = jnp.sum(arrived, axis=0)
     return (gradient, current[None])
 
 

time: 318 us -> 224 us (0.70)
  waiting for transfers between devices: 110 us -> 35.8 us
  blocking collectives: 0 us -> 23.2 us
  local copies, waits for them, and re-layouts: 36.7 us -> 21.9 us
  between operations: 15 us -> 1.61 us
  other arithmetic: 109 us -> 98.7 us
    add x12 -> x0, other arithmetic: 77.2 us -> none  [the longest x6 69.4 us: local(): advanced = 2.0 * current - previous + speed_sq * laplace(pad_sides(rimmed))]
    reduce_scatter x1 -> x0, waiting for transfers between devices: 73.1 us -> none  [local(): lax.psum_scatter(jnp.where(inside[:, None, None], chosen, 0.0), 'shot', s...]
    select_n x1 -> x6, other arithmetic: 1.32 us -> 57.3 us  [the longest x5 57 us: local(): jnp.where(depth == 0, advanced + source[moment][:, :, None], advanced)]
    all_to_all x0 -> x1, blocking collectives: none -> 23.2 us  [local(): lax.all_to_all(placed, 'shot', split_axis=0, concat_axis=0, tiled=True)]
    scatter-add x6 -> x0, local copies, waits for them, and re-layouts: 14.4 us -> none  [local(): advanced = advanced.at[:, :, 0].add(source[moment])]
    add x1, other arithmetic: 5.05 us -> 14.3 us  [local(): imaging = imaging + forward[moment] * advanced]
    slice x6 -> x5, local copies, waits for them, and re-layouts: 7.75 us -> 6.47 us  [extended(): leading = lax.slice_in_dim(shard, 0, width, axis=dim)]
  transfers between devices with their start and end apart: 15 -> 14, of which waited for: 12 -> 10; matrix products, arithmetic and copies ran while one was open for 5% -> 7% of each run, Pallas kernels for 0% -> 0%
where the time goes in v1:
time: 224 us; the launch traced here: 223 us
  other arithmetic  98.7 us (44%)
  starting transfers between devices  40.4 us (18%)
  waiting for transfers between devices  35.8 us (16%)
  blocking collectives  23.2 us (10%)
  local copies, waits for them, and re-layouts  21.9 us (10%)
    select_n x5, other arithmetic, local(): jnp.where(depth == 0, advanced + source[moment][:, :, None], advanced)  57 us
    ppermute x6, waiting for transfers between devices, extended(): after = lax.ppermute(leading, axis, down)  29.4 us
    all_to_all x1, blocking collectives, local(): lax.all_to_all(placed, 'shot', split_axis=0, concat_axis=0, tiled=True)  23.2 us
    concatenate x6, other arithmetic, extended(): shard = jnp.concatenate([before, shard, after], axis=dim)  15.3 us
    ppermute x6, starting transfers between devices, extended(): before = lax.ppermute(last, axis, up)  14.8 us
    add x1, other arithmetic, local(): imaging = imaging + forward[moment] * advanced  14.3 us
    ppermute x6, starting transfers between devices, extended(): after = lax.ppermute(leading, axis, down)  13.9 us
    scatter-add x1, other arithmetic, local(): jax.ops.segment_sum(values.reshape(-1, step_count), arrived_cells.reshape...  6.81 us
  transfers between devices with their start and end apart: 14, of which 10 were waited for; matrix products, arithmetic and copies ran while one was open for 7% of the time, Pallas kernels for 0%

profile of v1, /device:TPU:97, one launch (start us, length us, event | category | flops | bytes accessed | tf_op | source)
XLA Modules:
  0.0 222.8 jit_solution(9446211093606745184)
XLA Ops:
  0.6 0.8 fusion.196
  1.4 0.6 reduce-window.6
  2.2 0.8 fusion.195
  3.0 0.7 compare_select_fusion.1
  3.7 1.6 scatter_custom_fusion
  5.2 0.7 all_to_all.12
  5.9 5.8 %all-to-all-start = ((s32[16,1,48]{2,1,0:T(1,128)}), s32[16,1,48]{2,1,0:T(1,128)S(1)}, u32[]{:S(2)}, u32[]{:S(2)}) async-start(s32[16,1,48]{2,1,0:T(1,128)} %all_to_all.12), calls=%async_computation | async-start | bytes 16384 | tf_op jit(solution)/shard_map/all_to_all | solution.py:90
  11.7 1.3 fusion.211
  13.0 3.4 %collective-permute-start = (f32[64,4,256]{2,1,0:T(4,128)S(1)}, f32[64,4,256]{2,1,0:T(4,128)S(1)}, u32[]{:S(2)}, u32[]{:S(2)}) collective-permute-start(f32[64,4,256]{2,1,0:T(4,128)S(1)} %get-tuple-element.21), channel_id=1, source_target_pairs={{0,1},{1,2},{2,3},{3,4},{4,5},{5,6},{6,7},{7,8},{8,9},{9,10},{10,1... | collective-permute-start | bytes 786440 | tf_op jit(solution)/shard_map/ppermute | solution.py:16
  16.4 1.9 collective-permute-start.1
  18.3 1.1 fusion.188
  19.4 1.2 scatter_custom_fusion.1
  20.9 0.7 reshape.206
  21.6 6.0 %all-to-all-start.1 = ((f32[16,1,288]{2,1,0:T(1,128)}), f32[16,1,288]{2,1,0:T(1,128)S(1)}, u32[]{:S(2)}, u32[]{:S(2)}) async-start(f32[16,1,288]{2,1,0:T(1,128)} %reshape.206), calls=%async_computation.1 | async-start | bytes 49152 | tf_op jit(solution)/shard_map/all_to_all | solution.py:89
  28.1 0.7 reduce.17
  28.9 2.9 %all-to-all-done.1 = f32[16,1,288]{2,1,0:T(1,128)S(1)} async-done(((f32[16,1,288]{2,1,0:T(1,128)}), f32[16,1,288]{2,1,0:T(1,128)S(1)}, u32[]{:S(2)}, u32[]{:S(2)}) %all-to-all-start.1) | async-done | bytes 18464 | tf_op jit(solution)/shard_map/all_to_all | solution.py:89
  32.3 0.7 reduce.18
  33.3 6.8 %scatter_custom_fusion.2 = f32[1025,6]{1,0:T(8,128)S(1)} fusion(s32[768]{0:T(1024)S(1)} %reshape.177, f32[768,6]{1,0:T(8,128)S(1)} %bitcast.79, f32[]{:T(128)} %constant.22.clone.1), kind=kCustom, calls=%fused_computation.351 | custom fusion | flops 4608 | bytes 24604 | tf_op jit(solution)/shard_map/scatter-add | solution.py:92
  40.1 1.6 slice_reduce_fusion
  41.8 0.7 copy-done.1
  42.5 2.6 %select_maximum_fusion.10 = f32[72,24,264]{2,1,0:T(8,128)S(1)} fusion(f32[64,4,256]{2,1,0:T(4,128)} %collective-permute-done.1, f32[64,16,256]{2,1,0:T(8,128)} %bitcast.74, f32[64,4,256]{2,1,0:T(4,128)} %copy-done.1), kind=kLoop, calls=%fused_computation.54 | loop fusion | flops 6842880 | bytes 3397632 | tf_op jit(solution)/shard_map/concatenate | solution.py:18
  45.1 11.6 %add_select_fusion.5 = f32[64,16,256]{2,1,0:T(8,128)} fusion(f32[64,16,256]{2,1,0:T(8,128)} %bitcast.75, f32[64,4,256]{2,1,0:T(4,128)} %copy-done.1, f32[64,4,256]{2,1,0:T(4,128)} %collective-permute-done.1, f32[72,24,264]{2,1,0:T(8,128)S(1)} %select_maximum_fusion.10, f32[1,64,16,256]{3,2,1,0:T(8,128)} %param.14, f32[1,64,16,256]{3,2,1,0:T(8,128)} %param.15, ...), kind=kLoop, calls=%fused_computation.100 | loop fusion | flops 11272192 | bytes 21500160 | tf_op jit(solution)/shard_map/jit(_where)/select_n | solution.py:106
  56.6 1.3 fusion.210
  57.9 3.7 %collective-permute-start.2 = (f32[64,4,256]{2,1,0:T(4,128)S(1)}, f32[64,4,256]{2,1,0:T(4,128)S(1)}, u32[]{:S(2)}, u32[]{:S(2)}) collective-permute-start(f32[64,4,256]{2,1,0:T(4,128)S(1)} %get-tuple-element.19), channel_id=1, source_target_pairs={{0,1},{1,2},{2,3},{3,4},{4,5},{5,6},{6,7},{7,8},{8,9},{9,10},{10,1... | collective-permute-start | bytes 786440 | tf_op jit(solution)/shard_map/ppermute | solution.py:16
  61.7 2.1 collective-permute-start.3
  63.8 1.1 collective-permute-done.2
  65.0 0.7 copy-done.4
  65.7 5.9 %collective-permute-done.3 = f32[64,4,256]{2,1,0:T(4,128)} collective-permute-done((f32[64,4,256]{2,1,0:T(4,128)S(1)}, f32[64,4,256]{2,1,0:T(4,128)}, u32[]{:S(2)}, u32[]{:S(2)}) %collective-permute-start.3) | collective-permute-done | bytes 262176 | tf_op jit(solution)/shard_map/ppermute | solution.py:17
  71.6 2.6 %select_maximum_fusion.8 = f32[72,24,264]{2,1,0:T(8,128)S(1)} fusion(f32[64,4,256]{2,1,0:T(4,128)} %collective-permute-done.3, f32[64,16,256]{2,1,0:T(8,128)} %add_select_fusion.5, f32[64,4,256]{2,1,0:T(4,128)} %copy-done.4), kind=kLoop, calls=%fused_computation.52 | loop fusion | flops 6842880 | bytes 3397632 | tf_op jit(solution)/shard_map/concatenate | solution.py:18
  74.1 11.7 %add_select_fusion.4 = f32[64,16,256]{2,1,0:T(8,128)} fusion(f32[64,16,256]{2,1,0:T(8,128)} %add_select_fusion.5, f32[64,4,256]{2,1,0:T(4,128)} %copy-done.4, f32[64,4,256]{2,1,0:T(4,128)} %collective-permute-done.3, f32[72,24,264]{2,1,0:T(8,128)S(1)} %select_maximum_fusion.8, f32[1,64,16,256]{3,2,1,0:T(8,128)} %param.14, f32[64,16]{1,0:T(8,128)S(1)} %add.639, ...), kind=kLoop, calls=%fused_computation.99 | loop fusion | flops 11272192 | bytes 21500160 | tf_op jit(solution)/shard_map/jit(_where)/select_n | solution.py:106
  85.8 1.3 fusion.209
  87.1 1.9 collective-permute-start.4
  89.1 2.4 %collective-permute-start.5 = (f32[64,4,256]{2,1,0:T(4,128)S(1)}, f32[64,4,256]{2,1,0:T(4,128)}, u32[]{:S(2)}, u32[]{:S(2)}) collective-permute-start(f32[64,4,256]{2,1,0:T(4,128)S(1)} %get-tuple-element.16), channel_id=1, source_target_pairs={{1,0},{2,1},{3,2},{4,3},{5,4},{6,5},{7,6},{8,7},{9,8},{10,9},{11,1... | collective-permute-start | bytes 786440 | tf_op jit(solution)/shard_map/ppermute | solution.py:17
  91.6 0.8 collective-permute-done.4
  92.4 0.7 copy-done.5
  93.1 5.9 %collective-permute-done.5 = f32[64,4,256]{2,1,0:T(4,128)} collective-permute-done((f32[64,4,256]{2,1,0:T(4,128)S(1)}, f32[64,4,256]{2,1,0:T(4,128)}, u32[]{:S(2)}, u32[]{:S(2)}) %collective-permute-start.5) | collective-permute-done | bytes 262176 | tf_op jit(solution)/shard_map/ppermute | solution.py:17
  99.0 2.6 %select_maximum_fusion.6 = f32[72,24,264]{2,1,0:T(8,128)S(1)} fusion(f32[64,4,256]{2,1,0:T(4,128)} %collective-permute-done.5, f32[64,16,256]{2,1,0:T(8,128)} %add_select_fusion.4, f32[64,4,256]{2,1,0:T(4,128)} %copy-done.5), kind=kLoop, calls=%fused_computation.50 | loop fusion | flops 6842880 | bytes 3397632 | tf_op jit(solution)/shard_map/concatenate | solution.py:18
  101.5 11.2 %add_select_fusion.3 = f32[64,16,256]{2,1,0:T(8,128)} fusion(f32[64,16,256]{2,1,0:T(8,128)} %add_select_fusion.4, f32[64,4,256]{2,1,0:T(4,128)} %copy-done.5, f32[64,4,256]{2,1,0:T(4,128)} %collective-permute-done.5, f32[72,24,264]{2,1,0:T(8,128)S(1)} %select_maximum_fusion.6, f32[1,64,16,256]{3,2,1,0:T(8,128)} %param.14, ...), kind=kLoop, calls=%fused_computation.98 | loop fusion | flops 11272192 | bytes 21500160 | tf_op jit(solution)/shard_map/jit(_where)/select_n | solution.py:106
  112.8 1.3 fusion.208
  114.1 1.9 collective-permute-start.6
  116.0 2.4 %collective-permute-start.7 = (f32[64,4,256]{2,1,0:T(4,128)S(1)}, f32[64,4,256]{2,1,0:T(4,128)}, u32[]{:S(2)}, u32[]{:S(2)}) collective-permute-start(f32[64,4,256]{2,1,0:T(4,128)S(1)} %get-tuple-element.14), channel_id=1, source_target_pairs={{1,0},{2,1},{3,2},{4,3},{5,4},{6,5},{7,6},{8,7},{9,8},{10,9},{11,1... | collective-permute-start | bytes 786440 | tf_op jit(solution)/shard_map/ppermute | solution.py:17
  118.5 0.8 collective-permute-done.6
  119.3 0.7 copy-done.6
  120.0 5.9 %collective-permute-done.7 = f32[64,4,256]{2,1,0:T(4,128)} collective-permute-done((f32[64,4,256]{2,1,0:T(4,128)S(1)}, f32[64,4,256]{2,1,0:T(4,128)}, u32[]{:S(2)}, u32[]{:S(2)}) %collective-permute-start.7) | collective-permute-done | bytes 262176 | tf_op jit(solution)/shard_map/ppermute | solution.py:17
  125.9 2.6 %select_maximum_fusion.4 = f32[72,24,264]{2,1,0:T(8,128)S(1)} fusion(f32[64,4,256]{2,1,0:T(4,128)} %collective-permute-done.7, f32[64,16,256]{2,1,0:T(8,128)} %add_select_fusion.3, f32[64,4,256]{2,1,0:T(4,128)} %copy-done.6), kind=kLoop, calls=%fused_computation.48 | loop fusion | flops 6842880 | bytes 3397632 | tf_op jit(solution)/shard_map/concatenate | solution.py:18
  128.4 11.3 %add_select_fusion.2 = f32[64,16,256]{2,1,0:T(8,128)} fusion(f32[64,16,256]{2,1,0:T(8,128)} %add_select_fusion.3, f32[64,4,256]{2,1,0:T(4,128)} %copy-done.6, f32[64,4,256]{2,1,0:T(4,128)} %collective-permute-done.7, f32[72,24,264]{2,1,0:T(8,128)S(1)} %select_maximum_fusion.4, f32[1,64,16,256]{3,2,1,0:T(8,128)} %param.14, ...), kind=kLoop, calls=%fused_computation.97 | loop fusion | flops 11272192 | bytes 21500160 | tf_op jit(solution)/shard_map/jit(_where)/select_n | solution.py:106
  139.7 1.3 fusion.207
  141.0 1.9 collective-permute-start.8
  142.9 2.6 %collective-permute-start.9 = (f32[64,4,256]{2,1,0:T(4,128)S(1)}, f32[64,4,256]{2,1,0:T(4,128)}, u32[]{:S(2)}, u32[]{:S(2)}) collective-permute-start(f32[64,4,256]{2,1,0:T(4,128)S(1)} %get-tuple-element.12), channel_id=1, source_target_pairs={{1,0},{2,1},{3,2},{4,3},{5,4},{6,5},{7,6},{8,7},{9,8},{10,9},{11,1... | collective-permute-start | bytes 786440 | tf_op jit(solution)/shard_map/ppermute | solution.py:17
  146.3 0.7 copy-done.3
  147.0 5.9 %collective-permute-done.9 = f32[64,4,256]{2,1,0:T(4,128)} collective-permute-done((f32[64,4,256]{2,1,0:T(4,128)S(1)}, f32[64,4,256]{2,1,0:T(4,128)}, u32[]{:S(2)}, u32[]{:S(2)}) %collective-permute-start.9) | collective-permute-done | bytes 262176 | tf_op jit(solution)/shard_map/ppermute | solution.py:17
  152.8 2.6 %select_maximum_fusion.2 = f32[72,24,264]{2,1,0:T(8,128)S(1)} fusion(f32[64,4,256]{2,1,0:T(4,128)} %collective-permute-done.9, f32[64,16,256]{2,1,0:T(8,128)} %add_select_fusion.2, f32[64,4,256]{2,1,0:T(4,128)} %copy-done.3), kind=kLoop, calls=%fused_computation.46 | loop fusion | flops 6842880 | bytes 3397632 | tf_op jit(solution)/shard_map/concatenate | solution.py:18
  155.4 11.3 %add_select_fusion.1 = f32[64,16,256]{2,1,0:T(8,128)} fusion(f32[64,16,256]{2,1,0:T(8,128)} %add_select_fusion.2, f32[64,4,256]{2,1,0:T(4,128)} %copy-done.3, f32[64,4,256]{2,1,0:T(4,128)} %collective-permute-done.9, f32[72,24,264]{2,1,0:T(8,128)S(1)} %select_maximum_fusion.2, f32[1,64,16,256]{3,2,1,0:T(8,128)} %param.14, ...), kind=kLoop, calls=%fused_computation.96 | loop fusion | flops 11272192 | bytes 21500160 | tf_op jit(solution)/shard_map/jit(_where)/select_n | solution.py:106
  166.7 1.3 fusion.206
  168.0 1.9 collective-permute-start.10
  169.9 2.4 %collective-permute-start.11 = (f32[64,4,256]{2,1,0:T(4,128)S(1)}, f32[64,4,256]{2,1,0:T(4,128)}, u32[]{:S(2)}, u32[]{:S(2)}) collective-permute-start(f32[64,4,256]{2,1,0:T(4,128)S(1)} %get-tuple-element.11), channel_id=1, source_target_pairs={{1,0},{2,1},{3,2},{4,3},{5,4},{6,5},{7,6},{8,7},{9,8},{10,9},{11,1... | collective-permute-start | bytes 786440 | tf_op jit(solution)/shard_map/ppermute | solution.py:17
  172.4 0.8 collective-permute-done.10
  173.2 0.7 copy-done.2
  173.9 5.9 %collective-permute-done.11 = f32[64,4,256]{2,1,0:T(4,128)} collective-permute-done((f32[64,4,256]{2,1,0:T(4,128)S(1)}, f32[64,4,256]{2,1,0:T(4,128)}, u32[]{:S(2)}, u32[]{:S(2)}) %collective-permute-start.11) | collective-permute-done | bytes 262176 | tf_op jit(solution)/shard_map/ppermute | solution.py:17
  179.8 2.6 %select_maximum_fusion = f32[72,24,264]{2,1,0:T(8,128)S(1)} fusion(f32[64,4,256]{2,1,0:T(4,128)} %collective-permute-done.11, f32[64,16,256]{2,1,0:T(8,128)} %add_select_fusion.1, f32[64,4,256]{2,1,0:T(4,128)} %copy-done.2), kind=kLoop, calls=%fused_computation.44 | loop fusion | flops 6842880 | bytes 3397632 | tf_op jit(solution)/shard_map/concatenate | solution.py:18
  182.4 14.3 %fusion.183 = (f32[64,16,256]{2,1,0:T(8,128)}, f32[64,16,256]{2,1,0:T(8,128)}) fusion(f32[64,16,256]{2,1,0:T(8,128)} %add_select_fusion.1, f32[64,16,256]{2,1,0:T(8,128)} %add_select_fusion.2, f32[64,16,256]{2,1,0:T(8,128)} %add_select_fusion.3, f32[64,16,256]{2,1,0:T(8,128)} %add_select_fusion.4, f32[64,16,256]{2,1,0:T(8,128)} %add_select_fusion.5, ...), kind=kLoop, calls=%fused_computation.331 | loop fusion | flops 15728640 | bytes 28840192 | tf_op jit(solution)/shard_map/add | solution.py:107
  196.7 1.9 gather_fusion
  198.8 23.2 %all_to_all.19 = f32[8,10,16,256]{3,2,1,0:T(8,128)S(1)} all-to-all(f32[8,10,16,256]{3,2,1,0:T(8,128)S(1)} %select_select_fusion), channel_id=1, replica_groups=mesh['shot'=8,'space'=16] {'shot'}, dimensions={0} | all-to-all | bytes 2621440 | tf_op jit(solution)/shard_map/all_to_all | solution.py:115
  222.0 0.8 reduce_sum.22
  (33 shorter events, 2.6 us)
Async XLA Ops:
  0.6 17.7 %copy-start = (bf16[1,256,1536]{2,1,0:T(8,128)(2,1)S(1)}, bf16[1,256,1536]{2,1,0:T(8,128)(2,1)}, u32[]{:S(2)}) copy-start(bf16[1,256,1536]{2,1,0:T(8,128)(2,1)} %param.9) | copy-start | bytes 2359300
  5.9 15.7 %all-to-all-start = ((s32[16,1,48]{2,1,0:T(1,128)}), s32[16,1,48]{2,1,0:T(1,128)S(1)}, u32[]{:S(2)}, u32[]{:S(2)}) async-start(s32[16,1,48]{2,1,0:T(1,128)} %all_to_all.12), calls=%async_computation | async-start | bytes 16384 | tf_op jit(solution)/shard_map/all_to_all | solution.py:90
  13.0 28.8 %collective-permute-start = (f32[64,4,256]{2,1,0:T(4,128)S(1)}, f32[64,4,256]{2,1,0:T(4,128)S(1)}, u32[]{:S(2)}, u32[]{:S(2)}) collective-permute-start(f32[64,4,256]{2,1,0:T(4,128)S(1)} %get-tuple-element.21), channel_id=1, source_target_pairs={{0,1},{1,2},{2,3},{3,4},{4,5},{5,6},{6,7},{7,8},{8,9},{9,10},{10,1... | collective-permute-start | bytes 786440 | tf_op jit(solution)/shard_map/ppermute | solution.py:16
  16.4 26.1 %collective-permute-start.1 = (f32[64,4,256]{2,1,0:T(4,128)S(1)}, f32[64,4,256]{2,1,0:T(4,128)}, u32[]{:S(2)}, u32[]{:S(2)}) collective-permute-start(f32[64,4,256]{2,1,0:T(4,128)S(1)} %get-tuple-element.20), channel_id=1, source_target_pairs={{1,0},{2,1},{3,2},{4,3},{5,4},{6,5},{7,6},{8,7},{9,8},{10,9},{11,1... | collective-permute-start | bytes 786440 | tf_op jit(solution)/shard_map/ppermute | solution.py:17
  21.6 10.2 %all-to-all-start.1 = ((f32[16,1,288]{2,1,0:T(1,128)}), f32[16,1,288]{2,1,0:T(1,128)S(1)}, u32[]{:S(2)}, u32[]{:S(2)}) async-start(f32[16,1,288]{2,1,0:T(1,128)} %reshape.206), calls=%async_computation.1 | async-start | bytes 49152 | tf_op jit(solution)/shard_map/all_to_all | solution.py:89
  41.8 0.7 copy-start.1
  57.9 7.0 %collective-permute-start.2 = (f32[64,4,256]{2,1,0:T(4,128)S(1)}, f32[64,4,256]{2,1,0:T(4,128)S(1)}, u32[]{:S(2)}, u32[]{:S(2)}) collective-permute-start(f32[64,4,256]{2,1,0:T(4,128)S(1)} %get-tuple-element.19), channel_id=1, source_target_pairs={{0,1},{1,2},{2,3},{3,4},{4,5},{5,6},{6,7},{7,8},{8,9},{9,10},{10,1... | collective-permute-start | bytes 786440 | tf_op jit(solution)/shard_map/ppermute | solution.py:16
  61.7 9.9 %collective-permute-start.3 = (f32[64,4,256]{2,1,0:T(4,128)S(1)}, f32[64,4,256]{2,1,0:T(4,128)}, u32[]{:S(2)}, u32[]{:S(2)}) collective-permute-start(f32[64,4,256]{2,1,0:T(4,128)S(1)} %get-tuple-element.18), channel_id=1, source_target_pairs={{1,0},{2,1},{3,2},{4,3},{5,4},{6,5},{7,6},{8,7},{9,8},{10,9},{11,1... | collective-permute-start | bytes 786440 | tf_op jit(solution)/shard_map/ppermute | solution.py:17
  65.0 0.7 copy-start.4
  87.1 5.2 %collective-permute-start.4 = (f32[64,4,256]{2,1,0:T(4,128)S(1)}, f32[64,4,256]{2,1,0:T(4,128)S(1)}, u32[]{:S(2)}, u32[]{:S(2)}) collective-permute-start(f32[64,4,256]{2,1,0:T(4,128)S(1)} %get-tuple-element.17), channel_id=1, source_target_pairs={{0,1},{1,2},{2,3},{3,4},{4,5},{5,6},{6,7},{7,8},{8,9},{9,10},{10,1... | collective-permute-start | bytes 786440 | tf_op jit(solution)/shard_map/ppermute | solution.py:16
  89.1 9.9 %collective-permute-start.5 = (f32[64,4,256]{2,1,0:T(4,128)S(1)}, f32[64,4,256]{2,1,0:T(4,128)}, u32[]{:S(2)}, u32[]{:S(2)}) collective-permute-start(f32[64,4,256]{2,1,0:T(4,128)S(1)} %get-tuple-element.16), channel_id=1, source_target_pairs={{1,0},{2,1},{3,2},{4,3},{5,4},{6,5},{7,6},{8,7},{9,8},{10,9},{11,1... | collective-permute-start | bytes 786440 | tf_op jit(solution)/shard_map/ppermute | solution.py:17
  92.4 0.7 copy-start.5
  114.1 5.2 %collective-permute-start.6 = (f32[64,4,256]{2,1,0:T(4,128)S(1)}, f32[64,4,256]{2,1,0:T(4,128)S(1)}, u32[]{:S(2)}, u32[]{:S(2)}) collective-permute-start(f32[64,4,256]{2,1,0:T(4,128)S(1)} %get-tuple-element.15), channel_id=1, source_target_pairs={{0,1},{1,2},{2,3},{3,4},{4,5},{5,6},{6,7},{7,8},{8,9},{9,10},{10,1... | collective-permute-start | bytes 786440 | tf_op jit(solution)/shard_map/ppermute | solution.py:16
  116.0 9.9 %collective-permute-start.7 = (f32[64,4,256]{2,1,0:T(4,128)S(1)}, f32[64,4,256]{2,1,0:T(4,128)}, u32[]{:S(2)}, u32[]{:S(2)}) collective-permute-start(f32[64,4,256]{2,1,0:T(4,128)S(1)} %get-tuple-element.14), channel_id=1, source_target_pairs={{1,0},{2,1},{3,2},{4,3},{5,4},{6,5},{7,6},{8,7},{9,8},{10,9},{11,1... | collective-permute-start | bytes 786440 | tf_op jit(solution)/shard_map/ppermute | solution.py:17
  119.3 0.7 copy-start.6
  141.0 5.3 %collective-permute-start.8 = (f32[64,4,256]{2,1,0:T(4,128)S(1)}, f32[64,4,256]{2,1,0:T(4,128)S(1)}, u32[]{:S(2)}, u32[]{:S(2)}) collective-permute-start(f32[64,4,256]{2,1,0:T(4,128)S(1)} %get-tuple-element.13), channel_id=1, source_target_pairs={{0,1},{1,2},{2,3},{3,4},{4,5},{5,6},{6,7},{7,8},{8,9},{9,10},{10,1... | collective-permute-start | bytes 786440 | tf_op jit(solution)/shard_map/ppermute | solution.py:16
  142.9 9.9 %collective-permute-start.9 = (f32[64,4,256]{2,1,0:T(4,128)S(1)}, f32[64,4,256]{2,1,0:T(4,128)}, u32[]{:S(2)}, u32[]{:S(2)}) collective-permute-start(f32[64,4,256]{2,1,0:T(4,128)S(1)} %get-tuple-element.12), channel_id=1, source_target_pairs={{1,0},{2,1},{3,2},{4,3},{5,4},{6,5},{7,6},{8,7},{9,8},{10,9},{11,1... | collective-permute-start | bytes 786440 | tf_op jit(solution)/shard_map/ppermute | solution.py:17
  146.3 0.7 copy-start.3
  168.0 5.2 %collective-permute-start.10 = (f32[64,4,256]{2,1,0:T(4,128)S(1)}, f32[64,4,256]{2,1,0:T(4,128)S(1)}, u32[]{:S(2)}, u32[]{:S(2)}) collective-permute-start(f32[64,4,256]{2,1,0:T(4,128)S(1)} %get-tuple-element.10), channel_id=1, source_target_pairs={{0,1},{1,2},{2,3},{3,4},{4,5},{5,6},{6,7},{7,8},{8,9},{9,10},{10,1... | collective-permute-start | bytes 786440 | tf_op jit(solution)/shard_map/ppermute | solution.py:16
  169.9 9.9 %collective-permute-start.11 = (f32[64,4,256]{2,1,0:T(4,128)S(1)}, f32[64,4,256]{2,1,0:T(4,128)}, u32[]{:S(2)}, u32[]{:S(2)}) collective-permute-start(f32[64,4,256]{2,1,0:T(4,128)S(1)} %get-tuple-element.11), channel_id=1, source_target_pairs={{1,0},{2,1},{3,2},{4,3},{5,4},{6,5},{7,6},{8,7},{9,8},{10,9},{11,1... | collective-permute-start | bytes 786440 | tf_op jit(solution)/shard_map/ppermute | solution.py:17
  173.2 0.7 copy-start.2

commit v2 on v1

--- a/solution.py
+++ b/solution.py
@@ -2,6 +2,8 @@
 import jax.numpy as jnp
 from jax import lax
 from jax.sharding import PartitionSpec as P
+from jax.experimental import pallas as pl
+from jax.experimental.pallas import tpu as pltpu
 
 STENCIL = (-205.0 / 72.0, 8.0 / 5.0, -1.0 / 5.0, 8.0 / 315.0, -1.0 / 560.0)
 
@@ -47,6 +49,95 @@
 
 def pad_sides(field):
     return jnp.pad(field, ((4, 4), (0, 0), (4, 4)))
+
+
+ROWS = 2
+
+
+def step_kernel(cur_ref, prev_ref, lo_ref, hi_ref, vel_ref, fwd_ref, src_ref, img_ref,
+                next_ref, img_out_ref, first_ref, last_ref, pad_ref):
+    cells_y, cells_x, cells_z = cur_ref.shape
+    width = lo_ref.shape[1]
+    zeros = jnp.zeros((4, pad_ref.shape[1], cells_z), jnp.float32)
+    pad_ref[0:4] = zeros
+    pad_ref[4 + cells_y : 8 + cells_y] = zeros
+    pad_ref[4 : 4 + cells_y, 8 - width : 8] = lo_ref[...]
+    pad_ref[4 : 4 + cells_y, 8 : 8 + cells_x] = cur_ref[...]
+    pad_ref[4 : 4 + cells_y, 8 + cells_x : 8 + cells_x + width] = hi_ref[...]
+
+    def body(chunk, carry):
+        y0 = pl.multiple_of(chunk * ROWS, ROWS)
+
+        def window(shift_y, shift_x):
+            return pad_ref[pl.ds(y0 + 4 + shift_y, ROWS), 8 + shift_x : 8 + shift_x + cells_x, :]
+
+        center = window(0, 0)
+        depth = lax.broadcasted_iota(jnp.int32, center.shape, 2)
+
+        def along_z(reach):
+            up = pltpu.roll(center, cells_z - reach, 2)
+            down = pltpu.roll(center, reach, 2)
+            return (
+                jnp.where(depth + reach < cells_z, up, 0.0),
+                jnp.where(depth - reach >= 0, down, 0.0),
+            )
+
+        summed = 3.0 * STENCIL[0] * center
+        for reach in range(1, 5):
+            z_up, z_down = along_z(reach)
+            beside_all = (
+                window(reach, 0)
+                + window(-reach, 0)
+                + window(0, reach)
+                + window(0, -reach)
+                + z_up
+                + z_down
+            )
+            summed = summed + STENCIL[reach] * beside_all
+        rows = pl.ds(y0, ROWS)
+        advanced = 2.0 * center - prev_ref[rows] + vel_ref[rows] * summed
+        source = jnp.broadcast_to(src_ref[rows], advanced.shape)
+        advanced = jnp.where(depth == 0, advanced + source, advanced)
+        next_ref[rows] = advanced
+        img_out_ref[rows] = img_ref[rows] + fwd_ref[rows].astype(jnp.float32) * advanced
+        first_ref[rows] = advanced[:, :width]
+        last_ref[rows] = advanced[:, cells_x - width :]
+        return carry
+
+    lax.fori_loop(0, cells_y // ROWS, body, 0)
+
+
+def step_call(moment, current, previous, lo, hi, speed_sq, forward, source, imaging):
+    cells_y, cells_x, cells_z = current.shape
+    width = lo.shape[1]
+    field = pl.BlockSpec((cells_y, cells_x, cells_z), lambda i: (0, 0, 0))
+    rim = pl.BlockSpec((cells_y, width, cells_z), lambda i: (0, 0, 0))
+    fwd_spec = pl.BlockSpec((None, cells_y, cells_x, cells_z), lambda i: (moment, 0, 0, 0))
+    src_spec = pl.BlockSpec((None, cells_y, cells_x, 1), lambda i: (moment, 0, 0, 0))
+    f32 = jnp.float32
+    return pl.pallas_call(
+        step_kernel,
+        grid=(1,),
+        out_shape=(
+            jax.ShapeDtypeStruct(current.shape, f32),
+            jax.ShapeDtypeStruct(current.shape, f32),
+            jax.ShapeDtypeStruct(lo.shape, f32),
+            jax.ShapeDtypeStruct(lo.shape, f32),
+        ),
+        in_specs=[field, field, rim, rim, field, fwd_spec, src_spec, field],
+        out_specs=(field, field, rim, rim),
+        scratch_shapes=[pltpu.VMEM((cells_y + 8, cells_x + 16, cells_z), f32)],
+        input_output_aliases={7: 1},
+        compiler_params=pltpu.CompilerParams(vmem_limit_bytes=48 * 1024 * 1024),
+    )(current, previous, lo, hi, speed_sq, forward, source, imaging)
+
+
+def halo(first, last):
+    axis = "space"
+    devices = lax.axis_size(axis)
+    up = [(i, (i + 1) % devices) for i in range(devices - 1)]
+    down = [(j, i) for i, j in up]
+    return lax.ppermute(last, axis, up), lax.ppermute(first, axis, down)
 
 
 def local(
@@ -99,12 +190,15 @@
     current = adjoint_now[0]
     forward = forward_accel[0]
     imaging = jnp.zeros_like(current)
+    source = source.reshape(source.shape + (1,))
+    width = 4
+    first = current[:, :width]
+    last = current[:, cells_x - width :]
     for moment in range(step_count):
-        rimmed = extended(current, (("space", 1),), 4)
-        advanced = 2.0 * current - previous + speed_sq * laplace(pad_sides(rimmed))
-        depth = lax.broadcasted_iota(jnp.int32, advanced.shape, 2)
-        advanced = jnp.where(depth == 0, advanced + source[moment][:, :, None], advanced)
-        imaging = imaging + forward[moment] * advanced
+        lo, hi = halo(first, last)
+        advanced, imaging, first, last = step_call(
+            moment, current, previous, lo, hi, speed_sq, forward, source, imaging
+        )
         previous, current = (current, advanced)
     row_index = jnp.arange(lax.axis_size("shot") * block_rows, dtype=jnp.int32) - shift_rows
     inside = (row_index >= 0) & (row_index < cells_y)

time: 224 us -> 180 us (0.80)
  other arithmetic: 98.7 us -> 11.8 us
  Pallas kernels: 0 us -> 39.9 us
  waiting for transfers between devices: 35.8 us -> 39.6 us
    select_n x5 -> x0, other arithmetic: 57 us -> none  [local(): jnp.where(depth == 0, advanced + source[moment][:, :, None], advanced)]
    pallas_call x0 -> x6, Pallas kernels: none -> 39.9 us  [step_call(): pl.pallas_call(step_kernel, grid=(1,), out_shape=(jax.ShapeDtypeStruct(cu...]
    concatenate x6 -> x0, other arithmetic: 15.3 us -> none  [extended(): shard = jnp.concatenate([before, shard, after], axis=dim)]
    add x1 -> x0, other arithmetic: 14.3 us -> none  [local(): imaging = imaging + forward[moment] * advanced]
    another operation x1 -> x2, local copies, waits for them, and re-layouts: 0.01 us -> 10.3 us  [the longest x1 10.3 us: local(): source = source.reshape(source.shape + (1,))]
    slice x8 -> x3, local copies, waits for them, and re-layouts: 9.52 us -> 3.09 us  [the longest x1 2.08 us: local(): first = current[:, :width]]
    ppermute x12, waiting for transfers between devices: 32.9 us -> 36.7 us  [halo(): return (lax.ppermute(last, axis, up), lax.ppermute(first, axis, down))]
    unnamed x16 -> x10, local copies, waits for them, and re-layouts: 5.06 us -> 1.91 us
  transfers between devices with their start and end apart: 14 -> 14, of which waited for: 10 -> 11; matrix products, arithmetic and copies ran while one was open for 7% -> 14% of each run, Pallas kernels for 0% -> 0%
where the time goes in v2:
time: 180 us; the launch traced here: 179 us
  starting transfers between devices  40.5 us (22%)
  Pallas kernels  39.9 us (22%)
  waiting for transfers between devices  39.6 us (22%)
  blocking collectives  23.3 us (13%)
  local copies, waits for them, and re-layouts  21 us (12%)
  other arithmetic  11.8 us (7%)
    pallas_call x6, Pallas kernels, step_call(): pl.pallas_call(step_kernel, grid=(1,), out_shape=(jax.ShapeDtypeStruct(cu...  39.9 us
    ppermute x12, waiting for transfers between devices, halo(): return (lax.ppermute(last, axis, up), lax.ppermute(first, axis, down))  36.7 us
    ppermute x12, starting transfers between devices, halo(): return (lax.ppermute(last, axis, up), lax.ppermute(first, axis, down))  28.7 us
    all_to_all x1, blocking collectives, local(): lax.all_to_all(placed, 'shot', split_axis=0, concat_axis=0, tiled=True)  23.3 us
    another operation x1, local copies, waits for them, and re-layouts, local(): source = source.reshape(source.shape + (1,))  10.3 us
    scatter-add x1, other arithmetic, local(): jax.ops.segment_sum(values.reshape(-1, step_count), arrived_cells.reshape...  6.6 us
    all_to_all x1, starting transfers between devices, local(): lax.all_to_all(value_buffer, 'space', split_axis=0, concat_axis=0, tiled=...  5.99 us
    all_to_all x1, starting transfers between devices, local(): lax.all_to_all(cell_buffer, 'space', split_axis=0, concat_axis=0, tiled=T...  5.82 us
  transfers between devices with their start and end apart: 14, of which 11 were waited for; matrix products, arithmetic and copies ran while one was open for 14% of the time, Pallas kernels for 0%

profile of v2, /device:TPU:97, one launch (start us, length us, event | category | flops | bytes accessed | tf_op | source)
XLA Modules:
  0.0 178.8 jit_solution(14668182349723574757)
XLA Ops:
  0.6 0.0 copy-start
  0.6 0.8 fusion.8
  1.4 0.6 reduce-window.6
  2.0 0.2 slice_reduce_fusion
  2.2 0.8 fusion.7
  3.0 0.7 compare_select_fusion.1
  3.7 1.6 scatter_custom_fusion
  5.2 0.7 all_to_all.12
  5.9 5.8 %all-to-all-start = ((s32[16,1,48]{2,1,0:T(1,128)}), s32[16,1,48]{2,1,0:T(1,128)S(1)}, u32[]{:S(2)}, u32[]{:S(2)}) async-start(s32[16,1,48]{2,1,0:T(1,128)} %all_to_all.12), calls=%async_computation | async-start | bytes 16384 | tf_op jit(solution)/shard_map/all_to_all | solution.py:181
  11.7 2.1 %fusion.18 = (f32[64,4,256]{2,1,0:T(4,128)}, f32[64,4,256]{2,1,0:T(4,128)}) fusion(f32[64,16,256]{2,1,0:T(8,128)} %bitcast.52), kind=kLoop, calls=%fused_computation.34 | loop fusion | bytes 1048576 | tf_op jit(solution)/shard_map/slice | solution.py:195
  13.8 3.4 %collective-permute-start = (f32[64,4,256]{2,1,0:T(4,128)}, f32[64,4,256]{2,1,0:T(4,128)S(1)}, u32[]{:S(2)}, u32[]{:S(2)}) collective-permute-start(f32[64,4,256]{2,1,0:T(4,128)} %get-tuple-element.47), channel_id=1, source_target_pairs={{0,1},{1,2},{2,3},{3,4},{4,5},{5,6},{6,7},{7,8},{8,9},{9,10},{10,1... | collective-permute-start | bytes 786440 | tf_op jit(solution)/shard_map/ppermute | solution.py:140
  17.2 1.9 %collective-permute-start.1 = (f32[64,4,256]{2,1,0:T(4,128)}, f32[64,4,256]{2,1,0:T(4,128)S(1)}, u32[]{:S(2)}, u32[]{:S(2)}) collective-permute-start(f32[64,4,256]{2,1,0:T(4,128)} %get-tuple-element.46), channel_id=1, source_target_pairs={{1,0},{2,1},{3,2},{4,3},{5,4},{6,5},{7,6},{8,7},{9,8},{10,9},{11,1... | collective-permute-start | bytes 786440 | tf_op jit(solution)/shard_map/ppermute | solution.py:140
  19.1 1.1 fusion
  20.2 1.2 scatter_custom_fusion.1
  21.4 0.2 copy.38
  21.6 0.7 reshape.151
  22.4 0.0 all-to-all-done
  22.4 6.0 %all-to-all-start.1 = ((f32[16,1,288]{2,1,0:T(1,128)}), f32[16,1,288]{2,1,0:T(1,128)S(1)}, u32[]{:S(2)}, u32[]{:S(2)}) async-start(f32[16,1,288]{2,1,0:T(1,128)} %reshape.151), calls=%async_computation.1 | async-start | bytes 49152 | tf_op jit(solution)/shard_map/all_to_all | solution.py:180
  28.4 0.5 broadcast.146
  28.9 0.7 reduce.5
  29.6 0.1 reshape.128
  29.6 2.9 %all-to-all-done.1 = f32[16,1,288]{2,1,0:T(1,128)S(1)} async-done(((f32[16,1,288]{2,1,0:T(1,128)}), f32[16,1,288]{2,1,0:T(1,128)S(1)}, u32[]{:S(2)}, u32[]{:S(2)}) %all-to-all-start.1) | async-done | bytes 18464 | tf_op jit(solution)/shard_map/all_to_all | solution.py:180
  32.5 0.5 broadcast.149
  33.0 0.7 reduce.6
  33.8 0.1 reshape.152
  33.8 0.2 copy.49
  34.0 6.6 %scatter_custom_fusion.2 = f32[1025,6]{1,0:T(8,128)S(1)} fusion(s32[768]{0:T(1024)S(1)} %reshape.128, f32[768,6]{1,0:T(8,128)S(1)} %bitcast.65, f32[]{:T(128)} %constant.17.clone.1), kind=kCustom, calls=%fused_computation.7 | custom fusion | flops 4608 | bytes 24604 | tf_op jit(solution)/shard_map/scatter-add | solution.py:183
  40.7 0.8 slice.25
  41.5 10.3 %copy.42.src_ref = f32[6,64,16,1]{3,2,1,0:T(8,128)} copy(f32[6,64,16,1]{0,2,1,3:T(8,128)} %bitcast.63) | data formatting | bytes 49152 | tf_op jit(solution)/shard_map/reshape;reshape | solution.py:193
  51.7 0.0 collective-permute-done.lo_ref
  51.8 0.0 collective-permute-done.1.hi_ref
  51.8 0.1 broadcast_in_dim.46.img_ref
  51.9 0.0 copy-done.3
  51.9 1.1 copy-done.2
  53.0 6.5 %shard_map.104 = (f32[64,16,256]{2,1,0:T(8,128)S(1)}, f32[64,16,256]{2,1,0:T(8,128)S(1)}, f32[64,4,256]{2,1,0:T(4,128)S(1)}, f32[64,4,256]{2,1,0:T(4,128)S(1)}) custom-call(f32[64,16,256]{2,1,0:T(8,128)S(1)} %bitcast.53, f32[64,16,256]{2,1,0:T(8,128)S(1)} %bitcast.55, ...), custom_call_target="tpu_custom_call", output_to_operand_aliasing={{1}: (7, {})} | custom-call | tf_op jit(solution)/shard_map/pallas_call | solution.py:118
  59.5 4.2 %collective-permute-start.2 = (f32[64,4,256]{2,1,0:T(4,128)S(1)}, f32[64,4,256]{2,1,0:T(4,128)S(1)}, u32[]{:S(2)}, u32[]{:S(2)}) collective-permute-start(f32[64,4,256]{2,1,0:T(4,128)S(1)} %get-tuple-element.25), channel_id=1, source_target_pairs={{0,1},{1,2},{2,3},{3,4},{4,5},{5,6},{6,7},{7,8},{8,9},{9,10},{10,1... | collective-permute-start | bytes 786440 | tf_op jit(solution)/shard_map/ppermute | solution.py:140
  63.7 1.9 %collective-permute-start.3 = (f32[64,4,256]{2,1,0:T(4,128)S(1)}, f32[64,4,256]{2,1,0:T(4,128)S(1)}, u32[]{:S(2)}, u32[]{:S(2)}) collective-permute-start(f32[64,4,256]{2,1,0:T(4,128)S(1)} %get-tuple-element.26), channel_id=1, source_target_pairs={{1,0},{2,1},{3,2},{4,3},{5,4},{6,5},{7,6},{8,7},{9,8},{10,9},{11,1... | collective-permute-start | bytes 786440 | tf_op jit(solution)/shard_map/ppermute | solution.py:140
  65.6 1.4 collective-permute-done.2.lo_ref
  67.0 6.5 %collective-permute-done.3.hi_ref = f32[64,4,256]{2,1,0:T(4,128)S(1)} collective-permute-done((f32[64,4,256]{2,1,0:T(4,128)S(1)}, f32[64,4,256]{2,1,0:T(4,128)S(1)}, u32[]{:S(2)}, u32[]{:S(2)}) %collective-permute-start.3) | collective-permute-done | bytes 262176 | tf_op jit(solution)/shard_map/ppermute | solution.py:140
  73.5 6.5 %shard_map.105 = (f32[64,16,256]{2,1,0:T(8,128)S(1)}, f32[64,16,256]{2,1,0:T(8,128)S(1)}, f32[64,4,256]{2,1,0:T(4,128)S(1)}, f32[64,4,256]{2,1,0:T(4,128)S(1)}) custom-call(f32[64,16,256]{2,1,0:T(8,128)S(1)} %get-tuple-element.24.cur_ref.prev_ref, f32[64,16,256]{2,1,0:T(8,128)S(1)} %bitcast.54, ...), custom_call_target="tpu_custom_call", output_to_operand_aliasing={{1}: (7, {})} | custom-call | tf_op jit(solution)/shard_map/pallas_call | solution.py:118
  80.0 1.9 %collective-permute-start.4 = (f32[64,4,256]{2,1,0:T(4,128)S(1)}, f32[64,4,256]{2,1,0:T(4,128)S(1)}, u32[]{:S(2)}, u32[]{:S(2)}) collective-permute-start(f32[64,4,256]{2,1,0:T(4,128)S(1)} %get-tuple-element.29), channel_id=1, source_target_pairs={{0,1},{1,2},{2,3},{3,4},{4,5},{5,6},{6,7},{7,8},{8,9},{9,10},{10,1... | collective-permute-start | bytes 786440 | tf_op jit(solution)/shard_map/ppermute | solution.py:140
  81.9 2.4 %collective-permute-start.5 = (f32[64,4,256]{2,1,0:T(4,128)S(1)}, f32[64,4,256]{2,1,0:T(4,128)S(1)}, u32[]{:S(2)}, u32[]{:S(2)}) collective-permute-start(f32[64,4,256]{2,1,0:T(4,128)S(1)} %get-tuple-element.30), channel_id=1, source_target_pairs={{1,0},{2,1},{3,2},{4,3},{5,4},{6,5},{7,6},{8,7},{9,8},{10,9},{11,1... | collective-permute-start | bytes 786440 | tf_op jit(solution)/shard_map/ppermute | solution.py:140
  84.3 0.9 collective-permute-done.4.lo_ref
  85.2 6.5 %collective-permute-done.5.hi_ref = f32[64,4,256]{2,1,0:T(4,128)S(1)} collective-permute-done((f32[64,4,256]{2,1,0:T(4,128)S(1)}, f32[64,4,256]{2,1,0:T(4,128)S(1)}, u32[]{:S(2)}, u32[]{:S(2)}) %collective-permute-start.5) | collective-permute-done | bytes 262176 | tf_op jit(solution)/shard_map/ppermute | solution.py:140
  91.7 6.5 %shard_map.106 = (f32[64,16,256]{2,1,0:T(8,128)S(1)}, f32[64,16,256]{2,1,0:T(8,128)S(1)}, f32[64,4,256]{2,1,0:T(4,128)S(1)}, f32[64,4,256]{2,1,0:T(4,128)S(1)}) custom-call(f32[64,16,256]{2,1,0:T(8,128)S(1)} %get-tuple-element.28.cur_ref.prev_ref, f32[64,16,256]{2,1,0:T(8,128)S(1)} %get-tuple-element.24.cur_ref.prev_ref, ...), custom_call_target="tpu_custom_call", output_to_operand_aliasing={{1}: (7, {})} | custom-call | tf_op jit(solution)/shard_map/pallas_call | solution.py:118
  98.2 1.9 %collective-permute-start.6 = (f32[64,4,256]{2,1,0:T(4,128)S(1)}, f32[64,4,256]{2,1,0:T(4,128)S(1)}, u32[]{:S(2)}, u32[]{:S(2)}) collective-permute-start(f32[64,4,256]{2,1,0:T(4,128)S(1)} %get-tuple-element.33), channel_id=1, source_target_pairs={{0,1},{1,2},{2,3},{3,4},{4,5},{5,6},{6,7},{7,8},{8,9},{9,10},{10,1... | collective-permute-start | bytes 786440 | tf_op jit(solution)/shard_map/ppermute | solution.py:140
  100.1 2.4 %collective-permute-start.7 = (f32[64,4,256]{2,1,0:T(4,128)S(1)}, f32[64,4,256]{2,1,0:T(4,128)S(1)}, u32[]{:S(2)}, u32[]{:S(2)}) collective-permute-start(f32[64,4,256]{2,1,0:T(4,128)S(1)} %get-tuple-element.34), channel_id=1, source_target_pairs={{1,0},{2,1},{3,2},{4,3},{5,4},{6,5},{7,6},{8,7},{9,8},{10,9},{11,1... | collective-permute-start | bytes 786440 | tf_op jit(solution)/shard_map/ppermute | solution.py:140
  102.6 0.9 collective-permute-done.6.lo_ref
  103.4 6.5 %collective-permute-done.7.hi_ref = f32[64,4,256]{2,1,0:T(4,128)S(1)} collective-permute-done((f32[64,4,256]{2,1,0:T(4,128)S(1)}, f32[64,4,256]{2,1,0:T(4,128)S(1)}, u32[]{:S(2)}, u32[]{:S(2)}) %collective-permute-start.7) | collective-permute-done | bytes 262176 | tf_op jit(solution)/shard_map/ppermute | solution.py:140
  109.9 6.5 %shard_map.107 = (f32[64,16,256]{2,1,0:T(8,128)S(1)}, f32[64,16,256]{2,1,0:T(8,128)S(1)}, f32[64,4,256]{2,1,0:T(4,128)S(1)}, f32[64,4,256]{2,1,0:T(4,128)S(1)}) custom-call(f32[64,16,256]{2,1,0:T(8,128)S(1)} %get-tuple-element.32.cur_ref.prev_ref, f32[64,16,256]{2,1,0:T(8,128)S(1)} %get-tuple-element.28.cur_ref.prev_ref, ...), custom_call_target="tpu_custom_call", output_to_operand_aliasing={{1}: (7, {})} | custom-call | tf_op jit(solution)/shard_map/pallas_call | solution.py:118
  116.5 1.9 %collective-permute-start.8 = (f32[64,4,256]{2,1,0:T(4,128)S(1)}, f32[64,4,256]{2,1,0:T(4,128)S(1)}, u32[]{:S(2)}, u32[]{:S(2)}) collective-permute-start(f32[64,4,256]{2,1,0:T(4,128)S(1)} %get-tuple-element.37), channel_id=1, source_target_pairs={{0,1},{1,2},{2,3},{3,4},{4,5},{5,6},{6,7},{7,8},{8,9},{9,10},{10,1... | collective-permute-start | bytes 786440 | tf_op jit(solution)/shard_map/ppermute | solution.py:140
  118.4 2.4 %collective-permute-start.9 = (f32[64,4,256]{2,1,0:T(4,128)S(1)}, f32[64,4,256]{2,1,0:T(4,128)S(1)}, u32[]{:S(2)}, u32[]{:S(2)}) collective-permute-start(f32[64,4,256]{2,1,0:T(4,128)S(1)} %get-tuple-element.38), channel_id=1, source_target_pairs={{1,0},{2,1},{3,2},{4,3},{5,4},{6,5},{7,6},{8,7},{9,8},{10,9},{11,1... | collective-permute-start | bytes 786440 | tf_op jit(solution)/shard_map/ppermute | solution.py:140
  121.4 0.2 collective-permute-done.8.lo_ref
  121.7 6.5 %collective-permute-done.9.hi_ref = f32[64,4,256]{2,1,0:T(4,128)S(1)} collective-permute-done((f32[64,4,256]{2,1,0:T(4,128)S(1)}, f32[64,4,256]{2,1,0:T(4,128)S(1)}, u32[]{:S(2)}, u32[]{:S(2)}) %collective-permute-start.9) | collective-permute-done | bytes 262176 | tf_op jit(solution)/shard_map/ppermute | solution.py:140
  128.2 6.6 %shard_map.108 = (f32[64,16,256]{2,1,0:T(8,128)S(1)}, f32[64,16,256]{2,1,0:T(8,128)S(1)}, f32[64,4,256]{2,1,0:T(4,128)S(1)}, f32[64,4,256]{2,1,0:T(4,128)S(1)}) custom-call(f32[64,16,256]{2,1,0:T(8,128)S(1)} %get-tuple-element.36.cur_ref.prev_ref, f32[64,16,256]{2,1,0:T(8,128)S(1)} %get-tuple-element.32.cur_ref.prev_ref, ...), custom_call_target="tpu_custom_call", output_to_operand_aliasing={{1}: (7, {})} | custom-call | tf_op jit(solution)/shard_map/pallas_call | solution.py:118
  134.8 1.9 %collective-permute-start.10 = (f32[64,4,256]{2,1,0:T(4,128)S(1)}, f32[64,4,256]{2,1,0:T(4,128)S(1)}, u32[]{:S(2)}, u32[]{:S(2)}) collective-permute-start(f32[64,4,256]{2,1,0:T(4,128)S(1)} %get-tuple-element.41), channel_id=1, source_target_pairs={{0,1},{1,2},{2,3},{3,4},{4,5},{5,6},{6,7},{7,8},{8,9},{9,10},{10,1... | collective-permute-start | bytes 786440 | tf_op jit(solution)/shard_map/ppermute | solution.py:140
  136.7 2.4 %collective-permute-start.11 = (f32[64,4,256]{2,1,0:T(4,128)S(1)}, f32[64,4,256]{2,1,0:T(4,128)S(1)}, u32[]{:S(2)}, u32[]{:S(2)}) collective-permute-start(f32[64,4,256]{2,1,0:T(4,128)S(1)} %get-tuple-element.42), channel_id=1, source_target_pairs={{1,0},{2,1},{3,2},{4,3},{5,4},{6,5},{7,6},{8,7},{9,8},{10,9},{11,1... | collective-permute-start | bytes 786440 | tf_op jit(solution)/shard_map/ppermute | solution.py:140
  139.2 0.8 collective-permute-done.10.lo_ref
  140.0 6.5 %collective-permute-done.11.hi_ref = f32[64,4,256]{2,1,0:T(4,128)S(1)} collective-permute-done((f32[64,4,256]{2,1,0:T(4,128)S(1)}, f32[64,4,256]{2,1,0:T(4,128)S(1)}, u32[]{:S(2)}, u32[]{:S(2)}) %collective-permute-start.11) | collective-permute-done | bytes 262176 | tf_op jit(solution)/shard_map/ppermute | solution.py:140
  146.5 7.3 %shard_map.109 = (f32[64,16,256]{2,1,0:T(8,128)}, f32[64,16,256]{2,1,0:T(8,128)S(1)}, f32[64,4,256]{2,1,0:T(4,128)}, f32[64,4,256]{2,1,0:T(4,128)}) custom-call(f32[64,16,256]{2,1,0:T(8,128)S(1)} %get-tuple-element.40.cur_ref, f32[64,16,256]{2,1,0:T(8,128)S(1)} %get-tuple-element.36.cur_ref.prev_ref, ...), custom_call_target="tpu_custom_call", output_to_operand_aliasing={{1}: (7, {})} | custom-call | tf_op jit(solution)/shard_map/pallas_call | solution.py:118
  153.8 0.7 gather_fusion
  154.5 0.2 select_select_fusion
  154.8 23.3 %all_to_all.19 = f32[8,10,16,256]{3,2,1,0:T(8,128)S(1)} all-to-all(f32[8,10,16,256]{3,2,1,0:T(8,128)S(1)} %select_select_fusion), channel_id=1, replica_groups=mesh['shot'=8,'space'=16] {'shot'}, dimensions={0} | all-to-all | bytes 2621440 | tf_op jit(solution)/shard_map/all_to_all | solution.py:209
  178.0 0.8 reduce_sum.22
  (10 shorter events, 0.1 us)
Async XLA Ops:
  0.6 18.5 %copy-start = (bf16[1,256,1536]{2,1,0:T(8,128)(2,1)S(1)}, bf16[1,256,1536]{2,1,0:T(8,128)(2,1)}, u32[]{:S(2)}) copy-start(bf16[1,256,1536]{2,1,0:T(8,128)(2,1)} %param.9) | copy-start | bytes 2359300
  5.9 16.5 %all-to-all-start = ((s32[16,1,48]{2,1,0:T(1,128)}), s32[16,1,48]{2,1,0:T(1,128)S(1)}, u32[]{:S(2)}, u32[]{:S(2)}) async-start(s32[16,1,48]{2,1,0:T(1,128)} %all_to_all.12), calls=%async_computation | async-start | bytes 16384 | tf_op jit(solution)/shard_map/all_to_all | solution.py:181
  13.8 37.9 %collective-permute-start = (f32[64,4,256]{2,1,0:T(4,128)}, f32[64,4,256]{2,1,0:T(4,128)S(1)}, u32[]{:S(2)}, u32[]{:S(2)}) collective-permute-start(f32[64,4,256]{2,1,0:T(4,128)} %get-tuple-element.47), channel_id=1, source_target_pairs={{0,1},{1,2},{2,3},{3,4},{4,5},{5,6},{6,7},{7,8},{8,9},{9,10},{10,1... | collective-permute-start | bytes 786440 | tf_op jit(solution)/shard_map/ppermute | solution.py:140
  17.2 34.6 %collective-permute-start.1 = (f32[64,4,256]{2,1,0:T(4,128)}, f32[64,4,256]{2,1,0:T(4,128)S(1)}, u32[]{:S(2)}, u32[]{:S(2)}) collective-permute-start(f32[64,4,256]{2,1,0:T(4,128)} %get-tuple-element.46), channel_id=1, source_target_pairs={{1,0},{2,1},{3,2},{4,3},{5,4},{6,5},{7,6},{8,7},{9,8},{10,9},{11,1... | collective-permute-start | bytes 786440 | tf_op jit(solution)/shard_map/ppermute | solution.py:140
  22.4 10.2 %all-to-all-start.1 = ((f32[16,1,288]{2,1,0:T(1,128)}), f32[16,1,288]{2,1,0:T(1,128)S(1)}, u32[]{:S(2)}, u32[]{:S(2)}) async-start(f32[16,1,288]{2,1,0:T(1,128)} %reshape.151), calls=%async_computation.1 | async-start | bytes 49152 | tf_op jit(solution)/shard_map/all_to_all | solution.py:180
  41.5 10.4 %copy-start.3 = (f32[1,64,16,256]{3,2,1,0:T(8,128)S(1)}, f32[1,64,16,256]{3,2,1,0:T(8,128)}, u32[]{:S(2)}) copy-start(f32[1,64,16,256]{3,2,1,0:T(8,128)} %param.15) | copy-start | bytes 3145732
  51.7 1.2 copy-start.2
  59.5 7.5 %collective-permute-start.2 = (f32[64,4,256]{2,1,0:T(4,128)S(1)}, f32[64,4,256]{2,1,0:T(4,128)S(1)}, u32[]{:S(2)}, u32[]{:S(2)}) collective-permute-start(f32[64,4,256]{2,1,0:T(4,128)S(1)} %get-tuple-element.25), channel_id=1, source_target_pairs={{0,1},{1,2},{2,3},{3,4},{4,5},{5,6},{6,7},{7,8},{8,9},{9,10},{10,1... | collective-permute-start | bytes 786440 | tf_op jit(solution)/shard_map/ppermute | solution.py:140
  63.7 9.8 %collective-permute-start.3 = (f32[64,4,256]{2,1,0:T(4,128)S(1)}, f32[64,4,256]{2,1,0:T(4,128)S(1)}, u32[]{:S(2)}, u32[]{:S(2)}) collective-permute-start(f32[64,4,256]{2,1,0:T(4,128)S(1)} %get-tuple-element.26), channel_id=1, source_target_pairs={{1,0},{2,1},{3,2},{4,3},{5,4},{6,5},{7,6},{8,7},{9,8},{10,9},{11,1... | collective-permute-start | bytes 786440 | tf_op jit(solution)/shard_map/ppermute | solution.py:140
  80.0 5.2 %collective-permute-start.4 = (f32[64,4,256]{2,1,0:T(4,128)S(1)}, f32[64,4,256]{2,1,0:T(4,128)S(1)}, u32[]{:S(2)}, u32[]{:S(2)}) collective-permute-start(f32[64,4,256]{2,1,0:T(4,128)S(1)} %get-tuple-element.29), channel_id=1, source_target_pairs={{0,1},{1,2},{2,3},{3,4},{4,5},{5,6},{6,7},{7,8},{8,9},{9,10},{10,1... | collective-permute-start | bytes 786440 | tf_op jit(solution)/shard_map/ppermute | solution.py:140
  81.9 9.8 %collective-permute-start.5 = (f32[64,4,256]{2,1,0:T(4,128)S(1)}, f32[64,4,256]{2,1,0:T(4,128)S(1)}, u32[]{:S(2)}, u32[]{:S(2)}) collective-permute-start(f32[64,4,256]{2,1,0:T(4,128)S(1)} %get-tuple-element.30), channel_id=1, source_target_pairs={{1,0},{2,1},{3,2},{4,3},{5,4},{6,5},{7,6},{8,7},{9,8},{10,9},{11,1... | collective-permute-start | bytes 786440 | tf_op jit(solution)/shard_map/ppermute | solution.py:140
  98.2 5.2 %collective-permute-start.6 = (f32[64,4,256]{2,1,0:T(4,128)S(1)}, f32[64,4,256]{2,1,0:T(4,128)S(1)}, u32[]{:S(2)}, u32[]{:S(2)}) collective-permute-start(f32[64,4,256]{2,1,0:T(4,128)S(1)} %get-tuple-element.33), channel_id=1, source_target_pairs={{0,1},{1,2},{2,3},{3,4},{4,5},{5,6},{6,7},{7,8},{8,9},{9,10},{10,1... | collective-permute-start | bytes 786440 | tf_op jit(solution)/shard_map/ppermute | solution.py:140
  100.1 9.8 %collective-permute-start.7 = (f32[64,4,256]{2,1,0:T(4,128)S(1)}, f32[64,4,256]{2,1,0:T(4,128)S(1)}, u32[]{:S(2)}, u32[]{:S(2)}) collective-permute-start(f32[64,4,256]{2,1,0:T(4,128)S(1)} %get-tuple-element.34), channel_id=1, source_target_pairs={{1,0},{2,1},{3,2},{4,3},{5,4},{6,5},{7,6},{8,7},{9,8},{10,9},{11,1... | collective-permute-start | bytes 786440 | tf_op jit(solution)/shard_map/ppermute | solution.py:140
  116.5 5.2 %collective-permute-start.8 = (f32[64,4,256]{2,1,0:T(4,128)S(1)}, f32[64,4,256]{2,1,0:T(4,128)S(1)}, u32[]{:S(2)}, u32[]{:S(2)}) collective-permute-start(f32[64,4,256]{2,1,0:T(4,128)S(1)} %get-tuple-element.37), channel_id=1, source_target_pairs={{0,1},{1,2},{2,3},{3,4},{4,5},{5,6},{6,7},{7,8},{8,9},{9,10},{10,1... | collective-permute-start | bytes 786440 | tf_op jit(solution)/shard_map/ppermute | solution.py:140
  118.4 9.8 %collective-permute-start.9 = (f32[64,4,256]{2,1,0:T(4,128)S(1)}, f32[64,4,256]{2,1,0:T(4,128)S(1)}, u32[]{:S(2)}, u32[]{:S(2)}) collective-permute-start(f32[64,4,256]{2,1,0:T(4,128)S(1)} %get-tuple-element.38), channel_id=1, source_target_pairs={{1,0},{2,1},{3,2},{4,3},{5,4},{6,5},{7,6},{8,7},{9,8},{10,9},{11,1... | collective-permute-start | bytes 786440 | tf_op jit(solution)/shard_map/ppermute | solution.py:140
  128.2 18.3 %copy-start.1 = (f32[1,64,16,256]{3,2,1,0:T(8,128)S(1)}, f32[1,64,16,256]{3,2,1,0:T(8,128)}, u32[]{:S(2)}) copy-start(f32[1,64,16,256]{3,2,1,0:T(8,128)} %param.14) | copy-start | bytes 3145732
  134.8 5.2 %collective-permute-start.10 = (f32[64,4,256]{2,1,0:T(4,128)S(1)}, f32[64,4,256]{2,1,0:T(4,128)S(1)}, u32[]{:S(2)}, u32[]{:S(2)}) collective-permute-start(f32[64,4,256]{2,1,0:T(4,128)S(1)} %get-tuple-element.41), channel_id=1, source_target_pairs={{0,1},{1,2},{2,3},{3,4},{4,5},{5,6},{6,7},{7,8},{8,9},{9,10},{10,1... | collective-permute-start | bytes 786440 | tf_op jit(solution)/shard_map/ppermute | solution.py:140
  136.7 9.8 %collective-permute-start.11 = (f32[64,4,256]{2,1,0:T(4,128)S(1)}, f32[64,4,256]{2,1,0:T(4,128)S(1)}, u32[]{:S(2)}, u32[]{:S(2)}) collective-permute-start(f32[64,4,256]{2,1,0:T(4,128)S(1)} %get-tuple-element.42), channel_id=1, source_target_pairs={{1,0},{2,1},{3,2},{4,3},{5,4},{6,5},{7,6},{8,7},{9,8},{10,9},{11,1... | collective-permute-start | bytes 786440 | tf_op jit(solution)/shard_map/ppermute | solution.py:140

commit v3 on v2

--- a/solution.py
+++ b/solution.py
@@ -1,3 +1,5 @@
+import functools
+
 import jax
 import jax.numpy as jnp
 from jax import lax
@@ -54,7 +56,7 @@
 ROWS = 2
 
 
-def step_kernel(cur_ref, prev_ref, lo_ref, hi_ref, vel_ref, fwd_ref, src_ref, img_ref,
+def step_kernel(moment, cur_ref, prev_ref, lo_ref, hi_ref, vel_ref, fwd_ref, src_ref, img_ref,
                 next_ref, img_out_ref, first_ref, last_ref, pad_ref):
     cells_y, cells_x, cells_z = cur_ref.shape
     width = lo_ref.shape[1]
@@ -96,7 +98,7 @@
             summed = summed + STENCIL[reach] * beside_all
         rows = pl.ds(y0, ROWS)
         advanced = 2.0 * center - prev_ref[rows] + vel_ref[rows] * summed
-        source = jnp.broadcast_to(src_ref[rows], advanced.shape)
+        source = jnp.broadcast_to(src_ref[rows, :, pl.ds(moment, 1)], advanced.shape)
         advanced = jnp.where(depth == 0, advanced + source, advanced)
         next_ref[rows] = advanced
         img_out_ref[rows] = img_ref[rows] + fwd_ref[rows].astype(jnp.float32) * advanced
@@ -113,10 +115,10 @@
     field = pl.BlockSpec((cells_y, cells_x, cells_z), lambda i: (0, 0, 0))
     rim = pl.BlockSpec((cells_y, width, cells_z), lambda i: (0, 0, 0))
     fwd_spec = pl.BlockSpec((None, cells_y, cells_x, cells_z), lambda i: (moment, 0, 0, 0))
-    src_spec = pl.BlockSpec((None, cells_y, cells_x, 1), lambda i: (moment, 0, 0, 0))
+    src_spec = pl.BlockSpec(source.shape, lambda i: (0, 0, 0))
     f32 = jnp.float32
     return pl.pallas_call(
-        step_kernel,
+        functools.partial(step_kernel, moment),
         grid=(1,),
         out_shape=(
             jax.ShapeDtypeStruct(current.shape, f32),
@@ -167,30 +169,35 @@
     )
     order_rank = jnp.sum((jnp.cumsum(one_hot, axis=0) - 1) * one_hot, axis=1)
     slot_index = tile_ids * slot_count + order_rank
-    cell_buffer = (
-        jnp.full((tiles_count * slot_count,), surface, jnp.int32).at[slot_index].set(cell_ids)
-    )
-    cell_buffer = cell_buffer.reshape(tiles_count, slot_count)
     filtered = jnp.dot(trace_rows, time_filter.T, preferred_element_type=jnp.float32)
-    value_buffer = (
-        jnp.zeros((tiles_count * slot_count, step_count), jnp.float32).at[slot_index].set(filtered)
-    )
-    value_buffer = value_buffer.reshape(tiles_count, slot_count, step_count)
-    values, arrived_cells = (
-        lax.all_to_all(value_buffer, "space", split_axis=0, concat_axis=0, tiled=True),
-        lax.all_to_all(cell_buffer, "space", split_axis=0, concat_axis=0, tiled=True),
-    )
-    source = jax.ops.segment_sum(
-        values.reshape(-1, step_count), arrived_cells.reshape(-1), num_segments=surface + 1
-    )[:surface]
-    source = source.T.reshape(step_count, cells_y, cells_x)
+    payload = jnp.concatenate(
+        [filtered, (cell_ids + 1).astype(jnp.float32)[:, None]], axis=1
+    )
+    slots = tiles_count * slot_count
+    placing = (
+        slot_index[None, :] == jnp.arange(slots, dtype=jnp.int32)[:, None]
+    ).astype(jnp.float32)
+    buffer = jnp.dot(placing, payload, precision=lax.Precision.HIGHEST)
+    buffer = buffer.reshape(tiles_count, slot_count, step_count + 1)
+    arrived = lax.all_to_all(buffer, "space", split_axis=0, concat_axis=0, tiled=True)
+    arrived = arrived.reshape(slots, step_count + 1)
+    cell_of = arrived[:, step_count].astype(jnp.int32)
+    gathering = (
+        cell_of[:, None] == jnp.arange(1, surface + 1, dtype=jnp.int32)[None, :]
+    ).astype(jnp.float32)
+    source = lax.dot_general(
+        gathering,
+        arrived[:, :step_count],
+        (((0,), (0,)), ((), ())),
+        precision=lax.Precision.HIGHEST,
+    )
+    source = source.reshape(cells_y, cells_x, step_count)
     shift_rows = offsets[0]
     speed_sq = velocity[0]
     previous = adjoint_prev[0]
     current = adjoint_now[0]
     forward = forward_accel[0]
     imaging = jnp.zeros_like(current)
-    source = source.reshape(source.shape + (1,))
     width = 4
     first = current[:, :width]
     last = current[:, cells_x - width :]

time: 180 us -> 151 us (0.84)
  local copies, waits for them, and re-layouts: 21 us -> 3.86 us
  starting transfers between devices: 40.5 us -> 32.7 us
  other arithmetic: 11.8 us -> 5.32 us
  matrix products: 1.06 us -> 3.39 us
    another operation x3 -> x1, local copies, waits for them, and re-layouts: 10.3 us -> 0.01 us  [the longest x1 10.3 us: local(): source = source.reshape(source.shape + (1,))]
    scatter-add x1 -> x0, other arithmetic: 6.6 us -> none  [local(): jax.ops.segment_sum(values.reshape(-1, step_count), arrived_cells.reshape...]
    all_to_all x2 -> x1, starting transfers between devices: 11.8 us -> 5.82 us  [local(): lax.all_to_all(buffer, 'space', split_axis=0, concat_axis=0, tiled=True)]
    ppermute x12, waiting for transfers between devices: 36.7 us -> 40.7 us  [halo(): return (lax.ppermute(last, axis, up), lax.ppermute(first, axis, down))]
    all_to_all x2 -> x1, waiting for transfers between devices: 2.91 us -> 0.01 us  [local(): lax.all_to_all(buffer, 'space', split_axis=0, concat_axis=0, tiled=True)]
    scatter x2 -> x0, local copies, waits for them, and re-layouts: 2.81 us -> none  [the longest x1 1.56 us: local(): jnp.full((tiles_count * slot_count,), surface, jnp.int32).at[slot_index]]
    dot_general x0 -> x2, matrix products: none -> 2.38 us  [the longest x1 1.88 us: local(): lax.dot_general(gathering, arrived[:, :step_count], (((0,), (0,)), ((), (...]
    slice x1, local copies, waits for them, and re-layouts: 2.08 us -> 0.09 us  [local(): first = current[:, :width]]
  transfers between devices with their start and end apart: 14 -> 13, of which waited for: 11 -> 11; matrix products, arithmetic and copies ran while one was open for 14% -> 2% of each run, Pallas kernels for 0% -> 0%
where the time goes in v3:
time: 151 us; the launch traced here: 150 us
  waiting for transfers between devices  40.7 us (27%)
  Pallas kernels  38.9 us (26%)
  starting transfers between devices  32.7 us (22%)
  blocking collectives  23.3 us (15%)
  other arithmetic  5.32 us (4%)
  local copies, waits for them, and re-layouts  3.86 us (3%)
  matrix products  3.39 us (2%)
  between operations  1.58 us (1%)
    ppermute x12, waiting for transfers between devices, halo(): return (lax.ppermute(last, axis, up), lax.ppermute(first, axis, down))  40.7 us
    pallas_call x6, Pallas kernels, step_call(): pl.pallas_call(functools.partial(step_kernel, moment), grid=(1,), out_sha...  38.9 us
    ppermute x12, starting transfers between devices, halo(): return (lax.ppermute(last, axis, up), lax.ppermute(first, axis, down))  26.9 us
    all_to_all x1, blocking collectives, local(): lax.all_to_all(placed, 'shot', split_axis=0, concat_axis=0, tiled=True)  23.3 us
    all_to_all x1, starting transfers between devices, local(): lax.all_to_all(buffer, 'space', split_axis=0, concat_axis=0, tiled=True)  5.82 us
  transfers between devices with their start and end apart: 13, of which 11 were waited for; matrix products, arithmetic and copies ran while one was open for 2% of the time, Pallas kernels for 0%

profile of v3, /device:TPU:97, one launch (start us, length us, event | category | flops | bytes accessed | tf_op | source)
XLA Modules:
  0.0 149.9 jit_solution(10522287149705093902)
XLA Ops:
  0.6 0.0 copy-start
  0.6 0.0 copy-start.2
  0.7 0.8 fusion.10
  1.5 0.6 reduce-window.6
  2.0 0.2 slice_reduce_fusion
  2.3 0.8 fusion.9
  3.0 0.7 multiply_add_fusion
  3.7 0.7 convert_bitcast_fusion
  4.4 0.0 copy-done
  4.4 1.0 fusion.3
  5.4 0.5 fusion.5
  5.9 0.1 reshape.98
  6.1 0.7 reshape.111
  6.8 5.8 %all-to-all-start = ((f32[16,1,336]{2,1,0:T(1,128)}), f32[16,1,336]{2,1,0:T(1,128)S(1)}, u32[]{:S(2)}, u32[]{:S(2)}) async-start(f32[16,1,336]{2,1,0:T(1,128)} %reshape.111), calls=%async_computation | async-start | bytes 49152 | tf_op jit(solution)/shard_map/all_to_all | solution.py:182
  12.6 0.0 copy-done.2
  12.6 0.1 fusion.23
  12.7 3.4 %collective-permute-start = (f32[64,4,256]{2,1,0:T(4,128)S(1)}, f32[64,4,256]{2,1,0:T(4,128)S(1)}, u32[]{:S(2)}, u32[]{:S(2)}) collective-permute-start(f32[64,4,256]{2,1,0:T(4,128)S(1)} %get-tuple-element.47), channel_id=1, source_target_pairs={{0,1},{1,2},{2,3},{3,4},{4,5},{5,6},{6,7},{7,8},{8,9},{9,10},{10,1... | collective-permute-start | bytes 786440 | tf_op jit(solution)/shard_map/ppermute | solution.py:142
  16.1 1.9 %collective-permute-start.1 = (f32[64,4,256]{2,1,0:T(4,128)S(1)}, f32[64,4,256]{2,1,0:T(4,128)S(1)}, u32[]{:S(2)}, u32[]{:S(2)}) collective-permute-start(f32[64,4,256]{2,1,0:T(4,128)S(1)} %get-tuple-element.46), channel_id=1, source_target_pairs={{1,0},{2,1},{3,2},{4,3},{5,4},{6,5},{7,6},{8,7},{9,8},{10,9},{11,1... | collective-permute-start | bytes 786440 | tf_op jit(solution)/shard_map/ppermute | solution.py:142
  18.0 0.0 all-to-all-done
  18.0 0.5 broadcast.130
  18.6 0.7 reduce.4
  19.3 0.1 reshape.112
  19.4 0.1 reshape.99
  19.5 1.9 %fusion = f32[1024,6]{1,0:T(8,128)S(1)} fusion(s32[1024]{0:T(1024)S(1)} %iota_add_fusion, s32[768]{0:T(1024)S(1)} %fusion.20, f32[768,7]{0,1:T(8,128)S(1)} %reshape.99), kind=kOutput, calls=%fused_computation.2 | convolution fusion | flops 58195968 | bytes 53248 | tf_op jit(solution)/shard_map/dot_general | solution.py:188
  21.4 0.0 collective-permute-done.lo_ref
  21.4 4.5 %collective-permute-done.1.hi_ref = f32[64,4,256]{2,1,0:T(4,128)S(1)} collective-permute-done((f32[64,4,256]{2,1,0:T(4,128)S(1)}, f32[64,4,256]{2,1,0:T(4,128)S(1)}, u32[]{:S(2)}, u32[]{:S(2)}) %collective-permute-start.1) | collective-permute-done | bytes 262176 | tf_op jit(solution)/shard_map/ppermute | solution.py:142
  25.9 0.1 broadcast_in_dim.37.img_ref
  26.0 0.0 copy-start.3
  26.0 1.2 copy-done.3
  27.3 6.3 %shard_map.104 = (f32[64,16,256]{2,1,0:T(8,128)S(1)}, f32[64,16,256]{2,1,0:T(8,128)S(1)}, f32[64,4,256]{2,1,0:T(4,128)S(1)}, f32[64,4,256]{2,1,0:T(4,128)S(1)}) custom-call(f32[64,16,256]{2,1,0:T(8,128)S(1)} %bitcast.56, f32[64,16,256]{2,1,0:T(8,128)S(1)} %bitcast.58, ...), custom_call_target="tpu_custom_call", output_to_operand_aliasing={{1}: (7, {})} | custom-call | tf_op jit(solution)/shard_map/pallas_call | solution.py:120
  33.6 1.9 %collective-permute-start.2 = (f32[64,4,256]{2,1,0:T(4,128)S(1)}, f32[64,4,256]{2,1,0:T(4,128)S(1)}, u32[]{:S(2)}, u32[]{:S(2)}) collective-permute-start(f32[64,4,256]{2,1,0:T(4,128)S(1)} %get-tuple-element.25), channel_id=1, source_target_pairs={{0,1},{1,2},{2,3},{3,4},{4,5},{5,6},{6,7},{7,8},{8,9},{9,10},{10,1... | collective-permute-start | bytes 786440 | tf_op jit(solution)/shard_map/ppermute | solution.py:142
  35.5 2.4 %collective-permute-start.3 = (f32[64,4,256]{2,1,0:T(4,128)S(1)}, f32[64,4,256]{2,1,0:T(4,128)S(1)}, u32[]{:S(2)}, u32[]{:S(2)}) collective-permute-start(f32[64,4,256]{2,1,0:T(4,128)S(1)} %get-tuple-element.26), channel_id=1, source_target_pairs={{1,0},{2,1},{3,2},{4,3},{5,4},{6,5},{7,6},{8,7},{9,8},{10,9},{11,1... | collective-permute-start | bytes 786440 | tf_op jit(solution)/shard_map/ppermute | solution.py:142
  37.9 0.9 collective-permute-done.2.lo_ref
  38.8 6.5 %collective-permute-done.3.hi_ref = f32[64,4,256]{2,1,0:T(4,128)S(1)} collective-permute-done((f32[64,4,256]{2,1,0:T(4,128)S(1)}, f32[64,4,256]{2,1,0:T(4,128)S(1)}, u32[]{:S(2)}, u32[]{:S(2)}) %collective-permute-start.3) | collective-permute-done | bytes 262176 | tf_op jit(solution)/shard_map/ppermute | solution.py:142
  45.3 6.3 %shard_map.105 = (f32[64,16,256]{2,1,0:T(8,128)S(1)}, f32[64,16,256]{2,1,0:T(8,128)S(1)}, f32[64,4,256]{2,1,0:T(4,128)S(1)}, f32[64,4,256]{2,1,0:T(4,128)S(1)}) custom-call(f32[64,16,256]{2,1,0:T(8,128)S(1)} %get-tuple-element.24.cur_ref.prev_ref, f32[64,16,256]{2,1,0:T(8,128)S(1)} %bitcast.57, ...), custom_call_target="tpu_custom_call", output_to_operand_aliasing={{1}: (7, {})} | custom-call | tf_op jit(solution)/shard_map/pallas_call | solution.py:120
  51.7 1.9 %collective-permute-start.4 = (f32[64,4,256]{2,1,0:T(4,128)S(1)}, f32[64,4,256]{2,1,0:T(4,128)S(1)}, u32[]{:S(2)}, u32[]{:S(2)}) collective-permute-start(f32[64,4,256]{2,1,0:T(4,128)S(1)} %get-tuple-element.29), channel_id=1, source_target_pairs={{0,1},{1,2},{2,3},{3,4},{4,5},{5,6},{6,7},{7,8},{8,9},{9,10},{10,1... | collective-permute-start | bytes 786440 | tf_op jit(solution)/shard_map/ppermute | solution.py:142
  53.6 2.4 %collective-permute-start.5 = (f32[64,4,256]{2,1,0:T(4,128)S(1)}, f32[64,4,256]{2,1,0:T(4,128)S(1)}, u32[]{:S(2)}, u32[]{:S(2)}) collective-permute-start(f32[64,4,256]{2,1,0:T(4,128)S(1)} %get-tuple-element.30), channel_id=1, source_target_pairs={{1,0},{2,1},{3,2},{4,3},{5,4},{6,5},{7,6},{8,7},{9,8},{10,9},{11,1... | collective-permute-start | bytes 786440 | tf_op jit(solution)/shard_map/ppermute | solution.py:142
  56.0 0.9 collective-permute-done.4.lo_ref
  56.9 6.5 %collective-permute-done.5.hi_ref = f32[64,4,256]{2,1,0:T(4,128)S(1)} collective-permute-done((f32[64,4,256]{2,1,0:T(4,128)S(1)}, f32[64,4,256]{2,1,0:T(4,128)S(1)}, u32[]{:S(2)}, u32[]{:S(2)}) %collective-permute-start.5) | collective-permute-done | bytes 262176 | tf_op jit(solution)/shard_map/ppermute | solution.py:142
  63.4 6.3 %shard_map.106 = (f32[64,16,256]{2,1,0:T(8,128)S(1)}, f32[64,16,256]{2,1,0:T(8,128)S(1)}, f32[64,4,256]{2,1,0:T(4,128)S(1)}, f32[64,4,256]{2,1,0:T(4,128)S(1)}) custom-call(f32[64,16,256]{2,1,0:T(8,128)S(1)} %get-tuple-element.28.cur_ref.prev_ref, f32[64,16,256]{2,1,0:T(8,128)S(1)} %get-tuple-element.24.cur_ref.prev_ref, ...), custom_call_target="tpu_custom_call", output_to_operand_aliasing={{1}: (7, {})} | custom-call | tf_op jit(solution)/shard_map/pallas_call | solution.py:120
  69.8 1.9 %collective-permute-start.6 = (f32[64,4,256]{2,1,0:T(4,128)S(1)}, f32[64,4,256]{2,1,0:T(4,128)S(1)}, u32[]{:S(2)}, u32[]{:S(2)}) collective-permute-start(f32[64,4,256]{2,1,0:T(4,128)S(1)} %get-tuple-element.33), channel_id=1, source_target_pairs={{0,1},{1,2},{2,3},{3,4},{4,5},{5,6},{6,7},{7,8},{8,9},{9,10},{10,1... | collective-permute-start | bytes 786440 | tf_op jit(solution)/shard_map/ppermute | solution.py:142
  71.7 2.4 %collective-permute-start.7 = (f32[64,4,256]{2,1,0:T(4,128)S(1)}, f32[64,4,256]{2,1,0:T(4,128)S(1)}, u32[]{:S(2)}, u32[]{:S(2)}) collective-permute-start(f32[64,4,256]{2,1,0:T(4,128)S(1)} %get-tuple-element.34), channel_id=1, source_target_pairs={{1,0},{2,1},{3,2},{4,3},{5,4},{6,5},{7,6},{8,7},{9,8},{10,9},{11,1... | collective-permute-start | bytes 786440 | tf_op jit(solution)/shard_map/ppermute | solution.py:142
  74.1 0.9 collective-permute-done.6.lo_ref
  75.0 6.5 %collective-permute-done.7.hi_ref = f32[64,4,256]{2,1,0:T(4,128)S(1)} collective-permute-done((f32[64,4,256]{2,1,0:T(4,128)S(1)}, f32[64,4,256]{2,1,0:T(4,128)S(1)}, u32[]{:S(2)}, u32[]{:S(2)}) %collective-permute-start.7) | collective-permute-done | bytes 262176 | tf_op jit(solution)/shard_map/ppermute | solution.py:142
  81.5 6.3 %shard_map.107 = (f32[64,16,256]{2,1,0:T(8,128)S(1)}, f32[64,16,256]{2,1,0:T(8,128)S(1)}, f32[64,4,256]{2,1,0:T(4,128)S(1)}, f32[64,4,256]{2,1,0:T(4,128)S(1)}) custom-call(f32[64,16,256]{2,1,0:T(8,128)S(1)} %get-tuple-element.32.cur_ref.prev_ref, f32[64,16,256]{2,1,0:T(8,128)S(1)} %get-tuple-element.28.cur_ref.prev_ref, ...), custom_call_target="tpu_custom_call", output_to_operand_aliasing={{1}: (7, {})} | custom-call | tf_op jit(solution)/shard_map/pallas_call | solution.py:120
  87.8 1.9 %collective-permute-start.8 = (f32[64,4,256]{2,1,0:T(4,128)S(1)}, f32[64,4,256]{2,1,0:T(4,128)S(1)}, u32[]{:S(2)}, u32[]{:S(2)}) collective-permute-start(f32[64,4,256]{2,1,0:T(4,128)S(1)} %get-tuple-element.37), channel_id=1, source_target_pairs={{0,1},{1,2},{2,3},{3,4},{4,5},{5,6},{6,7},{7,8},{8,9},{9,10},{10,1... | collective-permute-start | bytes 786440 | tf_op jit(solution)/shard_map/ppermute | solution.py:142
  89.8 2.4 %collective-permute-start.9 = (f32[64,4,256]{2,1,0:T(4,128)S(1)}, f32[64,4,256]{2,1,0:T(4,128)S(1)}, u32[]{:S(2)}, u32[]{:S(2)}) collective-permute-start(f32[64,4,256]{2,1,0:T(4,128)S(1)} %get-tuple-element.38), channel_id=1, source_target_pairs={{1,0},{2,1},{3,2},{4,3},{5,4},{6,5},{7,6},{8,7},{9,8},{10,9},{11,1... | collective-permute-start | bytes 786440 | tf_op jit(solution)/shard_map/ppermute | solution.py:142
  92.8 0.2 collective-permute-done.8.lo_ref
  93.1 6.5 %collective-permute-done.9.hi_ref = f32[64,4,256]{2,1,0:T(4,128)S(1)} collective-permute-done((f32[64,4,256]{2,1,0:T(4,128)S(1)}, f32[64,4,256]{2,1,0:T(4,128)S(1)}, u32[]{:S(2)}, u32[]{:S(2)}) %collective-permute-start.9) | collective-permute-done | bytes 262176 | tf_op jit(solution)/shard_map/ppermute | solution.py:142
  99.6 0.0 copy-start.1
  99.6 6.4 %shard_map.108 = (f32[64,16,256]{2,1,0:T(8,128)S(1)}, f32[64,16,256]{2,1,0:T(8,128)S(1)}, f32[64,4,256]{2,1,0:T(4,128)S(1)}, f32[64,4,256]{2,1,0:T(4,128)S(1)}) custom-call(f32[64,16,256]{2,1,0:T(8,128)S(1)} %get-tuple-element.36.cur_ref.prev_ref, f32[64,16,256]{2,1,0:T(8,128)S(1)} %get-tuple-element.32.cur_ref.prev_ref, ...), custom_call_target="tpu_custom_call", output_to_operand_aliasing={{1}: (7, {})} | custom-call | tf_op jit(solution)/shard_map/pallas_call | solution.py:120
  106.0 1.9 %collective-permute-start.10 = (f32[64,4,256]{2,1,0:T(4,128)S(1)}, f32[64,4,256]{2,1,0:T(4,128)S(1)}, u32[]{:S(2)}, u32[]{:S(2)}) collective-permute-start(f32[64,4,256]{2,1,0:T(4,128)S(1)} %get-tuple-element.41), channel_id=1, source_target_pairs={{0,1},{1,2},{2,3},{3,4},{4,5},{5,6},{6,7},{7,8},{8,9},{9,10},{10,1... | collective-permute-start | bytes 786440 | tf_op jit(solution)/shard_map/ppermute | solution.py:142
  107.9 2.4 %collective-permute-start.11 = (f32[64,4,256]{2,1,0:T(4,128)S(1)}, f32[64,4,256]{2,1,0:T(4,128)S(1)}, u32[]{:S(2)}, u32[]{:S(2)}) collective-permute-start(f32[64,4,256]{2,1,0:T(4,128)S(1)} %get-tuple-element.42), channel_id=1, source_target_pairs={{1,0},{2,1},{3,2},{4,3},{5,4},{6,5},{7,6},{8,7},{9,8},{10,9},{11,1... | collective-permute-start | bytes 786440 | tf_op jit(solution)/shard_map/ppermute | solution.py:142
  110.4 0.8 collective-permute-done.10.lo_ref
  111.2 6.5 %collective-permute-done.11.hi_ref = f32[64,4,256]{2,1,0:T(4,128)S(1)} collective-permute-done((f32[64,4,256]{2,1,0:T(4,128)S(1)}, f32[64,4,256]{2,1,0:T(4,128)S(1)}, u32[]{:S(2)}, u32[]{:S(2)}) %collective-permute-start.11) | collective-permute-done | bytes 262176 | tf_op jit(solution)/shard_map/ppermute | solution.py:142
  117.7 0.0 copy-done.1
  117.7 7.1 %shard_map.109 = (f32[64,16,256]{2,1,0:T(8,128)}, f32[64,16,256]{2,1,0:T(8,128)S(1)}, f32[64,4,256]{2,1,0:T(4,128)}, f32[64,4,256]{2,1,0:T(4,128)}) custom-call(f32[64,16,256]{2,1,0:T(8,128)S(1)} %get-tuple-element.40.cur_ref, f32[64,16,256]{2,1,0:T(8,128)S(1)} %get-tuple-element.36.cur_ref.prev_ref, ...), custom_call_target="tpu_custom_call", output_to_operand_aliasing={{1}: (7, {})} | custom-call | tf_op jit(solution)/shard_map/pallas_call | solution.py:120
  124.9 0.7 gather_fusion
  125.6 0.2 select_select_fusion
  125.8 23.3 %all_to_all.10 = f32[8,10,16,256]{3,2,1,0:T(8,128)S(1)} all-to-all(f32[8,10,16,256]{3,2,1,0:T(8,128)S(1)} %select_select_fusion), channel_id=1, replica_groups=mesh['shot'=8,'space'=16] {'shot'}, dimensions={0} | all-to-all | bytes 2621440 | tf_op jit(solution)/shard_map/all_to_all | solution.py:216
  149.1 0.8 reduce_sum.19
  (9 shorter events, 0.1 us)
Async XLA Ops:
  0.6 3.8 %copy-start = (bf16[1,256,1536]{2,1,0:T(8,128)(2,1)S(1)}, bf16[1,256,1536]{2,1,0:T(8,128)(2,1)}, u32[]{:S(2)}) copy-start(bf16[1,256,1536]{2,1,0:T(8,128)(2,1)} %param.9) | copy-start | bytes 2359300
  0.6 12.0 %copy-start.2 = (f32[1,64,16,256]{3,2,1,0:T(8,128)S(1)}, f32[1,64,16,256]{3,2,1,0:T(8,128)}, u32[]{:S(2)}) copy-start(f32[1,64,16,256]{3,2,1,0:T(8,128)} %param.16) | copy-start | bytes 3145732
  6.8 11.2 %all-to-all-start = ((f32[16,1,336]{2,1,0:T(1,128)}), f32[16,1,336]{2,1,0:T(1,128)S(1)}, u32[]{:S(2)}, u32[]{:S(2)}) async-start(f32[16,1,336]{2,1,0:T(1,128)} %reshape.111), calls=%async_computation | async-start | bytes 49152 | tf_op jit(solution)/shard_map/all_to_all | solution.py:182
  12.7 8.7 %collective-permute-start = (f32[64,4,256]{2,1,0:T(4,128)S(1)}, f32[64,4,256]{2,1,0:T(4,128)S(1)}, u32[]{:S(2)}, u32[]{:S(2)}) collective-permute-start(f32[64,4,256]{2,1,0:T(4,128)S(1)} %get-tuple-element.47), channel_id=1, source_target_pairs={{0,1},{1,2},{2,3},{3,4},{4,5},{5,6},{6,7},{7,8},{8,9},{9,10},{10,1... | collective-permute-start | bytes 786440 | tf_op jit(solution)/shard_map/ppermute | solution.py:142
  16.1 9.8 %collective-permute-start.1 = (f32[64,4,256]{2,1,0:T(4,128)S(1)}, f32[64,4,256]{2,1,0:T(4,128)S(1)}, u32[]{:S(2)}, u32[]{:S(2)}) collective-permute-start(f32[64,4,256]{2,1,0:T(4,128)S(1)} %get-tuple-element.46), channel_id=1, source_target_pairs={{1,0},{2,1},{3,2},{4,3},{5,4},{6,5},{7,6},{8,7},{9,8},{10,9},{11,1... | collective-permute-start | bytes 786440 | tf_op jit(solution)/shard_map/ppermute | solution.py:142
  26.0 1.2 copy-start.3
  33.6 5.2 %collective-permute-start.2 = (f32[64,4,256]{2,1,0:T(4,128)S(1)}, f32[64,4,256]{2,1,0:T(4,128)S(1)}, u32[]{:S(2)}, u32[]{:S(2)}) collective-permute-start(f32[64,4,256]{2,1,0:T(4,128)S(1)} %get-tuple-element.25), channel_id=1, source_target_pairs={{0,1},{1,2},{2,3},{3,4},{4,5},{5,6},{6,7},{7,8},{8,9},{9,10},{10,1... | collective-permute-start | bytes 786440 | tf_op jit(solution)/shard_map/ppermute | solution.py:142
  35.5 9.8 %collective-permute-start.3 = (f32[64,4,256]{2,1,0:T(4,128)S(1)}, f32[64,4,256]{2,1,0:T(4,128)S(1)}, u32[]{:S(2)}, u32[]{:S(2)}) collective-permute-start(f32[64,4,256]{2,1,0:T(4,128)S(1)} %get-tuple-element.26), channel_id=1, source_target_pairs={{1,0},{2,1},{3,2},{4,3},{5,4},{6,5},{7,6},{8,7},{9,8},{10,9},{11,1... | collective-permute-start | bytes 786440 | tf_op jit(solution)/shard_map/ppermute | solution.py:142
  51.7 5.2 %collective-permute-start.4 = (f32[64,4,256]{2,1,0:T(4,128)S(1)}, f32[64,4,256]{2,1,0:T(4,128)S(1)}, u32[]{:S(2)}, u32[]{:S(2)}) collective-permute-start(f32[64,4,256]{2,1,0:T(4,128)S(1)} %get-tuple-element.29), channel_id=1, source_target_pairs={{0,1},{1,2},{2,3},{3,4},{4,5},{5,6},{6,7},{7,8},{8,9},{9,10},{10,1... | collective-permute-start | bytes 786440 | tf_op jit(solution)/shard_map/ppermute | solution.py:142
  53.6 9.8 %collective-permute-start.5 = (f32[64,4,256]{2,1,0:T(4,128)S(1)}, f32[64,4,256]{2,1,0:T(4,128)S(1)}, u32[]{:S(2)}, u32[]{:S(2)}) collective-permute-start(f32[64,4,256]{2,1,0:T(4,128)S(1)} %get-tuple-element.30), channel_id=1, source_target_pairs={{1,0},{2,1},{3,2},{4,3},{5,4},{6,5},{7,6},{8,7},{9,8},{10,9},{11,1... | collective-permute-start | bytes 786440 | tf_op jit(solution)/shard_map/ppermute | solution.py:142
  69.8 5.2 %collective-permute-start.6 = (f32[64,4,256]{2,1,0:T(4,128)S(1)}, f32[64,4,256]{2,1,0:T(4,128)S(1)}, u32[]{:S(2)}, u32[]{:S(2)}) collective-permute-start(f32[64,4,256]{2,1,0:T(4,128)S(1)} %get-tuple-element.33), channel_id=1, source_target_pairs={{0,1},{1,2},{2,3},{3,4},{4,5},{5,6},{6,7},{7,8},{8,9},{9,10},{10,1... | collective-permute-start | bytes 786440 | tf_op jit(solution)/shard_map/ppermute | solution.py:142
  71.7 9.8 %collective-permute-start.7 = (f32[64,4,256]{2,1,0:T(4,128)S(1)}, f32[64,4,256]{2,1,0:T(4,128)S(1)}, u32[]{:S(2)}, u32[]{:S(2)}) collective-permute-start(f32[64,4,256]{2,1,0:T(4,128)S(1)} %get-tuple-element.34), channel_id=1, source_target_pairs={{1,0},{2,1},{3,2},{4,3},{5,4},{6,5},{7,6},{8,7},{9,8},{10,9},{11,1... | collective-permute-start | bytes 786440 | tf_op jit(solution)/shard_map/ppermute | solution.py:142
  87.8 5.2 %collective-permute-start.8 = (f32[64,4,256]{2,1,0:T(4,128)S(1)}, f32[64,4,256]{2,1,0:T(4,128)S(1)}, u32[]{:S(2)}, u32[]{:S(2)}) collective-permute-start(f32[64,4,256]{2,1,0:T(4,128)S(1)} %get-tuple-element.37), channel_id=1, source_target_pairs={{0,1},{1,2},{2,3},{3,4},{4,5},{5,6},{6,7},{7,8},{8,9},{9,10},{10,1... | collective-permute-start | bytes 786440 | tf_op jit(solution)/shard_map/ppermute | solution.py:142
  89.8 9.8 %collective-permute-start.9 = (f32[64,4,256]{2,1,0:T(4,128)S(1)}, f32[64,4,256]{2,1,0:T(4,128)S(1)}, u32[]{:S(2)}, u32[]{:S(2)}) collective-permute-start(f32[64,4,256]{2,1,0:T(4,128)S(1)} %get-tuple-element.38), channel_id=1, source_target_pairs={{1,0},{2,1},{3,2},{4,3},{5,4},{6,5},{7,6},{8,7},{9,8},{10,9},{11,1... | collective-permute-start | bytes 786440 | tf_op jit(solution)/shard_map/ppermute | solution.py:142
  99.6 18.2 %copy-start.1 = (f32[1,64,16,256]{3,2,1,0:T(8,128)S(1)}, f32[1,64,16,256]{3,2,1,0:T(8,128)}, u32[]{:S(2)}) copy-start(f32[1,64,16,256]{3,2,1,0:T(8,128)} %param.14) | copy-start | bytes 3145732
  106.0 5.2 %collective-permute-start.10 = (f32[64,4,256]{2,1,0:T(4,128)S(1)}, f32[64,4,256]{2,1,0:T(4,128)S(1)}, u32[]{:S(2)}, u32[]{:S(2)}) collective-permute-start(f32[64,4,256]{2,1,0:T(4,128)S(1)} %get-tuple-element.41), channel_id=1, source_target_pairs={{0,1},{1,2},{2,3},{3,4},{4,5},{5,6},{6,7},{7,8},{8,9},{9,10},{10,1... | collective-permute-start | bytes 786440 | tf_op jit(solution)/shard_map/ppermute | solution.py:142
  107.9 9.8 %collective-permute-start.11 = (f32[64,4,256]{2,1,0:T(4,128)S(1)}, f32[64,4,256]{2,1,0:T(4,128)S(1)}, u32[]{:S(2)}, u32[]{:S(2)}) collective-permute-start(f32[64,4,256]{2,1,0:T(4,128)S(1)} %get-tuple-element.42), channel_id=1, source_target_pairs={{1,0},{2,1},{3,2},{4,3},{5,4},{6,5},{7,6},{8,7},{9,8},{10,9},{11,1... | collective-permute-start | bytes 786440 | tf_op jit(solution)/shard_map/ppermute | solution.py:142

commit v4 on v3

--- a/solution.py
+++ b/solution.py
@@ -53,36 +53,52 @@
     return jnp.pad(field, ((4, 4), (0, 0), (4, 4)))
 
 
-ROWS = 2
+ROWS = 1
+BLOCK = 8
 
 
 def step_kernel(moment, cur_ref, prev_ref, lo_ref, hi_ref, vel_ref, fwd_ref, src_ref, img_ref,
                 next_ref, img_out_ref, first_ref, last_ref, pad_ref):
     cells_y, cells_x, cells_z = cur_ref.shape
     width = lo_ref.shape[1]
-    zeros = jnp.zeros((4, pad_ref.shape[1], cells_z), jnp.float32)
-    pad_ref[0:4] = zeros
-    pad_ref[4 + cells_y : 8 + cells_y] = zeros
-    pad_ref[4 : 4 + cells_y, 8 - width : 8] = lo_ref[...]
-    pad_ref[4 : 4 + cells_y, 8 : 8 + cells_x] = cur_ref[...]
-    pad_ref[4 : 4 + cells_y, 8 + cells_x : 8 + cells_x + width] = hi_ref[...]
+    block = pl.program_id(0)
+
+    @pl.when(block == 0)
+    def _():
+        zeros = jnp.zeros((4, pad_ref.shape[1], cells_z), jnp.float32)
+        pad_ref[0:4] = zeros
+        pad_ref[4 + cells_y : 8 + cells_y] = zeros
+        pad_ref[4 : 4 + cells_y, 8 - width : 8] = lo_ref[...]
+        pad_ref[4 : 4 + cells_y, 8 : 8 + cells_x] = cur_ref[...]
+        pad_ref[4 : 4 + cells_y, 8 + cells_x : 8 + cells_x + width] = hi_ref[...]
 
     def body(chunk, carry):
         y0 = pl.multiple_of(chunk * ROWS, ROWS)
+        base = block * BLOCK + y0 + 4
 
         def window(shift_y, shift_x):
-            return pad_ref[pl.ds(y0 + 4 + shift_y, ROWS), 8 + shift_x : 8 + shift_x + cells_x, :]
+            return pad_ref[pl.ds(base + shift_y, ROWS), 8 + shift_x : 8 + shift_x + cells_x, :]
 
         center = window(0, 0)
         depth = lax.broadcasted_iota(jnp.int32, center.shape, 2)
+        half = cells_z // 2
+        low, high = center[..., :half], center[..., half:]
+        lane = lax.broadcasted_iota(jnp.int32, low.shape, 2)
 
         def along_z(reach):
-            up = pltpu.roll(center, cells_z - reach, 2)
-            down = pltpu.roll(center, reach, 2)
-            return (
-                jnp.where(depth + reach < cells_z, up, 0.0),
-                jnp.where(depth - reach >= 0, down, 0.0),
+            low_up = pltpu.roll(low, half - reach, 2)
+            high_up = pltpu.roll(high, half - reach, 2)
+            low_down = pltpu.roll(low, reach, 2)
+            high_down = pltpu.roll(high, reach, 2)
+            head = lane < half - reach
+            tail = lane >= reach
+            up = jnp.concatenate(
+                [jnp.where(head, low_up, high_up), jnp.where(head, high_up, 0.0)], axis=2
             )
+            down = jnp.concatenate(
+                [jnp.where(tail, low_down, 0.0), jnp.where(tail, high_down, low_down)], axis=2
+            )
+            return up, down
 
         summed = 3.0 * STENCIL[0] * center
         for reach in range(1, 5):
@@ -98,7 +114,8 @@
             summed = summed + STENCIL[reach] * beside_all
         rows = pl.ds(y0, ROWS)
         advanced = 2.0 * center - prev_ref[rows] + vel_ref[rows] * summed
-        source = jnp.broadcast_to(src_ref[rows, :, pl.ds(moment, 1)], advanced.shape)
+        source_rows = pl.ds(block * BLOCK + y0, ROWS)
+        source = jnp.broadcast_to(src_ref[source_rows, :, pl.ds(moment, 1)], advanced.shape)
         advanced = jnp.where(depth == 0, advanced + source, advanced)
         next_ref[rows] = advanced
         img_out_ref[rows] = img_ref[rows] + fwd_ref[rows].astype(jnp.float32) * advanced
@@ -106,40 +123,49 @@
         last_ref[rows] = advanced[:, cells_x - width :]
         return carry
 
-    lax.fori_loop(0, cells_y // ROWS, body, 0)
+    lax.fori_loop(0, BLOCK // ROWS, body, 0, unroll=4)
 
 
 def step_call(moment, current, previous, lo, hi, speed_sq, forward, source, imaging):
     cells_y, cells_x, cells_z = current.shape
     width = lo.shape[1]
-    field = pl.BlockSpec((cells_y, cells_x, cells_z), lambda i: (0, 0, 0))
-    rim = pl.BlockSpec((cells_y, width, cells_z), lambda i: (0, 0, 0))
-    fwd_spec = pl.BlockSpec((None, cells_y, cells_x, cells_z), lambda i: (moment, 0, 0, 0))
+    whole = pl.BlockSpec((cells_y, cells_x, cells_z), lambda i: (0, 0, 0))
+    whole_rim = pl.BlockSpec((cells_y, width, cells_z), lambda i: (0, 0, 0))
+    field = pl.BlockSpec((BLOCK, cells_x, cells_z), lambda i: (i, 0, 0))
+    rim = pl.BlockSpec((BLOCK, width, cells_z), lambda i: (i, 0, 0))
+    fwd_spec = pl.BlockSpec((None, BLOCK, cells_x, cells_z), lambda i: (moment, i, 0, 0))
     src_spec = pl.BlockSpec(source.shape, lambda i: (0, 0, 0))
     f32 = jnp.float32
     return pl.pallas_call(
         functools.partial(step_kernel, moment),
-        grid=(1,),
+        grid=(cells_y // BLOCK,),
         out_shape=(
             jax.ShapeDtypeStruct(current.shape, f32),
             jax.ShapeDtypeStruct(current.shape, f32),
             jax.ShapeDtypeStruct(lo.shape, f32),
             jax.ShapeDtypeStruct(lo.shape, f32),
         ),
-        in_specs=[field, field, rim, rim, field, fwd_spec, src_spec, field],
+        in_specs=[whole, field, whole_rim, whole_rim, field, fwd_spec, src_spec, field],
         out_specs=(field, field, rim, rim),
         scratch_shapes=[pltpu.VMEM((cells_y + 8, cells_x + 16, cells_z), f32)],
         input_output_aliases={7: 1},
-        compiler_params=pltpu.CompilerParams(vmem_limit_bytes=48 * 1024 * 1024),
+        compiler_params=pltpu.CompilerParams(
+            dimension_semantics=("arbitrary",), vmem_limit_bytes=48 * 1024 * 1024
+        ),
     )(current, previous, lo, hi, speed_sq, forward, source, imaging)
 
 
 def halo(first, last):
     axis = "space"
     devices = lax.axis_size(axis)
-    up = [(i, (i + 1) % devices) for i in range(devices - 1)]
-    down = [(j, i) for i, j in up]
-    return lax.ppermute(last, axis, up), lax.ppermute(first, axis, down)
+    even = lax.axis_index(axis) % 2 == 0
+    within = [(i, i ^ 1) for i in range(devices)]
+    across = [(i, i + 1 - 2 * ((i + 1) % 2)) for i in range(1, devices - 1)]
+    got_within = lax.ppermute(jnp.where(even, last, first), axis, within)
+    got_across = lax.ppermute(jnp.where(even, first, last), axis, across)
+    lo = jnp.where(even, got_across, got_within)
+    hi = jnp.where(even, got_within, got_across)
+    return lo, hi
 
 
 def local(

time: 151 us -> 143 us (0.947)
  waiting for transfers between devices: 40.7 us -> 34.1 us
  starting transfers between devices: 32.7 us -> 28.2 us
  blocking collectives: 23.3 us -> 25.1 us
  other arithmetic: 5.32 us -> 6.98 us
    ppermute x12, waiting for transfers between devices: 40.7 us -> 29.9 us  [the longest x6 29.9 us: halo(): got_across = lax.ppermute(jnp.where(even, first, last), axis, across)]
    ppermute x12, starting transfers between devices: 26.9 us -> 21.9 us  [the longest x6 20.3 us: halo(): got_across = lax.ppermute(jnp.where(even, first, last), axis, across)]
    all_to_all x1, waiting for transfers between devices: 0.01 us -> 4.16 us  [local(): lax.all_to_all(buffer, 'space', split_axis=0, concat_axis=0, tiled=True)]
    select_n x0 -> x12, other arithmetic: none -> 1.79 us  [the longest x6 1.57 us: halo(): got_within = lax.ppermute(jnp.where(even, last, first), axis, within)]
    all_to_all x1, blocking collectives: 23.3 us -> 25.1 us  [local(): lax.all_to_all(placed, 'shot', split_axis=0, concat_axis=0, tiled=True)]
  transfers between devices with their start and end apart: 13 -> 13, of which waited for: 11 -> 6; matrix products, arithmetic and copies ran while one was open for 2% -> 7% of each run, Pallas kernels for 0% -> 0%
where the time goes in v4:
time: 143 us; the launch traced here: 141 us
  Pallas kernels  37.6 us (26%)
  waiting for transfers between devices  34.1 us (24%)
  starting transfers between devices  28.2 us (20%)
  blocking collectives  25.1 us (18%)
  other arithmetic  6.98 us (5%)
  local copies, waits for them, and re-layouts  3.88 us (3%)
  matrix products  3.39 us (2%)
  between operations  1.68 us (1%)
    pallas_call x6, Pallas kernels, step_call(): pl.pallas_call(functools.partial(step_kernel, moment), grid=(cells_y // B...  37.6 us
    ppermute x6, waiting for transfers between devices, halo(): got_across = lax.ppermute(jnp.where(even, first, last), axis, across)  29.9 us
    all_to_all x1, blocking collectives, local(): lax.all_to_all(placed, 'shot', split_axis=0, concat_axis=0, tiled=True)  25.1 us
    ppermute x6, starting transfers between devices, halo(): got_across = lax.ppermute(jnp.where(even, first, last), axis, across)  20.3 us
    all_to_all x1, starting transfers between devices, local(): lax.all_to_all(buffer, 'space', split_axis=0, concat_axis=0, tiled=True)  6.34 us
    all_to_all x1, waiting for transfers between devices, local(): lax.all_to_all(buffer, 'space', split_axis=0, concat_axis=0, tiled=True)  4.16 us
  transfers between devices with their start and end apart: 13, of which 6 were waited for; matrix products, arithmetic and copies ran while one was open for 7% of the time, Pallas kernels for 0%

profile of v4, /device:TPU:97, one launch (start us, length us, event | category | flops | bytes accessed | tf_op | source)
XLA Modules:
  0.0 140.9 jit_solution(11576111769634045022)
XLA Ops:
  0.6 0.0 copy-start
  0.7 1.4 slice_select_fusion
  2.0 0.8 collective-permute-start.1
  2.8 1.9 %collective-permute-start = (f32[64,4,256]{2,1,0:T(4,128)S(1)}, f32[64,4,256]{2,1,0:T(4,128)S(1)}, u32[]{:S(2)}, u32[]{:S(2)}) collective-permute-start(f32[64,4,256]{2,1,0:T(4,128)S(1)} %get-tuple-element.47), channel_id=1, source_target_pairs={{1,2},{2,1},{3,4},{4,3},{5,6},{6,5},{7,8},{8,7},{9,10},{10,9},{11,... | collective-permute-start | bytes 786440 | tf_op jit(solution)/shard_map/ppermute | solution.py:165
  4.7 0.7 fusion.10
  5.4 0.6 reduce-window.6
  6.0 0.2 slice_reduce_fusion
  6.2 0.8 fusion.9
  7.0 0.7 multiply_add_fusion
  7.6 0.7 convert_bitcast_fusion
  8.3 0.0 copy-done
  8.3 1.0 fusion.3
  9.3 0.5 fusion.5
  9.8 0.1 reshape.98
  10.0 0.7 reshape.111
  10.7 6.3 %all-to-all-start = ((f32[16,1,336]{2,1,0:T(1,128)}), f32[16,1,336]{2,1,0:T(1,128)S(1)}, u32[]{:S(2)}, u32[]{:S(2)}) async-start(f32[16,1,336]{2,1,0:T(1,128)} %reshape.111), calls=%async_computation | async-start | bytes 49152 | tf_op jit(solution)/shard_map/all_to_all | solution.py:208
  17.1 4.2 %all-to-all-done = f32[16,1,336]{2,1,0:T(1,128)S(1)} async-done(((f32[16,1,336]{2,1,0:T(1,128)}), f32[16,1,336]{2,1,0:T(1,128)S(1)}, u32[]{:S(2)}, u32[]{:S(2)}) %all-to-all-start) | async-done | bytes 21536 | tf_op jit(solution)/shard_map/all_to_all | solution.py:208
  21.2 0.5 broadcast.131
  21.7 0.7 reduce.4
  22.4 0.1 reshape.112
  22.5 0.1 reshape.99
  22.7 1.9 %fusion = f32[1024,6]{1,0:T(8,128)S(1)} fusion(s32[1024]{0:T(1024)S(1)} %iota_add_fusion, s32[768]{0:T(1024)S(1)} %fusion.20, f32[768,7]{0,1:T(8,128)S(1)} %reshape.99), kind=kOutput, calls=%fused_computation.2 | convolution fusion | flops 58195968 | bytes 53248 | tf_op jit(solution)/shard_map/dot_general | solution.py:214
  24.5 0.0 copy-start.2
  24.6 0.0 copy-start.3
  24.6 0.0 collective-permute-done.1
  24.6 0.0 collective-permute-done
  24.6 0.1 broadcast_in_dim.37.img_ref
  24.8 1.0 copy-done.2
  25.8 0.3 copy-done.3
  26.1 6.1 %shard_map.104 = (f32[64,16,256]{2,1,0:T(8,128)S(1)}, f32[64,16,256]{2,1,0:T(8,128)S(1)}, f32[64,4,256]{2,1,0:T(4,128)S(1)}, f32[64,4,256]{2,1,0:T(4,128)S(1)}) custom-call(f32[64,16,256]{2,1,0:T(8,128)S(1)} %bitcast.100, f32[64,16,256]{2,1,0:T(8,128)S(1)} %bitcast.114, f32[64,4,256]{2,1,0:T(4,128)S(1)} %bitcast.113, ...), custom_call_target="tpu_custom_call", output_to_operand_aliasing={{1}: (7, {})} | custom-call | tf_op jit(solution)/shard_map/pallas_call | solution.py:139
  32.3 0.5 collective-permute-start.3
  32.8 3.6 %collective-permute-start.2 = (f32[64,4,256]{2,1,0:T(4,128)S(1)}, f32[64,4,256]{2,1,0:T(4,128)S(1)}, u32[]{:S(2)}, u32[]{:S(2)}) collective-permute-start(f32[64,4,256]{2,1,0:T(4,128)S(1)} %bitcast.145), channel_id=1, source_target_pairs={{1,2},{2,1},{3,4},{4,3},{5,6},{6,5},{7,8},{8,7},{9,10},{10,9},{11,... | collective-permute-start | bytes 786440 | tf_op jit(solution)/shard_map/ppermute | solution.py:165
  36.4 0.0 collective-permute-done.3
  36.4 6.1 %collective-permute-done.2 = f32[64,4,256]{2,1,0:T(4,128)S(1)} collective-permute-done((f32[64,4,256]{2,1,0:T(4,128)S(1)}, f32[64,4,256]{2,1,0:T(4,128)S(1)}, u32[]{:S(2)}, u32[]{:S(2)}) %collective-permute-start.2) | collective-permute-done | bytes 262176 | tf_op jit(solution)/shard_map/ppermute | solution.py:165
  42.6 6.2 %shard_map.105 = (f32[64,16,256]{2,1,0:T(8,128)S(1)}, f32[64,16,256]{2,1,0:T(8,128)S(1)}, f32[64,4,256]{2,1,0:T(4,128)S(1)}, f32[64,4,256]{2,1,0:T(4,128)S(1)}) custom-call(f32[64,16,256]{2,1,0:T(8,128)S(1)} %get-tuple-element.24.cur_ref.prev_ref, f32[64,16,256]{2,1,0:T(8,128)S(1)} %bitcast.101, ...), custom_call_target="tpu_custom_call", output_to_operand_aliasing={{1}: (7, {})} | custom-call | tf_op jit(solution)/shard_map/pallas_call | solution.py:139
  48.8 0.1 collective-permute-start.5
  48.9 3.7 %collective-permute-start.4 = (f32[64,4,256]{2,1,0:T(4,128)S(1)}, f32[64,4,256]{2,1,0:T(4,128)S(1)}, u32[]{:S(2)}, u32[]{:S(2)}) collective-permute-start(f32[64,4,256]{2,1,0:T(4,128)S(1)} %bitcast.146), channel_id=1, source_target_pairs={{1,2},{2,1},{3,4},{4,3},{5,6},{6,5},{7,8},{8,7},{9,10},{10,9},{11,... | collective-permute-start | bytes 786440 | tf_op jit(solution)/shard_map/ppermute | solution.py:165
  52.6 0.0 collective-permute-done.5
  52.6 6.1 %collective-permute-done.4 = f32[64,4,256]{2,1,0:T(4,128)S(1)} collective-permute-done((f32[64,4,256]{2,1,0:T(4,128)S(1)}, f32[64,4,256]{2,1,0:T(4,128)S(1)}, u32[]{:S(2)}, u32[]{:S(2)}) %collective-permute-start.4) | collective-permute-done | bytes 262176 | tf_op jit(solution)/shard_map/ppermute | solution.py:165
  58.7 6.2 %shard_map.106 = (f32[64,16,256]{2,1,0:T(8,128)S(1)}, f32[64,16,256]{2,1,0:T(8,128)S(1)}, f32[64,4,256]{2,1,0:T(4,128)S(1)}, f32[64,4,256]{2,1,0:T(4,128)S(1)}) custom-call(f32[64,16,256]{2,1,0:T(8,128)S(1)} %get-tuple-element.28.cur_ref.prev_ref, f32[64,16,256]{2,1,0:T(8,128)S(1)} %get-tuple-element.24.cur_ref.prev_ref, ...), custom_call_target="tpu_custom_call", output_to_operand_aliasing={{1}: (7, {})} | custom-call | tf_op jit(solution)/shard_map/pallas_call | solution.py:139
  64.9 0.1 collective-permute-start.7
  65.0 3.7 %collective-permute-start.6 = (f32[64,4,256]{2,1,0:T(4,128)S(1)}, f32[64,4,256]{2,1,0:T(4,128)S(1)}, u32[]{:S(2)}, u32[]{:S(2)}) collective-permute-start(f32[64,4,256]{2,1,0:T(4,128)S(1)} %bitcast.147), channel_id=1, source_target_pairs={{1,2},{2,1},{3,4},{4,3},{5,6},{6,5},{7,8},{8,7},{9,10},{10,9},{11,... | collective-permute-start | bytes 786440 | tf_op jit(solution)/shard_map/ppermute | solution.py:165
  68.7 0.0 collective-permute-done.7
  68.7 6.1 %collective-permute-done.6 = f32[64,4,256]{2,1,0:T(4,128)S(1)} collective-permute-done((f32[64,4,256]{2,1,0:T(4,128)S(1)}, f32[64,4,256]{2,1,0:T(4,128)S(1)}, u32[]{:S(2)}, u32[]{:S(2)}) %collective-permute-start.6) | collective-permute-done | bytes 262176 | tf_op jit(solution)/shard_map/ppermute | solution.py:165
  74.9 6.2 %shard_map.107 = (f32[64,16,256]{2,1,0:T(8,128)S(1)}, f32[64,16,256]{2,1,0:T(8,128)S(1)}, f32[64,4,256]{2,1,0:T(4,128)S(1)}, f32[64,4,256]{2,1,0:T(4,128)S(1)}) custom-call(f32[64,16,256]{2,1,0:T(8,128)S(1)} %get-tuple-element.32.cur_ref.prev_ref, f32[64,16,256]{2,1,0:T(8,128)S(1)} %get-tuple-element.28.cur_ref.prev_ref, ...), custom_call_target="tpu_custom_call", output_to_operand_aliasing={{1}: (7, {})} | custom-call | tf_op jit(solution)/shard_map/pallas_call | solution.py:139
  81.1 0.1 collective-permute-start.9
  81.2 3.7 %collective-permute-start.8 = (f32[64,4,256]{2,1,0:T(4,128)S(1)}, f32[64,4,256]{2,1,0:T(4,128)S(1)}, u32[]{:S(2)}, u32[]{:S(2)}) collective-permute-start(f32[64,4,256]{2,1,0:T(4,128)S(1)} %bitcast.144), channel_id=1, source_target_pairs={{1,2},{2,1},{3,4},{4,3},{5,6},{6,5},{7,8},{8,7},{9,10},{10,9},{11,... | collective-permute-start | bytes 786440 | tf_op jit(solution)/shard_map/ppermute | solution.py:165
  85.5 0.0 collective-permute-done.9
  85.5 5.5 %collective-permute-done.8 = f32[64,4,256]{2,1,0:T(4,128)S(1)} collective-permute-done((f32[64,4,256]{2,1,0:T(4,128)S(1)}, f32[64,4,256]{2,1,0:T(4,128)S(1)}, u32[]{:S(2)}, u32[]{:S(2)}) %collective-permute-start.8) | collective-permute-done | bytes 262176 | tf_op jit(solution)/shard_map/ppermute | solution.py:165
  91.0 6.2 %shard_map.108 = (f32[64,16,256]{2,1,0:T(8,128)S(1)}, f32[64,16,256]{2,1,0:T(8,128)S(1)}, f32[64,4,256]{2,1,0:T(4,128)S(1)}, f32[64,4,256]{2,1,0:T(4,128)S(1)}) custom-call(f32[64,16,256]{2,1,0:T(8,128)S(1)} %get-tuple-element.36.cur_ref.prev_ref, f32[64,16,256]{2,1,0:T(8,128)S(1)} %get-tuple-element.32.cur_ref.prev_ref, ...), custom_call_target="tpu_custom_call", output_to_operand_aliasing={{1}: (7, {})} | custom-call | tf_op jit(solution)/shard_map/pallas_call | solution.py:139
  97.2 0.0 copy-start.1
  97.2 0.1 collective-permute-start.11
  97.3 3.8 %collective-permute-start.10 = (f32[64,4,256]{2,1,0:T(4,128)S(1)}, f32[64,4,256]{2,1,0:T(4,128)S(1)}, u32[]{:S(2)}, u32[]{:S(2)}) collective-permute-start(f32[64,4,256]{2,1,0:T(4,128)S(1)} %bitcast.137), channel_id=1, source_target_pairs={{1,2},{2,1},{3,4},{4,3},{5,6},{6,5},{7,8},{8,7},{9,10},{10,9},{11,... | collective-permute-start | bytes 786440 | tf_op jit(solution)/shard_map/ppermute | solution.py:165
  101.2 0.0 collective-permute-done.11
  101.2 6.1 %collective-permute-done.10 = f32[64,4,256]{2,1,0:T(4,128)S(1)} collective-permute-done((f32[64,4,256]{2,1,0:T(4,128)S(1)}, f32[64,4,256]{2,1,0:T(4,128)S(1)}, u32[]{:S(2)}, u32[]{:S(2)}) %collective-permute-start.10) | collective-permute-done | bytes 262176 | tf_op jit(solution)/shard_map/ppermute | solution.py:165
  107.3 0.0 copy-done.1
  107.3 6.8 %shard_map.109 = (f32[64,16,256]{2,1,0:T(8,128)}, f32[64,16,256]{2,1,0:T(8,128)S(1)}, f32[64,4,256]{2,1,0:T(4,128)}, f32[64,4,256]{2,1,0:T(4,128)}) custom-call(f32[64,16,256]{2,1,0:T(8,128)S(1)} %get-tuple-element.40.cur_ref, f32[64,16,256]{2,1,0:T(8,128)S(1)} %get-tuple-element.36.cur_ref.prev_ref, ...), custom_call_target="tpu_custom_call", output_to_operand_aliasing={{1}: (7, {})} | custom-call | tf_op jit(solution)/shard_map/pallas_call | solution.py:139
  114.1 0.7 gather_fusion
  114.8 0.2 select_select_fusion
  115.1 25.1 %all_to_all.10 = f32[8,10,16,256]{3,2,1,0:T(8,128)S(1)} all-to-all(f32[8,10,16,256]{3,2,1,0:T(8,128)S(1)} %select_select_fusion), channel_id=1, replica_groups=mesh['shot'=8,'space'=16] {'shot'}, dimensions={0} | all-to-all | bytes 2621440 | tf_op jit(solution)/shard_map/all_to_all | solution.py:242
  140.1 0.8 reduce_sum.19
  (20 shorter events, 0.5 us)
Async XLA Ops:
  0.6 7.7 %copy-start = (bf16[1,256,1536]{2,1,0:T(8,128)(2,1)S(1)}, bf16[1,256,1536]{2,1,0:T(8,128)(2,1)}, u32[]{:S(2)}) copy-start(bf16[1,256,1536]{2,1,0:T(8,128)(2,1)} %param.9) | copy-start | bytes 2359300
  2.0 22.5 %collective-permute-start.1 = (f32[64,4,256]{2,1,0:T(4,128)S(1)}, f32[64,4,256]{2,1,0:T(4,128)S(1)}, u32[]{:S(2)}, u32[]{:S(2)}) collective-permute-start(f32[64,4,256]{2,1,0:T(4,128)S(1)} %get-tuple-element.46), channel_id=1, source_target_pairs={{0,1},{1,0},{2,3},{3,2},{4,5},{5,4},{6,7},{7,6},{8,9},{9,8},{10,11... | collective-permute-start | bytes 786440 | tf_op jit(solution)/shard_map/ppermute | solution.py:164
  2.8 21.8 %collective-permute-start = (f32[64,4,256]{2,1,0:T(4,128)S(1)}, f32[64,4,256]{2,1,0:T(4,128)S(1)}, u32[]{:S(2)}, u32[]{:S(2)}) collective-permute-start(f32[64,4,256]{2,1,0:T(4,128)S(1)} %get-tuple-element.47), channel_id=1, source_target_pairs={{1,2},{2,1},{3,4},{4,3},{5,6},{6,5},{7,8},{8,7},{9,10},{10,9},{11,... | collective-permute-start | bytes 786440 | tf_op jit(solution)/shard_map/ppermute | solution.py:165
  10.7 10.5 %all-to-all-start = ((f32[16,1,336]{2,1,0:T(1,128)}), f32[16,1,336]{2,1,0:T(1,128)S(1)}, u32[]{:S(2)}, u32[]{:S(2)}) async-start(f32[16,1,336]{2,1,0:T(1,128)} %reshape.111), calls=%async_computation | async-start | bytes 49152 | tf_op jit(solution)/shard_map/all_to_all | solution.py:208
  24.5 1.2 copy-start.2
  24.6 1.5 %copy-start.3 = (f32[1,64,16,256]{3,2,1,0:T(8,128)S(1)}, f32[1,64,16,256]{3,2,1,0:T(8,128)}, u32[]{:S(2)}) copy-start(f32[1,64,16,256]{3,2,1,0:T(8,128)} %param.15) | copy-start | bytes 3145732
  32.3 4.1 %collective-permute-start.3 = (f32[64,4,256]{2,1,0:T(4,128)S(1)}, f32[64,4,256]{2,1,0:T(4,128)S(1)}, u32[]{:S(2)}, u32[]{:S(2)}) collective-permute-start(f32[64,4,256]{2,1,0:T(4,128)S(1)} %bitcast.150), channel_id=1, source_target_pairs={{0,1},{1,0},{2,3},{3,2},{4,5},{5,4},{6,7},{7,6},{8,9},{9,8},{10,11... | collective-permute-start | bytes 786440 | tf_op jit(solution)/shard_map/ppermute | solution.py:164
  32.8 9.8 %collective-permute-start.2 = (f32[64,4,256]{2,1,0:T(4,128)S(1)}, f32[64,4,256]{2,1,0:T(4,128)S(1)}, u32[]{:S(2)}, u32[]{:S(2)}) collective-permute-start(f32[64,4,256]{2,1,0:T(4,128)S(1)} %bitcast.145), channel_id=1, source_target_pairs={{1,2},{2,1},{3,4},{4,3},{5,6},{6,5},{7,8},{8,7},{9,10},{10,9},{11,... | collective-permute-start | bytes 786440 | tf_op jit(solution)/shard_map/ppermute | solution.py:165
  48.8 3.8 %collective-permute-start.5 = (f32[64,4,256]{2,1,0:T(4,128)S(1)}, f32[64,4,256]{2,1,0:T(4,128)S(1)}, u32[]{:S(2)}, u32[]{:S(2)}) collective-permute-start(f32[64,4,256]{2,1,0:T(4,128)S(1)} %bitcast.152), channel_id=1, source_target_pairs={{0,1},{1,0},{2,3},{3,2},{4,5},{5,4},{6,7},{7,6},{8,9},{9,8},{10,11... | collective-permute-start | bytes 786440 | tf_op jit(solution)/shard_map/ppermute | solution.py:164
  48.9 9.8 %collective-permute-start.4 = (f32[64,4,256]{2,1,0:T(4,128)S(1)}, f32[64,4,256]{2,1,0:T(4,128)S(1)}, u32[]{:S(2)}, u32[]{:S(2)}) collective-permute-start(f32[64,4,256]{2,1,0:T(4,128)S(1)} %bitcast.146), channel_id=1, source_target_pairs={{1,2},{2,1},{3,4},{4,3},{5,6},{6,5},{7,8},{8,7},{9,10},{10,9},{11,... | collective-permute-start | bytes 786440 | tf_op jit(solution)/shard_map/ppermute | solution.py:165
  64.9 3.8 %collective-permute-start.7 = (f32[64,4,256]{2,1,0:T(4,128)S(1)}, f32[64,4,256]{2,1,0:T(4,128)S(1)}, u32[]{:S(2)}, u32[]{:S(2)}) collective-permute-start(f32[64,4,256]{2,1,0:T(4,128)S(1)} %bitcast.154), channel_id=1, source_target_pairs={{0,1},{1,0},{2,3},{3,2},{4,5},{5,4},{6,7},{7,6},{8,9},{9,8},{10,11... | collective-permute-start | bytes 786440 | tf_op jit(solution)/shard_map/ppermute | solution.py:164
  65.0 9.8 %collective-permute-start.6 = (f32[64,4,256]{2,1,0:T(4,128)S(1)}, f32[64,4,256]{2,1,0:T(4,128)S(1)}, u32[]{:S(2)}, u32[]{:S(2)}) collective-permute-start(f32[64,4,256]{2,1,0:T(4,128)S(1)} %bitcast.147), channel_id=1, source_target_pairs={{1,2},{2,1},{3,4},{4,3},{5,6},{6,5},{7,8},{8,7},{9,10},{10,9},{11,... | collective-permute-start | bytes 786440 | tf_op jit(solution)/shard_map/ppermute | solution.py:165
  81.1 4.4 %collective-permute-start.9 = (f32[64,4,256]{2,1,0:T(4,128)S(1)}, f32[64,4,256]{2,1,0:T(4,128)S(1)}, u32[]{:S(2)}, u32[]{:S(2)}) collective-permute-start(f32[64,4,256]{2,1,0:T(4,128)S(1)} %bitcast.148), channel_id=1, source_target_pairs={{0,1},{1,0},{2,3},{3,2},{4,5},{5,4},{6,7},{7,6},{8,9},{9,8},{10,11... | collective-permute-start | bytes 786440 | tf_op jit(solution)/shard_map/ppermute | solution.py:164
  81.2 9.8 %collective-permute-start.8 = (f32[64,4,256]{2,1,0:T(4,128)S(1)}, f32[64,4,256]{2,1,0:T(4,128)S(1)}, u32[]{:S(2)}, u32[]{:S(2)}) collective-permute-start(f32[64,4,256]{2,1,0:T(4,128)S(1)} %bitcast.144), channel_id=1, source_target_pairs={{1,2},{2,1},{3,4},{4,3},{5,6},{6,5},{7,8},{8,7},{9,10},{10,9},{11,... | collective-permute-start | bytes 786440 | tf_op jit(solution)/shard_map/ppermute | solution.py:165
  97.2 10.1 %copy-start.1 = (f32[1,64,16,256]{3,2,1,0:T(8,128)S(1)}, f32[1,64,16,256]{3,2,1,0:T(8,128)}, u32[]{:S(2)}) copy-start(f32[1,64,16,256]{3,2,1,0:T(8,128)} %param.14) | copy-start | bytes 3145732
  97.2 3.9 %collective-permute-start.11 = (f32[64,4,256]{2,1,0:T(4,128)S(1)}, f32[64,4,256]{2,1,0:T(4,128)S(1)}, u32[]{:S(2)}, u32[]{:S(2)}) collective-permute-start(f32[64,4,256]{2,1,0:T(4,128)S(1)} %bitcast.139), channel_id=1, source_target_pairs={{0,1},{1,0},{2,3},{3,2},{4,5},{5,4},{6,7},{7,6},{8,9},{9,8},{10,11... | collective-permute-start | bytes 786440 | tf_op jit(solution)/shard_map/ppermute | solution.py:164
  97.3 9.9 %collective-permute-start.10 = (f32[64,4,256]{2,1,0:T(4,128)S(1)}, f32[64,4,256]{2,1,0:T(4,128)S(1)}, u32[]{:S(2)}, u32[]{:S(2)}) collective-permute-start(f32[64,4,256]{2,1,0:T(4,128)S(1)} %bitcast.137), channel_id=1, source_target_pairs={{1,2},{2,1},{3,4},{4,3},{5,6},{6,5},{7,8},{8,7},{9,10},{10,9},{11,... | collective-permute-start | bytes 786440 | tf_op jit(solution)/shard_map/ppermute | solution.py:165

commit v5 on v4

--- a/solution.py
+++ b/solution.py
@@ -153,6 +153,110 @@
             dimension_semantics=("arbitrary",), vmem_limit_bytes=48 * 1024 * 1024
         ),
     )(current, previous, lo, hi, speed_sq, forward, source, imaging)
+
+
+def tile_kernel(moment, tile_ref, cur_ref, prev_ref, halo_ref, vel_ref, fwd_ref, src_ref, img_ref,
+                chain_ref, next_ref, img_out_ref, edge_ref, pad_ref):
+    del chain_ref
+    cells_y, cells_x, cells_z = cur_ref.shape
+    width = halo_ref.shape[1]
+    part = cells_x // 2
+    zeros = jnp.zeros((4, pad_ref.shape[1], cells_z), jnp.float32)
+    pad_ref[0:4] = zeros
+    pad_ref[4 + cells_y : 8 + cells_y] = zeros
+    pad_ref[4 : 4 + cells_y, 8 : 8 + cells_x] = cur_ref[...]
+
+    def compute(tile):
+        if tile == 0:
+            pad_ref[4 : 4 + cells_y, 8 - width : 8] = halo_ref[...]
+        else:
+            pad_ref[4 : 4 + cells_y, 8 + cells_x : 8 + cells_x + width] = halo_ref[...]
+        start = 8 + tile * part
+
+        def body(chunk, carry):
+            y0 = chunk * ROWS
+            base = y0 + 4
+
+            def window(shift_y, shift_x):
+                return pad_ref[
+                    pl.ds(base + shift_y, ROWS), start + shift_x : start + shift_x + part, :
+                ]
+
+            center = window(0, 0)
+            depth = lax.broadcasted_iota(jnp.int32, center.shape, 2)
+
+            def along_z(reach):
+                up = pltpu.roll(center, cells_z - reach, 2)
+                down = pltpu.roll(center, reach, 2)
+                return (
+                    jnp.where(depth + reach < cells_z, up, 0.0),
+                    jnp.where(depth - reach >= 0, down, 0.0),
+                )
+
+            summed = 3.0 * STENCIL[0] * center
+            for reach in range(1, 5):
+                z_up, z_down = along_z(reach)
+                beside_all = (
+                    window(reach, 0)
+                    + window(-reach, 0)
+                    + window(0, reach)
+                    + window(0, -reach)
+                    + z_up
+                    + z_down
+                )
+                summed = summed + STENCIL[reach] * beside_all
+            rows = pl.ds(y0, ROWS)
+            advanced = 2.0 * center - prev_ref[rows] + vel_ref[rows] * summed
+            source = src_ref[rows, tile * part : (tile + 1) * part, pl.ds(moment, 1)]
+            source = jnp.broadcast_to(source, advanced.shape)
+            advanced = jnp.where(depth == 0, advanced + source, advanced)
+            next_ref[rows] = advanced
+            accel = fwd_ref[rows].astype(jnp.float32)[:, tile * part : (tile + 1) * part]
+            img_out_ref[rows] = img_ref[rows] + accel * advanced
+            if tile == 0:
+                edge_ref[rows] = advanced[:, :width]
+            else:
+                edge_ref[rows] = advanced[:, part - width :]
+            return carry
+
+        lax.fori_loop(0, cells_y // ROWS, body, 0, unroll=4)
+
+    for tile in range(2):
+        pl.when(tile_ref[0] == tile)(functools.partial(compute, tile))
+
+
+def tile_call(moment, tile, current, previous, halo_rim, speed_sq, forward, source, imaging, chain):
+    cells_y, cells_x, cells_z = current.shape
+    width = halo_rim.shape[1]
+    part = cells_x // 2
+    whole = pl.BlockSpec((cells_y, cells_x, cells_z), lambda i, t: (0, 0, 0))
+    rim = pl.BlockSpec((cells_y, width, cells_z), lambda i, t: (0, 0, 0))
+    half = pl.BlockSpec((cells_y, part, cells_z), lambda i, t: (0, t[0], 0))
+    fwd_spec = pl.BlockSpec((None, cells_y, cells_x, cells_z), lambda i, t: (moment, 0, 0, 0))
+    src_spec = pl.BlockSpec(source.shape, lambda i, t: (0, 0, 0))
+    f32 = jnp.float32
+    cells = cells_y * part * cells_z
+    return pl.pallas_call(
+        functools.partial(tile_kernel, moment),
+        grid_spec=pltpu.PrefetchScalarGridSpec(
+            num_scalar_prefetch=1,
+            grid=(1,),
+            in_specs=[whole, half, rim, half, fwd_spec, src_spec, half,
+                      pl.BlockSpec(memory_space=pl.ANY)],
+            out_specs=(half, half, rim),
+            scratch_shapes=[pltpu.VMEM((cells_y + 8, cells_x + 16, cells_z), f32)],
+        ),
+        out_shape=(
+            jax.ShapeDtypeStruct(current.shape, f32),
+            jax.ShapeDtypeStruct(current.shape, f32),
+            jax.ShapeDtypeStruct(halo_rim.shape, f32),
+        ),
+        input_output_aliases={7: 1, 8: 0},
+        cost_estimate=pl.CostEstimate(
+            flops=60 * cells, bytes_accessed=28 * cells, transcendentals=0
+        ),
+        compiler_params=pltpu.CompilerParams(vmem_limit_bytes=48 * 1024 * 1024),
+    )(tile, current, previous, halo_rim, speed_sq, forward, source, imaging, chain)
 
 
 def halo(first, last):
@@ -225,12 +329,27 @@
     forward = forward_accel[0]
     imaging = jnp.zeros_like(current)
     width = 4
+    odd = lax.axis_index("space") % 2
+    tile_near = (1 - odd).reshape(1).astype(jnp.int32)
+    tile_far = odd.reshape(1).astype(jnp.int32)
+    devices = lax.axis_size("space")
+    within = [(i, i ^ 1) for i in range(devices)]
+    across = [(i, i + 1 - 2 * ((i + 1) % 2)) for i in range(1, devices - 1)]
     first = current[:, :width]
     last = current[:, cells_x - width :]
+    even = odd == 0
+    near_edge = jnp.where(even, last, first)
+    far_edge = jnp.where(even, first, last)
     for moment in range(step_count):
-        lo, hi = halo(first, last)
-        advanced, imaging, first, last = step_call(
-            moment, current, previous, lo, hi, speed_sq, forward, source, imaging
+        near_halo = lax.ppermute(near_edge, "space", within)
+        far_halo = lax.ppermute(far_edge, "space", across)
+        partial_next, imaging, near_edge = tile_call(
+            moment, tile_near, current, previous, near_halo, speed_sq, forward, source,
+            imaging, jnp.zeros_like(current),
+        )
+        advanced, imaging, far_edge = tile_call(
+            moment, tile_far, current, previous, far_halo, speed_sq, forward, source,
+            imaging, partial_next,
         )
         previous, current = (current, advanced)
     row_index = jnp.arange(lax.axis_size("shot") * block_rows, dtype=jnp.int32) - shift_rows

time: 143 us -> 127 us (0.89)
  waiting for transfers between devices: 34.1 us -> 8.82 us
  Pallas kernels: 37.6 us -> 46.8 us
  local copies, waits for them, and re-layouts: 3.88 us -> 5.49 us
    ppermute x12, waiting for transfers between devices: 29.9 us -> 8.03 us  [the longest x6 8.01 us: local(): far_halo = lax.ppermute(far_edge, 'space', across)]
    pallas_call x6 -> x12, Pallas kernels: 37.6 us -> 46.8 us  [tile_call(): pl.pallas_call(functools.partial(tile_kernel, moment), grid_spec=pltpu.Pr...]
    all_to_all x1, waiting for transfers between devices: 4.16 us -> 0.79 us  [local(): lax.all_to_all(buffer, 'space', split_axis=0, concat_axis=0, tiled=True)]
    another operation x1 -> x8, local copies, waits for them, and re-layouts: 0.01 us -> 1.8 us
    ppermute x12, starting transfers between devices: 21.9 us -> 23.6 us  [the longest x6 22 us: local(): far_halo = lax.ppermute(far_edge, 'space', across)]
  transfers between devices with their start and end apart: 13 -> 13, of which waited for: 6 -> 6; matrix products, arithmetic and copies ran while one was open for 7% -> 9% of each run, Pallas kernels for 0% -> 34%
where the time goes in v5:
time: 127 us; the launch traced here: 125 us
  Pallas kernels  46.8 us (37%)
  starting transfers between devices  28.9 us (23%)
  blocking collectives  23.9 us (19%)
  waiting for transfers between devices  8.82 us (7%)
  other arithmetic  6.56 us (5%)
  local copies, waits for them, and re-layouts  5.49 us (4%)
  matrix products  3.4 us (3%)
  between operations  1.69 us (1%)
    pallas_call x12, Pallas kernels, tile_call(): pl.pallas_call(functools.partial(tile_kernel, moment), grid_spec=pltpu.Pr...  46.8 us
    all_to_all x1, blocking collectives, local(): lax.all_to_all(placed, 'shot', split_axis=0, concat_axis=0, tiled=True)  23.9 us
    ppermute x6, starting transfers between devices, local(): far_halo = lax.ppermute(far_edge, 'space', across)  22 us
    ppermute x6, waiting for transfers between devices, local(): far_halo = lax.ppermute(far_edge, 'space', across)  8.01 us
    all_to_all x1, starting transfers between devices, local(): lax.all_to_all(buffer, 'space', split_axis=0, concat_axis=0, tiled=True)  5.26 us
  transfers between devices with their start and end apart: 13, of which 6 were waited for; matrix products, arithmetic and copies ran while one was open for 9% of the time, Pallas kernels for 34%

profile of v5, /device:TPU:97, one launch (start us, length us, event | category | flops | bytes accessed | tf_op | source)
XLA Modules:
  0.0 125.4 jit_solution(3224459023456285350)
XLA Ops:
  0.6 0.0 copy-start
  0.7 1.4 %slice_select_fusion = (f32[64,4,256]{2,1,0:T(4,128)S(1)}, f32[64,4,256]{2,1,0:T(4,128)S(1)}) fusion(f32[64,16,256]{2,1,0:T(8,128)} %bitcast.69, pred[]{:T(512)S(6)} %eq.56), kind=kLoop, calls=%fused_computation.11 | loop fusion | flops 131072 | bytes 1048577 | tf_op jit(solution)/shard_map/jit(_where)/select_n | solution.py:341
  2.0 0.8 collective-permute-start.1
  2.8 0.7 fusion.10
  3.5 0.6 reduce-window.6
  4.0 0.2 slice_reduce_fusion
  4.3 0.8 fusion.9
  5.0 0.7 multiply_add_fusion
  5.7 0.7 convert_bitcast_fusion
  6.4 1.0 fusion.3
  7.4 0.5 fusion.5
  7.9 0.1 reshape.105
  8.1 0.7 reshape.119
  8.8 5.3 %all-to-all-start = ((f32[16,1,336]{2,1,0:T(1,128)}), f32[16,1,336]{2,1,0:T(1,128)S(1)}, u32[]{:S(2)}, u32[]{:S(2)}) async-start(f32[16,1,336]{2,1,0:T(1,128)} %reshape.119), calls=%async_computation | async-start | bytes 49152 | tf_op jit(solution)/shard_map/all_to_all | solution.py:312
  14.0 3.4 %collective-permute-start = (f32[64,4,256]{2,1,0:T(4,128)S(1)}, f32[64,4,256]{2,1,0:T(4,128)S(1)}, u32[]{:S(2)}, u32[]{:S(2)}) collective-permute-start(f32[64,4,256]{2,1,0:T(4,128)S(1)} %get-tuple-element.71), channel_id=1, source_target_pairs={{1,2},{2,1},{3,4},{4,3},{5,6},{6,5},{7,8},{8,7},{9,10},{10,9},{11,... | collective-permute-start | bytes 786440 | tf_op jit(solution)/shard_map/ppermute | solution.py:345
  17.4 0.8 all-to-all-done
  18.2 0.5 broadcast.132
  18.7 0.7 reduce.4
  19.4 0.1 reshape.120
  19.5 0.1 reshape.106
  19.7 1.9 %fusion = f32[1024,6]{1,0:T(8,128)S(1)} fusion(s32[1024]{0:T(1024)S(1)} %iota_add_fusion, s32[768]{0:T(1024)S(1)} %fusion.20, f32[768,7]{0,1:T(8,128)S(1)} %reshape.106), kind=kOutput, calls=%fused_computation.2 | convolution fusion | flops 58195968 | bytes 53248 | tf_op jit(solution)/shard_map/dot_general | solution.py:318
  21.6 0.0 copy-start.2
  21.6 0.0 copy-start.3
  21.6 0.1 broadcast_1_img_ref_chain_ref.2.clone.img_ref
  21.7 0.1 broadcast_1_img_ref_chain_ref.2.clone.1.chain_ref
  21.8 0.9 copy-done.2
  22.8 0.3 copy-done.3
  23.1 3.8 %shard_map.104 = (f32[64,16,256]{2,1,0:T(8,128)S(1)}, f32[64,16,256]{2,1,0:T(8,128)S(1)}, f32[64,4,256]{2,1,0:T(4,128)S(1)}) custom-call(s32[1]{0:T(128)} %bitcast.12.tile_ref, f32[64,16,256]{2,1,0:T(8,128)S(1)} %bitcast.70, f32[64,16,256]{2,1,0:T(8,128)S(1)} %bitcast.74, ...), custom_call_target="tpu_custom_call", output_to_operand_aliasing={{1}: (7, {}), {0}: (8, {})} | custom-call | flops 7864320 | bytes 3670016 | tf_op jit(solution)/shard_map/pallas_call | solution.py:239
  26.9 0.5 collective-permute-start.3
  27.4 3.8 %shard_map.105 = (f32[64,16,256]{2,1,0:T(8,128)S(1)}, f32[64,16,256]{2,1,0:T(8,128)S(1)}, f32[64,4,256]{2,1,0:T(4,128)S(1)}) custom-call(s32[1]{0:T(128)} %bitcast.1.tile_ref, f32[64,16,256]{2,1,0:T(8,128)S(1)} %bitcast.71, f32[64,16,256]{2,1,0:T(8,128)S(1)} %bitcast.75, ...), custom_call_target="tpu_custom_call", output_to_operand_aliasing={{1}: (7, {}), {0}: (8, {})} | custom-call | flops 7864320 | bytes 3670016 | tf_op jit(solution)/shard_map/pallas_call | solution.py:239
  31.2 3.7 %collective-permute-start.2 = (f32[64,4,256]{2,1,0:T(4,128)S(1)}, f32[64,4,256]{2,1,0:T(4,128)S(1)}, u32[]{:S(2)}, u32[]{:S(2)}) collective-permute-start(f32[64,4,256]{2,1,0:T(4,128)S(1)} %get-tuple-element.39), channel_id=1, source_target_pairs={{1,2},{2,1},{3,4},{4,3},{5,6},{6,5},{7,8},{8,7},{9,10},{10,9},{11,... | collective-permute-start | bytes 786440 | tf_op jit(solution)/shard_map/ppermute | solution.py:345
  34.9 0.1 broadcast_1_img_ref_chain_ref.2.clone.2.chain_ref
  35.0 3.8 %shard_map.106 = (f32[64,16,256]{2,1,0:T(8,128)S(1)}, f32[64,16,256]{2,1,0:T(8,128)S(1)}, f32[64,4,256]{2,1,0:T(4,128)S(1)}) custom-call(s32[1]{0:T(128)} %bitcast.12.tile_ref, f32[64,16,256]{2,1,0:T(8,128)S(1)} %get-tuple-element.38.cur_ref.prev_ref, f32[64,16,256]{2,1,0:T(8,128)S(1)} %bitcast.72, ...), custom_call_target="tpu_custom_call", output_to_operand_aliasing={{1}: (7, {}), {0}: (8, {})} | custom-call | flops 7864320 | bytes 3670016 | tf_op jit(solution)/shard_map/pallas_call | solution.py:239
  38.8 0.1 collective-permute-start.5
  38.9 2.1 %collective-permute-done.2.halo_ref = f32[64,4,256]{2,1,0:T(4,128)S(1)} collective-permute-done((f32[64,4,256]{2,1,0:T(4,128)S(1)}, f32[64,4,256]{2,1,0:T(4,128)S(1)}, u32[]{:S(2)}, u32[]{:S(2)}) %collective-permute-start.2) | collective-permute-done | bytes 262176 | tf_op jit(solution)/shard_map/ppermute | solution.py:345
  41.0 3.8 %shard_map.107 = (f32[64,16,256]{2,1,0:T(8,128)S(1)}, f32[64,16,256]{2,1,0:T(8,128)S(1)}, f32[64,4,256]{2,1,0:T(4,128)S(1)}) custom-call(s32[1]{0:T(128)} %bitcast.1.tile_ref, f32[64,16,256]{2,1,0:T(8,128)S(1)} %get-tuple-element.38.cur_ref.prev_ref, f32[64,16,256]{2,1,0:T(8,128)S(1)} %bitcast.73, ...), custom_call_target="tpu_custom_call", output_to_operand_aliasing={{1}: (7, {}), {0}: (8, {})} | custom-call | flops 7864320 | bytes 3670016 | tf_op jit(solution)/shard_map/pallas_call | solution.py:239
  44.8 3.7 %collective-permute-start.4 = (f32[64,4,256]{2,1,0:T(4,128)S(1)}, f32[64,4,256]{2,1,0:T(4,128)S(1)}, u32[]{:S(2)}, u32[]{:S(2)}) collective-permute-start(f32[64,4,256]{2,1,0:T(4,128)S(1)} %get-tuple-element.45), channel_id=1, source_target_pairs={{1,2},{2,1},{3,4},{4,3},{5,6},{6,5},{7,8},{8,7},{9,10},{10,9},{11,... | collective-permute-start | bytes 786440 | tf_op jit(solution)/shard_map/ppermute | solution.py:345
  48.5 0.1 broadcast_1_img_ref_chain_ref.2.clone.3.chain_ref
  48.6 3.8 %shard_map.108 = (f32[64,16,256]{2,1,0:T(8,128)S(1)}, f32[64,16,256]{2,1,0:T(8,128)S(1)}, f32[64,4,256]{2,1,0:T(4,128)S(1)}) custom-call(s32[1]{0:T(128)} %bitcast.12.tile_ref, f32[64,16,256]{2,1,0:T(8,128)S(1)} %get-tuple-element.44.cur_ref.prev_ref, ...), custom_call_target="tpu_custom_call", output_to_operand_aliasing={{1}: (7, {}), {0}: (8, {})} | custom-call | flops 7864320 | bytes 3670016 | tf_op jit(solution)/shard_map/pallas_call | solution.py:239
  52.4 0.1 collective-permute-start.7
  52.5 2.1 %collective-permute-done.4.halo_ref = f32[64,4,256]{2,1,0:T(4,128)S(1)} collective-permute-done((f32[64,4,256]{2,1,0:T(4,128)S(1)}, f32[64,4,256]{2,1,0:T(4,128)S(1)}, u32[]{:S(2)}, u32[]{:S(2)}) %collective-permute-start.4) | collective-permute-done | bytes 262176 | tf_op jit(solution)/shard_map/ppermute | solution.py:345
  54.6 3.8 %shard_map.109 = (f32[64,16,256]{2,1,0:T(8,128)S(1)}, f32[64,16,256]{2,1,0:T(8,128)S(1)}, f32[64,4,256]{2,1,0:T(4,128)S(1)}) custom-call(s32[1]{0:T(128)} %bitcast.1.tile_ref, f32[64,16,256]{2,1,0:T(8,128)S(1)} %get-tuple-element.44.cur_ref.prev_ref, ...), custom_call_target="tpu_custom_call", output_to_operand_aliasing={{1}: (7, {}), {0}: (8, {})} | custom-call | flops 7864320 | bytes 3670016 | tf_op jit(solution)/shard_map/pallas_call | solution.py:239
  58.3 3.7 %collective-permute-start.6 = (f32[64,4,256]{2,1,0:T(4,128)S(1)}, f32[64,4,256]{2,1,0:T(4,128)S(1)}, u32[]{:S(2)}, u32[]{:S(2)}) collective-permute-start(f32[64,4,256]{2,1,0:T(4,128)S(1)} %get-tuple-element.51), channel_id=1, source_target_pairs={{1,2},{2,1},{3,4},{4,3},{5,6},{6,5},{7,8},{8,7},{9,10},{10,9},{11,... | collective-permute-start | bytes 786440 | tf_op jit(solution)/shard_map/ppermute | solution.py:345
  62.1 0.1 broadcast_1_img_ref_chain_ref.2.clone.4.chain_ref
  62.2 3.8 %shard_map.110 = (f32[64,16,256]{2,1,0:T(8,128)S(1)}, f32[64,16,256]{2,1,0:T(8,128)S(1)}, f32[64,4,256]{2,1,0:T(4,128)S(1)}) custom-call(s32[1]{0:T(128)} %bitcast.12.tile_ref, f32[64,16,256]{2,1,0:T(8,128)S(1)} %get-tuple-element.50.cur_ref.prev_ref, ...), custom_call_target="tpu_custom_call", output_to_operand_aliasing={{1}: (7, {}), {0}: (8, {})} | custom-call | flops 7864320 | bytes 3670016 | tf_op jit(solution)/shard_map/pallas_call | solution.py:239
  66.0 0.1 collective-permute-start.9
  66.1 2.0 %collective-permute-done.6.halo_ref = f32[64,4,256]{2,1,0:T(4,128)S(1)} collective-permute-done((f32[64,4,256]{2,1,0:T(4,128)S(1)}, f32[64,4,256]{2,1,0:T(4,128)S(1)}, u32[]{:S(2)}, u32[]{:S(2)}) %collective-permute-start.6) | collective-permute-done | bytes 262176 | tf_op jit(solution)/shard_map/ppermute | solution.py:345
  68.1 3.8 %shard_map.111 = (f32[64,16,256]{2,1,0:T(8,128)S(1)}, f32[64,16,256]{2,1,0:T(8,128)S(1)}, f32[64,4,256]{2,1,0:T(4,128)S(1)}) custom-call(s32[1]{0:T(128)} %bitcast.1.tile_ref, f32[64,16,256]{2,1,0:T(8,128)S(1)} %get-tuple-element.50.cur_ref.prev_ref, ...), custom_call_target="tpu_custom_call", output_to_operand_aliasing={{1}: (7, {}), {0}: (8, {})} | custom-call | flops 7864320 | bytes 3670016 | tf_op jit(solution)/shard_map/pallas_call | solution.py:239
  71.9 3.7 %collective-permute-start.8 = (f32[64,4,256]{2,1,0:T(4,128)S(1)}, f32[64,4,256]{2,1,0:T(4,128)S(1)}, u32[]{:S(2)}, u32[]{:S(2)}) collective-permute-start(f32[64,4,256]{2,1,0:T(4,128)S(1)} %get-tuple-element.57), channel_id=1, source_target_pairs={{1,2},{2,1},{3,4},{4,3},{5,6},{6,5},{7,8},{8,7},{9,10},{10,9},{11,... | collective-permute-start | bytes 786440 | tf_op jit(solution)/shard_map/ppermute | solution.py:345
  76.3 0.1 broadcast_1_img_ref_chain_ref.2.clone.5.chain_ref
  76.4 3.8 %shard_map.112 = (f32[64,16,256]{2,1,0:T(8,128)S(1)}, f32[64,16,256]{2,1,0:T(8,128)S(1)}, f32[64,4,256]{2,1,0:T(4,128)S(1)}) custom-call(s32[1]{0:T(128)} %bitcast.12.tile_ref, f32[64,16,256]{2,1,0:T(8,128)S(1)} %get-tuple-element.56.cur_ref.prev_ref, ...), custom_call_target="tpu_custom_call", output_to_operand_aliasing={{1}: (7, {}), {0}: (8, {})} | custom-call | flops 7864320 | bytes 3670016 | tf_op jit(solution)/shard_map/pallas_call | solution.py:239
  80.3 0.1 collective-permute-start.11
  80.4 1.4 %collective-permute-done.8.halo_ref = f32[64,4,256]{2,1,0:T(4,128)S(1)} collective-permute-done((f32[64,4,256]{2,1,0:T(4,128)S(1)}, f32[64,4,256]{2,1,0:T(4,128)S(1)}, u32[]{:S(2)}, u32[]{:S(2)}) %collective-permute-start.8) | collective-permute-done | bytes 262176 | tf_op jit(solution)/shard_map/ppermute | solution.py:345
  81.7 3.8 %shard_map.113 = (f32[64,16,256]{2,1,0:T(8,128)S(1)}, f32[64,16,256]{2,1,0:T(8,128)S(1)}, f32[64,4,256]{2,1,0:T(4,128)S(1)}) custom-call(s32[1]{0:T(128)} %bitcast.1.tile_ref, f32[64,16,256]{2,1,0:T(8,128)S(1)} %get-tuple-element.56.cur_ref.prev_ref, ...), custom_call_target="tpu_custom_call", output_to_operand_aliasing={{1}: (7, {}), {0}: (8, {})} | custom-call | flops 7864320 | bytes 3670016 | tf_op jit(solution)/shard_map/pallas_call | solution.py:239
  85.5 0.0 copy-start.1
  85.5 3.9 %collective-permute-start.10 = (f32[64,4,256]{2,1,0:T(4,128)S(1)}, f32[64,4,256]{2,1,0:T(4,128)S(1)}, u32[]{:S(2)}, u32[]{:S(2)}) collective-permute-start(f32[64,4,256]{2,1,0:T(4,128)S(1)} %get-tuple-element.63), channel_id=1, source_target_pairs={{1,2},{2,1},{3,4},{4,3},{5,6},{6,5},{7,8},{8,7},{9,10},{10,9},{11,... | collective-permute-start | bytes 786440 | tf_op jit(solution)/shard_map/ppermute | solution.py:345
  89.5 1.1 broadcast_1_img_ref_chain_ref.2.chain_ref
  90.6 4.4 %shard_map.114 = (f32[64,16,256]{2,1,0:T(8,128)}, f32[64,16,256]{2,1,0:T(8,128)S(1)}, f32[64,4,256]{2,1,0:T(4,128)}) custom-call(s32[1]{0:T(128)} %bitcast.12.tile_ref, f32[64,16,256]{2,1,0:T(8,128)S(1)} %get-tuple-element.62.cur_ref, f32[64,16,256]{2,1,0:T(8,128)S(1)} %get-tuple-element.56.cur_ref.prev_ref, ...), custom_call_target="tpu_custom_call", output_to_operand_aliasing={{1}: (7, {}), {0}: (8, {})} | custom-call | flops 7864320 | bytes 3670016 | tf_op jit(solution)/shard_map/pallas_call | solution.py:239
  95.0 0.5 collective-permute-done.10.halo_ref
  95.5 4.4 %shard_map.115 = (f32[64,16,256]{2,1,0:T(8,128)}, f32[64,16,256]{2,1,0:T(8,128)S(1)}, f32[64,4,256]{2,1,0:T(4,128)}) custom-call(s32[1]{0:T(128)} %bitcast.1.tile_ref, f32[64,16,256]{2,1,0:T(8,128)S(1)} %get-tuple-element.62.cur_ref, f32[64,16,256]{2,1,0:T(8,128)S(1)} %get-tuple-element.56.cur_ref.prev_ref, ...), custom_call_target="tpu_custom_call", output_to_operand_aliasing={{1}: (7, {}), {0}: (8, {})} | custom-call | flops 7864320 | bytes 3670016 | tf_op jit(solution)/shard_map/pallas_call | solution.py:239
  99.9 0.7 gather_fusion
  100.6 0.2 select_select_fusion
  100.8 23.9 %all_to_all.10 = f32[8,10,16,256]{3,2,1,0:T(8,128)S(1)} all-to-all(f32[8,10,16,256]{3,2,1,0:T(8,128)S(1)} %select_select_fusion), channel_id=1, replica_groups=mesh['shot'=8,'space'=16] {'shot'}, dimensions={0} | all-to-all | bytes 2621440 | tf_op jit(solution)/shard_map/all_to_all | solution.py:361
  124.7 0.8 reduce_sum.19
  (18 shorter events, 0.2 us)
Async XLA Ops:
  0.6 5.8 %copy-start = (bf16[1,256,1536]{2,1,0:T(8,128)(2,1)S(1)}, bf16[1,256,1536]{2,1,0:T(8,128)(2,1)}, u32[]{:S(2)}) copy-start(bf16[1,256,1536]{2,1,0:T(8,128)(2,1)} %param.9) | copy-start | bytes 2359300
  2.0 19.5 %collective-permute-start.1 = (f32[64,4,256]{2,1,0:T(4,128)S(1)}, f32[64,4,256]{2,1,0:T(4,128)S(1)}, u32[]{:S(2)}, u32[]{:S(2)}) collective-permute-start(f32[64,4,256]{2,1,0:T(4,128)S(1)} %get-tuple-element.70), channel_id=1, source_target_pairs={{0,1},{1,0},{2,3},{3,2},{4,5},{5,4},{6,7},{7,6},{8,9},{9,8},{10,11... | collective-permute-start | bytes 786440 | tf_op jit(solution)/shard_map/ppermute | solution.py:344
  8.8 9.4 %all-to-all-start = ((f32[16,1,336]{2,1,0:T(1,128)}), f32[16,1,336]{2,1,0:T(1,128)S(1)}, u32[]{:S(2)}, u32[]{:S(2)}) async-start(f32[16,1,336]{2,1,0:T(1,128)} %reshape.119), calls=%async_computation | async-start | bytes 49152 | tf_op jit(solution)/shard_map/all_to_all | solution.py:312
  14.0 13.3 %collective-permute-start = (f32[64,4,256]{2,1,0:T(4,128)S(1)}, f32[64,4,256]{2,1,0:T(4,128)S(1)}, u32[]{:S(2)}, u32[]{:S(2)}) collective-permute-start(f32[64,4,256]{2,1,0:T(4,128)S(1)} %get-tuple-element.71), channel_id=1, source_target_pairs={{1,2},{2,1},{3,4},{4,3},{5,6},{6,5},{7,8},{8,7},{9,10},{10,9},{11,... | collective-permute-start | bytes 786440 | tf_op jit(solution)/shard_map/ppermute | solution.py:345
  21.6 1.2 copy-start.2
  21.6 1.5 %copy-start.3 = (f32[1,64,16,256]{3,2,1,0:T(8,128)S(1)}, f32[1,64,16,256]{3,2,1,0:T(8,128)}, u32[]{:S(2)}) copy-start(f32[1,64,16,256]{3,2,1,0:T(8,128)} %param.15) | copy-start | bytes 3145732
  26.9 8.0 %collective-permute-start.3 = (f32[64,4,256]{2,1,0:T(4,128)S(1)}, f32[64,4,256]{2,1,0:T(4,128)S(1)}, u32[]{:S(2)}, u32[]{:S(2)}) collective-permute-start(f32[64,4,256]{2,1,0:T(4,128)S(1)} %get-tuple-element.40), channel_id=1, source_target_pairs={{0,1},{1,0},{2,3},{3,2},{4,5},{5,4},{6,7},{7,6},{8,9},{9,8},{10,11... | collective-permute-start | bytes 786440 | tf_op jit(solution)/shard_map/ppermute | solution.py:344
  31.2 9.8 %collective-permute-start.2 = (f32[64,4,256]{2,1,0:T(4,128)S(1)}, f32[64,4,256]{2,1,0:T(4,128)S(1)}, u32[]{:S(2)}, u32[]{:S(2)}) collective-permute-start(f32[64,4,256]{2,1,0:T(4,128)S(1)} %get-tuple-element.39), channel_id=1, source_target_pairs={{1,2},{2,1},{3,4},{4,3},{5,6},{6,5},{7,8},{8,7},{9,10},{10,9},{11,... | collective-permute-start | bytes 786440 | tf_op jit(solution)/shard_map/ppermute | solution.py:345
  38.8 9.7 %collective-permute-start.5 = (f32[64,4,256]{2,1,0:T(4,128)S(1)}, f32[64,4,256]{2,1,0:T(4,128)S(1)}, u32[]{:S(2)}, u32[]{:S(2)}) collective-permute-start(f32[64,4,256]{2,1,0:T(4,128)S(1)} %get-tuple-element.46), channel_id=1, source_target_pairs={{0,1},{1,0},{2,3},{3,2},{4,5},{5,4},{6,7},{7,6},{8,9},{9,8},{10,11... | collective-permute-start | bytes 786440 | tf_op jit(solution)/shard_map/ppermute | solution.py:344
  44.8 9.8 %collective-permute-start.4 = (f32[64,4,256]{2,1,0:T(4,128)S(1)}, f32[64,4,256]{2,1,0:T(4,128)S(1)}, u32[]{:S(2)}, u32[]{:S(2)}) collective-permute-start(f32[64,4,256]{2,1,0:T(4,128)S(1)} %get-tuple-element.45), channel_id=1, source_target_pairs={{1,2},{2,1},{3,4},{4,3},{5,6},{6,5},{7,8},{8,7},{9,10},{10,9},{11,... | collective-permute-start | bytes 786440 | tf_op jit(solution)/shard_map/ppermute | solution.py:345
  52.4 9.7 %collective-permute-start.7 = (f32[64,4,256]{2,1,0:T(4,128)S(1)}, f32[64,4,256]{2,1,0:T(4,128)S(1)}, u32[]{:S(2)}, u32[]{:S(2)}) collective-permute-start(f32[64,4,256]{2,1,0:T(4,128)S(1)} %get-tuple-element.52), channel_id=1, source_target_pairs={{0,1},{1,0},{2,3},{3,2},{4,5},{5,4},{6,7},{7,6},{8,9},{9,8},{10,11... | collective-permute-start | bytes 786440 | tf_op jit(solution)/shard_map/ppermute | solution.py:344
  58.3 9.8 %collective-permute-start.6 = (f32[64,4,256]{2,1,0:T(4,128)S(1)}, f32[64,4,256]{2,1,0:T(4,128)S(1)}, u32[]{:S(2)}, u32[]{:S(2)}) collective-permute-start(f32[64,4,256]{2,1,0:T(4,128)S(1)} %get-tuple-element.51), channel_id=1, source_target_pairs={{1,2},{2,1},{3,4},{4,3},{5,6},{6,5},{7,8},{8,7},{9,10},{10,9},{11,... | collective-permute-start | bytes 786440 | tf_op jit(solution)/shard_map/ppermute | solution.py:345
  66.0 10.3 %collective-permute-start.9 = (f32[64,4,256]{2,1,0:T(4,128)S(1)}, f32[64,4,256]{2,1,0:T(4,128)S(1)}, u32[]{:S(2)}, u32[]{:S(2)}) collective-permute-start(f32[64,4,256]{2,1,0:T(4,128)S(1)} %get-tuple-element.58), channel_id=1, source_target_pairs={{0,1},{1,0},{2,3},{3,2},{4,5},{5,4},{6,7},{7,6},{8,9},{9,8},{10,11... | collective-permute-start | bytes 786440 | tf_op jit(solution)/shard_map/ppermute | solution.py:344
  71.9 9.8 %collective-permute-start.8 = (f32[64,4,256]{2,1,0:T(4,128)S(1)}, f32[64,4,256]{2,1,0:T(4,128)S(1)}, u32[]{:S(2)}, u32[]{:S(2)}) collective-permute-start(f32[64,4,256]{2,1,0:T(4,128)S(1)} %get-tuple-element.57), channel_id=1, source_target_pairs={{1,2},{2,1},{3,4},{4,3},{5,6},{6,5},{7,8},{8,7},{9,10},{10,9},{11,... | collective-permute-start | bytes 786440 | tf_op jit(solution)/shard_map/ppermute | solution.py:345
  80.3 9.2 %collective-permute-start.11 = (f32[64,4,256]{2,1,0:T(4,128)S(1)}, f32[64,4,256]{2,1,0:T(4,128)S(1)}, u32[]{:S(2)}, u32[]{:S(2)}) collective-permute-start(f32[64,4,256]{2,1,0:T(4,128)S(1)} %get-tuple-element.64), channel_id=1, source_target_pairs={{0,1},{1,0},{2,3},{3,2},{4,5},{5,4},{6,7},{7,6},{8,9},{9,8},{10,11... | collective-permute-start | bytes 786440 | tf_op jit(solution)/shard_map/ppermute | solution.py:344
  85.5 5.0 %copy-start.1 = (f32[1,64,16,256]{3,2,1,0:T(8,128)S(1)}, f32[1,64,16,256]{3,2,1,0:T(8,128)}, u32[]{:S(2)}) copy-start(f32[1,64,16,256]{3,2,1,0:T(8,128)} %param.14) | copy-start | bytes 3145732
  85.5 9.9 %collective-permute-start.10 = (f32[64,4,256]{2,1,0:T(4,128)S(1)}, f32[64,4,256]{2,1,0:T(4,128)S(1)}, u32[]{:S(2)}, u32[]{:S(2)}) collective-permute-start(f32[64,4,256]{2,1,0:T(4,128)S(1)} %get-tuple-element.63), channel_id=1, source_target_pairs={{1,2},{2,1},{3,4},{4,3},{5,6},{6,5},{7,8},{8,7},{9,10},{10,9},{11,... | collective-permute-start | bytes 786440 | tf_op jit(solution)/shard_map/ppermute | solution.py:345

commit v6 on v5

--- a/solution.py
+++ b/solution.py
@@ -55,6 +55,8 @@
 
 ROWS = 1
 BLOCK = 8
+SLAB_ROWS = 4
+SLAB_UNROLL = 2
 
 
 def step_kernel(moment, cur_ref, prev_ref, lo_ref, hi_ref, vel_ref, fwd_ref, src_ref, img_ref,
@@ -174,12 +176,15 @@
         start = 8 + tile * part
 
         def body(chunk, carry):
-            y0 = chunk * ROWS
+            y0 = chunk * SLAB_ROWS
             base = y0 + 4
+            slab = pad_ref[pl.ds(base - 4, SLAB_ROWS + 8), start : start + part, :]
 
             def window(shift_y, shift_x):
+                if shift_x == 0:
+                    return slab[4 + shift_y : 4 + shift_y + SLAB_ROWS]
                 return pad_ref[
-                    pl.ds(base + shift_y, ROWS), start + shift_x : start + shift_x + part, :
+                    pl.ds(base + shift_y, SLAB_ROWS), start + shift_x : start + shift_x + part, :
                 ]
 
             center = window(0, 0)
@@ -205,7 +210,7 @@
                     + z_down
                 )
                 summed = summed + STENCIL[reach] * beside_all
-            rows = pl.ds(y0, ROWS)
+            rows = pl.ds(y0, SLAB_ROWS)
             advanced = 2.0 * center - prev_ref[rows] + vel_ref[rows] * summed
             source = src_ref[rows, tile * part : (tile + 1) * part, pl.ds(moment, 1)]
             source = jnp.broadcast_to(source, advanced.shape)
@@ -219,7 +224,7 @@
                 edge_ref[rows] = advanced[:, part - width :]
             return carry
 
-        lax.fori_loop(0, cells_y // ROWS, body, 0, unroll=4)
+        lax.fori_loop(0, cells_y // SLAB_ROWS, body, 0, unroll=SLAB_UNROLL)
 
     for tile in range(2):
         pl.when(tile_ref[0] == tile)(functools.partial(compute, tile))

time: 127 us -> 123 us (0.969)
  Pallas kernels: 46.8 us -> 40.5 us
  waiting for transfers between devices: 8.82 us -> 11.3 us
    pallas_call x12, Pallas kernels: 46.8 us -> 40.5 us  [tile_call(): pl.pallas_call(functools.partial(tile_kernel, moment), grid_spec=pltpu.Pr...]
    ppermute x6, waiting for transfers between devices: 8.01 us -> 10.5 us  [local(): far_halo = lax.ppermute(far_edge, 'space', across)]
  transfers between devices with their start and end apart: 13 -> 13, of which waited for: 6 -> 6; matrix products, arithmetic and copies ran while one was open for 9% -> 9% of each run, Pallas kernels for 34% -> 30%
where the time goes in v6:
time: 123 us; the launch traced here: 121 us
  Pallas kernels  40.5 us (33%)
  starting transfers between devices  28.9 us (23%)
  blocking collectives  23.5 us (19%)
  waiting for transfers between devices  11.3 us (9%)
  other arithmetic  6.56 us (5%)
  local copies, waits for them, and re-layouts  5.49 us (4%)
  matrix products  3.4 us (3%)
  between operations  1.69 us (1%)
    pallas_call x12, Pallas kernels, tile_call(): pl.pallas_call(functools.partial(tile_kernel, moment), grid_spec=pltpu.Pr...  40.5 us
    all_to_all x1, blocking collectives, local(): lax.all_to_all(placed, 'shot', split_axis=0, concat_axis=0, tiled=True)  23.5 us
    ppermute x6, starting transfers between devices, local(): far_halo = lax.ppermute(far_edge, 'space', across)  22 us
    ppermute x6, waiting for transfers between devices, local(): far_halo = lax.ppermute(far_edge, 'space', across)  10.5 us
    all_to_all x1, starting transfers between devices, local(): lax.all_to_all(buffer, 'space', split_axis=0, concat_axis=0, tiled=True)  5.26 us
  transfers between devices with their start and end apart: 13, of which 6 were waited for; matrix products, arithmetic and copies ran while one was open for 9% of the time, Pallas kernels for 30%

profile of v6, /device:TPU:97, one launch (start us, length us, event | category | flops | bytes accessed | tf_op | source)
XLA Modules:
  0.0 121.4 jit_solution(5861639935531805602)
XLA Ops:
  0.6 0.0 copy-start
  0.7 1.4 %slice_select_fusion = (f32[64,4,256]{2,1,0:T(4,128)S(1)}, f32[64,4,256]{2,1,0:T(4,128)S(1)}) fusion(f32[64,16,256]{2,1,0:T(8,128)} %bitcast.69, pred[]{:T(512)S(6)} %eq.56), kind=kLoop, calls=%fused_computation.11 | loop fusion | flops 131072 | bytes 1048577 | tf_op jit(solution)/shard_map/jit(_where)/select_n | solution.py:346
  2.0 0.8 collective-permute-start.1
  2.8 0.7 fusion.10
  3.5 0.6 reduce-window.6
  4.0 0.2 slice_reduce_fusion
  4.3 0.8 fusion.9
  5.0 0.7 multiply_add_fusion
  5.7 0.7 convert_bitcast_fusion
  6.4 1.0 fusion.3
  7.4 0.5 fusion.5
  7.9 0.1 reshape.105
  8.1 0.7 reshape.119
  8.8 5.3 %all-to-all-start = ((f32[16,1,336]{2,1,0:T(1,128)}), f32[16,1,336]{2,1,0:T(1,128)S(1)}, u32[]{:S(2)}, u32[]{:S(2)}) async-start(f32[16,1,336]{2,1,0:T(1,128)} %reshape.119), calls=%async_computation | async-start | bytes 49152 | tf_op jit(solution)/shard_map/all_to_all | solution.py:317
  14.0 3.4 %collective-permute-start = (f32[64,4,256]{2,1,0:T(4,128)S(1)}, f32[64,4,256]{2,1,0:T(4,128)S(1)}, u32[]{:S(2)}, u32[]{:S(2)}) collective-permute-start(f32[64,4,256]{2,1,0:T(4,128)S(1)} %get-tuple-element.71), channel_id=1, source_target_pairs={{1,2},{2,1},{3,4},{4,3},{5,6},{6,5},{7,8},{8,7},{9,10},{10,9},{11,... | collective-permute-start | bytes 786440 | tf_op jit(solution)/shard_map/ppermute | solution.py:350
  17.4 0.8 all-to-all-done
  18.2 0.5 broadcast.132
  18.7 0.7 reduce.4
  19.4 0.1 reshape.120
  19.5 0.1 reshape.106
  19.7 1.9 %fusion = f32[1024,6]{1,0:T(8,128)S(1)} fusion(s32[1024]{0:T(1024)S(1)} %iota_add_fusion, s32[768]{0:T(1024)S(1)} %fusion.20, f32[768,7]{0,1:T(8,128)S(1)} %reshape.106), kind=kOutput, calls=%fused_computation.2 | convolution fusion | flops 58195968 | bytes 53248 | tf_op jit(solution)/shard_map/dot_general | solution.py:323
  21.6 0.0 copy-start.2
  21.6 0.0 copy-start.3
  21.6 0.1 broadcast_1_img_ref_chain_ref.2.clone.img_ref
  21.7 0.1 broadcast_1_img_ref_chain_ref.2.clone.1.chain_ref
  21.8 0.9 copy-done.2
  22.8 0.3 copy-done.3
  23.1 3.3 %shard_map.104 = (f32[64,16,256]{2,1,0:T(8,128)S(1)}, f32[64,16,256]{2,1,0:T(8,128)S(1)}, f32[64,4,256]{2,1,0:T(4,128)S(1)}) custom-call(s32[1]{0:T(128)} %bitcast.12.tile_ref, f32[64,16,256]{2,1,0:T(8,128)S(1)} %bitcast.70, f32[64,16,256]{2,1,0:T(8,128)S(1)} %bitcast.74, ...), custom_call_target="tpu_custom_call", output_to_operand_aliasing={{1}: (7, {}), {0}: (8, {})} | custom-call | flops 7864320 | bytes 3670016 | tf_op jit(solution)/shard_map/pallas_call | solution.py:244
  26.4 0.5 collective-permute-start.3
  26.8 3.2 %shard_map.105 = (f32[64,16,256]{2,1,0:T(8,128)S(1)}, f32[64,16,256]{2,1,0:T(8,128)S(1)}, f32[64,4,256]{2,1,0:T(4,128)S(1)}) custom-call(s32[1]{0:T(128)} %bitcast.1.tile_ref, f32[64,16,256]{2,1,0:T(8,128)S(1)} %bitcast.71, f32[64,16,256]{2,1,0:T(8,128)S(1)} %bitcast.75, ...), custom_call_target="tpu_custom_call", output_to_operand_aliasing={{1}: (7, {}), {0}: (8, {})} | custom-call | flops 7864320 | bytes 3670016 | tf_op jit(solution)/shard_map/pallas_call | solution.py:244
  30.1 3.7 %collective-permute-start.2 = (f32[64,4,256]{2,1,0:T(4,128)S(1)}, f32[64,4,256]{2,1,0:T(4,128)S(1)}, u32[]{:S(2)}, u32[]{:S(2)}) collective-permute-start(f32[64,4,256]{2,1,0:T(4,128)S(1)} %get-tuple-element.39), channel_id=1, source_target_pairs={{1,2},{2,1},{3,4},{4,3},{5,6},{6,5},{7,8},{8,7},{9,10},{10,9},{11,... | collective-permute-start | bytes 786440 | tf_op jit(solution)/shard_map/ppermute | solution.py:350
  33.8 0.1 broadcast_1_img_ref_chain_ref.2.clone.2.chain_ref
  33.9 3.3 %shard_map.106 = (f32[64,16,256]{2,1,0:T(8,128)S(1)}, f32[64,16,256]{2,1,0:T(8,128)S(1)}, f32[64,4,256]{2,1,0:T(4,128)S(1)}) custom-call(s32[1]{0:T(128)} %bitcast.12.tile_ref, f32[64,16,256]{2,1,0:T(8,128)S(1)} %get-tuple-element.38.cur_ref.prev_ref, f32[64,16,256]{2,1,0:T(8,128)S(1)} %bitcast.72, ...), custom_call_target="tpu_custom_call", output_to_operand_aliasing={{1}: (7, {}), {0}: (8, {})} | custom-call | flops 7864320 | bytes 3670016 | tf_op jit(solution)/shard_map/pallas_call | solution.py:244
  37.2 0.1 collective-permute-start.5
  37.3 2.6 %collective-permute-done.2.halo_ref = f32[64,4,256]{2,1,0:T(4,128)S(1)} collective-permute-done((f32[64,4,256]{2,1,0:T(4,128)S(1)}, f32[64,4,256]{2,1,0:T(4,128)S(1)}, u32[]{:S(2)}, u32[]{:S(2)}) %collective-permute-start.2) | collective-permute-done | bytes 262176 | tf_op jit(solution)/shard_map/ppermute | solution.py:350
  39.9 3.2 %shard_map.107 = (f32[64,16,256]{2,1,0:T(8,128)S(1)}, f32[64,16,256]{2,1,0:T(8,128)S(1)}, f32[64,4,256]{2,1,0:T(4,128)S(1)}) custom-call(s32[1]{0:T(128)} %bitcast.1.tile_ref, f32[64,16,256]{2,1,0:T(8,128)S(1)} %get-tuple-element.38.cur_ref.prev_ref, f32[64,16,256]{2,1,0:T(8,128)S(1)} %bitcast.73, ...), custom_call_target="tpu_custom_call", output_to_operand_aliasing={{1}: (7, {}), {0}: (8, {})} | custom-call | flops 7864320 | bytes 3670016 | tf_op jit(solution)/shard_map/pallas_call | solution.py:244
  43.1 3.7 %collective-permute-start.4 = (f32[64,4,256]{2,1,0:T(4,128)S(1)}, f32[64,4,256]{2,1,0:T(4,128)S(1)}, u32[]{:S(2)}, u32[]{:S(2)}) collective-permute-start(f32[64,4,256]{2,1,0:T(4,128)S(1)} %get-tuple-element.45), channel_id=1, source_target_pairs={{1,2},{2,1},{3,4},{4,3},{5,6},{6,5},{7,8},{8,7},{9,10},{10,9},{11,... | collective-permute-start | bytes 786440 | tf_op jit(solution)/shard_map/ppermute | solution.py:350
  46.9 0.1 broadcast_1_img_ref_chain_ref.2.clone.3.chain_ref
  47.0 3.3 %shard_map.108 = (f32[64,16,256]{2,1,0:T(8,128)S(1)}, f32[64,16,256]{2,1,0:T(8,128)S(1)}, f32[64,4,256]{2,1,0:T(4,128)S(1)}) custom-call(s32[1]{0:T(128)} %bitcast.12.tile_ref, f32[64,16,256]{2,1,0:T(8,128)S(1)} %get-tuple-element.44.cur_ref.prev_ref, ...), custom_call_target="tpu_custom_call", output_to_operand_aliasing={{1}: (7, {}), {0}: (8, {})} | custom-call | flops 7864320 | bytes 3670016 | tf_op jit(solution)/shard_map/pallas_call | solution.py:244
  50.3 0.1 collective-permute-start.7
  50.4 2.6 %collective-permute-done.4.halo_ref = f32[64,4,256]{2,1,0:T(4,128)S(1)} collective-permute-done((f32[64,4,256]{2,1,0:T(4,128)S(1)}, f32[64,4,256]{2,1,0:T(4,128)S(1)}, u32[]{:S(2)}, u32[]{:S(2)}) %collective-permute-start.4) | collective-permute-done | bytes 262176 | tf_op jit(solution)/shard_map/ppermute | solution.py:350
  52.9 3.2 %shard_map.109 = (f32[64,16,256]{2,1,0:T(8,128)S(1)}, f32[64,16,256]{2,1,0:T(8,128)S(1)}, f32[64,4,256]{2,1,0:T(4,128)S(1)}) custom-call(s32[1]{0:T(128)} %bitcast.1.tile_ref, f32[64,16,256]{2,1,0:T(8,128)S(1)} %get-tuple-element.44.cur_ref.prev_ref, ...), custom_call_target="tpu_custom_call", output_to_operand_aliasing={{1}: (7, {}), {0}: (8, {})} | custom-call | flops 7864320 | bytes 3670016 | tf_op jit(solution)/shard_map/pallas_call | solution.py:244
  56.2 3.7 %collective-permute-start.6 = (f32[64,4,256]{2,1,0:T(4,128)S(1)}, f32[64,4,256]{2,1,0:T(4,128)S(1)}, u32[]{:S(2)}, u32[]{:S(2)}) collective-permute-start(f32[64,4,256]{2,1,0:T(4,128)S(1)} %get-tuple-element.51), channel_id=1, source_target_pairs={{1,2},{2,1},{3,4},{4,3},{5,6},{6,5},{7,8},{8,7},{9,10},{10,9},{11,... | collective-permute-start | bytes 786440 | tf_op jit(solution)/shard_map/ppermute | solution.py:350
  59.9 0.1 broadcast_1_img_ref_chain_ref.2.clone.4.chain_ref
  60.1 3.3 %shard_map.110 = (f32[64,16,256]{2,1,0:T(8,128)S(1)}, f32[64,16,256]{2,1,0:T(8,128)S(1)}, f32[64,4,256]{2,1,0:T(4,128)S(1)}) custom-call(s32[1]{0:T(128)} %bitcast.12.tile_ref, f32[64,16,256]{2,1,0:T(8,128)S(1)} %get-tuple-element.50.cur_ref.prev_ref, ...), custom_call_target="tpu_custom_call", output_to_operand_aliasing={{1}: (7, {}), {0}: (8, {})} | custom-call | flops 7864320 | bytes 3670016 | tf_op jit(solution)/shard_map/pallas_call | solution.py:244
  63.3 0.1 collective-permute-start.9
  63.4 2.6 %collective-permute-done.6.halo_ref = f32[64,4,256]{2,1,0:T(4,128)S(1)} collective-permute-done((f32[64,4,256]{2,1,0:T(4,128)S(1)}, f32[64,4,256]{2,1,0:T(4,128)S(1)}, u32[]{:S(2)}, u32[]{:S(2)}) %collective-permute-start.6) | collective-permute-done | bytes 262176 | tf_op jit(solution)/shard_map/ppermute | solution.py:350
  66.0 3.2 %shard_map.111 = (f32[64,16,256]{2,1,0:T(8,128)S(1)}, f32[64,16,256]{2,1,0:T(8,128)S(1)}, f32[64,4,256]{2,1,0:T(4,128)S(1)}) custom-call(s32[1]{0:T(128)} %bitcast.1.tile_ref, f32[64,16,256]{2,1,0:T(8,128)S(1)} %get-tuple-element.50.cur_ref.prev_ref, ...), custom_call_target="tpu_custom_call", output_to_operand_aliasing={{1}: (7, {}), {0}: (8, {})} | custom-call | flops 7864320 | bytes 3670016 | tf_op jit(solution)/shard_map/pallas_call | solution.py:244
  69.3 3.7 %collective-permute-start.8 = (f32[64,4,256]{2,1,0:T(4,128)S(1)}, f32[64,4,256]{2,1,0:T(4,128)S(1)}, u32[]{:S(2)}, u32[]{:S(2)}) collective-permute-start(f32[64,4,256]{2,1,0:T(4,128)S(1)} %get-tuple-element.57), channel_id=1, source_target_pairs={{1,2},{2,1},{3,4},{4,3},{5,6},{6,5},{7,8},{8,7},{9,10},{10,9},{11,... | collective-permute-start | bytes 786440 | tf_op jit(solution)/shard_map/ppermute | solution.py:350
  73.7 0.1 broadcast_1_img_ref_chain_ref.2.clone.5.chain_ref
  73.8 3.4 %shard_map.112 = (f32[64,16,256]{2,1,0:T(8,128)S(1)}, f32[64,16,256]{2,1,0:T(8,128)S(1)}, f32[64,4,256]{2,1,0:T(4,128)S(1)}) custom-call(s32[1]{0:T(128)} %bitcast.12.tile_ref, f32[64,16,256]{2,1,0:T(8,128)S(1)} %get-tuple-element.56.cur_ref.prev_ref, ...), custom_call_target="tpu_custom_call", output_to_operand_aliasing={{1}: (7, {}), {0}: (8, {})} | custom-call | flops 7864320 | bytes 3670016 | tf_op jit(solution)/shard_map/pallas_call | solution.py:244
  77.2 0.1 collective-permute-start.11
  77.3 1.7 %collective-permute-done.8.halo_ref = f32[64,4,256]{2,1,0:T(4,128)S(1)} collective-permute-done((f32[64,4,256]{2,1,0:T(4,128)S(1)}, f32[64,4,256]{2,1,0:T(4,128)S(1)}, u32[]{:S(2)}, u32[]{:S(2)}) %collective-permute-start.8) | collective-permute-done | bytes 262176 | tf_op jit(solution)/shard_map/ppermute | solution.py:350
  79.1 3.2 %shard_map.113 = (f32[64,16,256]{2,1,0:T(8,128)S(1)}, f32[64,16,256]{2,1,0:T(8,128)S(1)}, f32[64,4,256]{2,1,0:T(4,128)S(1)}) custom-call(s32[1]{0:T(128)} %bitcast.1.tile_ref, f32[64,16,256]{2,1,0:T(8,128)S(1)} %get-tuple-element.56.cur_ref.prev_ref, ...), custom_call_target="tpu_custom_call", output_to_operand_aliasing={{1}: (7, {}), {0}: (8, {})} | custom-call | flops 7864320 | bytes 3670016 | tf_op jit(solution)/shard_map/pallas_call | solution.py:244
  82.3 0.0 copy-start.1
  82.3 3.9 %collective-permute-start.10 = (f32[64,4,256]{2,1,0:T(4,128)S(1)}, f32[64,4,256]{2,1,0:T(4,128)S(1)}, u32[]{:S(2)}, u32[]{:S(2)}) collective-permute-start(f32[64,4,256]{2,1,0:T(4,128)S(1)} %get-tuple-element.63), channel_id=1, source_target_pairs={{1,2},{2,1},{3,4},{4,3},{5,6},{6,5},{7,8},{8,7},{9,10},{10,9},{11,... | collective-permute-start | bytes 786440 | tf_op jit(solution)/shard_map/ppermute | solution.py:350
  86.3 1.1 broadcast_1_img_ref_chain_ref.2.chain_ref
  87.4 3.9 %shard_map.114 = (f32[64,16,256]{2,1,0:T(8,128)}, f32[64,16,256]{2,1,0:T(8,128)S(1)}, f32[64,4,256]{2,1,0:T(4,128)}) custom-call(s32[1]{0:T(128)} %bitcast.12.tile_ref, f32[64,16,256]{2,1,0:T(8,128)S(1)} %get-tuple-element.62.cur_ref, f32[64,16,256]{2,1,0:T(8,128)S(1)} %get-tuple-element.56.cur_ref.prev_ref, ...), custom_call_target="tpu_custom_call", output_to_operand_aliasing={{1}: (7, {}), {0}: (8, {})} | custom-call | flops 7864320 | bytes 3670016 | tf_op jit(solution)/shard_map/pallas_call | solution.py:244
  91.3 1.0 collective-permute-done.10.halo_ref
  92.3 3.9 %shard_map.115 = (f32[64,16,256]{2,1,0:T(8,128)}, f32[64,16,256]{2,1,0:T(8,128)S(1)}, f32[64,4,256]{2,1,0:T(4,128)}) custom-call(s32[1]{0:T(128)} %bitcast.1.tile_ref, f32[64,16,256]{2,1,0:T(8,128)S(1)} %get-tuple-element.62.cur_ref, f32[64,16,256]{2,1,0:T(8,128)S(1)} %get-tuple-element.56.cur_ref.prev_ref, ...), custom_call_target="tpu_custom_call", output_to_operand_aliasing={{1}: (7, {}), {0}: (8, {})} | custom-call | flops 7864320 | bytes 3670016 | tf_op jit(solution)/shard_map/pallas_call | solution.py:244
  96.1 0.7 gather_fusion
  96.8 0.2 select_select_fusion
  97.1 23.5 %all_to_all.10 = f32[8,10,16,256]{3,2,1,0:T(8,128)S(1)} all-to-all(f32[8,10,16,256]{3,2,1,0:T(8,128)S(1)} %select_select_fusion), channel_id=1, replica_groups=mesh['shot'=8,'space'=16] {'shot'}, dimensions={0} | all-to-all | bytes 2621440 | tf_op jit(solution)/shard_map/all_to_all | solution.py:366
  120.6 0.8 reduce_sum.19
  (18 shorter events, 0.2 us)
Async XLA Ops:
  0.6 5.8 %copy-start = (bf16[1,256,1536]{2,1,0:T(8,128)(2,1)S(1)}, bf16[1,256,1536]{2,1,0:T(8,128)(2,1)}, u32[]{:S(2)}) copy-start(bf16[1,256,1536]{2,1,0:T(8,128)(2,1)} %param.9) | copy-start | bytes 2359300
  2.0 19.5 %collective-permute-start.1 = (f32[64,4,256]{2,1,0:T(4,128)S(1)}, f32[64,4,256]{2,1,0:T(4,128)S(1)}, u32[]{:S(2)}, u32[]{:S(2)}) collective-permute-start(f32[64,4,256]{2,1,0:T(4,128)S(1)} %get-tuple-element.70), channel_id=1, source_target_pairs={{0,1},{1,0},{2,3},{3,2},{4,5},{5,4},{6,7},{7,6},{8,9},{9,8},{10,11... | collective-permute-start | bytes 786440 | tf_op jit(solution)/shard_map/ppermute | solution.py:349
  8.8 9.4 %all-to-all-start = ((f32[16,1,336]{2,1,0:T(1,128)}), f32[16,1,336]{2,1,0:T(1,128)S(1)}, u32[]{:S(2)}, u32[]{:S(2)}) async-start(f32[16,1,336]{2,1,0:T(1,128)} %reshape.119), calls=%async_computation | async-start | bytes 49152 | tf_op jit(solution)/shard_map/all_to_all | solution.py:317
  14.0 12.8 %collective-permute-start = (f32[64,4,256]{2,1,0:T(4,128)S(1)}, f32[64,4,256]{2,1,0:T(4,128)S(1)}, u32[]{:S(2)}, u32[]{:S(2)}) collective-permute-start(f32[64,4,256]{2,1,0:T(4,128)S(1)} %get-tuple-element.71), channel_id=1, source_target_pairs={{1,2},{2,1},{3,4},{4,3},{5,6},{6,5},{7,8},{8,7},{9,10},{10,9},{11,... | collective-permute-start | bytes 786440 | tf_op jit(solution)/shard_map/ppermute | solution.py:350
  21.6 1.2 %copy-start.2 = (f32[1,64,16,256]{3,2,1,0:T(8,128)S(1)}, f32[1,64,16,256]{3,2,1,0:T(8,128)}, u32[]{:S(2)}) copy-start(f32[1,64,16,256]{3,2,1,0:T(8,128)} %param.16) | copy-start | bytes 3145732
  21.6 1.5 %copy-start.3 = (f32[1,64,16,256]{3,2,1,0:T(8,128)S(1)}, f32[1,64,16,256]{3,2,1,0:T(8,128)}, u32[]{:S(2)}) copy-start(f32[1,64,16,256]{3,2,1,0:T(8,128)} %param.15) | copy-start | bytes 3145732
  26.4 7.4 %collective-permute-start.3 = (f32[64,4,256]{2,1,0:T(4,128)S(1)}, f32[64,4,256]{2,1,0:T(4,128)S(1)}, u32[]{:S(2)}, u32[]{:S(2)}) collective-permute-start(f32[64,4,256]{2,1,0:T(4,128)S(1)} %get-tuple-element.40), channel_id=1, source_target_pairs={{0,1},{1,0},{2,3},{3,2},{4,5},{5,4},{6,7},{7,6},{8,9},{9,8},{10,11... | collective-permute-start | bytes 786440 | tf_op jit(solution)/shard_map/ppermute | solution.py:349
  30.1 9.8 %collective-permute-start.2 = (f32[64,4,256]{2,1,0:T(4,128)S(1)}, f32[64,4,256]{2,1,0:T(4,128)S(1)}, u32[]{:S(2)}, u32[]{:S(2)}) collective-permute-start(f32[64,4,256]{2,1,0:T(4,128)S(1)} %get-tuple-element.39), channel_id=1, source_target_pairs={{1,2},{2,1},{3,4},{4,3},{5,6},{6,5},{7,8},{8,7},{9,10},{10,9},{11,... | collective-permute-start | bytes 786440 | tf_op jit(solution)/shard_map/ppermute | solution.py:350
  37.2 9.7 %collective-permute-start.5 = (f32[64,4,256]{2,1,0:T(4,128)S(1)}, f32[64,4,256]{2,1,0:T(4,128)S(1)}, u32[]{:S(2)}, u32[]{:S(2)}) collective-permute-start(f32[64,4,256]{2,1,0:T(4,128)S(1)} %get-tuple-element.46), channel_id=1, source_target_pairs={{0,1},{1,0},{2,3},{3,2},{4,5},{5,4},{6,7},{7,6},{8,9},{9,8},{10,11... | collective-permute-start | bytes 786440 | tf_op jit(solution)/shard_map/ppermute | solution.py:349
  43.1 9.8 %collective-permute-start.4 = (f32[64,4,256]{2,1,0:T(4,128)S(1)}, f32[64,4,256]{2,1,0:T(4,128)S(1)}, u32[]{:S(2)}, u32[]{:S(2)}) collective-permute-start(f32[64,4,256]{2,1,0:T(4,128)S(1)} %get-tuple-element.45), channel_id=1, source_target_pairs={{1,2},{2,1},{3,4},{4,3},{5,6},{6,5},{7,8},{8,7},{9,10},{10,9},{11,... | collective-permute-start | bytes 786440 | tf_op jit(solution)/shard_map/ppermute | solution.py:350
  50.3 9.7 %collective-permute-start.7 = (f32[64,4,256]{2,1,0:T(4,128)S(1)}, f32[64,4,256]{2,1,0:T(4,128)S(1)}, u32[]{:S(2)}, u32[]{:S(2)}) collective-permute-start(f32[64,4,256]{2,1,0:T(4,128)S(1)} %get-tuple-element.52), channel_id=1, source_target_pairs={{0,1},{1,0},{2,3},{3,2},{4,5},{5,4},{6,7},{7,6},{8,9},{9,8},{10,11... | collective-permute-start | bytes 786440 | tf_op jit(solution)/shard_map/ppermute | solution.py:349
  56.2 9.8 %collective-permute-start.6 = (f32[64,4,256]{2,1,0:T(4,128)S(1)}, f32[64,4,256]{2,1,0:T(4,128)S(1)}, u32[]{:S(2)}, u32[]{:S(2)}) collective-permute-start(f32[64,4,256]{2,1,0:T(4,128)S(1)} %get-tuple-element.51), channel_id=1, source_target_pairs={{1,2},{2,1},{3,4},{4,3},{5,6},{6,5},{7,8},{8,7},{9,10},{10,9},{11,... | collective-permute-start | bytes 786440 | tf_op jit(solution)/shard_map/ppermute | solution.py:350
  63.3 10.3 %collective-permute-start.9 = (f32[64,4,256]{2,1,0:T(4,128)S(1)}, f32[64,4,256]{2,1,0:T(4,128)S(1)}, u32[]{:S(2)}, u32[]{:S(2)}) collective-permute-start(f32[64,4,256]{2,1,0:T(4,128)S(1)} %get-tuple-element.58), channel_id=1, source_target_pairs={{0,1},{1,0},{2,3},{3,2},{4,5},{5,4},{6,7},{7,6},{8,9},{9,8},{10,11... | collective-permute-start | bytes 786440 | tf_op jit(solution)/shard_map/ppermute | solution.py:349
  69.3 9.8 %collective-permute-start.8 = (f32[64,4,256]{2,1,0:T(4,128)S(1)}, f32[64,4,256]{2,1,0:T(4,128)S(1)}, u32[]{:S(2)}, u32[]{:S(2)}) collective-permute-start(f32[64,4,256]{2,1,0:T(4,128)S(1)} %get-tuple-element.57), channel_id=1, source_target_pairs={{1,2},{2,1},{3,4},{4,3},{5,6},{6,5},{7,8},{8,7},{9,10},{10,9},{11,... | collective-permute-start | bytes 786440 | tf_op jit(solution)/shard_map/ppermute | solution.py:350
  77.2 9.0 %collective-permute-start.11 = (f32[64,4,256]{2,1,0:T(4,128)S(1)}, f32[64,4,256]{2,1,0:T(4,128)S(1)}, u32[]{:S(2)}, u32[]{:S(2)}) collective-permute-start(f32[64,4,256]{2,1,0:T(4,128)S(1)} %get-tuple-element.64), channel_id=1, source_target_pairs={{0,1},{1,0},{2,3},{3,2},{4,5},{5,4},{6,7},{7,6},{8,9},{9,8},{10,11... | collective-permute-start | bytes 786440 | tf_op jit(solution)/shard_map/ppermute | solution.py:349
  82.3 5.0 %copy-start.1 = (f32[1,64,16,256]{3,2,1,0:T(8,128)S(1)}, f32[1,64,16,256]{3,2,1,0:T(8,128)}, u32[]{:S(2)}) copy-start(f32[1,64,16,256]{3,2,1,0:T(8,128)} %param.14) | copy-start | bytes 3145732
  82.3 9.9 %collective-permute-start.10 = (f32[64,4,256]{2,1,0:T(4,128)S(1)}, f32[64,4,256]{2,1,0:T(4,128)S(1)}, u32[]{:S(2)}, u32[]{:S(2)}) collective-permute-start(f32[64,4,256]{2,1,0:T(4,128)S(1)} %get-tuple-element.63), channel_id=1, source_target_pairs={{1,2},{2,1},{3,4},{4,3},{5,6},{6,5},{7,8},{8,7},{9,10},{10,9},{11,... | collective-permute-start | bytes 786440 | tf_op jit(solution)/shard_map/ppermute | solution.py:350

commit v7 on v6

--- a/solution.py
+++ b/solution.py
@@ -157,9 +157,11 @@
     )(current, previous, lo, hi, speed_sq, forward, source, imaging)
 
 
-def tile_kernel(moment, tile_ref, cur_ref, prev_ref, halo_ref, vel_ref, fwd_ref, src_ref, img_ref,
-                chain_ref, next_ref, img_out_ref, edge_ref, pad_ref):
-    del chain_ref
+def tile_kernel(moment, chained, tile_ref, cur_ref, prev_ref, halo_ref, vel_ref, fwd_ref, src_ref,
+                img_ref, *rest):
+    if chained:
+        rest = rest[1:]
+    next_ref, img_out_ref, edge_ref, pad_ref = rest
     cells_y, cells_x, cells_z = cur_ref.shape
     width = halo_ref.shape[1]
     part = cells_x // 2
@@ -241,13 +243,20 @@
     src_spec = pl.BlockSpec(source.shape, lambda i, t: (0, 0, 0))
     f32 = jnp.float32
     cells = cells_y * part * cells_z
+    chained = chain is not None
+    in_specs = [whole, half, rim, half, fwd_spec, src_spec, half]
+    operands = [tile, current, previous, halo_rim, speed_sq, forward, source, imaging]
+    aliases = {7: 1}
+    if chained:
+        in_specs.append(pl.BlockSpec(memory_space=pl.ANY))
+        operands.append(chain)
+        aliases[8] = 0
     return pl.pallas_call(
-        functools.partial(tile_kernel, moment),
+        functools.partial(tile_kernel, moment, chained),
         grid_spec=pltpu.PrefetchScalarGridSpec(
             num_scalar_prefetch=1,
             grid=(1,),
-            in_specs=[whole, half, rim, half, fwd_spec, src_spec, half,
-                      pl.BlockSpec(memory_space=pl.ANY)],
+            in_specs=in_specs,
             out_specs=(half, half, rim),
             scratch_shapes=[pltpu.VMEM((cells_y + 8, cells_x + 16, cells_z), f32)],
         ),
@@ -256,12 +265,12 @@
             jax.ShapeDtypeStruct(current.shape, f32),
             jax.ShapeDtypeStruct(halo_rim.shape, f32),
         ),
-        input_output_aliases={7: 1, 8: 0},
+        input_output_aliases=aliases,
         cost_estimate=pl.CostEstimate(
             flops=60 * cells, bytes_accessed=28 * cells, transcendentals=0
         ),
         compiler_params=pltpu.CompilerParams(vmem_limit_bytes=48 * 1024 * 1024),
-    )(tile, current, previous, halo_rim, speed_sq, forward, source, imaging, chain)
+    )(*operands)
 
 
 def halo(first, last):
@@ -350,7 +359,7 @@
         far_halo = lax.ppermute(far_edge, "space", across)
         partial_next, imaging, near_edge = tile_call(
             moment, tile_near, current, previous, near_halo, speed_sq, forward, source,
-            imaging, jnp.zeros_like(current),
+            imaging, None,
         )
         advanced, imaging, far_edge = tile_call(
             moment, tile_far, current, previous, far_halo, speed_sq, forward, source,

time: 123 us -> 123 us (level)
  local copies, waits for them, and re-layouts: 5.49 us -> 3.76 us
  waiting for transfers between devices: 11.3 us -> 12.9 us
    another operation x8 -> x1, local copies, waits for them, and re-layouts: 1.8 us -> 0.01 us
    ppermute x6, waiting for transfers between devices: 10.5 us -> 12.1 us  [local(): far_halo = lax.ppermute(far_edge, 'space', across)]
  transfers between devices with their start and end apart: 13 -> 13, of which waited for: 6 -> 6; matrix products, arithmetic and copies ran while one was open for 9% -> 8% of each run, Pallas kernels for 30% -> 30%
where the time goes in v7:
time: 123 us; the launch traced here: 122 us
  Pallas kernels  40.6 us (33%)
  starting transfers between devices  28.7 us (23%)
  blocking collectives  23.4 us (19%)
  waiting for transfers between devices  12.9 us (10%)
  other arithmetic  7.26 us (6%)
  local copies, waits for them, and re-layouts  3.76 us (3%)
  matrix products  3.4 us (3%)
  between operations  1.65 us (1%)
    pallas_call x12, Pallas kernels, tile_call(): pl.pallas_call(functools.partial(tile_kernel, moment, chained), grid_spec...  40.6 us
    all_to_all x1, blocking collectives, local(): lax.all_to_all(placed, 'shot', split_axis=0, concat_axis=0, tiled=True)  23.4 us
    ppermute x6, starting transfers between devices, local(): far_halo = lax.ppermute(far_edge, 'space', across)  21.9 us
    ppermute x6, waiting for transfers between devices, local(): far_halo = lax.ppermute(far_edge, 'space', across)  12.1 us
    all_to_all x1, starting transfers between devices, local(): lax.all_to_all(buffer, 'space', split_axis=0, concat_axis=0, tiled=True)  5.26 us
  transfers between devices with their start and end apart: 13, of which 6 were waited for; matrix products, arithmetic and copies ran while one was open for 8% of the time, Pallas kernels for 30%

profile of v7, /device:TPU:97, one launch (start us, length us, event | category | flops | bytes accessed | tf_op | source)
XLA Modules:
  0.0 121.6 jit_solution(11821749962360937070)
XLA Ops:
  0.6 0.0 copy-start
  0.7 2.1 %slice_select_fusion = (f32[64,4,256]{2,1,0:T(4,128)S(1)}, f32[64,4,256]{2,1,0:T(4,128)}) fusion(f32[64,16,256]{2,1,0:T(8,128)} %bitcast.69, pred[]{:T(512)S(6)} %eq.56), kind=kLoop, calls=%fused_computation.11 | loop fusion | flops 131072 | bytes 1048577 | tf_op jit(solution)/shard_map/jit(_where)/select_n | solution.py:355
  2.7 0.7 collective-permute-start.1
  3.4 0.7 fusion.10
  4.1 0.6 reduce-window.6
  4.7 0.2 slice_reduce_fusion
  4.9 0.8 fusion.9
  5.7 0.7 multiply_add_fusion
  6.3 0.7 convert_bitcast_fusion
  7.0 0.0 copy-done
  7.0 1.0 fusion.3
  8.0 0.5 fusion.5
  8.5 0.1 reshape.105
  8.7 0.7 reshape.119
  9.4 5.3 %all-to-all-start = ((f32[16,1,336]{2,1,0:T(1,128)}), f32[16,1,336]{2,1,0:T(1,128)S(1)}, u32[]{:S(2)}, u32[]{:S(2)}) async-start(f32[16,1,336]{2,1,0:T(1,128)} %reshape.119), calls=%async_computation | async-start | bytes 49152 | tf_op jit(solution)/shard_map/all_to_all | solution.py:326
  14.7 3.4 %collective-permute-start = (f32[64,4,256]{2,1,0:T(4,128)}, f32[64,4,256]{2,1,0:T(4,128)S(1)}, u32[]{:S(2)}, u32[]{:S(2)}) collective-permute-start(f32[64,4,256]{2,1,0:T(4,128)} %get-tuple-element.71), channel_id=1, source_target_pairs={{1,2},{2,1},{3,4},{4,3},{5,6},{6,5},{7,8},{8,7},{9,10},{10,9},{11,... | collective-permute-start | bytes 786440 | tf_op jit(solution)/shard_map/ppermute | solution.py:359
  18.0 0.8 all-to-all-done
  18.8 0.5 broadcast.131
  19.3 0.7 reduce.4
  20.1 0.1 reshape.120
  20.1 0.0 copy-start.2
  20.2 0.1 reshape.106
  20.3 1.9 %fusion = f32[1024,6]{1,0:T(8,128)S(1)} fusion(s32[1024]{0:T(1024)S(1)} %iota_add_fusion, s32[768]{0:T(1024)S(1)} %fusion.20, f32[768,7]{0,1:T(8,128)S(1)} %reshape.106), kind=kOutput, calls=%fused_computation.2 | convolution fusion | flops 58195968 | bytes 53248 | tf_op jit(solution)/shard_map/dot_general | solution.py:332
  22.2 0.0 collective-permute-done.1.halo_ref
  22.2 0.1 broadcast_in_dim.37.img_ref
  22.3 0.0 copy-start.3
  22.3 1.2 copy-done.3
  23.6 3.3 %shard_map.104 = (f32[64,16,256]{2,1,0:T(8,128)S(1)}, f32[64,16,256]{2,1,0:T(8,128)S(1)}, f32[64,4,256]{2,1,0:T(4,128)S(1)}) custom-call(s32[1]{0:T(128)} %bitcast.12.tile_ref, f32[64,16,256]{2,1,0:T(8,128)S(1)} %bitcast.70, f32[64,16,256]{2,1,0:T(8,128)S(1)} %bitcast.74, ...), custom_call_target="tpu_custom_call", output_to_operand_aliasing={{1}: (7, {})} | custom-call | flops 7864320 | bytes 3670016 | tf_op jit(solution)/shard_map/pallas_call | solution.py:254
  26.8 0.5 collective-permute-start.3
  27.3 0.0 collective-permute-done.halo_ref
  27.3 3.2 %shard_map.105 = (f32[64,16,256]{2,1,0:T(8,128)S(1)}, f32[64,16,256]{2,1,0:T(8,128)S(1)}, f32[64,4,256]{2,1,0:T(4,128)S(1)}) custom-call(s32[1]{0:T(128)} %bitcast.1.tile_ref, f32[64,16,256]{2,1,0:T(8,128)S(1)} %bitcast.71, f32[64,16,256]{2,1,0:T(8,128)S(1)} %bitcast.75, ...), custom_call_target="tpu_custom_call", output_to_operand_aliasing={{1}: (7, {}), {0}: (8, {})} | custom-call | flops 7864320 | bytes 3670016 | tf_op jit(solution)/shard_map/pallas_call | solution.py:254
  30.5 3.7 %collective-permute-start.2 = (f32[64,4,256]{2,1,0:T(4,128)S(1)}, f32[64,4,256]{2,1,0:T(4,128)S(1)}, u32[]{:S(2)}, u32[]{:S(2)}) collective-permute-start(f32[64,4,256]{2,1,0:T(4,128)S(1)} %get-tuple-element.39), channel_id=1, source_target_pairs={{1,2},{2,1},{3,4},{4,3},{5,6},{6,5},{7,8},{8,7},{9,10},{10,9},{11,... | collective-permute-start | bytes 786440 | tf_op jit(solution)/shard_map/ppermute | solution.py:359
  34.2 0.0 collective-permute-done.3.halo_ref
  34.2 3.3 %shard_map.106 = (f32[64,16,256]{2,1,0:T(8,128)S(1)}, f32[64,16,256]{2,1,0:T(8,128)S(1)}, f32[64,4,256]{2,1,0:T(4,128)S(1)}) custom-call(s32[1]{0:T(128)} %bitcast.12.tile_ref, f32[64,16,256]{2,1,0:T(8,128)S(1)} %get-tuple-element.38.cur_ref.prev_ref, f32[64,16,256]{2,1,0:T(8,128)S(1)} %bitcast.72, ...), custom_call_target="tpu_custom_call", output_to_operand_aliasing={{1}: (7, {})} | custom-call | flops 7864320 | bytes 3670016 | tf_op jit(solution)/shard_map/pallas_call | solution.py:254
  37.5 0.1 collective-permute-start.5
  37.6 2.7 %collective-permute-done.2.halo_ref = f32[64,4,256]{2,1,0:T(4,128)S(1)} collective-permute-done((f32[64,4,256]{2,1,0:T(4,128)S(1)}, f32[64,4,256]{2,1,0:T(4,128)S(1)}, u32[]{:S(2)}, u32[]{:S(2)}) %collective-permute-start.2) | collective-permute-done | bytes 262176 | tf_op jit(solution)/shard_map/ppermute | solution.py:359
  40.3 3.2 %shard_map.107 = (f32[64,16,256]{2,1,0:T(8,128)S(1)}, f32[64,16,256]{2,1,0:T(8,128)S(1)}, f32[64,4,256]{2,1,0:T(4,128)S(1)}) custom-call(s32[1]{0:T(128)} %bitcast.1.tile_ref, f32[64,16,256]{2,1,0:T(8,128)S(1)} %get-tuple-element.38.cur_ref.prev_ref, f32[64,16,256]{2,1,0:T(8,128)S(1)} %bitcast.73, ...), custom_call_target="tpu_custom_call", output_to_operand_aliasing={{1}: (7, {}), {0}: (8, {})} | custom-call | flops 7864320 | bytes 3670016 | tf_op jit(solution)/shard_map/pallas_call | solution.py:254
  43.6 3.7 %collective-permute-start.4 = (f32[64,4,256]{2,1,0:T(4,128)S(1)}, f32[64,4,256]{2,1,0:T(4,128)S(1)}, u32[]{:S(2)}, u32[]{:S(2)}) collective-permute-start(f32[64,4,256]{2,1,0:T(4,128)S(1)} %get-tuple-element.45), channel_id=1, source_target_pairs={{1,2},{2,1},{3,4},{4,3},{5,6},{6,5},{7,8},{8,7},{9,10},{10,9},{11,... | collective-permute-start | bytes 786440 | tf_op jit(solution)/shard_map/ppermute | solution.py:359
  47.3 0.0 collective-permute-done.5.halo_ref
  47.3 3.3 %shard_map.108 = (f32[64,16,256]{2,1,0:T(8,128)S(1)}, f32[64,16,256]{2,1,0:T(8,128)S(1)}, f32[64,4,256]{2,1,0:T(4,128)S(1)}) custom-call(s32[1]{0:T(128)} %bitcast.12.tile_ref, f32[64,16,256]{2,1,0:T(8,128)S(1)} %get-tuple-element.44.cur_ref.prev_ref, f32[64,16,256]{2,1,0:T(8,128)S(1)} %get-tuple-element.38.cur_ref.prev_ref, ...), custom_call_target="tpu_custom_call", output_to_operand_aliasing={{1}: (7, {})} | custom-call | flops 7864320 | bytes 3670016 | tf_op jit(solution)/shard_map/pallas_call | solution.py:254
  50.6 0.1 collective-permute-start.7
  50.7 2.7 %collective-permute-done.4.halo_ref = f32[64,4,256]{2,1,0:T(4,128)S(1)} collective-permute-done((f32[64,4,256]{2,1,0:T(4,128)S(1)}, f32[64,4,256]{2,1,0:T(4,128)S(1)}, u32[]{:S(2)}, u32[]{:S(2)}) %collective-permute-start.4) | collective-permute-done | bytes 262176 | tf_op jit(solution)/shard_map/ppermute | solution.py:359
  53.4 3.2 %shard_map.109 = (f32[64,16,256]{2,1,0:T(8,128)S(1)}, f32[64,16,256]{2,1,0:T(8,128)S(1)}, f32[64,4,256]{2,1,0:T(4,128)S(1)}) custom-call(s32[1]{0:T(128)} %bitcast.1.tile_ref, f32[64,16,256]{2,1,0:T(8,128)S(1)} %get-tuple-element.44.cur_ref.prev_ref, ...), custom_call_target="tpu_custom_call", output_to_operand_aliasing={{1}: (7, {}), {0}: (8, {})} | custom-call | flops 7864320 | bytes 3670016 | tf_op jit(solution)/shard_map/pallas_call | solution.py:254
  56.7 3.7 %collective-permute-start.6 = (f32[64,4,256]{2,1,0:T(4,128)S(1)}, f32[64,4,256]{2,1,0:T(4,128)S(1)}, u32[]{:S(2)}, u32[]{:S(2)}) collective-permute-start(f32[64,4,256]{2,1,0:T(4,128)S(1)} %get-tuple-element.51), channel_id=1, source_target_pairs={{1,2},{2,1},{3,4},{4,3},{5,6},{6,5},{7,8},{8,7},{9,10},{10,9},{11,... | collective-permute-start | bytes 786440 | tf_op jit(solution)/shard_map/ppermute | solution.py:359
  60.4 0.0 collective-permute-done.7.halo_ref
  60.4 3.3 %shard_map.110 = (f32[64,16,256]{2,1,0:T(8,128)S(1)}, f32[64,16,256]{2,1,0:T(8,128)S(1)}, f32[64,4,256]{2,1,0:T(4,128)S(1)}) custom-call(s32[1]{0:T(128)} %bitcast.12.tile_ref, f32[64,16,256]{2,1,0:T(8,128)S(1)} %get-tuple-element.50.cur_ref.prev_ref, f32[64,16,256]{2,1,0:T(8,128)S(1)} %get-tuple-element.44.cur_ref.prev_ref, ...), custom_call_target="tpu_custom_call", output_to_operand_aliasing={{1}: (7, {})} | custom-call | flops 7864320 | bytes 3670016 | tf_op jit(solution)/shard_map/pallas_call | solution.py:254
  63.7 0.1 collective-permute-start.9
  63.8 2.7 %collective-permute-done.6.halo_ref = f32[64,4,256]{2,1,0:T(4,128)S(1)} collective-permute-done((f32[64,4,256]{2,1,0:T(4,128)S(1)}, f32[64,4,256]{2,1,0:T(4,128)S(1)}, u32[]{:S(2)}, u32[]{:S(2)}) %collective-permute-start.6) | collective-permute-done | bytes 262176 | tf_op jit(solution)/shard_map/ppermute | solution.py:359
  66.5 3.2 %shard_map.111 = (f32[64,16,256]{2,1,0:T(8,128)S(1)}, f32[64,16,256]{2,1,0:T(8,128)S(1)}, f32[64,4,256]{2,1,0:T(4,128)S(1)}) custom-call(s32[1]{0:T(128)} %bitcast.1.tile_ref, f32[64,16,256]{2,1,0:T(8,128)S(1)} %get-tuple-element.50.cur_ref.prev_ref, ...), custom_call_target="tpu_custom_call", output_to_operand_aliasing={{1}: (7, {}), {0}: (8, {})} | custom-call | flops 7864320 | bytes 3670016 | tf_op jit(solution)/shard_map/pallas_call | solution.py:254
  69.7 3.7 %collective-permute-start.8 = (f32[64,4,256]{2,1,0:T(4,128)S(1)}, f32[64,4,256]{2,1,0:T(4,128)S(1)}, u32[]{:S(2)}, u32[]{:S(2)}) collective-permute-start(f32[64,4,256]{2,1,0:T(4,128)S(1)} %get-tuple-element.57), channel_id=1, source_target_pairs={{1,2},{2,1},{3,4},{4,3},{5,6},{6,5},{7,8},{8,7},{9,10},{10,9},{11,... | collective-permute-start | bytes 786440 | tf_op jit(solution)/shard_map/ppermute | solution.py:359
  74.1 0.0 collective-permute-done.9.halo_ref
  74.1 3.5 %shard_map.112 = (f32[64,16,256]{2,1,0:T(8,128)S(1)}, f32[64,16,256]{2,1,0:T(8,128)S(1)}, f32[64,4,256]{2,1,0:T(4,128)S(1)}) custom-call(s32[1]{0:T(128)} %bitcast.12.tile_ref, f32[64,16,256]{2,1,0:T(8,128)S(1)} %get-tuple-element.56.cur_ref.prev_ref, f32[64,16,256]{2,1,0:T(8,128)S(1)} %get-tuple-element.50.cur_ref.prev_ref, ...), custom_call_target="tpu_custom_call", output_to_operand_aliasing={{1}: (7, {})} | custom-call | flops 7864320 | bytes 3670016 | tf_op jit(solution)/shard_map/pallas_call | solution.py:254
  77.6 0.1 collective-permute-start.11
  77.7 1.9 %collective-permute-done.8.halo_ref = f32[64,4,256]{2,1,0:T(4,128)S(1)} collective-permute-done((f32[64,4,256]{2,1,0:T(4,128)S(1)}, f32[64,4,256]{2,1,0:T(4,128)S(1)}, u32[]{:S(2)}, u32[]{:S(2)}) %collective-permute-start.8) | collective-permute-done | bytes 262176 | tf_op jit(solution)/shard_map/ppermute | solution.py:359
  79.5 3.3 %shard_map.113 = (f32[64,16,256]{2,1,0:T(8,128)S(1)}, f32[64,16,256]{2,1,0:T(8,128)S(1)}, f32[64,4,256]{2,1,0:T(4,128)S(1)}) custom-call(s32[1]{0:T(128)} %bitcast.1.tile_ref, f32[64,16,256]{2,1,0:T(8,128)S(1)} %get-tuple-element.56.cur_ref.prev_ref, ...), custom_call_target="tpu_custom_call", output_to_operand_aliasing={{1}: (7, {}), {0}: (8, {})} | custom-call | flops 7864320 | bytes 3670016 | tf_op jit(solution)/shard_map/pallas_call | solution.py:254
  82.9 3.7 %collective-permute-start.10 = (f32[64,4,256]{2,1,0:T(4,128)S(1)}, f32[64,4,256]{2,1,0:T(4,128)S(1)}, u32[]{:S(2)}, u32[]{:S(2)}) collective-permute-start(f32[64,4,256]{2,1,0:T(4,128)S(1)} %get-tuple-element.63), channel_id=1, source_target_pairs={{1,2},{2,1},{3,4},{4,3},{5,6},{6,5},{7,8},{8,7},{9,10},{10,9},{11,... | collective-permute-start | bytes 786440 | tf_op jit(solution)/shard_map/ppermute | solution.py:359
  86.7 0.0 collective-permute-done.11.halo_ref
  86.7 3.9 %shard_map.114 = (f32[64,16,256]{2,1,0:T(8,128)}, f32[64,16,256]{2,1,0:T(8,128)S(1)}, f32[64,4,256]{2,1,0:T(4,128)}) custom-call(s32[1]{0:T(128)} %bitcast.12.tile_ref, f32[64,16,256]{2,1,0:T(8,128)S(1)} %get-tuple-element.62.cur_ref, f32[64,16,256]{2,1,0:T(8,128)S(1)} %get-tuple-element.56.cur_ref.prev_ref, ...), custom_call_target="tpu_custom_call", output_to_operand_aliasing={{1}: (7, {})} | custom-call | flops 7864320 | bytes 3670016 | tf_op jit(solution)/shard_map/pallas_call | solution.py:254
  90.6 2.1 %collective-permute-done.10.halo_ref = f32[64,4,256]{2,1,0:T(4,128)S(1)} collective-permute-done((f32[64,4,256]{2,1,0:T(4,128)S(1)}, f32[64,4,256]{2,1,0:T(4,128)S(1)}, u32[]{:S(2)}, u32[]{:S(2)}) %collective-permute-start.10) | collective-permute-done | bytes 262176 | tf_op jit(solution)/shard_map/ppermute | solution.py:359
  92.7 3.9 %shard_map.115 = (f32[64,16,256]{2,1,0:T(8,128)}, f32[64,16,256]{2,1,0:T(8,128)S(1)}, f32[64,4,256]{2,1,0:T(4,128)}) custom-call(s32[1]{0:T(128)} %bitcast.1.tile_ref, f32[64,16,256]{2,1,0:T(8,128)S(1)} %get-tuple-element.62.cur_ref, f32[64,16,256]{2,1,0:T(8,128)S(1)} %get-tuple-element.56.cur_ref.prev_ref, ...), custom_call_target="tpu_custom_call", output_to_operand_aliasing={{1}: (7, {}), {0}: (8, {})} | custom-call | flops 7864320 | bytes 3670016 | tf_op jit(solution)/shard_map/pallas_call | solution.py:254
  96.5 0.7 gather_fusion
  97.2 0.2 select_select_fusion
  97.5 23.4 %all_to_all.10 = f32[8,10,16,256]{3,2,1,0:T(8,128)S(1)} all-to-all(f32[8,10,16,256]{3,2,1,0:T(8,128)S(1)} %select_select_fusion), channel_id=1, replica_groups=mesh['shot'=8,'space'=16] {'shot'}, dimensions={0} | all-to-all | bytes 2621440 | tf_op jit(solution)/shard_map/all_to_all | solution.py:375
  120.9 0.8 reduce_sum.19
  (12 shorter events, 0.1 us)
Async XLA Ops:
  0.6 6.4 %copy-start = (bf16[1,256,1536]{2,1,0:T(8,128)(2,1)S(1)}, bf16[1,256,1536]{2,1,0:T(8,128)(2,1)}, u32[]{:S(2)}) copy-start(bf16[1,256,1536]{2,1,0:T(8,128)(2,1)} %param.9) | copy-start | bytes 2359300
  2.7 19.5 %collective-permute-start.1 = (f32[64,4,256]{2,1,0:T(4,128)S(1)}, f32[64,4,256]{2,1,0:T(4,128)S(1)}, u32[]{:S(2)}, u32[]{:S(2)}) collective-permute-start(f32[64,4,256]{2,1,0:T(4,128)S(1)} %get-tuple-element.70), channel_id=1, source_target_pairs={{0,1},{1,0},{2,3},{3,2},{4,5},{5,4},{6,7},{7,6},{8,9},{9,8},{10,11... | collective-permute-start | bytes 786440 | tf_op jit(solution)/shard_map/ppermute | solution.py:358
  9.4 9.4 %all-to-all-start = ((f32[16,1,336]{2,1,0:T(1,128)}), f32[16,1,336]{2,1,0:T(1,128)S(1)}, u32[]{:S(2)}, u32[]{:S(2)}) async-start(f32[16,1,336]{2,1,0:T(1,128)} %reshape.119), calls=%async_computation | async-start | bytes 49152 | tf_op jit(solution)/shard_map/all_to_all | solution.py:326
  14.7 12.6 %collective-permute-start = (f32[64,4,256]{2,1,0:T(4,128)}, f32[64,4,256]{2,1,0:T(4,128)S(1)}, u32[]{:S(2)}, u32[]{:S(2)}) collective-permute-start(f32[64,4,256]{2,1,0:T(4,128)} %get-tuple-element.71), channel_id=1, source_target_pairs={{1,2},{2,1},{3,4},{4,3},{5,6},{6,5},{7,8},{8,7},{9,10},{10,9},{11,... | collective-permute-start | bytes 786440 | tf_op jit(solution)/shard_map/ppermute | solution.py:359
  20.1 2.2 %copy-start.2 = (f32[1,64,16,256]{3,2,1,0:T(8,128)S(1)}, f32[1,64,16,256]{3,2,1,0:T(8,128)}, u32[]{:S(2)}) copy-start(f32[1,64,16,256]{3,2,1,0:T(8,128)} %param.16) | copy-start | bytes 3145732
  22.3 1.2 %copy-start.3 = (f32[1,64,16,256]{3,2,1,0:T(8,128)S(1)}, f32[1,64,16,256]{3,2,1,0:T(8,128)}, u32[]{:S(2)}) copy-start(f32[1,64,16,256]{3,2,1,0:T(8,128)} %param.15) | copy-start | bytes 3145732
  26.8 7.4 %collective-permute-start.3 = (f32[64,4,256]{2,1,0:T(4,128)S(1)}, f32[64,4,256]{2,1,0:T(4,128)S(1)}, u32[]{:S(2)}, u32[]{:S(2)}) collective-permute-start(f32[64,4,256]{2,1,0:T(4,128)S(1)} %get-tuple-element.40), channel_id=1, source_target_pairs={{0,1},{1,0},{2,3},{3,2},{4,5},{5,4},{6,7},{7,6},{8,9},{9,8},{10,11... | collective-permute-start | bytes 786440 | tf_op jit(solution)/shard_map/ppermute | solution.py:358
  30.5 9.8 %collective-permute-start.2 = (f32[64,4,256]{2,1,0:T(4,128)S(1)}, f32[64,4,256]{2,1,0:T(4,128)S(1)}, u32[]{:S(2)}, u32[]{:S(2)}) collective-permute-start(f32[64,4,256]{2,1,0:T(4,128)S(1)} %get-tuple-element.39), channel_id=1, source_target_pairs={{1,2},{2,1},{3,4},{4,3},{5,6},{6,5},{7,8},{8,7},{9,10},{10,9},{11,... | collective-permute-start | bytes 786440 | tf_op jit(solution)/shard_map/ppermute | solution.py:359
  37.5 9.8 %collective-permute-start.5 = (f32[64,4,256]{2,1,0:T(4,128)S(1)}, f32[64,4,256]{2,1,0:T(4,128)S(1)}, u32[]{:S(2)}, u32[]{:S(2)}) collective-permute-start(f32[64,4,256]{2,1,0:T(4,128)S(1)} %get-tuple-element.46), channel_id=1, source_target_pairs={{0,1},{1,0},{2,3},{3,2},{4,5},{5,4},{6,7},{7,6},{8,9},{9,8},{10,11... | collective-permute-start | bytes 786440 | tf_op jit(solution)/shard_map/ppermute | solution.py:358
  43.6 9.8 %collective-permute-start.4 = (f32[64,4,256]{2,1,0:T(4,128)S(1)}, f32[64,4,256]{2,1,0:T(4,128)S(1)}, u32[]{:S(2)}, u32[]{:S(2)}) collective-permute-start(f32[64,4,256]{2,1,0:T(4,128)S(1)} %get-tuple-element.45), channel_id=1, source_target_pairs={{1,2},{2,1},{3,4},{4,3},{5,6},{6,5},{7,8},{8,7},{9,10},{10,9},{11,... | collective-permute-start | bytes 786440 | tf_op jit(solution)/shard_map/ppermute | solution.py:359
  50.6 9.8 %collective-permute-start.7 = (f32[64,4,256]{2,1,0:T(4,128)S(1)}, f32[64,4,256]{2,1,0:T(4,128)S(1)}, u32[]{:S(2)}, u32[]{:S(2)}) collective-permute-start(f32[64,4,256]{2,1,0:T(4,128)S(1)} %get-tuple-element.52), channel_id=1, source_target_pairs={{0,1},{1,0},{2,3},{3,2},{4,5},{5,4},{6,7},{7,6},{8,9},{9,8},{10,11... | collective-permute-start | bytes 786440 | tf_op jit(solution)/shard_map/ppermute | solution.py:358
  56.7 9.8 %collective-permute-start.6 = (f32[64,4,256]{2,1,0:T(4,128)S(1)}, f32[64,4,256]{2,1,0:T(4,128)S(1)}, u32[]{:S(2)}, u32[]{:S(2)}) collective-permute-start(f32[64,4,256]{2,1,0:T(4,128)S(1)} %get-tuple-element.51), channel_id=1, source_target_pairs={{1,2},{2,1},{3,4},{4,3},{5,6},{6,5},{7,8},{8,7},{9,10},{10,9},{11,... | collective-permute-start | bytes 786440 | tf_op jit(solution)/shard_map/ppermute | solution.py:359
  63.7 10.4 %collective-permute-start.9 = (f32[64,4,256]{2,1,0:T(4,128)S(1)}, f32[64,4,256]{2,1,0:T(4,128)S(1)}, u32[]{:S(2)}, u32[]{:S(2)}) collective-permute-start(f32[64,4,256]{2,1,0:T(4,128)S(1)} %get-tuple-element.58), channel_id=1, source_target_pairs={{0,1},{1,0},{2,3},{3,2},{4,5},{5,4},{6,7},{7,6},{8,9},{9,8},{10,11... | collective-permute-start | bytes 786440 | tf_op jit(solution)/shard_map/ppermute | solution.py:358
  69.7 9.8 %collective-permute-start.8 = (f32[64,4,256]{2,1,0:T(4,128)S(1)}, f32[64,4,256]{2,1,0:T(4,128)S(1)}, u32[]{:S(2)}, u32[]{:S(2)}) collective-permute-start(f32[64,4,256]{2,1,0:T(4,128)S(1)} %get-tuple-element.57), channel_id=1, source_target_pairs={{1,2},{2,1},{3,4},{4,3},{5,6},{6,5},{7,8},{8,7},{9,10},{10,9},{11,... | collective-permute-start | bytes 786440 | tf_op jit(solution)/shard_map/ppermute | solution.py:359
  77.6 9.1 %collective-permute-start.11 = (f32[64,4,256]{2,1,0:T(4,128)S(1)}, f32[64,4,256]{2,1,0:T(4,128)S(1)}, u32[]{:S(2)}, u32[]{:S(2)}) collective-permute-start(f32[64,4,256]{2,1,0:T(4,128)S(1)} %get-tuple-element.64), channel_id=1, source_target_pairs={{0,1},{1,0},{2,3},{3,2},{4,5},{5,4},{6,7},{7,6},{8,9},{9,8},{10,11... | collective-permute-start | bytes 786440 | tf_op jit(solution)/shard_map/ppermute | solution.py:358
  79.5 7.1 %copy-start.1 = (f32[1,64,16,256]{3,2,1,0:T(8,128)S(1)}, f32[1,64,16,256]{3,2,1,0:T(8,128)}, u32[]{:S(2)}) copy-start(f32[1,64,16,256]{3,2,1,0:T(8,128)} %param.14) | copy-start | bytes 3145732
  82.9 9.8 %collective-permute-start.10 = (f32[64,4,256]{2,1,0:T(4,128)S(1)}, f32[64,4,256]{2,1,0:T(4,128)S(1)}, u32[]{:S(2)}, u32[]{:S(2)}) collective-permute-start(f32[64,4,256]{2,1,0:T(4,128)S(1)} %get-tuple-element.63), channel_id=1, source_target_pairs={{1,2},{2,1},{3,4},{4,3},{5,6},{6,5},{7,8},{8,7},{9,10},{10,9},{11,... | collective-permute-start | bytes 786440 | tf_op jit(solution)/shard_map/ppermute | solution.py:359

commit v8 on v7

--- a/solution.py
+++ b/solution.py
@@ -273,6 +273,44 @@
     )(*operands)
 
 
+def split_dot(select, table):
+    high = table.astype(jnp.bfloat16)
+    rest = table - high.astype(jnp.float32)
+    middle = rest.astype(jnp.bfloat16)
+    low = (rest - middle.astype(jnp.float32)).astype(jnp.bfloat16)
+    total = jnp.dot(select, high, preferred_element_type=jnp.float32)
+    total = total + jnp.dot(select, middle, preferred_element_type=jnp.float32)
+    return total + jnp.dot(select, low, preferred_element_type=jnp.float32)
+
+
+def route_kernel(slot_count, traces_ref, filter_ref, tile_col_ref, tile_row_ref, cell_ref, out_ref):
+    records = traces_ref.shape[0]
+    columns = filter_ref.shape[0]
+    values = lax.dot_general(
+        traces_ref[...], filter_ref[...], (((1,), (1,)), ((), ())),
+        preferred_element_type=jnp.float32,
+    )
+    lane = lax.broadcasted_iota(jnp.int32, (records, columns), 1)
+    cell = jnp.broadcast_to((cell_ref[...] + 1).astype(jnp.float32), (records, columns))
+    payload = jnp.where(lane == columns - 2, cell, values)
+    earlier = lax.broadcasted_iota(jnp.int32, (records, records), 0)
+    later = lax.broadcasted_iota(jnp.int32, (records, records), 1)
+    same = (tile_col_ref[...] == tile_row_ref[...]) & (earlier < later)
+    rank = jnp.sum(same.astype(jnp.int32), axis=0, keepdims=True)
+    slot = tile_row_ref[...] * slot_count + rank
+    slots = out_ref.shape[0]
+    placing = (lax.broadcasted_iota(jnp.int32, (slots, records), 0) == slot).astype(jnp.bfloat16)
+    out_ref[...] = split_dot(placing, payload)
+
+
+def gather_kernel(cells_ref, arrived_ref, out_ref):
+    surface = out_ref.shape[0]
+    slots = arrived_ref.shape[0]
+    cell_index = lax.broadcasted_iota(jnp.int32, (surface, slots), 0) + 1
+    gathering = (cell_index == cells_ref[...]).astype(jnp.bfloat16)
+    out_ref[...] = split_dot(gathering, arrived_ref[...])
+
+
 def halo(first, last):
     axis = "space"
     devices = lax.axis_size(axis)
@@ -308,34 +346,35 @@
     trace_rows = residual[0]
     tile_ids = record_tile[0, :, 0]
     cell_ids = record_cell[0]
-    one_hot = (tile_ids[:, None] == jnp.arange(tiles_count, dtype=jnp.int32)[None, :]).astype(
-        jnp.int32
+    slots = tiles_count * slot_count
+    columns = step_count + 2
+    filter_rows = jnp.concatenate(
+        [time_filter, jnp.zeros((columns - step_count,) + time_filter.shape[1:], time_filter.dtype)]
     )
-    order_rank = jnp.sum((jnp.cumsum(one_hot, axis=0) - 1) * one_hot, axis=1)
-    slot_index = tile_ids * slot_count + order_rank
-    filtered = jnp.dot(trace_rows, time_filter.T, preferred_element_type=jnp.float32)
-    payload = jnp.concatenate(
-        [filtered, (cell_ids + 1).astype(jnp.float32)[:, None]], axis=1
+    vmem = pl.BlockSpec(memory_space=pltpu.VMEM)
+    buffer = pl.pallas_call(
+        functools.partial(route_kernel, slot_count),
+        out_shape=jax.ShapeDtypeStruct((slots, columns), jnp.float32),
+        in_specs=[vmem] * 5,
+        out_specs=vmem,
+    )(
+        trace_rows,
+        filter_rows,
+        tile_ids.reshape(record_count, 1),
+        tile_ids.reshape(1, record_count),
+        cell_ids.reshape(record_count, 1),
     )
-    slots = tiles_count * slot_count
-    placing = (
-        slot_index[None, :] == jnp.arange(slots, dtype=jnp.int32)[:, None]
-    ).astype(jnp.float32)
-    buffer = jnp.dot(placing, payload, precision=lax.Precision.HIGHEST)
-    buffer = buffer.reshape(tiles_count, slot_count, step_count + 1)
+    buffer = buffer.reshape(tiles_count, slot_count, columns)
     arrived = lax.all_to_all(buffer, "space", split_axis=0, concat_axis=0, tiled=True)
-    arrived = arrived.reshape(slots, step_count + 1)
-    cell_of = arrived[:, step_count].astype(jnp.int32)
-    gathering = (
-        cell_of[:, None] == jnp.arange(1, surface + 1, dtype=jnp.int32)[None, :]
-    ).astype(jnp.float32)
-    source = lax.dot_general(
-        gathering,
-        arrived[:, :step_count],
-        (((0,), (0,)), ((), ())),
-        precision=lax.Precision.HIGHEST,
-    )
-    source = source.reshape(cells_y, cells_x, step_count)
+    arrived = arrived.reshape(slots, columns)
+    cells_row = arrived[:, step_count].astype(jnp.int32).reshape(1, slots)
+    source = pl.pallas_call(
+        gather_kernel,
+        out_shape=jax.ShapeDtypeStruct((surface, columns), jnp.float32),
+        in_specs=[vmem] * 2,
+        out_specs=vmem,
+    )(cells_row, arrived)
+    source = source.reshape(cells_y, cells_x, columns)
     shift_rows = offsets[0]
     speed_sq = velocity[0]
     previous = adjoint_prev[0]

time: 123 us -> 131 us (1.065)
  Pallas kernels: 40.6 us -> 46.8 us
  local copies, waits for them, and re-layouts: 3.76 us -> 9.51 us
  waiting for transfers between devices: 12.9 us -> 16.3 us
  matrix products: 3.4 us -> 0 us
  other arithmetic: 7.26 us -> 4.02 us
    pallas_call x0 -> x2, Pallas kernels: none -> 6.33 us  [the longest x1 3.2 us: local(): pl.pallas_call(gather_kernel, out_shape=jax.ShapeDtypeStruct((surface, co...]
    dot_general x3 -> x0, matrix products: 3.4 us -> none  [the longest x1 1.89 us: local(): lax.dot_general(gathering, arrived[:, :step_count], (((0,), (0,)), ((), (...]
    all_to_all x1, waiting for transfers between devices: 0.79 us -> 4.17 us  [local(): lax.all_to_all(buffer, 'space', split_axis=0, concat_axis=0, tiled=True)]
    another operation x1 -> x2, local copies, waits for them, and re-layouts: 0.01 us -> 2.94 us  [the longest x1 1.48 us: local(): tile_ids.reshape(record_count, 1)]
    ppermute x6, starting transfers between devices: 21.9 us -> 20.5 us  [local(): far_halo = lax.ppermute(far_edge, 'space', across)]
    unnamed x10 -> x18, local copies, waits for them, and re-layouts: 2.03 us -> 2.78 us
  transfers between devices with their start and end apart: 13 -> 13, of which waited for: 6 -> 6; matrix products, arithmetic and copies ran while one was open for 8% -> 6% of each run, Pallas kernels for 30% -> 33%
where the time goes in v8:
time: 131 us; the launch traced here: 130 us
  Pallas kernels  46.8 us (36%)
  starting transfers between devices  28.4 us (22%)
  blocking collectives  23.4 us (18%)
  waiting for transfers between devices  16.3 us (12%)
  local copies, waits for them, and re-layouts  9.51 us (7%)
  other arithmetic  4.02 us (3%)
  between operations  1.63 us (1%)
    pallas_call x12, Pallas kernels, tile_call(): pl.pallas_call(functools.partial(tile_kernel, moment, chained), grid_spec...  40.5 us
    all_to_all x1, blocking collectives, local(): lax.all_to_all(placed, 'shot', split_axis=0, concat_axis=0, tiled=True)  23.4 us
    ppermute x6, starting transfers between devices, local(): far_halo = lax.ppermute(far_edge, 'space', across)  20.5 us
    ppermute x6, waiting for transfers between devices, local(): far_halo = lax.ppermute(far_edge, 'space', across)  12.1 us
    all_to_all x1, starting transfers between devices, local(): lax.all_to_all(buffer, 'space', split_axis=0, concat_axis=0, tiled=True)  6.32 us
    all_to_all x1, waiting for transfers between devices, local(): lax.all_to_all(buffer, 'space', split_axis=0, concat_axis=0, tiled=True)  4.17 us
    pallas_call x1, Pallas kernels, local(): pl.pallas_call(gather_kernel, out_shape=jax.ShapeDtypeStruct((surface, co...  3.2 us
    pallas_call x1, Pallas kernels, local(): pl.pallas_call(functools.partial(route_kernel, slot_count), out_shape=jax...  3.13 us
  transfers between devices with their start and end apart: 13, of which 6 were waited for; matrix products, arithmetic and copies ran while one was open for 6% of the time, Pallas kernels for 33%

profile of v8, /device:TPU:97, one launch (start us, length us, event | category | flops | bytes accessed | tf_op | source)
XLA Modules:
  0.0 130.0 jit_solution(17501005571839272283)
XLA Ops:
  0.7 2.0 %slice_select_fusion = (f32[64,4,256]{2,1,0:T(4,128)S(1)}, f32[64,4,256]{2,1,0:T(4,128)}) fusion(f32[64,16,256]{2,1,0:T(8,128)} %bitcast.46, pred[]{:T(512)S(6)} %eq.5), kind=kLoop, calls=%fused_computation.4 | loop fusion | flops 131072 | bytes 1048577 | tf_op jit(solution)/shard_map/jit(_where)/select_n | solution.py:394
  2.6 0.7 collective-permute-start.1
  3.3 1.9 %collective-permute-start = (f32[64,4,256]{2,1,0:T(4,128)}, f32[64,4,256]{2,1,0:T(4,128)S(1)}, u32[]{:S(2)}, u32[]{:S(2)}) collective-permute-start(f32[64,4,256]{2,1,0:T(4,128)} %get-tuple-element.71), channel_id=1, source_target_pairs={{1,2},{2,1},{3,4},{4,3},{5,6},{6,5},{7,8},{8,7},{9,10},{10,9},{11,... | collective-permute-start | bytes 786440 | tf_op jit(solution)/shard_map/ppermute | solution.py:398
  5.2 1.5 %copy.31.tile_col_ref = s32[256,1]{1,0:T(8,128)} copy(s32[256,1]{0,1:T(1,128)} %bitcast.73) | data formatting | bytes 2048 | tf_op jit(solution)/shard_map/reshape;squeeze | solution.py:363
  6.7 1.5 %copy.32.cell_ref = s32[256,1]{1,0:T(8,128)} copy(s32[256,1]{0,1:T(1,128)} %bitcast.75) | data formatting | bytes 2048 | tf_op jit(solution)/shard_map/reshape;squeeze | solution.py:365
  8.2 0.6 concatenate.3.filter_ref
  8.8 3.1 %shard_map.104 = f32[768,8]{1,0:T(8,128)} custom-call(bf16[256,1536]{1,0:T(8,128)(2,1)} %bitcast.70, bf16[8,1536]{1,0:T(8,128)(2,1)} %concatenate.3.filter_ref, s32[256,1]{1,0:T(8,128)} %copy.31.tile_col_ref, s32[1,256]{1,0:T(1,128)} %bitcast.74, s32[256,1]{1,0:T(8,128)} %copy.32.cell_ref), custom_call_target="tpu_custom_call" | custom-call | tf_op jit(solution)/shard_map/pallas_call | solution.py:355
  11.9 1.1 copy.33
  13.0 0.7 reshape.82
  13.8 6.3 %all-to-all-start = ((f32[16,1,384]{2,1,0:T(1,128)}), f32[16,1,384]{2,1,0:T(1,128)S(1)}, u32[]{:S(2)}, u32[]{:S(2)}) async-start(f32[16,1,384]{2,1,0:T(1,128)} %reshape.82), calls=%async_computation | async-start | bytes 49152 | tf_op jit(solution)/shard_map/all_to_all | solution.py:368
  20.1 4.2 %all-to-all-done = f32[16,1,384]{2,1,0:T(1,128)S(1)} async-done(((f32[16,1,384]{2,1,0:T(1,128)}), f32[16,1,384]{2,1,0:T(1,128)S(1)}, u32[]{:S(2)}, u32[]{:S(2)}) %all-to-all-start) | async-done | bytes 24608 | tf_op jit(solution)/shard_map/all_to_all | solution.py:368
  24.3 0.5 broadcast.86
  24.8 0.7 reduce.2
  25.5 0.1 reshape.83
  25.6 0.0 copy-start.2
  25.6 0.0 copy-start.3
  25.6 0.2 copy.34
  25.8 0.3 fusion
  26.1 0.6 convert_element_type.14.cells_ref
  26.7 0.0 copy-done.6
  26.7 3.2 %shard_map.105 = f32[1024,8]{1,0:T(8,128)} custom-call(s32[1,768]{1,0:T(1,128)} %convert_element_type.14.cells_ref, f32[768,8]{1,0:T(8,128)} %bitcast.67), custom_call_target="tpu_custom_call" | custom-call | tf_op jit(solution)/shard_map/pallas_call | solution.py:371
  29.9 0.0 collective-permute-done.1.halo_ref
  29.9 0.7 copy-done.4
  30.6 0.1 broadcast_in_dim.32.img_ref
  30.7 0.0 copy-done.2
  30.7 0.3 copy-done.1
  31.0 0.9 copy-done.5
  32.0 3.3 %shard_map.106 = (f32[64,16,256]{2,1,0:T(8,128)S(1)}, f32[64,16,256]{2,1,0:T(8,128)S(1)}, f32[64,4,256]{2,1,0:T(4,128)S(1)}) custom-call(s32[1]{0:T(128)} %bitcast.13.tile_ref, f32[64,16,256]{2,1,0:T(8,128)S(1)} %bitcast.47, f32[64,16,256]{2,1,0:T(8,128)S(1)} %bitcast.51, f32[64,4,256]{2,1,0:T(4,128)S(1)} %copy-done.5, ...), custom_call_target="tpu_custom_call", output_to_operand_aliasing={{1}: (7, {})} | custom-call | flops 7864320 | bytes 3670016 | tf_op jit(solution)/shard_map/pallas_call | solution.py:254
  35.2 0.5 collective-permute-start.3
  35.7 0.0 collective-permute-done.halo_ref
  35.7 3.2 %shard_map.107 = (f32[64,16,256]{2,1,0:T(8,128)S(1)}, f32[64,16,256]{2,1,0:T(8,128)S(1)}, f32[64,4,256]{2,1,0:T(4,128)S(1)}) custom-call(s32[1]{0:T(128)} %bitcast.1.tile_ref, f32[64,16,256]{2,1,0:T(8,128)S(1)} %bitcast.48, f32[64,16,256]{2,1,0:T(8,128)S(1)} %bitcast.52, ...), custom_call_target="tpu_custom_call", output_to_operand_aliasing={{1}: (7, {}), {0}: (8, {})} | custom-call | flops 7864320 | bytes 3670016 | tf_op jit(solution)/shard_map/pallas_call | solution.py:254
  39.0 3.7 %collective-permute-start.2 = (f32[64,4,256]{2,1,0:T(4,128)S(1)}, f32[64,4,256]{2,1,0:T(4,128)S(1)}, u32[]{:S(2)}, u32[]{:S(2)}) collective-permute-start(f32[64,4,256]{2,1,0:T(4,128)S(1)} %get-tuple-element.39), channel_id=1, source_target_pairs={{1,2},{2,1},{3,4},{4,3},{5,6},{6,5},{7,8},{8,7},{9,10},{10,9},{11,... | collective-permute-start | bytes 786440 | tf_op jit(solution)/shard_map/ppermute | solution.py:398
  42.7 0.0 collective-permute-done.3.halo_ref
  42.7 3.3 %shard_map.108 = (f32[64,16,256]{2,1,0:T(8,128)S(1)}, f32[64,16,256]{2,1,0:T(8,128)S(1)}, f32[64,4,256]{2,1,0:T(4,128)S(1)}) custom-call(s32[1]{0:T(128)} %bitcast.13.tile_ref, f32[64,16,256]{2,1,0:T(8,128)S(1)} %get-tuple-element.38.cur_ref.prev_ref, f32[64,16,256]{2,1,0:T(8,128)S(1)} %bitcast.49, ...), custom_call_target="tpu_custom_call", output_to_operand_aliasing={{1}: (7, {})} | custom-call | flops 7864320 | bytes 3670016 | tf_op jit(solution)/shard_map/pallas_call | solution.py:254
  45.9 0.1 collective-permute-start.5
  46.0 2.7 %collective-permute-done.2.halo_ref = f32[64,4,256]{2,1,0:T(4,128)S(1)} collective-permute-done((f32[64,4,256]{2,1,0:T(4,128)S(1)}, f32[64,4,256]{2,1,0:T(4,128)S(1)}, u32[]{:S(2)}, u32[]{:S(2)}) %collective-permute-start.2) | collective-permute-done | bytes 262176 | tf_op jit(solution)/shard_map/ppermute | solution.py:398
  48.8 3.2 %shard_map.109 = (f32[64,16,256]{2,1,0:T(8,128)S(1)}, f32[64,16,256]{2,1,0:T(8,128)S(1)}, f32[64,4,256]{2,1,0:T(4,128)S(1)}) custom-call(s32[1]{0:T(128)} %bitcast.1.tile_ref, f32[64,16,256]{2,1,0:T(8,128)S(1)} %get-tuple-element.38.cur_ref.prev_ref, f32[64,16,256]{2,1,0:T(8,128)S(1)} %bitcast.50, ...), custom_call_target="tpu_custom_call", output_to_operand_aliasing={{1}: (7, {}), {0}: (8, {})} | custom-call | flops 7864320 | bytes 3670016 | tf_op jit(solution)/shard_map/pallas_call | solution.py:254
  52.0 3.7 %collective-permute-start.4 = (f32[64,4,256]{2,1,0:T(4,128)S(1)}, f32[64,4,256]{2,1,0:T(4,128)S(1)}, u32[]{:S(2)}, u32[]{:S(2)}) collective-permute-start(f32[64,4,256]{2,1,0:T(4,128)S(1)} %get-tuple-element.45), channel_id=1, source_target_pairs={{1,2},{2,1},{3,4},{4,3},{5,6},{6,5},{7,8},{8,7},{9,10},{10,9},{11,... | collective-permute-start | bytes 786440 | tf_op jit(solution)/shard_map/ppermute | solution.py:398
  55.7 0.0 collective-permute-done.5.halo_ref
  55.7 3.3 %shard_map.110 = (f32[64,16,256]{2,1,0:T(8,128)S(1)}, f32[64,16,256]{2,1,0:T(8,128)S(1)}, f32[64,4,256]{2,1,0:T(4,128)S(1)}) custom-call(s32[1]{0:T(128)} %bitcast.13.tile_ref, f32[64,16,256]{2,1,0:T(8,128)S(1)} %get-tuple-element.44.cur_ref.prev_ref, f32[64,16,256]{2,1,0:T(8,128)S(1)} %get-tuple-element.38.cur_ref.prev_ref, ...), custom_call_target="tpu_custom_call", output_to_operand_aliasing={{1}: (7, {})} | custom-call | flops 7864320 | bytes 3670016 | tf_op jit(solution)/shard_map/pallas_call | solution.py:254
  59.0 0.1 collective-permute-start.7
  59.1 2.7 %collective-permute-done.4.halo_ref = f32[64,4,256]{2,1,0:T(4,128)S(1)} collective-permute-done((f32[64,4,256]{2,1,0:T(4,128)S(1)}, f32[64,4,256]{2,1,0:T(4,128)S(1)}, u32[]{:S(2)}, u32[]{:S(2)}) %collective-permute-start.4) | collective-permute-done | bytes 262176 | tf_op jit(solution)/shard_map/ppermute | solution.py:398
  61.8 3.2 %shard_map.111 = (f32[64,16,256]{2,1,0:T(8,128)S(1)}, f32[64,16,256]{2,1,0:T(8,128)S(1)}, f32[64,4,256]{2,1,0:T(4,128)S(1)}) custom-call(s32[1]{0:T(128)} %bitcast.1.tile_ref, f32[64,16,256]{2,1,0:T(8,128)S(1)} %get-tuple-element.44.cur_ref.prev_ref, ...), custom_call_target="tpu_custom_call", output_to_operand_aliasing={{1}: (7, {}), {0}: (8, {})} | custom-call | flops 7864320 | bytes 3670016 | tf_op jit(solution)/shard_map/pallas_call | solution.py:254
  65.1 3.7 %collective-permute-start.6 = (f32[64,4,256]{2,1,0:T(4,128)S(1)}, f32[64,4,256]{2,1,0:T(4,128)S(1)}, u32[]{:S(2)}, u32[]{:S(2)}) collective-permute-start(f32[64,4,256]{2,1,0:T(4,128)S(1)} %get-tuple-element.51), channel_id=1, source_target_pairs={{1,2},{2,1},{3,4},{4,3},{5,6},{6,5},{7,8},{8,7},{9,10},{10,9},{11,... | collective-permute-start | bytes 786440 | tf_op jit(solution)/shard_map/ppermute | solution.py:398
  68.8 0.0 collective-permute-done.7.halo_ref
  68.8 3.3 %shard_map.112 = (f32[64,16,256]{2,1,0:T(8,128)S(1)}, f32[64,16,256]{2,1,0:T(8,128)S(1)}, f32[64,4,256]{2,1,0:T(4,128)S(1)}) custom-call(s32[1]{0:T(128)} %bitcast.13.tile_ref, f32[64,16,256]{2,1,0:T(8,128)S(1)} %get-tuple-element.50.cur_ref.prev_ref, f32[64,16,256]{2,1,0:T(8,128)S(1)} %get-tuple-element.44.cur_ref.prev_ref, ...), custom_call_target="tpu_custom_call", output_to_operand_aliasing={{1}: (7, {})} | custom-call | flops 7864320 | bytes 3670016 | tf_op jit(solution)/shard_map/pallas_call | solution.py:254
  72.1 0.1 collective-permute-start.9
  72.2 2.7 %collective-permute-done.6.halo_ref = f32[64,4,256]{2,1,0:T(4,128)S(1)} collective-permute-done((f32[64,4,256]{2,1,0:T(4,128)S(1)}, f32[64,4,256]{2,1,0:T(4,128)S(1)}, u32[]{:S(2)}, u32[]{:S(2)}) %collective-permute-start.6) | collective-permute-done | bytes 262176 | tf_op jit(solution)/shard_map/ppermute | solution.py:398
  74.9 3.2 %shard_map.113 = (f32[64,16,256]{2,1,0:T(8,128)S(1)}, f32[64,16,256]{2,1,0:T(8,128)S(1)}, f32[64,4,256]{2,1,0:T(4,128)S(1)}) custom-call(s32[1]{0:T(128)} %bitcast.1.tile_ref, f32[64,16,256]{2,1,0:T(8,128)S(1)} %get-tuple-element.50.cur_ref.prev_ref, ...), custom_call_target="tpu_custom_call", output_to_operand_aliasing={{1}: (7, {}), {0}: (8, {})} | custom-call | flops 7864320 | bytes 3670016 | tf_op jit(solution)/shard_map/pallas_call | solution.py:254
  78.1 3.7 %collective-permute-start.8 = (f32[64,4,256]{2,1,0:T(4,128)S(1)}, f32[64,4,256]{2,1,0:T(4,128)S(1)}, u32[]{:S(2)}, u32[]{:S(2)}) collective-permute-start(f32[64,4,256]{2,1,0:T(4,128)S(1)} %get-tuple-element.57), channel_id=1, source_target_pairs={{1,2},{2,1},{3,4},{4,3},{5,6},{6,5},{7,8},{8,7},{9,10},{10,9},{11,... | collective-permute-start | bytes 786440 | tf_op jit(solution)/shard_map/ppermute | solution.py:398
  82.5 0.0 collective-permute-done.9.halo_ref
  82.5 3.3 %shard_map.114 = (f32[64,16,256]{2,1,0:T(8,128)S(1)}, f32[64,16,256]{2,1,0:T(8,128)S(1)}, f32[64,4,256]{2,1,0:T(4,128)S(1)}) custom-call(s32[1]{0:T(128)} %bitcast.13.tile_ref, f32[64,16,256]{2,1,0:T(8,128)S(1)} %get-tuple-element.56.cur_ref.prev_ref, f32[64,16,256]{2,1,0:T(8,128)S(1)} %get-tuple-element.50.cur_ref.prev_ref, ...), custom_call_target="tpu_custom_call", output_to_operand_aliasing={{1}: (7, {})} | custom-call | flops 7864320 | bytes 3670016 | tf_op jit(solution)/shard_map/pallas_call | solution.py:254
  85.8 0.3 collective-permute-start.11
  86.1 1.9 %collective-permute-done.8.halo_ref = f32[64,4,256]{2,1,0:T(4,128)S(1)} collective-permute-done((f32[64,4,256]{2,1,0:T(4,128)S(1)}, f32[64,4,256]{2,1,0:T(4,128)S(1)}, u32[]{:S(2)}, u32[]{:S(2)}) %collective-permute-start.8) | collective-permute-done | bytes 262176 | tf_op jit(solution)/shard_map/ppermute | solution.py:398
  87.9 3.3 %shard_map.115 = (f32[64,16,256]{2,1,0:T(8,128)S(1)}, f32[64,16,256]{2,1,0:T(8,128)S(1)}, f32[64,4,256]{2,1,0:T(4,128)S(1)}) custom-call(s32[1]{0:T(128)} %bitcast.1.tile_ref, f32[64,16,256]{2,1,0:T(8,128)S(1)} %get-tuple-element.56.cur_ref.prev_ref, ...), custom_call_target="tpu_custom_call", output_to_operand_aliasing={{1}: (7, {}), {0}: (8, {})} | custom-call | flops 7864320 | bytes 3670016 | tf_op jit(solution)/shard_map/pallas_call | solution.py:254
  91.3 3.7 %collective-permute-start.10 = (f32[64,4,256]{2,1,0:T(4,128)S(1)}, f32[64,4,256]{2,1,0:T(4,128)S(1)}, u32[]{:S(2)}, u32[]{:S(2)}) collective-permute-start(f32[64,4,256]{2,1,0:T(4,128)S(1)} %get-tuple-element.63), channel_id=1, source_target_pairs={{1,2},{2,1},{3,4},{4,3},{5,6},{6,5},{7,8},{8,7},{9,10},{10,9},{11,... | collective-permute-start | bytes 786440 | tf_op jit(solution)/shard_map/ppermute | solution.py:398
  95.1 0.0 collective-permute-done.11.halo_ref
  95.1 3.9 %shard_map.116 = (f32[64,16,256]{2,1,0:T(8,128)}, f32[64,16,256]{2,1,0:T(8,128)S(1)}, f32[64,4,256]{2,1,0:T(4,128)}) custom-call(s32[1]{0:T(128)} %bitcast.13.tile_ref, f32[64,16,256]{2,1,0:T(8,128)S(1)} %get-tuple-element.62.cur_ref, f32[64,16,256]{2,1,0:T(8,128)S(1)} %get-tuple-element.56.cur_ref.prev_ref, ...), custom_call_target="tpu_custom_call", output_to_operand_aliasing={{1}: (7, {})} | custom-call | flops 7864320 | bytes 3670016 | tf_op jit(solution)/shard_map/pallas_call | solution.py:254
  99.0 2.1 %collective-permute-done.10.halo_ref = f32[64,4,256]{2,1,0:T(4,128)S(1)} collective-permute-done((f32[64,4,256]{2,1,0:T(4,128)S(1)}, f32[64,4,256]{2,1,0:T(4,128)S(1)}, u32[]{:S(2)}, u32[]{:S(2)}) %collective-permute-start.10) | collective-permute-done | bytes 262176 | tf_op jit(solution)/shard_map/ppermute | solution.py:398
  101.1 3.9 %shard_map.117 = (f32[64,16,256]{2,1,0:T(8,128)}, f32[64,16,256]{2,1,0:T(8,128)S(1)}, f32[64,4,256]{2,1,0:T(4,128)}) custom-call(s32[1]{0:T(128)} %bitcast.1.tile_ref, f32[64,16,256]{2,1,0:T(8,128)S(1)} %get-tuple-element.62.cur_ref, f32[64,16,256]{2,1,0:T(8,128)S(1)} %get-tuple-element.56.cur_ref.prev_ref, ...), custom_call_target="tpu_custom_call", output_to_operand_aliasing={{1}: (7, {}), {0}: (8, {})} | custom-call | flops 7864320 | bytes 3670016 | tf_op jit(solution)/shard_map/pallas_call | solution.py:254
  105.0 0.7 gather_fusion
  105.6 0.2 select_select_fusion
  105.9 23.4 %all_to_all.10 = f32[8,10,16,256]{3,2,1,0:T(8,128)S(1)} all-to-all(f32[8,10,16,256]{3,2,1,0:T(8,128)S(1)} %select_select_fusion), channel_id=1, replica_groups=mesh['shot'=8,'space'=16] {'shot'}, dimensions={0} | all-to-all | bytes 2621440 | tf_op jit(solution)/shard_map/all_to_all | solution.py:414
  129.3 0.8 reduce_sum.9
  (12 shorter events, 0.0 us)
Async XLA Ops:
  0.6 7.6 %copy-start.7 = (bf16[6,1536]{1,0:T(8,128)(2,1)S(1)}, bf16[6,1536]{1,0:T(8,128)(2,1)}, u32[]{:S(2)}) copy-start(bf16[6,1536]{1,0:T(8,128)(2,1)} %param.12) | copy-start | bytes 55300
  2.6 27.2 %collective-permute-start.1 = (f32[64,4,256]{2,1,0:T(4,128)S(1)}, f32[64,4,256]{2,1,0:T(4,128)S(1)}, u32[]{:S(2)}, u32[]{:S(2)}) collective-permute-start(f32[64,4,256]{2,1,0:T(4,128)S(1)} %get-tuple-element.70), channel_id=1, source_target_pairs={{0,1},{1,0},{2,3},{3,2},{4,5},{5,4},{6,7},{7,6},{8,9},{9,8},{10,11... | collective-permute-start | bytes 786440 | tf_op jit(solution)/shard_map/ppermute | solution.py:397
  3.3 32.4 %collective-permute-start = (f32[64,4,256]{2,1,0:T(4,128)}, f32[64,4,256]{2,1,0:T(4,128)S(1)}, u32[]{:S(2)}, u32[]{:S(2)}) collective-permute-start(f32[64,4,256]{2,1,0:T(4,128)} %get-tuple-element.71), channel_id=1, source_target_pairs={{1,2},{2,1},{3,4},{4,3},{5,6},{6,5},{7,8},{8,7},{9,10},{10,9},{11,... | collective-permute-start | bytes 786440 | tf_op jit(solution)/shard_map/ppermute | solution.py:398
  13.8 10.5 %all-to-all-start = ((f32[16,1,384]{2,1,0:T(1,128)}), f32[16,1,384]{2,1,0:T(1,128)S(1)}, u32[]{:S(2)}, u32[]{:S(2)}) async-start(f32[16,1,384]{2,1,0:T(1,128)} %reshape.82), calls=%async_computation | async-start | bytes 49152 | tf_op jit(solution)/shard_map/all_to_all | solution.py:368
  25.6 5.1 %copy-start.2 = (f32[1,64,16,256]{3,2,1,0:T(8,128)S(1)}, f32[1,64,16,256]{3,2,1,0:T(8,128)}, u32[]{:S(2)}) copy-start(f32[1,64,16,256]{3,2,1,0:T(8,128)} %param.16) | copy-start | bytes 3145732
  25.6 5.1 %copy-start.3 = (f32[1,64,16,256]{3,2,1,0:T(8,128)S(1)}, f32[1,64,16,256]{3,2,1,0:T(8,128)}, u32[]{:S(2)}) copy-start(f32[1,64,16,256]{3,2,1,0:T(8,128)} %param.15) | copy-start | bytes 3145732
  25.8 0.9 copy-start.6
  29.9 1.1 copy-start.1
  29.9 0.7 copy-start.4
  31.0 0.9 copy-start.5
  35.2 7.4 %collective-permute-start.3 = (f32[64,4,256]{2,1,0:T(4,128)S(1)}, f32[64,4,256]{2,1,0:T(4,128)S(1)}, u32[]{:S(2)}, u32[]{:S(2)}) collective-permute-start(f32[64,4,256]{2,1,0:T(4,128)S(1)} %get-tuple-element.40), channel_id=1, source_target_pairs={{0,1},{1,0},{2,3},{3,2},{4,5},{5,4},{6,7},{7,6},{8,9},{9,8},{10,11... | collective-permute-start | bytes 786440 | tf_op jit(solution)/shard_map/ppermute | solution.py:397
  39.0 9.8 %collective-permute-start.2 = (f32[64,4,256]{2,1,0:T(4,128)S(1)}, f32[64,4,256]{2,1,0:T(4,128)S(1)}, u32[]{:S(2)}, u32[]{:S(2)}) collective-permute-start(f32[64,4,256]{2,1,0:T(4,128)S(1)} %get-tuple-element.39), channel_id=1, source_target_pairs={{1,2},{2,1},{3,4},{4,3},{5,6},{6,5},{7,8},{8,7},{9,10},{10,9},{11,... | collective-permute-start | bytes 786440 | tf_op jit(solution)/shard_map/ppermute | solution.py:398
  45.9 9.8 %collective-permute-start.5 = (f32[64,4,256]{2,1,0:T(4,128)S(1)}, f32[64,4,256]{2,1,0:T(4,128)S(1)}, u32[]{:S(2)}, u32[]{:S(2)}) collective-permute-start(f32[64,4,256]{2,1,0:T(4,128)S(1)} %get-tuple-element.46), channel_id=1, source_target_pairs={{0,1},{1,0},{2,3},{3,2},{4,5},{5,4},{6,7},{7,6},{8,9},{9,8},{10,11... | collective-permute-start | bytes 786440 | tf_op jit(solution)/shard_map/ppermute | solution.py:397
  52.0 9.8 %collective-permute-start.4 = (f32[64,4,256]{2,1,0:T(4,128)S(1)}, f32[64,4,256]{2,1,0:T(4,128)S(1)}, u32[]{:S(2)}, u32[]{:S(2)}) collective-permute-start(f32[64,4,256]{2,1,0:T(4,128)S(1)} %get-tuple-element.45), channel_id=1, source_target_pairs={{1,2},{2,1},{3,4},{4,3},{5,6},{6,5},{7,8},{8,7},{9,10},{10,9},{11,... | collective-permute-start | bytes 786440 | tf_op jit(solution)/shard_map/ppermute | solution.py:398
  59.0 9.8 %collective-permute-start.7 = (f32[64,4,256]{2,1,0:T(4,128)S(1)}, f32[64,4,256]{2,1,0:T(4,128)S(1)}, u32[]{:S(2)}, u32[]{:S(2)}) collective-permute-start(f32[64,4,256]{2,1,0:T(4,128)S(1)} %get-tuple-element.52), channel_id=1, source_target_pairs={{0,1},{1,0},{2,3},{3,2},{4,5},{5,4},{6,7},{7,6},{8,9},{9,8},{10,11... | collective-permute-start | bytes 786440 | tf_op jit(solution)/shard_map/ppermute | solution.py:397
  65.1 9.8 %collective-permute-start.6 = (f32[64,4,256]{2,1,0:T(4,128)S(1)}, f32[64,4,256]{2,1,0:T(4,128)S(1)}, u32[]{:S(2)}, u32[]{:S(2)}) collective-permute-start(f32[64,4,256]{2,1,0:T(4,128)S(1)} %get-tuple-element.51), channel_id=1, source_target_pairs={{1,2},{2,1},{3,4},{4,3},{5,6},{6,5},{7,8},{8,7},{9,10},{10,9},{11,... | collective-permute-start | bytes 786440 | tf_op jit(solution)/shard_map/ppermute | solution.py:398
  72.1 10.4 %collective-permute-start.9 = (f32[64,4,256]{2,1,0:T(4,128)S(1)}, f32[64,4,256]{2,1,0:T(4,128)S(1)}, u32[]{:S(2)}, u32[]{:S(2)}) collective-permute-start(f32[64,4,256]{2,1,0:T(4,128)S(1)} %get-tuple-element.58), channel_id=1, source_target_pairs={{0,1},{1,0},{2,3},{3,2},{4,5},{5,4},{6,7},{7,6},{8,9},{9,8},{10,11... | collective-permute-start | bytes 786440 | tf_op jit(solution)/shard_map/ppermute | solution.py:397
  78.1 9.8 %collective-permute-start.8 = (f32[64,4,256]{2,1,0:T(4,128)S(1)}, f32[64,4,256]{2,1,0:T(4,128)S(1)}, u32[]{:S(2)}, u32[]{:S(2)}) collective-permute-start(f32[64,4,256]{2,1,0:T(4,128)S(1)} %get-tuple-element.57), channel_id=1, source_target_pairs={{1,2},{2,1},{3,4},{4,3},{5,6},{6,5},{7,8},{8,7},{9,10},{10,9},{11,... | collective-permute-start | bytes 786440 | tf_op jit(solution)/shard_map/ppermute | solution.py:398
  85.8 9.3 %collective-permute-start.11 = (f32[64,4,256]{2,1,0:T(4,128)S(1)}, f32[64,4,256]{2,1,0:T(4,128)S(1)}, u32[]{:S(2)}, u32[]{:S(2)}) collective-permute-start(f32[64,4,256]{2,1,0:T(4,128)S(1)} %get-tuple-element.64), channel_id=1, source_target_pairs={{0,1},{1,0},{2,3},{3,2},{4,5},{5,4},{6,7},{7,6},{8,9},{9,8},{10,11... | collective-permute-start | bytes 786440 | tf_op jit(solution)/shard_map/ppermute | solution.py:397
  87.9 7.1 %copy-start = (f32[1,64,16,256]{3,2,1,0:T(8,128)S(1)}, f32[1,64,16,256]{3,2,1,0:T(8,128)}, u32[]{:S(2)}) copy-start(f32[1,64,16,256]{3,2,1,0:T(8,128)} %param.14) | copy-start | bytes 3145732
  91.3 9.8 %collective-permute-start.10 = (f32[64,4,256]{2,1,0:T(4,128)S(1)}, f32[64,4,256]{2,1,0:T(4,128)S(1)}, u32[]{:S(2)}, u32[]{:S(2)}) collective-permute-start(f32[64,4,256]{2,1,0:T(4,128)S(1)} %get-tuple-element.63), channel_id=1, source_target_pairs={{1,2},{2,1},{3,4},{4,3},{5,6},{6,5},{7,8},{8,7},{9,10},{10,9},{11,... | collective-permute-start | bytes 786440 | tf_op jit(solution)/shard_map/ppermute | solution.py:398

commit v9 on v7

--- a/solution.py
+++ b/solution.py
@@ -301,6 +301,7 @@
     record_count = residual.shape[1]
     cells_y = velocity.shape[1]
     cells_x = velocity.shape[2]
+    cells_z = velocity.shape[3]
     step_count = forward_accel.shape[1]
     slot_count = record_count * 3 // 16
     surface = cells_y * cells_x
@@ -308,10 +309,11 @@
     trace_rows = residual[0]
     tile_ids = record_tile[0, :, 0]
     cell_ids = record_cell[0]
-    one_hot = (tile_ids[:, None] == jnp.arange(tiles_count, dtype=jnp.int32)[None, :]).astype(
-        jnp.int32
+    record_order = jnp.arange(record_count, dtype=jnp.int32)
+    same_before = (tile_ids[:, None] == tile_ids[None, :]) & (
+        record_order[:, None] < record_order[None, :]
     )
-    order_rank = jnp.sum((jnp.cumsum(one_hot, axis=0) - 1) * one_hot, axis=1)
+    order_rank = jnp.sum(same_before.astype(jnp.int32), axis=0)
     slot_index = tile_ids * slot_count + order_rank
     filtered = jnp.dot(trace_rows, time_filter.T, preferred_element_type=jnp.float32)
     payload = jnp.concatenate(
@@ -349,11 +351,11 @@
     devices = lax.axis_size("space")
     within = [(i, i ^ 1) for i in range(devices)]
     across = [(i, i + 1 - 2 * ((i + 1) % 2)) for i in range(1, devices - 1)]
-    first = current[:, :width]
-    last = current[:, cells_x - width :]
-    even = odd == 0
-    near_edge = jnp.where(even, last, first)
-    far_edge = jnp.where(even, first, last)
+    zero = jnp.zeros((), jnp.int32)
+    near_start = (1 - odd) * (cells_x - width)
+    near_edge = lax.dynamic_slice(current, (zero, near_start, zero), (cells_y, width, cells_z))
+    far_start = odd * (cells_x - width)
+    far_edge = lax.dynamic_slice(current, (zero, far_start, zero), (cells_y, width, cells_z))
     for moment in range(step_count):
         near_halo = lax.ppermute(near_edge, "space", within)
         far_halo = lax.ppermute(far_edge, "space", across)

time: 123 us -> 121 us (0.984)
  other arithmetic: 7.26 us -> 3.99 us
  local copies, waits for them, and re-layouts: 3.76 us -> 5.64 us
    select_n x1 -> x0, other arithmetic: 2.07 us -> none  [local(): near_edge = jnp.where(even, last, first)]
    dynamic_slice x0 -> x1, local copies, waits for them, and re-layouts: none -> 2.07 us  [local(): lax.dynamic_slice(current, (zero, near_start, zero), (cells_y, width, cel...]
  transfers between devices with their start and end apart: 13 -> 13, of which waited for: 6 -> 6; matrix products, arithmetic and copies ran while one was open for 8% -> 7% of each run, Pallas kernels for 30% -> 30%
where the time goes in v9:
time: 121 us; the launch traced here: 120 us
  Pallas kernels  40.5 us (33%)
  starting transfers between devices  28.8 us (24%)
  blocking collectives  23.4 us (19%)
  waiting for transfers between devices  12.9 us (11%)
  local copies, waits for them, and re-layouts  5.64 us (5%)
  other arithmetic  3.99 us (3%)
  matrix products  3.4 us (3%)
  between operations  1.66 us (1%)
    pallas_call x12, Pallas kernels, tile_call(): pl.pallas_call(functools.partial(tile_kernel, moment, chained), grid_spec...  40.5 us
    all_to_all x1, blocking collectives, local(): lax.all_to_all(placed, 'shot', split_axis=0, concat_axis=0, tiled=True)  23.4 us
    ppermute x6, starting transfers between devices, local(): far_halo = lax.ppermute(far_edge, 'space', across)  21.9 us
    ppermute x6, waiting for transfers between devices, local(): far_halo = lax.ppermute(far_edge, 'space', across)  12.1 us
    all_to_all x1, starting transfers between devices, local(): lax.all_to_all(buffer, 'space', split_axis=0, concat_axis=0, tiled=True)  5.26 us
  transfers between devices with their start and end apart: 13, of which 6 were waited for; matrix products, arithmetic and copies ran while one was open for 7% of the time, Pallas kernels for 30%

profile of v9, /device:TPU:97, one launch (start us, length us, event | category | flops | bytes accessed | tf_op | source)
XLA Modules:
  0.0 120.3 jit_solution(8355188253386474474)
XLA Ops:
  0.6 0.0 copy-start
  0.7 2.1 %dynamic-slice_bitcast_fusion = (f32[64,4,256]{2,1,0:T(4,128)S(1)}, f32[64,4,256]{2,1,0:T(4,128)}) fusion(f32[1,64,16,256]{3,2,1,0:T(8,128)} %param.16, s32[]{:T(128)S(6)} %select_n.43, s32[]{:T(128)S(6)} %select_n.42), kind=kLoop, calls=%fused_computation.11 | loop fusion | bytes 1048584 | tf_op jit(solution)/shard_map/dynamic_slice | solution.py:356
  2.7 0.7 collective-permute-start.1
  3.4 0.9 convert_reduce_fusion
  4.3 0.7 multiply_add_fusion
  5.0 0.7 convert_bitcast_fusion
  5.6 0.0 copy-done
  5.7 1.0 fusion.3
  6.7 0.5 fusion.5
  7.2 0.1 reshape.89
  7.3 0.7 reshape.102
  8.0 5.3 %all-to-all-start = ((f32[16,1,336]{2,1,0:T(1,128)}), f32[16,1,336]{2,1,0:T(1,128)S(1)}, u32[]{:S(2)}, u32[]{:S(2)}) async-start(f32[16,1,336]{2,1,0:T(1,128)} %reshape.102), calls=%async_computation | async-start | bytes 49152 | tf_op jit(solution)/shard_map/all_to_all | solution.py:328
  13.3 3.4 %collective-permute-start = (f32[64,4,256]{2,1,0:T(4,128)}, f32[64,4,256]{2,1,0:T(4,128)S(1)}, u32[]{:S(2)}, u32[]{:S(2)}) collective-permute-start(f32[64,4,256]{2,1,0:T(4,128)} %get-tuple-element.71), channel_id=1, source_target_pairs={{1,2},{2,1},{3,4},{4,3},{5,6},{6,5},{7,8},{8,7},{9,10},{10,9},{11,... | collective-permute-start | bytes 786440 | tf_op jit(solution)/shard_map/ppermute | solution.py:361
  16.7 0.8 all-to-all-done
  17.5 0.5 broadcast.101
  18.0 0.7 reduce.2
  18.7 0.1 reshape.103
  18.8 0.0 copy-start.2
  18.8 0.1 reshape.90
  18.9 1.9 %fusion = f32[1024,6]{1,0:T(8,128)S(1)} fusion(s32[1024]{0:T(1024)S(1)} %iota_add_fusion, s32[768]{0:T(1024)S(1)} %fusion.18, f32[768,7]{0,1:T(8,128)S(1)} %reshape.90), kind=kOutput, calls=%fused_computation.2 | convolution fusion | flops 58195968 | bytes 53248 | tf_op jit(solution)/shard_map/dot_general | solution.py:334
  20.8 0.0 collective-permute-done.1.halo_ref
  20.8 0.1 broadcast_in_dim.38.img_ref
  20.9 0.0 copy-done.2
  20.9 0.0 copy-start.3
  21.0 1.2 %copy-done.3 = f32[1,64,16,256]{3,2,1,0:T(8,128)S(1)} copy-done((f32[1,64,16,256]{3,2,1,0:T(8,128)S(1)}, f32[1,64,16,256]{3,2,1,0:T(8,128)}, u32[]{:S(2)}) %copy-start.3) | copy-done | bytes 1048600
  22.2 3.3 %shard_map.104 = (f32[64,16,256]{2,1,0:T(8,128)S(1)}, f32[64,16,256]{2,1,0:T(8,128)S(1)}, f32[64,4,256]{2,1,0:T(4,128)S(1)}) custom-call(s32[1]{0:T(128)} %bitcast.11.tile_ref, f32[64,16,256]{2,1,0:T(8,128)S(1)} %bitcast.57, f32[64,16,256]{2,1,0:T(8,128)S(1)} %bitcast.61, ...), custom_call_target="tpu_custom_call", output_to_operand_aliasing={{1}: (7, {})} | custom-call | flops 7864320 | bytes 3670016 | tf_op jit(solution)/shard_map/pallas_call | solution.py:254
  25.4 0.5 collective-permute-start.3
  25.9 0.0 collective-permute-done.halo_ref
  25.9 3.2 %shard_map.105 = (f32[64,16,256]{2,1,0:T(8,128)S(1)}, f32[64,16,256]{2,1,0:T(8,128)S(1)}, f32[64,4,256]{2,1,0:T(4,128)S(1)}) custom-call(s32[1]{0:T(128)} %bitcast.1.tile_ref, f32[64,16,256]{2,1,0:T(8,128)S(1)} %bitcast.58, f32[64,16,256]{2,1,0:T(8,128)S(1)} %bitcast.62, ...), custom_call_target="tpu_custom_call", output_to_operand_aliasing={{1}: (7, {}), {0}: (8, {})} | custom-call | flops 7864320 | bytes 3670016 | tf_op jit(solution)/shard_map/pallas_call | solution.py:254
  29.2 3.7 %collective-permute-start.2 = (f32[64,4,256]{2,1,0:T(4,128)S(1)}, f32[64,4,256]{2,1,0:T(4,128)S(1)}, u32[]{:S(2)}, u32[]{:S(2)}) collective-permute-start(f32[64,4,256]{2,1,0:T(4,128)S(1)} %get-tuple-element.39), channel_id=1, source_target_pairs={{1,2},{2,1},{3,4},{4,3},{5,6},{6,5},{7,8},{8,7},{9,10},{10,9},{11,... | collective-permute-start | bytes 786440 | tf_op jit(solution)/shard_map/ppermute | solution.py:361
  32.9 0.0 collective-permute-done.3.halo_ref
  32.9 3.3 %shard_map.106 = (f32[64,16,256]{2,1,0:T(8,128)S(1)}, f32[64,16,256]{2,1,0:T(8,128)S(1)}, f32[64,4,256]{2,1,0:T(4,128)S(1)}) custom-call(s32[1]{0:T(128)} %bitcast.11.tile_ref, f32[64,16,256]{2,1,0:T(8,128)S(1)} %get-tuple-element.38.cur_ref.prev_ref, f32[64,16,256]{2,1,0:T(8,128)S(1)} %bitcast.59, ...), custom_call_target="tpu_custom_call", output_to_operand_aliasing={{1}: (7, {})} | custom-call | flops 7864320 | bytes 3670016 | tf_op jit(solution)/shard_map/pallas_call | solution.py:254
  36.2 0.1 collective-permute-start.5
  36.2 2.7 %collective-permute-done.2.halo_ref = f32[64,4,256]{2,1,0:T(4,128)S(1)} collective-permute-done((f32[64,4,256]{2,1,0:T(4,128)S(1)}, f32[64,4,256]{2,1,0:T(4,128)S(1)}, u32[]{:S(2)}, u32[]{:S(2)}) %collective-permute-start.2) | collective-permute-done | bytes 262176 | tf_op jit(solution)/shard_map/ppermute | solution.py:361
  39.0 3.2 %shard_map.107 = (f32[64,16,256]{2,1,0:T(8,128)S(1)}, f32[64,16,256]{2,1,0:T(8,128)S(1)}, f32[64,4,256]{2,1,0:T(4,128)S(1)}) custom-call(s32[1]{0:T(128)} %bitcast.1.tile_ref, f32[64,16,256]{2,1,0:T(8,128)S(1)} %get-tuple-element.38.cur_ref.prev_ref, f32[64,16,256]{2,1,0:T(8,128)S(1)} %bitcast.60, ...), custom_call_target="tpu_custom_call", output_to_operand_aliasing={{1}: (7, {}), {0}: (8, {})} | custom-call | flops 7864320 | bytes 3670016 | tf_op jit(solution)/shard_map/pallas_call | solution.py:254
  42.2 3.7 %collective-permute-start.4 = (f32[64,4,256]{2,1,0:T(4,128)S(1)}, f32[64,4,256]{2,1,0:T(4,128)S(1)}, u32[]{:S(2)}, u32[]{:S(2)}) collective-permute-start(f32[64,4,256]{2,1,0:T(4,128)S(1)} %get-tuple-element.45), channel_id=1, source_target_pairs={{1,2},{2,1},{3,4},{4,3},{5,6},{6,5},{7,8},{8,7},{9,10},{10,9},{11,... | collective-permute-start | bytes 786440 | tf_op jit(solution)/shard_map/ppermute | solution.py:361
  45.9 0.0 collective-permute-done.5.halo_ref
  45.9 3.3 %shard_map.108 = (f32[64,16,256]{2,1,0:T(8,128)S(1)}, f32[64,16,256]{2,1,0:T(8,128)S(1)}, f32[64,4,256]{2,1,0:T(4,128)S(1)}) custom-call(s32[1]{0:T(128)} %bitcast.11.tile_ref, f32[64,16,256]{2,1,0:T(8,128)S(1)} %get-tuple-element.44.cur_ref.prev_ref, f32[64,16,256]{2,1,0:T(8,128)S(1)} %get-tuple-element.38.cur_ref.prev_ref, ...), custom_call_target="tpu_custom_call", output_to_operand_aliasing={{1}: (7, {})} | custom-call | flops 7864320 | bytes 3670016 | tf_op jit(solution)/shard_map/pallas_call | solution.py:254
  49.2 0.1 collective-permute-start.7
  49.3 2.7 %collective-permute-done.4.halo_ref = f32[64,4,256]{2,1,0:T(4,128)S(1)} collective-permute-done((f32[64,4,256]{2,1,0:T(4,128)S(1)}, f32[64,4,256]{2,1,0:T(4,128)S(1)}, u32[]{:S(2)}, u32[]{:S(2)}) %collective-permute-start.4) | collective-permute-done | bytes 262176 | tf_op jit(solution)/shard_map/ppermute | solution.py:361
  52.0 3.2 %shard_map.109 = (f32[64,16,256]{2,1,0:T(8,128)S(1)}, f32[64,16,256]{2,1,0:T(8,128)S(1)}, f32[64,4,256]{2,1,0:T(4,128)S(1)}) custom-call(s32[1]{0:T(128)} %bitcast.1.tile_ref, f32[64,16,256]{2,1,0:T(8,128)S(1)} %get-tuple-element.44.cur_ref.prev_ref, ...), custom_call_target="tpu_custom_call", output_to_operand_aliasing={{1}: (7, {}), {0}: (8, {})} | custom-call | flops 7864320 | bytes 3670016 | tf_op jit(solution)/shard_map/pallas_call | solution.py:254
  55.3 3.7 %collective-permute-start.6 = (f32[64,4,256]{2,1,0:T(4,128)S(1)}, f32[64,4,256]{2,1,0:T(4,128)S(1)}, u32[]{:S(2)}, u32[]{:S(2)}) collective-permute-start(f32[64,4,256]{2,1,0:T(4,128)S(1)} %get-tuple-element.51), channel_id=1, source_target_pairs={{1,2},{2,1},{3,4},{4,3},{5,6},{6,5},{7,8},{8,7},{9,10},{10,9},{11,... | collective-permute-start | bytes 786440 | tf_op jit(solution)/shard_map/ppermute | solution.py:361
  59.0 0.0 collective-permute-done.7.halo_ref
  59.0 3.3 %shard_map.110 = (f32[64,16,256]{2,1,0:T(8,128)S(1)}, f32[64,16,256]{2,1,0:T(8,128)S(1)}, f32[64,4,256]{2,1,0:T(4,128)S(1)}) custom-call(s32[1]{0:T(128)} %bitcast.11.tile_ref, f32[64,16,256]{2,1,0:T(8,128)S(1)} %get-tuple-element.50.cur_ref.prev_ref, f32[64,16,256]{2,1,0:T(8,128)S(1)} %get-tuple-element.44.cur_ref.prev_ref, ...), custom_call_target="tpu_custom_call", output_to_operand_aliasing={{1}: (7, {})} | custom-call | flops 7864320 | bytes 3670016 | tf_op jit(solution)/shard_map/pallas_call | solution.py:254
  62.3 0.1 collective-permute-start.9
  62.4 2.7 %collective-permute-done.6.halo_ref = f32[64,4,256]{2,1,0:T(4,128)S(1)} collective-permute-done((f32[64,4,256]{2,1,0:T(4,128)S(1)}, f32[64,4,256]{2,1,0:T(4,128)S(1)}, u32[]{:S(2)}, u32[]{:S(2)}) %collective-permute-start.6) | collective-permute-done | bytes 262176 | tf_op jit(solution)/shard_map/ppermute | solution.py:361
  65.1 3.2 %shard_map.111 = (f32[64,16,256]{2,1,0:T(8,128)S(1)}, f32[64,16,256]{2,1,0:T(8,128)S(1)}, f32[64,4,256]{2,1,0:T(4,128)S(1)}) custom-call(s32[1]{0:T(128)} %bitcast.1.tile_ref, f32[64,16,256]{2,1,0:T(8,128)S(1)} %get-tuple-element.50.cur_ref.prev_ref, ...), custom_call_target="tpu_custom_call", output_to_operand_aliasing={{1}: (7, {}), {0}: (8, {})} | custom-call | flops 7864320 | bytes 3670016 | tf_op jit(solution)/shard_map/pallas_call | solution.py:254
  68.3 3.7 %collective-permute-start.8 = (f32[64,4,256]{2,1,0:T(4,128)S(1)}, f32[64,4,256]{2,1,0:T(4,128)S(1)}, u32[]{:S(2)}, u32[]{:S(2)}) collective-permute-start(f32[64,4,256]{2,1,0:T(4,128)S(1)} %get-tuple-element.57), channel_id=1, source_target_pairs={{1,2},{2,1},{3,4},{4,3},{5,6},{6,5},{7,8},{8,7},{9,10},{10,9},{11,... | collective-permute-start | bytes 786440 | tf_op jit(solution)/shard_map/ppermute | solution.py:361
  72.7 0.0 collective-permute-done.9.halo_ref
  72.7 3.3 %shard_map.112 = (f32[64,16,256]{2,1,0:T(8,128)S(1)}, f32[64,16,256]{2,1,0:T(8,128)S(1)}, f32[64,4,256]{2,1,0:T(4,128)S(1)}) custom-call(s32[1]{0:T(128)} %bitcast.11.tile_ref, f32[64,16,256]{2,1,0:T(8,128)S(1)} %get-tuple-element.56.cur_ref.prev_ref, f32[64,16,256]{2,1,0:T(8,128)S(1)} %get-tuple-element.50.cur_ref.prev_ref, ...), custom_call_target="tpu_custom_call", output_to_operand_aliasing={{1}: (7, {})} | custom-call | flops 7864320 | bytes 3670016 | tf_op jit(solution)/shard_map/pallas_call | solution.py:254
  76.0 0.3 collective-permute-start.11
  76.3 1.9 %collective-permute-done.8.halo_ref = f32[64,4,256]{2,1,0:T(4,128)S(1)} collective-permute-done((f32[64,4,256]{2,1,0:T(4,128)S(1)}, f32[64,4,256]{2,1,0:T(4,128)S(1)}, u32[]{:S(2)}, u32[]{:S(2)}) %collective-permute-start.8) | collective-permute-done | bytes 262176 | tf_op jit(solution)/shard_map/ppermute | solution.py:361
  78.1 0.0 copy-start.1
  78.1 3.3 %shard_map.113 = (f32[64,16,256]{2,1,0:T(8,128)S(1)}, f32[64,16,256]{2,1,0:T(8,128)S(1)}, f32[64,4,256]{2,1,0:T(4,128)S(1)}) custom-call(s32[1]{0:T(128)} %bitcast.1.tile_ref, f32[64,16,256]{2,1,0:T(8,128)S(1)} %get-tuple-element.56.cur_ref.prev_ref, ...), custom_call_target="tpu_custom_call", output_to_operand_aliasing={{1}: (7, {}), {0}: (8, {})} | custom-call | flops 7864320 | bytes 3670016 | tf_op jit(solution)/shard_map/pallas_call | solution.py:254
  81.5 3.7 %collective-permute-start.10 = (f32[64,4,256]{2,1,0:T(4,128)S(1)}, f32[64,4,256]{2,1,0:T(4,128)S(1)}, u32[]{:S(2)}, u32[]{:S(2)}) collective-permute-start(f32[64,4,256]{2,1,0:T(4,128)S(1)} %get-tuple-element.63), channel_id=1, source_target_pairs={{1,2},{2,1},{3,4},{4,3},{5,6},{6,5},{7,8},{8,7},{9,10},{10,9},{11,... | collective-permute-start | bytes 786440 | tf_op jit(solution)/shard_map/ppermute | solution.py:361
  85.3 0.0 collective-permute-done.11.halo_ref
  85.3 0.0 copy-done.1
  85.3 3.9 %shard_map.114 = (f32[64,16,256]{2,1,0:T(8,128)}, f32[64,16,256]{2,1,0:T(8,128)S(1)}, f32[64,4,256]{2,1,0:T(4,128)}) custom-call(s32[1]{0:T(128)} %bitcast.11.tile_ref, f32[64,16,256]{2,1,0:T(8,128)S(1)} %get-tuple-element.62.cur_ref, f32[64,16,256]{2,1,0:T(8,128)S(1)} %get-tuple-element.56.cur_ref.prev_ref, ...), custom_call_target="tpu_custom_call", output_to_operand_aliasing={{1}: (7, {})} | custom-call | flops 7864320 | bytes 3670016 | tf_op jit(solution)/shard_map/pallas_call | solution.py:254
  89.2 2.1 %collective-permute-done.10.halo_ref = f32[64,4,256]{2,1,0:T(4,128)S(1)} collective-permute-done((f32[64,4,256]{2,1,0:T(4,128)S(1)}, f32[64,4,256]{2,1,0:T(4,128)S(1)}, u32[]{:S(2)}, u32[]{:S(2)}) %collective-permute-start.10) | collective-permute-done | bytes 262176 | tf_op jit(solution)/shard_map/ppermute | solution.py:361
  91.3 3.9 %shard_map.115 = (f32[64,16,256]{2,1,0:T(8,128)}, f32[64,16,256]{2,1,0:T(8,128)S(1)}, f32[64,4,256]{2,1,0:T(4,128)}) custom-call(s32[1]{0:T(128)} %bitcast.1.tile_ref, f32[64,16,256]{2,1,0:T(8,128)S(1)} %get-tuple-element.62.cur_ref, f32[64,16,256]{2,1,0:T(8,128)S(1)} %get-tuple-element.56.cur_ref.prev_ref, ...), custom_call_target="tpu_custom_call", output_to_operand_aliasing={{1}: (7, {}), {0}: (8, {})} | custom-call | flops 7864320 | bytes 3670016 | tf_op jit(solution)/shard_map/pallas_call | solution.py:254
  95.2 0.7 gather_fusion
  95.9 0.2 select_select_fusion
  96.1 23.4 %all_to_all.10 = f32[8,10,16,256]{3,2,1,0:T(8,128)S(1)} all-to-all(f32[8,10,16,256]{3,2,1,0:T(8,128)S(1)} %select_select_fusion), channel_id=1, replica_groups=mesh['shot'=8,'space'=16] {'shot'}, dimensions={0} | all-to-all | bytes 2621440 | tf_op jit(solution)/shard_map/all_to_all | solution.py:377
  119.5 0.8 reduce_sum.19
  (7 shorter events, 0.1 us)
Async XLA Ops:
  0.6 5.0 %copy-start = (bf16[1,256,1536]{2,1,0:T(8,128)(2,1)S(1)}, bf16[1,256,1536]{2,1,0:T(8,128)(2,1)}, u32[]{:S(2)}) copy-start(bf16[1,256,1536]{2,1,0:T(8,128)(2,1)} %param.9) | copy-start | bytes 2359300
  2.7 18.1 %collective-permute-start.1 = (f32[64,4,256]{2,1,0:T(4,128)S(1)}, f32[64,4,256]{2,1,0:T(4,128)S(1)}, u32[]{:S(2)}, u32[]{:S(2)}) collective-permute-start(f32[64,4,256]{2,1,0:T(4,128)S(1)} %get-tuple-element.70), channel_id=1, source_target_pairs={{0,1},{1,0},{2,3},{3,2},{4,5},{5,4},{6,7},{7,6},{8,9},{9,8},{10,11... | collective-permute-start | bytes 786440 | tf_op jit(solution)/shard_map/ppermute | solution.py:360
  8.0 9.4 %all-to-all-start = ((f32[16,1,336]{2,1,0:T(1,128)}), f32[16,1,336]{2,1,0:T(1,128)S(1)}, u32[]{:S(2)}, u32[]{:S(2)}) async-start(f32[16,1,336]{2,1,0:T(1,128)} %reshape.102), calls=%async_computation | async-start | bytes 49152 | tf_op jit(solution)/shard_map/all_to_all | solution.py:328
  13.3 12.6 %collective-permute-start = (f32[64,4,256]{2,1,0:T(4,128)}, f32[64,4,256]{2,1,0:T(4,128)S(1)}, u32[]{:S(2)}, u32[]{:S(2)}) collective-permute-start(f32[64,4,256]{2,1,0:T(4,128)} %get-tuple-element.71), channel_id=1, source_target_pairs={{1,2},{2,1},{3,4},{4,3},{5,6},{6,5},{7,8},{8,7},{9,10},{10,9},{11,... | collective-permute-start | bytes 786440 | tf_op jit(solution)/shard_map/ppermute | solution.py:361
  18.8 2.2 %copy-start.2 = (f32[1,64,16,256]{3,2,1,0:T(8,128)S(1)}, f32[1,64,16,256]{3,2,1,0:T(8,128)}, u32[]{:S(2)}) copy-start(f32[1,64,16,256]{3,2,1,0:T(8,128)} %param.16) | copy-start | bytes 3145732
  20.9 1.2 %copy-start.3 = (f32[1,64,16,256]{3,2,1,0:T(8,128)S(1)}, f32[1,64,16,256]{3,2,1,0:T(8,128)}, u32[]{:S(2)}) copy-start(f32[1,64,16,256]{3,2,1,0:T(8,128)} %param.15) | copy-start | bytes 3145732
  25.4 7.4 %collective-permute-start.3 = (f32[64,4,256]{2,1,0:T(4,128)S(1)}, f32[64,4,256]{2,1,0:T(4,128)S(1)}, u32[]{:S(2)}, u32[]{:S(2)}) collective-permute-start(f32[64,4,256]{2,1,0:T(4,128)S(1)} %get-tuple-element.40), channel_id=1, source_target_pairs={{0,1},{1,0},{2,3},{3,2},{4,5},{5,4},{6,7},{7,6},{8,9},{9,8},{10,11... | collective-permute-start | bytes 786440 | tf_op jit(solution)/shard_map/ppermute | solution.py:360
  29.2 9.8 %collective-permute-start.2 = (f32[64,4,256]{2,1,0:T(4,128)S(1)}, f32[64,4,256]{2,1,0:T(4,128)S(1)}, u32[]{:S(2)}, u32[]{:S(2)}) collective-permute-start(f32[64,4,256]{2,1,0:T(4,128)S(1)} %get-tuple-element.39), channel_id=1, source_target_pairs={{1,2},{2,1},{3,4},{4,3},{5,6},{6,5},{7,8},{8,7},{9,10},{10,9},{11,... | collective-permute-start | bytes 786440 | tf_op jit(solution)/shard_map/ppermute | solution.py:361
  36.2 9.8 %collective-permute-start.5 = (f32[64,4,256]{2,1,0:T(4,128)S(1)}, f32[64,4,256]{2,1,0:T(4,128)S(1)}, u32[]{:S(2)}, u32[]{:S(2)}) collective-permute-start(f32[64,4,256]{2,1,0:T(4,128)S(1)} %get-tuple-element.46), channel_id=1, source_target_pairs={{0,1},{1,0},{2,3},{3,2},{4,5},{5,4},{6,7},{7,6},{8,9},{9,8},{10,11... | collective-permute-start | bytes 786440 | tf_op jit(solution)/shard_map/ppermute | solution.py:360
  42.2 9.8 %collective-permute-start.4 = (f32[64,4,256]{2,1,0:T(4,128)S(1)}, f32[64,4,256]{2,1,0:T(4,128)S(1)}, u32[]{:S(2)}, u32[]{:S(2)}) collective-permute-start(f32[64,4,256]{2,1,0:T(4,128)S(1)} %get-tuple-element.45), channel_id=1, source_target_pairs={{1,2},{2,1},{3,4},{4,3},{5,6},{6,5},{7,8},{8,7},{9,10},{10,9},{11,... | collective-permute-start | bytes 786440 | tf_op jit(solution)/shard_map/ppermute | solution.py:361
  49.2 9.8 %collective-permute-start.7 = (f32[64,4,256]{2,1,0:T(4,128)S(1)}, f32[64,4,256]{2,1,0:T(4,128)S(1)}, u32[]{:S(2)}, u32[]{:S(2)}) collective-permute-start(f32[64,4,256]{2,1,0:T(4,128)S(1)} %get-tuple-element.52), channel_id=1, source_target_pairs={{0,1},{1,0},{2,3},{3,2},{4,5},{5,4},{6,7},{7,6},{8,9},{9,8},{10,11... | collective-permute-start | bytes 786440 | tf_op jit(solution)/shard_map/ppermute | solution.py:360
  55.3 9.8 %collective-permute-start.6 = (f32[64,4,256]{2,1,0:T(4,128)S(1)}, f32[64,4,256]{2,1,0:T(4,128)S(1)}, u32[]{:S(2)}, u32[]{:S(2)}) collective-permute-start(f32[64,4,256]{2,1,0:T(4,128)S(1)} %get-tuple-element.51), channel_id=1, source_target_pairs={{1,2},{2,1},{3,4},{4,3},{5,6},{6,5},{7,8},{8,7},{9,10},{10,9},{11,... | collective-permute-start | bytes 786440 | tf_op jit(solution)/shard_map/ppermute | solution.py:361
  62.3 10.4 %collective-permute-start.9 = (f32[64,4,256]{2,1,0:T(4,128)S(1)}, f32[64,4,256]{2,1,0:T(4,128)S(1)}, u32[]{:S(2)}, u32[]{:S(2)}) collective-permute-start(f32[64,4,256]{2,1,0:T(4,128)S(1)} %get-tuple-element.58), channel_id=1, source_target_pairs={{0,1},{1,0},{2,3},{3,2},{4,5},{5,4},{6,7},{7,6},{8,9},{9,8},{10,11... | collective-permute-start | bytes 786440 | tf_op jit(solution)/shard_map/ppermute | solution.py:360
  68.3 9.8 %collective-permute-start.8 = (f32[64,4,256]{2,1,0:T(4,128)S(1)}, f32[64,4,256]{2,1,0:T(4,128)S(1)}, u32[]{:S(2)}, u32[]{:S(2)}) collective-permute-start(f32[64,4,256]{2,1,0:T(4,128)S(1)} %get-tuple-element.57), channel_id=1, source_target_pairs={{1,2},{2,1},{3,4},{4,3},{5,6},{6,5},{7,8},{8,7},{9,10},{10,9},{11,... | collective-permute-start | bytes 786440 | tf_op jit(solution)/shard_map/ppermute | solution.py:361
  76.0 9.3 %collective-permute-start.11 = (f32[64,4,256]{2,1,0:T(4,128)S(1)}, f32[64,4,256]{2,1,0:T(4,128)S(1)}, u32[]{:S(2)}, u32[]{:S(2)}) collective-permute-start(f32[64,4,256]{2,1,0:T(4,128)S(1)} %get-tuple-element.64), channel_id=1, source_target_pairs={{0,1},{1,0},{2,3},{3,2},{4,5},{5,4},{6,7},{7,6},{8,9},{9,8},{10,11... | collective-permute-start | bytes 786440 | tf_op jit(solution)/shard_map/ppermute | solution.py:360
  78.1 7.1 %copy-start.1 = (f32[1,64,16,256]{3,2,1,0:T(8,128)S(1)}, f32[1,64,16,256]{3,2,1,0:T(8,128)}, u32[]{:S(2)}) copy-start(f32[1,64,16,256]{3,2,1,0:T(8,128)} %param.14) | copy-start | bytes 3145732
  81.5 9.8 %collective-permute-start.10 = (f32[64,4,256]{2,1,0:T(4,128)S(1)}, f32[64,4,256]{2,1,0:T(4,128)S(1)}, u32[]{:S(2)}, u32[]{:S(2)}) collective-permute-start(f32[64,4,256]{2,1,0:T(4,128)S(1)} %get-tuple-element.63), channel_id=1, source_target_pairs={{1,2},{2,1},{3,4},{4,3},{5,6},{6,5},{7,8},{8,7},{9,10},{10,9},{11,... | collective-permute-start | bytes 786440 | tf_op jit(solution)/shard_map/ppermute | solution.py:361

commit v10 on v9

--- a/solution.py
+++ b/solution.py
@@ -271,6 +271,38 @@
         ),
         compiler_params=pltpu.CompilerParams(vmem_limit_bytes=48 * 1024 * 1024),
     )(*operands)
+
+
+def edge_kernel(odd_ref, cur_ref, near_ref, far_ref):
+    width = near_ref.shape[1]
+    cells_x = cur_ref.shape[1]
+
+    @pl.when(odd_ref[0] == 0)
+    def _():
+        near_ref[...] = cur_ref[:, cells_x - width :, :]
+        far_ref[...] = cur_ref[:, :width, :]
+
+    @pl.when(odd_ref[0] == 1)
+    def _():
+        near_ref[...] = cur_ref[:, :width, :]
+        far_ref[...] = cur_ref[:, cells_x - width :, :]
+
+
+def edges_of(current, odd, width):
+    cells_y, cells_x, cells_z = current.shape
+    rim = jax.ShapeDtypeStruct((cells_y, width, cells_z), current.dtype)
+    whole = pl.BlockSpec((cells_y, cells_x, cells_z), lambda i, t: (0, 0, 0))
+    rim_spec = pl.BlockSpec((cells_y, width, cells_z), lambda i, t: (0, 0, 0))
+    return pl.pallas_call(
+        edge_kernel,
+        grid_spec=pltpu.PrefetchScalarGridSpec(
+            num_scalar_prefetch=1,
+            grid=(1,),
+            in_specs=[whole],
+            out_specs=(rim_spec, rim_spec),
+        ),
+        out_shape=(rim, rim),
+    )(odd, current)
 
 
 def halo(first, last):
@@ -351,11 +383,7 @@
     devices = lax.axis_size("space")
     within = [(i, i ^ 1) for i in range(devices)]
     across = [(i, i + 1 - 2 * ((i + 1) % 2)) for i in range(1, devices - 1)]
-    zero = jnp.zeros((), jnp.int32)
-    near_start = (1 - odd) * (cells_x - width)
-    near_edge = lax.dynamic_slice(current, (zero, near_start, zero), (cells_y, width, cells_z))
-    far_start = odd * (cells_x - width)
-    far_edge = lax.dynamic_slice(current, (zero, far_start, zero), (cells_y, width, cells_z))
+    near_edge, far_edge = edges_of(current, tile_far, width)
     for moment in range(step_count):
         near_halo = lax.ppermute(near_edge, "space", within)
         far_halo = lax.ppermute(far_edge, "space", across)

time: 121 us -> 122 us (level)
  Pallas kernels: 40.5 us -> 42.6 us
  local copies, waits for them, and re-layouts: 5.64 us -> 3.58 us
    pallas_call x0 -> x1, Pallas kernels: none -> 2.11 us  [edges_of(): pl.pallas_call(edge_kernel, grid_spec=pltpu.PrefetchScalarGridSpec(num_sc...]
    dynamic_slice x1 -> x0, local copies, waits for them, and re-layouts: 2.07 us -> none  [local(): lax.dynamic_slice(current, (zero, near_start, zero), (cells_y, width, cel...]
where the time goes in v10:
time: 122 us; the launch traced here: 120 us
  Pallas kernels  42.6 us (35%)
  starting transfers between devices  28.8 us (24%)
  blocking collectives  23.4 us (19%)
  waiting for transfers between devices  12.9 us (11%)
  other arithmetic  3.99 us (3%)
  local copies, waits for them, and re-layouts  3.58 us (3%)
  matrix products  3.4 us (3%)
  between operations  1.65 us (1%)
    pallas_call x12, Pallas kernels, tile_call(): pl.pallas_call(functools.partial(tile_kernel, moment, chained), grid_spec...  40.5 us
    all_to_all x1, blocking collectives, local(): lax.all_to_all(placed, 'shot', split_axis=0, concat_axis=0, tiled=True)  23.4 us
    ppermute x6, starting transfers between devices, local(): far_halo = lax.ppermute(far_edge, 'space', across)  21.9 us
    ppermute x6, waiting for transfers between devices, local(): far_halo = lax.ppermute(far_edge, 'space', across)  12.1 us
    all_to_all x1, starting transfers between devices, local(): lax.all_to_all(buffer, 'space', split_axis=0, concat_axis=0, tiled=True)  5.26 us
  transfers between devices with their start and end apart: 13, of which 6 were waited for; matrix products, arithmetic and copies ran while one was open for 7% of the time, Pallas kernels for 30%

profile of v10, /device:TPU:97, one launch (start us, length us, event | category | flops | bytes accessed | tf_op | source)
XLA Modules:
  0.0 120.4 jit_solution(9972100658114975050)
XLA Ops:
  0.6 0.0 copy-start
  0.7 2.1 %shard_map.104 = (f32[64,4,256]{2,1,0:T(4,128)}, f32[64,4,256]{2,1,0:T(4,128)}) custom-call(s32[1]{0:T(128)} %bitcast.1.odd_ref.tile_ref, f32[64,16,256]{2,1,0:T(8,128)} %bitcast.53), custom_call_target="tpu_custom_call" | custom-call | tf_op jit(solution)/shard_map/pallas_call | solution.py:296
  2.8 0.7 collective-permute-start.1
  3.4 0.9 convert_reduce_fusion
  4.3 0.7 multiply_add_fusion
  5.0 0.7 convert_bitcast_fusion
  5.7 0.0 copy-done
  5.7 1.0 fusion.3
  6.7 0.5 fusion.5
  7.2 0.1 reshape.87
  7.3 0.7 reshape.100
  8.1 5.3 %all-to-all-start = ((f32[16,1,336]{2,1,0:T(1,128)}), f32[16,1,336]{2,1,0:T(1,128)S(1)}, u32[]{:S(2)}, u32[]{:S(2)}) async-start(f32[16,1,336]{2,1,0:T(1,128)} %reshape.100), calls=%async_computation | async-start | bytes 49152 | tf_op jit(solution)/shard_map/all_to_all | solution.py:360
  13.3 3.4 %collective-permute-start = (f32[64,4,256]{2,1,0:T(4,128)}, f32[64,4,256]{2,1,0:T(4,128)S(1)}, u32[]{:S(2)}, u32[]{:S(2)}) collective-permute-start(f32[64,4,256]{2,1,0:T(4,128)} %get-tuple-element.38), channel_id=1, source_target_pairs={{1,2},{2,1},{3,4},{4,3},{5,6},{6,5},{7,8},{8,7},{9,10},{10,9},{11,... | collective-permute-start | bytes 786440 | tf_op jit(solution)/shard_map/ppermute | solution.py:389
  16.7 0.8 all-to-all-done
  17.5 0.5 broadcast.101
  18.0 0.7 reduce.2
  18.7 0.1 reshape.101
  18.8 0.0 copy-start.2
  18.8 0.1 reshape.88
  19.0 1.9 %fusion = f32[1024,6]{1,0:T(8,128)S(1)} fusion(s32[1024]{0:T(1024)S(1)} %iota_add_fusion, s32[768]{0:T(1024)S(1)} %fusion.18, f32[768,7]{0,1:T(8,128)S(1)} %reshape.88), kind=kOutput, calls=%fused_computation.2 | convolution fusion | flops 58195968 | bytes 53248 | tf_op jit(solution)/shard_map/dot_general | solution.py:366
  20.8 0.0 collective-permute-done.1.halo_ref
  20.9 0.1 broadcast_in_dim.38.img_ref
  21.0 0.0 copy-done.2
  21.0 0.0 copy-start.3
  21.0 1.2 %copy-done.3 = f32[1,64,16,256]{3,2,1,0:T(8,128)S(1)} copy-done((f32[1,64,16,256]{3,2,1,0:T(8,128)S(1)}, f32[1,64,16,256]{3,2,1,0:T(8,128)}, u32[]{:S(2)}) %copy-start.3) | copy-done | bytes 1048600
  22.2 3.3 %shard_map.105 = (f32[64,16,256]{2,1,0:T(8,128)S(1)}, f32[64,16,256]{2,1,0:T(8,128)S(1)}, f32[64,4,256]{2,1,0:T(4,128)S(1)}) custom-call(s32[1]{0:T(128)} %bitcast.10.tile_ref, f32[64,16,256]{2,1,0:T(8,128)S(1)} %bitcast.54, f32[64,16,256]{2,1,0:T(8,128)S(1)} %bitcast.58, ...), custom_call_target="tpu_custom_call", output_to_operand_aliasing={{1}: (7, {})} | custom-call | flops 7864320 | bytes 3670016 | tf_op jit(solution)/shard_map/pallas_call | solution.py:254
  25.6 0.5 collective-permute-start.3
  26.0 0.0 collective-permute-done.halo_ref
  26.0 0.0 copy-done.4
  26.0 3.2 %shard_map.106 = (f32[64,16,256]{2,1,0:T(8,128)S(1)}, f32[64,16,256]{2,1,0:T(8,128)S(1)}, f32[64,4,256]{2,1,0:T(4,128)S(1)}) custom-call(s32[1]{0:T(128)} %bitcast.1.odd_ref.tile_ref, f32[64,16,256]{2,1,0:T(8,128)S(1)} %bitcast.55, f32[64,16,256]{2,1,0:T(8,128)S(1)} %bitcast.59, ...), custom_call_target="tpu_custom_call", output_to_operand_aliasing={{1}: (7, {}), {0}: (8, {})} | custom-call | flops 7864320 | bytes 3670016 | tf_op jit(solution)/shard_map/pallas_call | solution.py:254
  29.3 3.7 %collective-permute-start.2 = (f32[64,4,256]{2,1,0:T(4,128)S(1)}, f32[64,4,256]{2,1,0:T(4,128)S(1)}, u32[]{:S(2)}, u32[]{:S(2)}) collective-permute-start(f32[64,4,256]{2,1,0:T(4,128)S(1)} %get-tuple-element.43), channel_id=1, source_target_pairs={{1,2},{2,1},{3,4},{4,3},{5,6},{6,5},{7,8},{8,7},{9,10},{10,9},{11,... | collective-permute-start | bytes 786440 | tf_op jit(solution)/shard_map/ppermute | solution.py:389
  33.0 0.0 collective-permute-done.3.halo_ref
  33.0 3.3 %shard_map.107 = (f32[64,16,256]{2,1,0:T(8,128)S(1)}, f32[64,16,256]{2,1,0:T(8,128)S(1)}, f32[64,4,256]{2,1,0:T(4,128)S(1)}) custom-call(s32[1]{0:T(128)} %bitcast.10.tile_ref, f32[64,16,256]{2,1,0:T(8,128)S(1)} %get-tuple-element.42.cur_ref.prev_ref, f32[64,16,256]{2,1,0:T(8,128)S(1)} %bitcast.56, ...), custom_call_target="tpu_custom_call", output_to_operand_aliasing={{1}: (7, {})} | custom-call | flops 7864320 | bytes 3670016 | tf_op jit(solution)/shard_map/pallas_call | solution.py:254
  36.3 0.1 collective-permute-start.5
  36.4 2.7 %collective-permute-done.2.halo_ref = f32[64,4,256]{2,1,0:T(4,128)S(1)} collective-permute-done((f32[64,4,256]{2,1,0:T(4,128)S(1)}, f32[64,4,256]{2,1,0:T(4,128)S(1)}, u32[]{:S(2)}, u32[]{:S(2)}) %collective-permute-start.2) | collective-permute-done | bytes 262176 | tf_op jit(solution)/shard_map/ppermute | solution.py:389
  39.1 3.2 %shard_map.108 = (f32[64,16,256]{2,1,0:T(8,128)S(1)}, f32[64,16,256]{2,1,0:T(8,128)S(1)}, f32[64,4,256]{2,1,0:T(4,128)S(1)}) custom-call(s32[1]{0:T(128)} %bitcast.1.odd_ref.tile_ref, f32[64,16,256]{2,1,0:T(8,128)S(1)} %get-tuple-element.42.cur_ref.prev_ref, f32[64,16,256]{2,1,0:T(8,128)S(1)} %bitcast.57, ...), custom_call_target="tpu_custom_call", output_to_operand_aliasing={{1}: (7, {}), {0}: (8, {})} | custom-call | flops 7864320 | bytes 3670016 | tf_op jit(solution)/shard_map/pallas_call | solution.py:254
  42.4 3.7 %collective-permute-start.4 = (f32[64,4,256]{2,1,0:T(4,128)S(1)}, f32[64,4,256]{2,1,0:T(4,128)S(1)}, u32[]{:S(2)}, u32[]{:S(2)}) collective-permute-start(f32[64,4,256]{2,1,0:T(4,128)S(1)} %get-tuple-element.49), channel_id=1, source_target_pairs={{1,2},{2,1},{3,4},{4,3},{5,6},{6,5},{7,8},{8,7},{9,10},{10,9},{11,... | collective-permute-start | bytes 786440 | tf_op jit(solution)/shard_map/ppermute | solution.py:389
  46.1 0.0 collective-permute-done.5.halo_ref
  46.1 3.3 %shard_map.109 = (f32[64,16,256]{2,1,0:T(8,128)S(1)}, f32[64,16,256]{2,1,0:T(8,128)S(1)}, f32[64,4,256]{2,1,0:T(4,128)S(1)}) custom-call(s32[1]{0:T(128)} %bitcast.10.tile_ref, f32[64,16,256]{2,1,0:T(8,128)S(1)} %get-tuple-element.48.cur_ref.prev_ref, f32[64,16,256]{2,1,0:T(8,128)S(1)} %get-tuple-element.42.cur_ref.prev_ref, ...), custom_call_target="tpu_custom_call", output_to_operand_aliasing={{1}: (7, {})} | custom-call | flops 7864320 | bytes 3670016 | tf_op jit(solution)/shard_map/pallas_call | solution.py:254
  49.3 0.1 collective-permute-start.7
  49.4 2.7 %collective-permute-done.4.halo_ref = f32[64,4,256]{2,1,0:T(4,128)S(1)} collective-permute-done((f32[64,4,256]{2,1,0:T(4,128)S(1)}, f32[64,4,256]{2,1,0:T(4,128)S(1)}, u32[]{:S(2)}, u32[]{:S(2)}) %collective-permute-start.4) | collective-permute-done | bytes 262176 | tf_op jit(solution)/shard_map/ppermute | solution.py:389
  52.2 3.2 %shard_map.110 = (f32[64,16,256]{2,1,0:T(8,128)S(1)}, f32[64,16,256]{2,1,0:T(8,128)S(1)}, f32[64,4,256]{2,1,0:T(4,128)S(1)}) custom-call(s32[1]{0:T(128)} %bitcast.1.odd_ref.tile_ref, f32[64,16,256]{2,1,0:T(8,128)S(1)} %get-tuple-element.48.cur_ref.prev_ref, ...), custom_call_target="tpu_custom_call", output_to_operand_aliasing={{1}: (7, {}), {0}: (8, {})} | custom-call | flops 7864320 | bytes 3670016 | tf_op jit(solution)/shard_map/pallas_call | solution.py:254
  55.4 3.7 %collective-permute-start.6 = (f32[64,4,256]{2,1,0:T(4,128)S(1)}, f32[64,4,256]{2,1,0:T(4,128)S(1)}, u32[]{:S(2)}, u32[]{:S(2)}) collective-permute-start(f32[64,4,256]{2,1,0:T(4,128)S(1)} %get-tuple-element.55), channel_id=1, source_target_pairs={{1,2},{2,1},{3,4},{4,3},{5,6},{6,5},{7,8},{8,7},{9,10},{10,9},{11,... | collective-permute-start | bytes 786440 | tf_op jit(solution)/shard_map/ppermute | solution.py:389
  59.1 0.0 collective-permute-done.7.halo_ref
  59.1 3.3 %shard_map.111 = (f32[64,16,256]{2,1,0:T(8,128)S(1)}, f32[64,16,256]{2,1,0:T(8,128)S(1)}, f32[64,4,256]{2,1,0:T(4,128)S(1)}) custom-call(s32[1]{0:T(128)} %bitcast.10.tile_ref, f32[64,16,256]{2,1,0:T(8,128)S(1)} %get-tuple-element.54.cur_ref.prev_ref, f32[64,16,256]{2,1,0:T(8,128)S(1)} %get-tuple-element.48.cur_ref.prev_ref, ...), custom_call_target="tpu_custom_call", output_to_operand_aliasing={{1}: (7, {})} | custom-call | flops 7864320 | bytes 3670016 | tf_op jit(solution)/shard_map/pallas_call | solution.py:254
  62.4 0.1 collective-permute-start.9
  62.5 2.7 %collective-permute-done.6.halo_ref = f32[64,4,256]{2,1,0:T(4,128)S(1)} collective-permute-done((f32[64,4,256]{2,1,0:T(4,128)S(1)}, f32[64,4,256]{2,1,0:T(4,128)S(1)}, u32[]{:S(2)}, u32[]{:S(2)}) %collective-permute-start.6) | collective-permute-done | bytes 262176 | tf_op jit(solution)/shard_map/ppermute | solution.py:389
  65.2 3.2 %shard_map.112 = (f32[64,16,256]{2,1,0:T(8,128)S(1)}, f32[64,16,256]{2,1,0:T(8,128)S(1)}, f32[64,4,256]{2,1,0:T(4,128)S(1)}) custom-call(s32[1]{0:T(128)} %bitcast.1.odd_ref.tile_ref, f32[64,16,256]{2,1,0:T(8,128)S(1)} %get-tuple-element.54.cur_ref.prev_ref, ...), custom_call_target="tpu_custom_call", output_to_operand_aliasing={{1}: (7, {}), {0}: (8, {})} | custom-call | flops 7864320 | bytes 3670016 | tf_op jit(solution)/shard_map/pallas_call | solution.py:254
  68.5 3.7 %collective-permute-start.8 = (f32[64,4,256]{2,1,0:T(4,128)S(1)}, f32[64,4,256]{2,1,0:T(4,128)S(1)}, u32[]{:S(2)}, u32[]{:S(2)}) collective-permute-start(f32[64,4,256]{2,1,0:T(4,128)S(1)} %get-tuple-element.61), channel_id=1, source_target_pairs={{1,2},{2,1},{3,4},{4,3},{5,6},{6,5},{7,8},{8,7},{9,10},{10,9},{11,... | collective-permute-start | bytes 786440 | tf_op jit(solution)/shard_map/ppermute | solution.py:389
  72.8 0.0 collective-permute-done.9.halo_ref
  72.9 3.3 %shard_map.113 = (f32[64,16,256]{2,1,0:T(8,128)S(1)}, f32[64,16,256]{2,1,0:T(8,128)S(1)}, f32[64,4,256]{2,1,0:T(4,128)S(1)}) custom-call(s32[1]{0:T(128)} %bitcast.10.tile_ref, f32[64,16,256]{2,1,0:T(8,128)S(1)} %get-tuple-element.60.cur_ref.prev_ref, f32[64,16,256]{2,1,0:T(8,128)S(1)} %get-tuple-element.54.cur_ref.prev_ref, ...), custom_call_target="tpu_custom_call", output_to_operand_aliasing={{1}: (7, {})} | custom-call | flops 7864320 | bytes 3670016 | tf_op jit(solution)/shard_map/pallas_call | solution.py:254
  76.1 0.3 collective-permute-start.11
  76.4 1.9 %collective-permute-done.8.halo_ref = f32[64,4,256]{2,1,0:T(4,128)S(1)} collective-permute-done((f32[64,4,256]{2,1,0:T(4,128)S(1)}, f32[64,4,256]{2,1,0:T(4,128)S(1)}, u32[]{:S(2)}, u32[]{:S(2)}) %collective-permute-start.8) | collective-permute-done | bytes 262176 | tf_op jit(solution)/shard_map/ppermute | solution.py:389
  78.3 3.3 %shard_map.114 = (f32[64,16,256]{2,1,0:T(8,128)S(1)}, f32[64,16,256]{2,1,0:T(8,128)S(1)}, f32[64,4,256]{2,1,0:T(4,128)S(1)}) custom-call(s32[1]{0:T(128)} %bitcast.1.odd_ref.tile_ref, f32[64,16,256]{2,1,0:T(8,128)S(1)} %get-tuple-element.60.cur_ref.prev_ref, ...), custom_call_target="tpu_custom_call", output_to_operand_aliasing={{1}: (7, {}), {0}: (8, {})} | custom-call | flops 7864320 | bytes 3670016 | tf_op jit(solution)/shard_map/pallas_call | solution.py:254
  81.6 3.7 %collective-permute-start.10 = (f32[64,4,256]{2,1,0:T(4,128)S(1)}, f32[64,4,256]{2,1,0:T(4,128)S(1)}, u32[]{:S(2)}, u32[]{:S(2)}) collective-permute-start(f32[64,4,256]{2,1,0:T(4,128)S(1)} %get-tuple-element.67), channel_id=1, source_target_pairs={{1,2},{2,1},{3,4},{4,3},{5,6},{6,5},{7,8},{8,7},{9,10},{10,9},{11,... | collective-permute-start | bytes 786440 | tf_op jit(solution)/shard_map/ppermute | solution.py:389
  85.4 0.0 collective-permute-done.11.halo_ref
  85.4 0.0 copy-done.1
  85.4 3.9 %shard_map.115 = (f32[64,16,256]{2,1,0:T(8,128)}, f32[64,16,256]{2,1,0:T(8,128)S(1)}, f32[64,4,256]{2,1,0:T(4,128)}) custom-call(s32[1]{0:T(128)} %bitcast.10.tile_ref, f32[64,16,256]{2,1,0:T(8,128)S(1)} %get-tuple-element.66.cur_ref, f32[64,16,256]{2,1,0:T(8,128)S(1)} %get-tuple-element.60.cur_ref.prev_ref, ...), custom_call_target="tpu_custom_call", output_to_operand_aliasing={{1}: (7, {})} | custom-call | flops 7864320 | bytes 3670016 | tf_op jit(solution)/shard_map/pallas_call | solution.py:254
  89.3 2.1 %collective-permute-done.10.halo_ref = f32[64,4,256]{2,1,0:T(4,128)S(1)} collective-permute-done((f32[64,4,256]{2,1,0:T(4,128)S(1)}, f32[64,4,256]{2,1,0:T(4,128)S(1)}, u32[]{:S(2)}, u32[]{:S(2)}) %collective-permute-start.10) | collective-permute-done | bytes 262176 | tf_op jit(solution)/shard_map/ppermute | solution.py:389
  91.4 3.9 %shard_map.116 = (f32[64,16,256]{2,1,0:T(8,128)}, f32[64,16,256]{2,1,0:T(8,128)S(1)}, f32[64,4,256]{2,1,0:T(4,128)}) custom-call(s32[1]{0:T(128)} %bitcast.1.odd_ref.tile_ref, f32[64,16,256]{2,1,0:T(8,128)S(1)} %get-tuple-element.66.cur_ref, f32[64,16,256]{2,1,0:T(8,128)S(1)} %get-tuple-element.60.cur_ref.prev_ref, ...), custom_call_target="tpu_custom_call", output_to_operand_aliasing={{1}: (7, {}), {0}: (8, {})} | custom-call | flops 7864320 | bytes 3670016 | tf_op jit(solution)/shard_map/pallas_call | solution.py:254
  95.3 0.7 gather_fusion
  96.0 0.2 select_select_fusion
  96.2 23.4 %all_to_all.10 = f32[8,10,16,256]{3,2,1,0:T(8,128)S(1)} all-to-all(f32[8,10,16,256]{3,2,1,0:T(8,128)S(1)} %select_select_fusion), channel_id=1, replica_groups=mesh['shot'=8,'space'=16] {'shot'}, dimensions={0} | all-to-all | bytes 2621440 | tf_op jit(solution)/shard_map/all_to_all | solution.py:405
  119.6 0.8 reduce_sum.19
  (9 shorter events, 0.1 us)
Async XLA Ops:
  0.6 5.1 %copy-start = (bf16[1,256,1536]{2,1,0:T(8,128)(2,1)S(1)}, bf16[1,256,1536]{2,1,0:T(8,128)(2,1)}, u32[]{:S(2)}) copy-start(bf16[1,256,1536]{2,1,0:T(8,128)(2,1)} %param.9) | copy-start | bytes 2359300
  2.8 18.1 %collective-permute-start.1 = (f32[64,4,256]{2,1,0:T(4,128)}, f32[64,4,256]{2,1,0:T(4,128)S(1)}, u32[]{:S(2)}, u32[]{:S(2)}) collective-permute-start(f32[64,4,256]{2,1,0:T(4,128)} %get-tuple-element.39), channel_id=1, source_target_pairs={{0,1},{1,0},{2,3},{3,2},{4,5},{5,4},{6,7},{7,6},{8,9},{9,8},{10,11... | collective-permute-start | bytes 786440 | tf_op jit(solution)/shard_map/ppermute | solution.py:388
  8.1 9.4 %all-to-all-start = ((f32[16,1,336]{2,1,0:T(1,128)}), f32[16,1,336]{2,1,0:T(1,128)S(1)}, u32[]{:S(2)}, u32[]{:S(2)}) async-start(f32[16,1,336]{2,1,0:T(1,128)} %reshape.100), calls=%async_computation | async-start | bytes 49152 | tf_op jit(solution)/shard_map/all_to_all | solution.py:360
  13.3 12.7 %collective-permute-start = (f32[64,4,256]{2,1,0:T(4,128)}, f32[64,4,256]{2,1,0:T(4,128)S(1)}, u32[]{:S(2)}, u32[]{:S(2)}) collective-permute-start(f32[64,4,256]{2,1,0:T(4,128)} %get-tuple-element.38), channel_id=1, source_target_pairs={{1,2},{2,1},{3,4},{4,3},{5,6},{6,5},{7,8},{8,7},{9,10},{10,9},{11,... | collective-permute-start | bytes 786440 | tf_op jit(solution)/shard_map/ppermute | solution.py:389
  18.8 2.2 %copy-start.2 = (f32[1,64,16,256]{3,2,1,0:T(8,128)S(1)}, f32[1,64,16,256]{3,2,1,0:T(8,128)}, u32[]{:S(2)}) copy-start(f32[1,64,16,256]{3,2,1,0:T(8,128)} %param.16) | copy-start | bytes 3145732
  21.0 1.2 %copy-start.3 = (f32[1,64,16,256]{3,2,1,0:T(8,128)S(1)}, f32[1,64,16,256]{3,2,1,0:T(8,128)}, u32[]{:S(2)}) copy-start(f32[1,64,16,256]{3,2,1,0:T(8,128)} %param.15) | copy-start | bytes 3145732
  22.2 3.8 %copy-start.4 = (f32[1,64,16,256]{3,2,1,0:T(8,128)S(1)}, f32[1,64,16,256]{3,2,1,0:T(8,128)}, u32[]{:S(2)}) copy-start(f32[1,64,16,256]{3,2,1,0:T(8,128)} %param.15) | copy-start | bytes 3145732
  25.6 7.4 %collective-permute-start.3 = (f32[64,4,256]{2,1,0:T(4,128)S(1)}, f32[64,4,256]{2,1,0:T(4,128)S(1)}, u32[]{:S(2)}, u32[]{:S(2)}) collective-permute-start(f32[64,4,256]{2,1,0:T(4,128)S(1)} %get-tuple-element.44), channel_id=1, source_target_pairs={{0,1},{1,0},{2,3},{3,2},{4,5},{5,4},{6,7},{7,6},{8,9},{9,8},{10,11... | collective-permute-start | bytes 786440 | tf_op jit(solution)/shard_map/ppermute | solution.py:388
  29.3 9.8 %collective-permute-start.2 = (f32[64,4,256]{2,1,0:T(4,128)S(1)}, f32[64,4,256]{2,1,0:T(4,128)S(1)}, u32[]{:S(2)}, u32[]{:S(2)}) collective-permute-start(f32[64,4,256]{2,1,0:T(4,128)S(1)} %get-tuple-element.43), channel_id=1, source_target_pairs={{1,2},{2,1},{3,4},{4,3},{5,6},{6,5},{7,8},{8,7},{9,10},{10,9},{11,... | collective-permute-start | bytes 786440 | tf_op jit(solution)/shard_map/ppermute | solution.py:389
  36.3 9.8 %collective-permute-start.5 = (f32[64,4,256]{2,1,0:T(4,128)S(1)}, f32[64,4,256]{2,1,0:T(4,128)S(1)}, u32[]{:S(2)}, u32[]{:S(2)}) collective-permute-start(f32[64,4,256]{2,1,0:T(4,128)S(1)} %get-tuple-element.50), channel_id=1, source_target_pairs={{0,1},{1,0},{2,3},{3,2},{4,5},{5,4},{6,7},{7,6},{8,9},{9,8},{10,11... | collective-permute-start | bytes 786440 | tf_op jit(solution)/shard_map/ppermute | solution.py:388
  42.4 9.8 %collective-permute-start.4 = (f32[64,4,256]{2,1,0:T(4,128)S(1)}, f32[64,4,256]{2,1,0:T(4,128)S(1)}, u32[]{:S(2)}, u32[]{:S(2)}) collective-permute-start(f32[64,4,256]{2,1,0:T(4,128)S(1)} %get-tuple-element.49), channel_id=1, source_target_pairs={{1,2},{2,1},{3,4},{4,3},{5,6},{6,5},{7,8},{8,7},{9,10},{10,9},{11,... | collective-permute-start | bytes 786440 | tf_op jit(solution)/shard_map/ppermute | solution.py:389
  49.3 9.8 %collective-permute-start.7 = (f32[64,4,256]{2,1,0:T(4,128)S(1)}, f32[64,4,256]{2,1,0:T(4,128)S(1)}, u32[]{:S(2)}, u32[]{:S(2)}) collective-permute-start(f32[64,4,256]{2,1,0:T(4,128)S(1)} %get-tuple-element.56), channel_id=1, source_target_pairs={{0,1},{1,0},{2,3},{3,2},{4,5},{5,4},{6,7},{7,6},{8,9},{9,8},{10,11... | collective-permute-start | bytes 786440 | tf_op jit(solution)/shard_map/ppermute | solution.py:388
  55.4 9.8 %collective-permute-start.6 = (f32[64,4,256]{2,1,0:T(4,128)S(1)}, f32[64,4,256]{2,1,0:T(4,128)S(1)}, u32[]{:S(2)}, u32[]{:S(2)}) collective-permute-start(f32[64,4,256]{2,1,0:T(4,128)S(1)} %get-tuple-element.55), channel_id=1, source_target_pairs={{1,2},{2,1},{3,4},{4,3},{5,6},{6,5},{7,8},{8,7},{9,10},{10,9},{11,... | collective-permute-start | bytes 786440 | tf_op jit(solution)/shard_map/ppermute | solution.py:389
  62.4 10.4 %collective-permute-start.9 = (f32[64,4,256]{2,1,0:T(4,128)S(1)}, f32[64,4,256]{2,1,0:T(4,128)S(1)}, u32[]{:S(2)}, u32[]{:S(2)}) collective-permute-start(f32[64,4,256]{2,1,0:T(4,128)S(1)} %get-tuple-element.62), channel_id=1, source_target_pairs={{0,1},{1,0},{2,3},{3,2},{4,5},{5,4},{6,7},{7,6},{8,9},{9,8},{10,11... | collective-permute-start | bytes 786440 | tf_op jit(solution)/shard_map/ppermute | solution.py:388
  68.5 9.8 %collective-permute-start.8 = (f32[64,4,256]{2,1,0:T(4,128)S(1)}, f32[64,4,256]{2,1,0:T(4,128)S(1)}, u32[]{:S(2)}, u32[]{:S(2)}) collective-permute-start(f32[64,4,256]{2,1,0:T(4,128)S(1)} %get-tuple-element.61), channel_id=1, source_target_pairs={{1,2},{2,1},{3,4},{4,3},{5,6},{6,5},{7,8},{8,7},{9,10},{10,9},{11,... | collective-permute-start | bytes 786440 | tf_op jit(solution)/shard_map/ppermute | solution.py:389
  76.1 9.3 %collective-permute-start.11 = (f32[64,4,256]{2,1,0:T(4,128)S(1)}, f32[64,4,256]{2,1,0:T(4,128)S(1)}, u32[]{:S(2)}, u32[]{:S(2)}) collective-permute-start(f32[64,4,256]{2,1,0:T(4,128)S(1)} %get-tuple-element.68), channel_id=1, source_target_pairs={{0,1},{1,0},{2,3},{3,2},{4,5},{5,4},{6,7},{7,6},{8,9},{9,8},{10,11... | collective-permute-start | bytes 786440 | tf_op jit(solution)/shard_map/ppermute | solution.py:388
  78.3 7.1 %copy-start.1 = (f32[1,64,16,256]{3,2,1,0:T(8,128)S(1)}, f32[1,64,16,256]{3,2,1,0:T(8,128)}, u32[]{:S(2)}) copy-start(f32[1,64,16,256]{3,2,1,0:T(8,128)} %param.14) | copy-start | bytes 3145732
  81.6 9.8 %collective-permute-start.10 = (f32[64,4,256]{2,1,0:T(4,128)S(1)}, f32[64,4,256]{2,1,0:T(4,128)S(1)}, u32[]{:S(2)}, u32[]{:S(2)}) collective-permute-start(f32[64,4,256]{2,1,0:T(4,128)S(1)} %get-tuple-element.67), channel_id=1, source_target_pairs={{1,2},{2,1},{3,4},{4,3},{5,6},{6,5},{7,8},{8,7},{9,10},{10,9},{11,... | collective-permute-start | bytes 786440 | tf_op jit(solution)/shard_map/ppermute | solution.py:389

commit v11 on v9

--- a/solution.py
+++ b/solution.py
@@ -358,11 +358,12 @@
     far_edge = lax.dynamic_slice(current, (zero, far_start, zero), (cells_y, width, cells_z))
     for moment in range(step_count):
         near_halo = lax.ppermute(near_edge, "space", within)
-        far_halo = lax.ppermute(far_edge, "space", across)
         partial_next, imaging, near_edge = tile_call(
             moment, tile_near, current, previous, near_halo, speed_sq, forward, source,
             imaging, None,
         )
+        far_edge, partial_next = lax.optimization_barrier((far_edge, partial_next))
+        far_halo = lax.ppermute(far_edge, "space", across)
         advanced, imaging, far_edge = tile_call(
             moment, tile_far, current, previous, far_halo, speed_sq, forward, source,
             imaging, partial_next,

time: 121 us -> 145 us (1.20)
  waiting for transfers between devices: 12.9 us -> 38 us
  blocking collectives: 23.4 us -> 20.3 us
    ppermute x6, waiting for transfers between devices: 12.1 us -> 33.9 us  [local(): far_halo = lax.ppermute(far_edge, 'space', across)]
    all_to_all x1, waiting for transfers between devices: 0.79 us -> 4.16 us  [local(): lax.all_to_all(buffer, 'space', split_axis=0, concat_axis=0, tiled=True)]
    all_to_all x1, blocking collectives: 23.4 us -> 20.3 us  [local(): lax.all_to_all(placed, 'shot', split_axis=0, concat_axis=0, tiled=True)]
    ppermute x6, starting transfers between devices: 21.9 us -> 23.5 us  [local(): far_halo = lax.ppermute(far_edge, 'space', across)]
  transfers between devices with their start and end apart: 13 -> 13, of which waited for: 6 -> 7; matrix products, arithmetic and copies ran while one was open for 7% -> 6% of each run, Pallas kernels for 30% -> 11%
where the time goes in v11:
time: 145 us; the launch traced here: 143 us
  Pallas kernels  40.5 us (28%)
  waiting for transfers between devices  38 us (26%)
  starting transfers between devices  30.2 us (21%)
  blocking collectives  20.3 us (14%)
  local copies, waits for them, and re-layouts  4.94 us (3%)
  other arithmetic  3.99 us (3%)
  matrix products  3.4 us (2%)
  between operations  1.66 us (1%)
    pallas_call x12, Pallas kernels, tile_call(): pl.pallas_call(functools.partial(tile_kernel, moment, chained), grid_spec...  40.5 us
    ppermute x6, waiting for transfers between devices, local(): far_halo = lax.ppermute(far_edge, 'space', across)  33.9 us
    ppermute x6, starting transfers between devices, local(): far_halo = lax.ppermute(far_edge, 'space', across)  23.5 us
    all_to_all x1, blocking collectives, local(): lax.all_to_all(placed, 'shot', split_axis=0, concat_axis=0, tiled=True)  20.3 us
    all_to_all x1, starting transfers between devices, local(): lax.all_to_all(buffer, 'space', split_axis=0, concat_axis=0, tiled=True)  5.26 us
    all_to_all x1, waiting for transfers between devices, local(): lax.all_to_all(buffer, 'space', split_axis=0, concat_axis=0, tiled=True)  4.16 us
  transfers between devices with their start and end apart: 13, of which 7 were waited for; matrix products, arithmetic and copies ran while one was open for 6% of the time, Pallas kernels for 11%

profile of v11, /device:TPU:97, one launch (start us, length us, event | category | flops | bytes accessed | tf_op | source)
XLA Modules:
  0.0 143.0 jit_solution(4153304890372792829)
XLA Ops:
  0.6 0.0 copy-start
  0.7 1.4 dynamic-slice_bitcast_fusion
  2.0 0.8 collective-permute-start
  2.8 0.9 convert_reduce_fusion
  3.7 0.7 multiply_add_fusion
  4.3 0.7 convert_bitcast_fusion
  5.0 0.0 copy-done
  5.0 1.0 fusion.3
  6.0 0.5 fusion.5
  6.5 0.1 reshape.90
  6.7 0.7 reshape.102
  7.4 5.3 %all-to-all-start = ((f32[16,1,336]{2,1,0:T(1,128)}), f32[16,1,336]{2,1,0:T(1,128)S(1)}, u32[]{:S(2)}, u32[]{:S(2)}) async-start(f32[16,1,336]{2,1,0:T(1,128)} %reshape.102), calls=%async_computation | async-start | bytes 49152 | tf_op jit(solution)/shard_map/all_to_all | solution.py:328
  12.7 4.2 %all-to-all-done = f32[16,1,336]{2,1,0:T(1,128)S(1)} async-done(((f32[16,1,336]{2,1,0:T(1,128)}), f32[16,1,336]{2,1,0:T(1,128)S(1)}, u32[]{:S(2)}, u32[]{:S(2)}) %all-to-all-start) | async-done | bytes 21536 | tf_op jit(solution)/shard_map/all_to_all | solution.py:328
  16.8 0.5 broadcast.101
  17.4 0.7 reduce.2
  18.1 0.1 reshape.103
  18.1 0.0 copy-start.2
  18.2 0.1 reshape.91
  18.3 1.9 %fusion = f32[1024,6]{1,0:T(8,128)S(1)} fusion(s32[1024]{0:T(1024)S(1)} %iota_add_fusion, s32[768]{0:T(1024)S(1)} %fusion.18, f32[768,7]{0,1:T(8,128)S(1)} %reshape.91), kind=kOutput, calls=%fused_computation.2 | convolution fusion | flops 58195968 | bytes 53248 | tf_op jit(solution)/shard_map/dot_general | solution.py:334
  20.2 0.0 collective-permute-done.halo_ref
  20.2 0.1 broadcast_in_dim.38.img_ref
  20.3 0.0 copy-done.2
  20.3 0.0 copy-start.3
  20.3 1.2 copy-done.3
  21.6 3.3 %shard_map.104 = (f32[64,16,256]{2,1,0:T(8,128)S(1)}, f32[64,16,256]{2,1,0:T(8,128)S(1)}, f32[64,4,256]{2,1,0:T(4,128)S(1)}) custom-call(s32[1]{0:T(128)} %bitcast.5.tile_ref, f32[64,16,256]{2,1,0:T(8,128)S(1)} %bitcast.57, f32[64,16,256]{2,1,0:T(8,128)S(1)} %bitcast.61, ...), custom_call_target="tpu_custom_call", output_to_operand_aliasing={{1}: (7, {})} | custom-call | flops 7864320 | bytes 3670016 | tf_op jit(solution)/shard_map/pallas_call | solution.py:254
  24.8 3.9 %collective-permute-start.1 = (f32[64,4,256]{2,1,0:T(4,128)S(1)}, f32[64,4,256]{2,1,0:T(4,128)S(1)}, u32[]{:S(2)}, u32[]{:S(2)}) collective-permute-start(f32[64,4,256]{2,1,0:T(4,128)S(1)} %get-tuple-element.49), channel_id=1, source_target_pairs={{1,2},{2,1},{3,4},{4,3},{5,6},{6,5},{7,8},{8,7},{9,10},{10,9},{11,... | collective-permute-start | bytes 786440 | tf_op jit(solution)/shard_map/ppermute | solution.py:366
  28.8 0.1 collective-permute-start.2
  28.9 5.8 %collective-permute-done.1.halo_ref = f32[64,4,256]{2,1,0:T(4,128)S(1)} collective-permute-done((f32[64,4,256]{2,1,0:T(4,128)S(1)}, f32[64,4,256]{2,1,0:T(4,128)S(1)}, u32[]{:S(2)}, u32[]{:S(2)}) %collective-permute-start.1) | collective-permute-done | bytes 262176 | tf_op jit(solution)/shard_map/ppermute | solution.py:366
  34.6 3.2 %shard_map.105 = (f32[64,16,256]{2,1,0:T(8,128)S(1)}, f32[64,16,256]{2,1,0:T(8,128)S(1)}, f32[64,4,256]{2,1,0:T(4,128)S(1)}) custom-call(s32[1]{0:T(128)} %bitcast.1.tile_ref, f32[64,16,256]{2,1,0:T(8,128)S(1)} %bitcast.58, f32[64,16,256]{2,1,0:T(8,128)S(1)} %bitcast.62, ...), custom_call_target="tpu_custom_call", output_to_operand_aliasing={{1}: (7, {}), {0}: (8, {})} | custom-call | flops 7864320 | bytes 3670016 | tf_op jit(solution)/shard_map/pallas_call | solution.py:254
  37.9 0.0 collective-permute-done.2.halo_ref
  37.9 3.3 %shard_map.106 = (f32[64,16,256]{2,1,0:T(8,128)S(1)}, f32[64,16,256]{2,1,0:T(8,128)S(1)}, f32[64,4,256]{2,1,0:T(4,128)S(1)}) custom-call(s32[1]{0:T(128)} %bitcast.5.tile_ref, f32[64,16,256]{2,1,0:T(8,128)S(1)} %get-tuple-element.52.cur_ref.prev_ref, f32[64,16,256]{2,1,0:T(8,128)S(1)} %bitcast.59, ...), custom_call_target="tpu_custom_call", output_to_operand_aliasing={{1}: (7, {})} | custom-call | flops 7864320 | bytes 3670016 | tf_op jit(solution)/shard_map/pallas_call | solution.py:254
  41.2 3.9 %collective-permute-start.3 = (f32[64,4,256]{2,1,0:T(4,128)S(1)}, f32[64,4,256]{2,1,0:T(4,128)S(1)}, u32[]{:S(2)}, u32[]{:S(2)}) collective-permute-start(f32[64,4,256]{2,1,0:T(4,128)S(1)} %get-tuple-element.57), channel_id=1, source_target_pairs={{1,2},{2,1},{3,4},{4,3},{5,6},{6,5},{7,8},{8,7},{9,10},{10,9},{11,... | collective-permute-start | bytes 786440 | tf_op jit(solution)/shard_map/ppermute | solution.py:366
  45.1 0.1 collective-permute-start.4
  45.2 5.8 %collective-permute-done.3.halo_ref = f32[64,4,256]{2,1,0:T(4,128)S(1)} collective-permute-done((f32[64,4,256]{2,1,0:T(4,128)S(1)}, f32[64,4,256]{2,1,0:T(4,128)S(1)}, u32[]{:S(2)}, u32[]{:S(2)}) %collective-permute-start.3) | collective-permute-done | bytes 262176 | tf_op jit(solution)/shard_map/ppermute | solution.py:366
  51.0 3.2 %shard_map.107 = (f32[64,16,256]{2,1,0:T(8,128)S(1)}, f32[64,16,256]{2,1,0:T(8,128)S(1)}, f32[64,4,256]{2,1,0:T(4,128)S(1)}) custom-call(s32[1]{0:T(128)} %bitcast.1.tile_ref, f32[64,16,256]{2,1,0:T(8,128)S(1)} %get-tuple-element.52.cur_ref.prev_ref, f32[64,16,256]{2,1,0:T(8,128)S(1)} %bitcast.60, ...), custom_call_target="tpu_custom_call", output_to_operand_aliasing={{1}: (7, {}), {0}: (8, {})} | custom-call | flops 7864320 | bytes 3670016 | tf_op jit(solution)/shard_map/pallas_call | solution.py:254
  54.2 0.0 collective-permute-done.4.halo_ref
  54.2 3.3 %shard_map.108 = (f32[64,16,256]{2,1,0:T(8,128)S(1)}, f32[64,16,256]{2,1,0:T(8,128)S(1)}, f32[64,4,256]{2,1,0:T(4,128)S(1)}) custom-call(s32[1]{0:T(128)} %bitcast.5.tile_ref, f32[64,16,256]{2,1,0:T(8,128)S(1)} %get-tuple-element.60.cur_ref.prev_ref, f32[64,16,256]{2,1,0:T(8,128)S(1)} %get-tuple-element.52.cur_ref.prev_ref, ...), custom_call_target="tpu_custom_call", output_to_operand_aliasing={{1}: (7, {})} | custom-call | flops 7864320 | bytes 3670016 | tf_op jit(solution)/shard_map/pallas_call | solution.py:254
  57.5 3.9 %collective-permute-start.5 = (f32[64,4,256]{2,1,0:T(4,128)S(1)}, f32[64,4,256]{2,1,0:T(4,128)S(1)}, u32[]{:S(2)}, u32[]{:S(2)}) collective-permute-start(f32[64,4,256]{2,1,0:T(4,128)S(1)} %get-tuple-element.65), channel_id=1, source_target_pairs={{1,2},{2,1},{3,4},{4,3},{5,6},{6,5},{7,8},{8,7},{9,10},{10,9},{11,... | collective-permute-start | bytes 786440 | tf_op jit(solution)/shard_map/ppermute | solution.py:366
  61.5 0.1 collective-permute-start.6
  61.5 5.8 %collective-permute-done.5.halo_ref = f32[64,4,256]{2,1,0:T(4,128)S(1)} collective-permute-done((f32[64,4,256]{2,1,0:T(4,128)S(1)}, f32[64,4,256]{2,1,0:T(4,128)S(1)}, u32[]{:S(2)}, u32[]{:S(2)}) %collective-permute-start.5) | collective-permute-done | bytes 262176 | tf_op jit(solution)/shard_map/ppermute | solution.py:366
  67.3 3.2 %shard_map.109 = (f32[64,16,256]{2,1,0:T(8,128)S(1)}, f32[64,16,256]{2,1,0:T(8,128)S(1)}, f32[64,4,256]{2,1,0:T(4,128)S(1)}) custom-call(s32[1]{0:T(128)} %bitcast.1.tile_ref, f32[64,16,256]{2,1,0:T(8,128)S(1)} %get-tuple-element.60.cur_ref.prev_ref, ...), custom_call_target="tpu_custom_call", output_to_operand_aliasing={{1}: (7, {}), {0}: (8, {})} | custom-call | flops 7864320 | bytes 3670016 | tf_op jit(solution)/shard_map/pallas_call | solution.py:254
  70.6 0.0 collective-permute-done.6.halo_ref
  70.6 3.3 %shard_map.110 = (f32[64,16,256]{2,1,0:T(8,128)S(1)}, f32[64,16,256]{2,1,0:T(8,128)S(1)}, f32[64,4,256]{2,1,0:T(4,128)S(1)}) custom-call(s32[1]{0:T(128)} %bitcast.5.tile_ref, f32[64,16,256]{2,1,0:T(8,128)S(1)} %get-tuple-element.68.cur_ref.prev_ref, f32[64,16,256]{2,1,0:T(8,128)S(1)} %get-tuple-element.60.cur_ref.prev_ref, ...), custom_call_target="tpu_custom_call", output_to_operand_aliasing={{1}: (7, {})} | custom-call | flops 7864320 | bytes 3670016 | tf_op jit(solution)/shard_map/pallas_call | solution.py:254
  73.9 3.9 %collective-permute-start.7 = (f32[64,4,256]{2,1,0:T(4,128)S(1)}, f32[64,4,256]{2,1,0:T(4,128)S(1)}, u32[]{:S(2)}, u32[]{:S(2)}) collective-permute-start(f32[64,4,256]{2,1,0:T(4,128)S(1)} %get-tuple-element.73), channel_id=1, source_target_pairs={{1,2},{2,1},{3,4},{4,3},{5,6},{6,5},{7,8},{8,7},{9,10},{10,9},{11,... | collective-permute-start | bytes 786440 | tf_op jit(solution)/shard_map/ppermute | solution.py:366
  77.8 0.1 collective-permute-start.8
  77.9 5.8 %collective-permute-done.7.halo_ref = f32[64,4,256]{2,1,0:T(4,128)S(1)} collective-permute-done((f32[64,4,256]{2,1,0:T(4,128)S(1)}, f32[64,4,256]{2,1,0:T(4,128)S(1)}, u32[]{:S(2)}, u32[]{:S(2)}) %collective-permute-start.7) | collective-permute-done | bytes 262176 | tf_op jit(solution)/shard_map/ppermute | solution.py:366
  83.7 3.2 %shard_map.111 = (f32[64,16,256]{2,1,0:T(8,128)S(1)}, f32[64,16,256]{2,1,0:T(8,128)S(1)}, f32[64,4,256]{2,1,0:T(4,128)S(1)}) custom-call(s32[1]{0:T(128)} %bitcast.1.tile_ref, f32[64,16,256]{2,1,0:T(8,128)S(1)} %get-tuple-element.68.cur_ref.prev_ref, ...), custom_call_target="tpu_custom_call", output_to_operand_aliasing={{1}: (7, {}), {0}: (8, {})} | custom-call | flops 7864320 | bytes 3670016 | tf_op jit(solution)/shard_map/pallas_call | solution.py:254
  86.9 0.0 collective-permute-done.8.halo_ref
  86.9 3.3 %shard_map.112 = (f32[64,16,256]{2,1,0:T(8,128)S(1)}, f32[64,16,256]{2,1,0:T(8,128)S(1)}, f32[64,4,256]{2,1,0:T(4,128)S(1)}) custom-call(s32[1]{0:T(128)} %bitcast.5.tile_ref, f32[64,16,256]{2,1,0:T(8,128)S(1)} %get-tuple-element.76.cur_ref.prev_ref, f32[64,16,256]{2,1,0:T(8,128)S(1)} %get-tuple-element.68.cur_ref.prev_ref, ...), custom_call_target="tpu_custom_call", output_to_operand_aliasing={{1}: (7, {})} | custom-call | flops 7864320 | bytes 3670016 | tf_op jit(solution)/shard_map/pallas_call | solution.py:254
  90.2 3.9 %collective-permute-start.9 = (f32[64,4,256]{2,1,0:T(4,128)S(1)}, f32[64,4,256]{2,1,0:T(4,128)S(1)}, u32[]{:S(2)}, u32[]{:S(2)}) collective-permute-start(f32[64,4,256]{2,1,0:T(4,128)S(1)} %get-tuple-element.81), channel_id=1, source_target_pairs={{1,2},{2,1},{3,4},{4,3},{5,6},{6,5},{7,8},{8,7},{9,10},{10,9},{11,... | collective-permute-start | bytes 786440 | tf_op jit(solution)/shard_map/ppermute | solution.py:366
  94.1 0.3 collective-permute-start.10
  95.1 4.9 %collective-permute-done.9.halo_ref = f32[64,4,256]{2,1,0:T(4,128)S(1)} collective-permute-done((f32[64,4,256]{2,1,0:T(4,128)S(1)}, f32[64,4,256]{2,1,0:T(4,128)S(1)}, u32[]{:S(2)}, u32[]{:S(2)}) %collective-permute-start.9) | collective-permute-done | bytes 262176 | tf_op jit(solution)/shard_map/ppermute | solution.py:366
  100.0 0.0 copy-start.1
  100.0 3.3 %shard_map.113 = (f32[64,16,256]{2,1,0:T(8,128)S(1)}, f32[64,16,256]{2,1,0:T(8,128)S(1)}, f32[64,4,256]{2,1,0:T(4,128)S(1)}) custom-call(s32[1]{0:T(128)} %bitcast.1.tile_ref, f32[64,16,256]{2,1,0:T(8,128)S(1)} %get-tuple-element.76.cur_ref.prev_ref, ...), custom_call_target="tpu_custom_call", output_to_operand_aliasing={{1}: (7, {}), {0}: (8, {})} | custom-call | flops 7864320 | bytes 3670016 | tf_op jit(solution)/shard_map/pallas_call | solution.py:254
  103.4 0.0 collective-permute-done.10.halo_ref
  103.4 0.0 copy-done.1
  103.4 3.9 %shard_map.114 = (f32[64,16,256]{2,1,0:T(8,128)}, f32[64,16,256]{2,1,0:T(8,128)S(1)}, f32[64,4,256]{2,1,0:T(4,128)}) custom-call(s32[1]{0:T(128)} %bitcast.5.tile_ref, f32[64,16,256]{2,1,0:T(8,128)S(1)} %get-tuple-element.84.cur_ref, f32[64,16,256]{2,1,0:T(8,128)S(1)} %get-tuple-element.76.cur_ref.prev_ref, ...), custom_call_target="tpu_custom_call", output_to_operand_aliasing={{1}: (7, {})} | custom-call | flops 7864320 | bytes 3670016 | tf_op jit(solution)/shard_map/pallas_call | solution.py:254
  107.3 3.9 %collective-permute-start.11 = (f32[64,4,256]{2,1,0:T(4,128)S(1)}, f32[64,4,256]{2,1,0:T(4,128)S(1)}, u32[]{:S(2)}, u32[]{:S(2)}) collective-permute-start(f32[64,4,256]{2,1,0:T(4,128)S(1)} %get-tuple-element.89), channel_id=1, source_target_pairs={{1,2},{2,1},{3,4},{4,3},{5,6},{6,5},{7,8},{8,7},{9,10},{10,9},{11,... | collective-permute-start | bytes 786440 | tf_op jit(solution)/shard_map/ppermute | solution.py:366
  111.2 5.8 %collective-permute-done.11.halo_ref = f32[64,4,256]{2,1,0:T(4,128)S(1)} collective-permute-done((f32[64,4,256]{2,1,0:T(4,128)S(1)}, f32[64,4,256]{2,1,0:T(4,128)S(1)}, u32[]{:S(2)}, u32[]{:S(2)}) %collective-permute-start.11) | collective-permute-done | bytes 262176 | tf_op jit(solution)/shard_map/ppermute | solution.py:366
  117.1 3.9 %shard_map.115 = (f32[64,16,256]{2,1,0:T(8,128)}, f32[64,16,256]{2,1,0:T(8,128)S(1)}, f32[64,4,256]{2,1,0:T(4,128)}) custom-call(s32[1]{0:T(128)} %bitcast.1.tile_ref, f32[64,16,256]{2,1,0:T(8,128)S(1)} %get-tuple-element.84.cur_ref, f32[64,16,256]{2,1,0:T(8,128)S(1)} %get-tuple-element.76.cur_ref.prev_ref, ...), custom_call_target="tpu_custom_call", output_to_operand_aliasing={{1}: (7, {}), {0}: (8, {})} | custom-call | flops 7864320 | bytes 3670016 | tf_op jit(solution)/shard_map/pallas_call | solution.py:254
  120.9 0.7 gather_fusion
  121.6 0.2 select_select_fusion
  121.9 20.3 %all_to_all.10 = f32[8,10,16,256]{3,2,1,0:T(8,128)S(1)} all-to-all(f32[8,10,16,256]{3,2,1,0:T(8,128)S(1)} %select_select_fusion), channel_id=1, replica_groups=mesh['shot'=8,'space'=16] {'shot'}, dimensions={0} | all-to-all | bytes 2621440 | tf_op jit(solution)/shard_map/all_to_all | solution.py:378
  142.2 0.8 reduce_sum.19
  (7 shorter events, 0.1 us)
Async XLA Ops:
  0.6 4.4 %copy-start = (bf16[1,256,1536]{2,1,0:T(8,128)(2,1)S(1)}, bf16[1,256,1536]{2,1,0:T(8,128)(2,1)}, u32[]{:S(2)}) copy-start(bf16[1,256,1536]{2,1,0:T(8,128)(2,1)} %param.9) | copy-start | bytes 2359300
  2.0 18.2 %collective-permute-start = (f32[64,4,256]{2,1,0:T(4,128)S(1)}, f32[64,4,256]{2,1,0:T(4,128)S(1)}, u32[]{:S(2)}, u32[]{:S(2)}) collective-permute-start(f32[64,4,256]{2,1,0:T(4,128)S(1)} %get-tuple-element.94), channel_id=1, source_target_pairs={{0,1},{1,0},{2,3},{3,2},{4,5},{5,4},{6,7},{7,6},{8,9},{9,8},{10,11... | collective-permute-start | bytes 786440 | tf_op jit(solution)/shard_map/ppermute | solution.py:360
  7.4 9.4 %all-to-all-start = ((f32[16,1,336]{2,1,0:T(1,128)}), f32[16,1,336]{2,1,0:T(1,128)S(1)}, u32[]{:S(2)}, u32[]{:S(2)}) async-start(f32[16,1,336]{2,1,0:T(1,128)} %reshape.102), calls=%async_computation | async-start | bytes 49152 | tf_op jit(solution)/shard_map/all_to_all | solution.py:328
  18.1 2.2 %copy-start.2 = (f32[1,64,16,256]{3,2,1,0:T(8,128)S(1)}, f32[1,64,16,256]{3,2,1,0:T(8,128)}, u32[]{:S(2)}) copy-start(f32[1,64,16,256]{3,2,1,0:T(8,128)} %param.16) | copy-start | bytes 3145732
  20.3 1.2 copy-start.3
  24.8 9.8 %collective-permute-start.1 = (f32[64,4,256]{2,1,0:T(4,128)S(1)}, f32[64,4,256]{2,1,0:T(4,128)S(1)}, u32[]{:S(2)}, u32[]{:S(2)}) collective-permute-start(f32[64,4,256]{2,1,0:T(4,128)S(1)} %get-tuple-element.49), channel_id=1, source_target_pairs={{1,2},{2,1},{3,4},{4,3},{5,6},{6,5},{7,8},{8,7},{9,10},{10,9},{11,... | collective-permute-start | bytes 786440 | tf_op jit(solution)/shard_map/ppermute | solution.py:366
  28.8 9.1 %collective-permute-start.2 = (f32[64,4,256]{2,1,0:T(4,128)S(1)}, f32[64,4,256]{2,1,0:T(4,128)S(1)}, u32[]{:S(2)}, u32[]{:S(2)}) collective-permute-start(f32[64,4,256]{2,1,0:T(4,128)S(1)} %get-tuple-element.54), channel_id=1, source_target_pairs={{0,1},{1,0},{2,3},{3,2},{4,5},{5,4},{6,7},{7,6},{8,9},{9,8},{10,11... | collective-permute-start | bytes 786440 | tf_op jit(solution)/shard_map/ppermute | solution.py:360
  41.2 9.8 %collective-permute-start.3 = (f32[64,4,256]{2,1,0:T(4,128)S(1)}, f32[64,4,256]{2,1,0:T(4,128)S(1)}, u32[]{:S(2)}, u32[]{:S(2)}) collective-permute-start(f32[64,4,256]{2,1,0:T(4,128)S(1)} %get-tuple-element.57), channel_id=1, source_target_pairs={{1,2},{2,1},{3,4},{4,3},{5,6},{6,5},{7,8},{8,7},{9,10},{10,9},{11,... | collective-permute-start | bytes 786440 | tf_op jit(solution)/shard_map/ppermute | solution.py:366
  45.1 9.1 %collective-permute-start.4 = (f32[64,4,256]{2,1,0:T(4,128)S(1)}, f32[64,4,256]{2,1,0:T(4,128)S(1)}, u32[]{:S(2)}, u32[]{:S(2)}) collective-permute-start(f32[64,4,256]{2,1,0:T(4,128)S(1)} %get-tuple-element.62), channel_id=1, source_target_pairs={{0,1},{1,0},{2,3},{3,2},{4,5},{5,4},{6,7},{7,6},{8,9},{9,8},{10,11... | collective-permute-start | bytes 786440 | tf_op jit(solution)/shard_map/ppermute | solution.py:360
  57.5 9.8 %collective-permute-start.5 = (f32[64,4,256]{2,1,0:T(4,128)S(1)}, f32[64,4,256]{2,1,0:T(4,128)S(1)}, u32[]{:S(2)}, u32[]{:S(2)}) collective-permute-start(f32[64,4,256]{2,1,0:T(4,128)S(1)} %get-tuple-element.65), channel_id=1, source_target_pairs={{1,2},{2,1},{3,4},{4,3},{5,6},{6,5},{7,8},{8,7},{9,10},{10,9},{11,... | collective-permute-start | bytes 786440 | tf_op jit(solution)/shard_map/ppermute | solution.py:366
  61.5 9.1 %collective-permute-start.6 = (f32[64,4,256]{2,1,0:T(4,128)S(1)}, f32[64,4,256]{2,1,0:T(4,128)S(1)}, u32[]{:S(2)}, u32[]{:S(2)}) collective-permute-start(f32[64,4,256]{2,1,0:T(4,128)S(1)} %get-tuple-element.70), channel_id=1, source_target_pairs={{0,1},{1,0},{2,3},{3,2},{4,5},{5,4},{6,7},{7,6},{8,9},{9,8},{10,11... | collective-permute-start | bytes 786440 | tf_op jit(solution)/shard_map/ppermute | solution.py:360
  73.9 9.8 %collective-permute-start.7 = (f32[64,4,256]{2,1,0:T(4,128)S(1)}, f32[64,4,256]{2,1,0:T(4,128)S(1)}, u32[]{:S(2)}, u32[]{:S(2)}) collective-permute-start(f32[64,4,256]{2,1,0:T(4,128)S(1)} %get-tuple-element.73), channel_id=1, source_target_pairs={{1,2},{2,1},{3,4},{4,3},{5,6},{6,5},{7,8},{8,7},{9,10},{10,9},{11,... | collective-permute-start | bytes 786440 | tf_op jit(solution)/shard_map/ppermute | solution.py:366
  77.8 9.1 %collective-permute-start.8 = (f32[64,4,256]{2,1,0:T(4,128)S(1)}, f32[64,4,256]{2,1,0:T(4,128)S(1)}, u32[]{:S(2)}, u32[]{:S(2)}) collective-permute-start(f32[64,4,256]{2,1,0:T(4,128)S(1)} %get-tuple-element.78), channel_id=1, source_target_pairs={{0,1},{1,0},{2,3},{3,2},{4,5},{5,4},{6,7},{7,6},{8,9},{9,8},{10,11... | collective-permute-start | bytes 786440 | tf_op jit(solution)/shard_map/ppermute | solution.py:360
  90.2 9.8 %collective-permute-start.9 = (f32[64,4,256]{2,1,0:T(4,128)S(1)}, f32[64,4,256]{2,1,0:T(4,128)S(1)}, u32[]{:S(2)}, u32[]{:S(2)}) collective-permute-start(f32[64,4,256]{2,1,0:T(4,128)S(1)} %get-tuple-element.81), channel_id=1, source_target_pairs={{1,2},{2,1},{3,4},{4,3},{5,6},{6,5},{7,8},{8,7},{9,10},{10,9},{11,... | collective-permute-start | bytes 786440 | tf_op jit(solution)/shard_map/ppermute | solution.py:366
  94.1 9.2 %collective-permute-start.10 = (f32[64,4,256]{2,1,0:T(4,128)S(1)}, f32[64,4,256]{2,1,0:T(4,128)S(1)}, u32[]{:S(2)}, u32[]{:S(2)}) collective-permute-start(f32[64,4,256]{2,1,0:T(4,128)S(1)} %get-tuple-element.86), channel_id=1, source_target_pairs={{0,1},{1,0},{2,3},{3,2},{4,5},{5,4},{6,7},{7,6},{8,9},{9,8},{10,11... | collective-permute-start | bytes 786440 | tf_op jit(solution)/shard_map/ppermute | solution.py:360
  100.0 3.4 %copy-start.1 = (f32[1,64,16,256]{3,2,1,0:T(8,128)S(1)}, f32[1,64,16,256]{3,2,1,0:T(8,128)}, u32[]{:S(2)}) copy-start(f32[1,64,16,256]{3,2,1,0:T(8,128)} %param.14) | copy-start | bytes 3145732
  107.3 9.8 %collective-permute-start.11 = (f32[64,4,256]{2,1,0:T(4,128)S(1)}, f32[64,4,256]{2,1,0:T(4,128)S(1)}, u32[]{:S(2)}, u32[]{:S(2)}) collective-permute-start(f32[64,4,256]{2,1,0:T(4,128)S(1)} %get-tuple-element.89), channel_id=1, source_target_pairs={{1,2},{2,1},{3,4},{4,3},{5,6},{6,5},{7,8},{8,7},{9,10},{10,9},{11,... | collective-permute-start | bytes 786440 | tf_op jit(solution)/shard_map/ppermute | solution.py:366

commit v12 on v9

--- a/solution.py
+++ b/solution.py
@@ -273,6 +273,22 @@
     )(*operands)
 
 
+def exact_select(select, table, dimension_numbers):
+    high = lax.reduce_precision(table, exponent_bits=8, mantissa_bits=7)
+    rest = table - high
+    middle = lax.reduce_precision(rest, exponent_bits=8, mantissa_bits=7)
+    low = rest - middle
+    select = select.astype(jnp.bfloat16)
+    parts = [
+        lax.dot_general(
+            select, part.astype(jnp.bfloat16), dimension_numbers,
+            preferred_element_type=jnp.float32,
+        )
+        for part in (high, middle, low)
+    ]
+    return (parts[0] + parts[1]) + parts[2]
+
+
 def halo(first, last):
     axis = "space"
     devices = lax.axis_size(axis)
@@ -323,7 +339,7 @@
     placing = (
         slot_index[None, :] == jnp.arange(slots, dtype=jnp.int32)[:, None]
     ).astype(jnp.float32)
-    buffer = jnp.dot(placing, payload, precision=lax.Precision.HIGHEST)
+    buffer = exact_select(placing, payload, (((1,), (0,)), ((), ())))
     buffer = buffer.reshape(tiles_count, slot_count, step_count + 1)
     arrived = lax.all_to_all(buffer, "space", split_axis=0, concat_axis=0, tiled=True)
     arrived = arrived.reshape(slots, step_count + 1)
@@ -331,12 +347,7 @@
     gathering = (
         cell_of[:, None] == jnp.arange(1, surface + 1, dtype=jnp.int32)[None, :]
     ).astype(jnp.float32)
-    source = lax.dot_general(
-        gathering,
-        arrived[:, :step_count],
-        (((0,), (0,)), ((), ())),
-        precision=lax.Precision.HIGHEST,
-    )
+    source = exact_select(gathering, arrived[:, :step_count], (((0,), (0,)), ((), ())))
     source = source.reshape(cells_y, cells_x, step_count)
     shift_rows = offsets[0]
     speed_sq = velocity[0]

time: 121 us -> 121 us (level)
  waiting for transfers between devices: 12.9 us -> 8.78 us
  starting transfers between devices: 28.8 us -> 32 us
    ppermute x6, waiting for transfers between devices: 12.1 us -> 8.76 us  [local(): far_halo = lax.ppermute(far_edge, 'space', across)]
    ppermute x6, starting transfers between devices: 21.9 us -> 25.2 us  [local(): far_halo = lax.ppermute(far_edge, 'space', across)]
    unnamed x10 -> x14, local copies, waits for them, and re-layouts: 2.03 us -> 3.68 us
    dynamic_slice x1, local copies, waits for them, and re-layouts: 2.07 us -> 0.84 us  [local(): lax.dynamic_slice(current, (zero, near_start, zero), (cells_y, width, cel...]
  transfers between devices with their start and end apart: 13 -> 13, of which waited for: 6 -> 5; matrix products, arithmetic and copies ran while one was open for 7% -> 3% of each run, Pallas kernels for 30% -> 30%
where the time goes in v12:
time: 121 us; the launch traced here: 120 us
  Pallas kernels  40.4 us (33%)
  starting transfers between devices  32 us (26%)
  blocking collectives  23.9 us (20%)
  waiting for transfers between devices  8.78 us (7%)
  local copies, waits for them, and re-layouts  6.29 us (5%)
  other arithmetic  4.07 us (3%)
  matrix products  2.95 us (2%)
  between operations  1.65 us (1%)
    pallas_call x12, Pallas kernels, tile_call(): pl.pallas_call(functools.partial(tile_kernel, moment, chained), grid_spec...  40.4 us
    ppermute x6, starting transfers between devices, local(): far_halo = lax.ppermute(far_edge, 'space', across)  25.2 us
    all_to_all x1, blocking collectives, local(): lax.all_to_all(placed, 'shot', split_axis=0, concat_axis=0, tiled=True)  23.9 us
    ppermute x6, waiting for transfers between devices, local(): far_halo = lax.ppermute(far_edge, 'space', across)  8.76 us
    all_to_all x1, starting transfers between devices, local(): lax.all_to_all(buffer, 'space', split_axis=0, concat_axis=0, tiled=True)  5.82 us
    unnamed x14, local copies, waits for them, and re-layouts  3.68 us
  transfers between devices with their start and end apart: 13, of which 5 were waited for; matrix products, arithmetic and copies ran while one was open for 3% of the time, Pallas kernels for 30%

profile of v12, /device:TPU:97, one launch (start us, length us, event | category | flops | bytes accessed | tf_op | source)
XLA Modules:
  0.0 120.1 jit_solution(4155024156942063074)
XLA Ops:
  0.6 0.0 copy-start
  0.7 0.9 convert_reduce_fusion
  1.6 0.7 multiply_add_fusion
  2.3 0.7 convert_bitcast_fusion
  3.0 1.0 fusion.11
  4.0 0.3 fusion.13
  4.3 0.3 convolution_add_fusion.1
  4.5 0.3 convolution_add_fusion
  4.8 0.1 reshape.89
  4.9 0.7 reshape.102
  5.6 5.8 %all-to-all-start = ((f32[16,1,336]{2,1,0:T(1,128)}), f32[16,1,336]{2,1,0:T(1,128)S(1)}, u32[]{:S(2)}, u32[]{:S(2)}) async-start(f32[16,1,336]{2,1,0:T(1,128)} %reshape.102), calls=%async_computation | async-start | bytes 49152 | tf_op jit(solution)/shard_map/all_to_all | solution.py:344
  11.5 0.8 dynamic-slice_bitcast_fusion
  12.3 0.4 collective-permute-start.1
  12.7 3.1 %collective-permute-start = (f32[64,4,256]{2,1,0:T(4,128)}, f32[64,4,256]{2,1,0:T(4,128)}, u32[]{:S(2)}, u32[]{:S(2)}) collective-permute-start(f32[64,4,256]{2,1,0:T(4,128)} %get-tuple-element.71), channel_id=1, source_target_pairs={{1,2},{2,1},{3,4},{4,3},{5,6},{6,5},{7,8},{8,7},{9,10},{10,9},{11,... | collective-permute-start | bytes 786440 | tf_op jit(solution)/shard_map/ppermute | solution.py:372
  15.8 0.0 all-to-all-done
  15.8 0.5 broadcast.101
  16.3 0.7 reduce.2
  17.0 0.1 reshape.103
  17.1 0.1 reshape.90
  17.2 0.4 fusion
  17.6 0.4 fusion.1
  18.0 0.4 fusion.10
  18.4 0.2 copy.37
  18.6 0.0 collective-permute-done.1.halo_ref
  18.7 0.7 copy-done.4
  19.4 0.1 broadcast_in_dim.38.img_ref
  19.5 0.0 copy-start.3
  19.5 1.2 %copy-done.3 = f32[1,64,16,256]{3,2,1,0:T(8,128)S(1)} copy-done((f32[1,64,16,256]{3,2,1,0:T(8,128)S(1)}, f32[1,64,16,256]{3,2,1,0:T(8,128)}, u32[]{:S(2)}) %copy-start.3) | copy-done | bytes 1048600
  20.7 0.9 copy-done.5
  21.7 3.2 %shard_map.104 = (f32[64,16,256]{2,1,0:T(8,128)S(1)}, f32[64,16,256]{2,1,0:T(8,128)S(1)}, f32[64,4,256]{2,1,0:T(4,128)S(1)}) custom-call(s32[1]{0:T(128)} %bitcast.11.tile_ref, f32[64,16,256]{2,1,0:T(8,128)S(1)} %bitcast.57, f32[64,16,256]{2,1,0:T(8,128)S(1)} %bitcast.61, f32[64,4,256]{2,1,0:T(4,128)S(1)} %copy-done.5, ...), custom_call_target="tpu_custom_call", output_to_operand_aliasing={{1}: (7, {})} | custom-call | flops 7864320 | bytes 3670016 | tf_op jit(solution)/shard_map/pallas_call | solution.py:254
  24.9 0.3 collective-permute-start.3
  25.2 0.0 collective-permute-done.halo_ref
  25.2 3.3 %shard_map.105 = (f32[64,16,256]{2,1,0:T(8,128)S(1)}, f32[64,16,256]{2,1,0:T(8,128)S(1)}, f32[64,4,256]{2,1,0:T(4,128)S(1)}) custom-call(s32[1]{0:T(128)} %bitcast.1.tile_ref, f32[64,16,256]{2,1,0:T(8,128)S(1)} %bitcast.58, f32[64,16,256]{2,1,0:T(8,128)S(1)} %bitcast.62, ...), custom_call_target="tpu_custom_call", output_to_operand_aliasing={{1}: (7, {}), {0}: (8, {})} | custom-call | flops 7864320 | bytes 3670016 | tf_op jit(solution)/shard_map/pallas_call | solution.py:254
  28.5 4.4 %collective-permute-start.2 = (f32[64,4,256]{2,1,0:T(4,128)S(1)}, f32[64,4,256]{2,1,0:T(4,128)S(1)}, u32[]{:S(2)}, u32[]{:S(2)}) collective-permute-start(f32[64,4,256]{2,1,0:T(4,128)S(1)} %get-tuple-element.39), channel_id=1, source_target_pairs={{1,2},{2,1},{3,4},{4,3},{5,6},{6,5},{7,8},{8,7},{9,10},{10,9},{11,... | collective-permute-start | bytes 786440 | tf_op jit(solution)/shard_map/ppermute | solution.py:372
  32.9 0.0 collective-permute-done.3.halo_ref
  33.0 3.3 %shard_map.106 = (f32[64,16,256]{2,1,0:T(8,128)S(1)}, f32[64,16,256]{2,1,0:T(8,128)S(1)}, f32[64,4,256]{2,1,0:T(4,128)S(1)}) custom-call(s32[1]{0:T(128)} %bitcast.11.tile_ref, f32[64,16,256]{2,1,0:T(8,128)S(1)} %get-tuple-element.38.cur_ref.prev_ref, f32[64,16,256]{2,1,0:T(8,128)S(1)} %bitcast.59, ...), custom_call_target="tpu_custom_call", output_to_operand_aliasing={{1}: (7, {})} | custom-call | flops 7864320 | bytes 3670016 | tf_op jit(solution)/shard_map/pallas_call | solution.py:254
  36.2 0.1 collective-permute-start.5
  36.3 2.0 %collective-permute-done.2.halo_ref = f32[64,4,256]{2,1,0:T(4,128)S(1)} collective-permute-done((f32[64,4,256]{2,1,0:T(4,128)S(1)}, f32[64,4,256]{2,1,0:T(4,128)S(1)}, u32[]{:S(2)}, u32[]{:S(2)}) %collective-permute-start.2) | collective-permute-done | bytes 262176 | tf_op jit(solution)/shard_map/ppermute | solution.py:372
  38.3 3.2 %shard_map.107 = (f32[64,16,256]{2,1,0:T(8,128)S(1)}, f32[64,16,256]{2,1,0:T(8,128)S(1)}, f32[64,4,256]{2,1,0:T(4,128)S(1)}) custom-call(s32[1]{0:T(128)} %bitcast.1.tile_ref, f32[64,16,256]{2,1,0:T(8,128)S(1)} %get-tuple-element.38.cur_ref.prev_ref, f32[64,16,256]{2,1,0:T(8,128)S(1)} %bitcast.60, ...), custom_call_target="tpu_custom_call", output_to_operand_aliasing={{1}: (7, {}), {0}: (8, {})} | custom-call | flops 7864320 | bytes 3670016 | tf_op jit(solution)/shard_map/pallas_call | solution.py:254
  41.6 4.4 %collective-permute-start.4 = (f32[64,4,256]{2,1,0:T(4,128)S(1)}, f32[64,4,256]{2,1,0:T(4,128)S(1)}, u32[]{:S(2)}, u32[]{:S(2)}) collective-permute-start(f32[64,4,256]{2,1,0:T(4,128)S(1)} %get-tuple-element.45), channel_id=1, source_target_pairs={{1,2},{2,1},{3,4},{4,3},{5,6},{6,5},{7,8},{8,7},{9,10},{10,9},{11,... | collective-permute-start | bytes 786440 | tf_op jit(solution)/shard_map/ppermute | solution.py:372
  46.0 3.3 %shard_map.108 = (f32[64,16,256]{2,1,0:T(8,128)S(1)}, f32[64,16,256]{2,1,0:T(8,128)S(1)}, f32[64,4,256]{2,1,0:T(4,128)S(1)}) custom-call(s32[1]{0:T(128)} %bitcast.11.tile_ref, f32[64,16,256]{2,1,0:T(8,128)S(1)} %get-tuple-element.44.cur_ref.prev_ref, f32[64,16,256]{2,1,0:T(8,128)S(1)} %get-tuple-element.38.cur_ref.prev_ref, ...), custom_call_target="tpu_custom_call", output_to_operand_aliasing={{1}: (7, {})} | custom-call | flops 7864320 | bytes 3670016 | tf_op jit(solution)/shard_map/pallas_call | solution.py:254
  49.3 0.1 collective-permute-start.7
  49.4 2.0 %collective-permute-done.4.halo_ref = f32[64,4,256]{2,1,0:T(4,128)S(1)} collective-permute-done((f32[64,4,256]{2,1,0:T(4,128)S(1)}, f32[64,4,256]{2,1,0:T(4,128)S(1)}, u32[]{:S(2)}, u32[]{:S(2)}) %collective-permute-start.4) | collective-permute-done | bytes 262176 | tf_op jit(solution)/shard_map/ppermute | solution.py:372
  51.4 3.2 %shard_map.109 = (f32[64,16,256]{2,1,0:T(8,128)S(1)}, f32[64,16,256]{2,1,0:T(8,128)S(1)}, f32[64,4,256]{2,1,0:T(4,128)S(1)}) custom-call(s32[1]{0:T(128)} %bitcast.1.tile_ref, f32[64,16,256]{2,1,0:T(8,128)S(1)} %get-tuple-element.44.cur_ref.prev_ref, ...), custom_call_target="tpu_custom_call", output_to_operand_aliasing={{1}: (7, {}), {0}: (8, {})} | custom-call | flops 7864320 | bytes 3670016 | tf_op jit(solution)/shard_map/pallas_call | solution.py:254
  54.6 4.4 %collective-permute-start.6 = (f32[64,4,256]{2,1,0:T(4,128)S(1)}, f32[64,4,256]{2,1,0:T(4,128)S(1)}, u32[]{:S(2)}, u32[]{:S(2)}) collective-permute-start(f32[64,4,256]{2,1,0:T(4,128)S(1)} %get-tuple-element.51), channel_id=1, source_target_pairs={{1,2},{2,1},{3,4},{4,3},{5,6},{6,5},{7,8},{8,7},{9,10},{10,9},{11,... | collective-permute-start | bytes 786440 | tf_op jit(solution)/shard_map/ppermute | solution.py:372
  59.1 0.0 collective-permute-done.7.halo_ref
  59.1 3.3 %shard_map.110 = (f32[64,16,256]{2,1,0:T(8,128)S(1)}, f32[64,16,256]{2,1,0:T(8,128)S(1)}, f32[64,4,256]{2,1,0:T(4,128)S(1)}) custom-call(s32[1]{0:T(128)} %bitcast.11.tile_ref, f32[64,16,256]{2,1,0:T(8,128)S(1)} %get-tuple-element.50.cur_ref.prev_ref, f32[64,16,256]{2,1,0:T(8,128)S(1)} %get-tuple-element.44.cur_ref.prev_ref, ...), custom_call_target="tpu_custom_call", output_to_operand_aliasing={{1}: (7, {})} | custom-call | flops 7864320 | bytes 3670016 | tf_op jit(solution)/shard_map/pallas_call | solution.py:254
  62.3 0.1 collective-permute-start.9
  62.4 2.0 %collective-permute-done.6.halo_ref = f32[64,4,256]{2,1,0:T(4,128)S(1)} collective-permute-done((f32[64,4,256]{2,1,0:T(4,128)S(1)}, f32[64,4,256]{2,1,0:T(4,128)S(1)}, u32[]{:S(2)}, u32[]{:S(2)}) %collective-permute-start.6) | collective-permute-done | bytes 262176 | tf_op jit(solution)/shard_map/ppermute | solution.py:372
  64.4 3.2 %shard_map.111 = (f32[64,16,256]{2,1,0:T(8,128)S(1)}, f32[64,16,256]{2,1,0:T(8,128)S(1)}, f32[64,4,256]{2,1,0:T(4,128)S(1)}) custom-call(s32[1]{0:T(128)} %bitcast.1.tile_ref, f32[64,16,256]{2,1,0:T(8,128)S(1)} %get-tuple-element.50.cur_ref.prev_ref, ...), custom_call_target="tpu_custom_call", output_to_operand_aliasing={{1}: (7, {}), {0}: (8, {})} | custom-call | flops 7864320 | bytes 3670016 | tf_op jit(solution)/shard_map/pallas_call | solution.py:254
  67.7 4.4 %collective-permute-start.8 = (f32[64,4,256]{2,1,0:T(4,128)S(1)}, f32[64,4,256]{2,1,0:T(4,128)S(1)}, u32[]{:S(2)}, u32[]{:S(2)}) collective-permute-start(f32[64,4,256]{2,1,0:T(4,128)S(1)} %get-tuple-element.57), channel_id=1, source_target_pairs={{1,2},{2,1},{3,4},{4,3},{5,6},{6,5},{7,8},{8,7},{9,10},{10,9},{11,... | collective-permute-start | bytes 786440 | tf_op jit(solution)/shard_map/ppermute | solution.py:372
  72.8 3.3 %shard_map.112 = (f32[64,16,256]{2,1,0:T(8,128)S(1)}, f32[64,16,256]{2,1,0:T(8,128)S(1)}, f32[64,4,256]{2,1,0:T(4,128)S(1)}) custom-call(s32[1]{0:T(128)} %bitcast.11.tile_ref, f32[64,16,256]{2,1,0:T(8,128)S(1)} %get-tuple-element.56.cur_ref.prev_ref, f32[64,16,256]{2,1,0:T(8,128)S(1)} %get-tuple-element.50.cur_ref.prev_ref, ...), custom_call_target="tpu_custom_call", output_to_operand_aliasing={{1}: (7, {})} | custom-call | flops 7864320 | bytes 3670016 | tf_op jit(solution)/shard_map/pallas_call | solution.py:254
  76.0 0.1 collective-permute-start.11
  76.1 1.3 %collective-permute-done.8.halo_ref = f32[64,4,256]{2,1,0:T(4,128)S(1)} collective-permute-done((f32[64,4,256]{2,1,0:T(4,128)S(1)}, f32[64,4,256]{2,1,0:T(4,128)S(1)}, u32[]{:S(2)}, u32[]{:S(2)}) %collective-permute-start.8) | collective-permute-done | bytes 262176 | tf_op jit(solution)/shard_map/ppermute | solution.py:372
  77.5 3.3 %shard_map.113 = (f32[64,16,256]{2,1,0:T(8,128)S(1)}, f32[64,16,256]{2,1,0:T(8,128)S(1)}, f32[64,4,256]{2,1,0:T(4,128)S(1)}) custom-call(s32[1]{0:T(128)} %bitcast.1.tile_ref, f32[64,16,256]{2,1,0:T(8,128)S(1)} %get-tuple-element.56.cur_ref.prev_ref, ...), custom_call_target="tpu_custom_call", output_to_operand_aliasing={{1}: (7, {}), {0}: (8, {})} | custom-call | flops 7864320 | bytes 3670016 | tf_op jit(solution)/shard_map/pallas_call | solution.py:254
  80.8 4.4 %collective-permute-start.10 = (f32[64,4,256]{2,1,0:T(4,128)S(1)}, f32[64,4,256]{2,1,0:T(4,128)S(1)}, u32[]{:S(2)}, u32[]{:S(2)}) collective-permute-start(f32[64,4,256]{2,1,0:T(4,128)S(1)} %get-tuple-element.63), channel_id=1, source_target_pairs={{1,2},{2,1},{3,4},{4,3},{5,6},{6,5},{7,8},{8,7},{9,10},{10,9},{11,... | collective-permute-start | bytes 786440 | tf_op jit(solution)/shard_map/ppermute | solution.py:372
  85.3 0.0 collective-permute-done.11.halo_ref
  85.3 3.9 %shard_map.114 = (f32[64,16,256]{2,1,0:T(8,128)}, f32[64,16,256]{2,1,0:T(8,128)S(1)}, f32[64,4,256]{2,1,0:T(4,128)}) custom-call(s32[1]{0:T(128)} %bitcast.11.tile_ref, f32[64,16,256]{2,1,0:T(8,128)S(1)} %get-tuple-element.62.cur_ref, f32[64,16,256]{2,1,0:T(8,128)S(1)} %get-tuple-element.56.cur_ref.prev_ref, ...), custom_call_target="tpu_custom_call", output_to_operand_aliasing={{1}: (7, {})} | custom-call | flops 7864320 | bytes 3670016 | tf_op jit(solution)/shard_map/pallas_call | solution.py:254
  89.2 1.4 %collective-permute-done.10.halo_ref = f32[64,4,256]{2,1,0:T(4,128)S(1)} collective-permute-done((f32[64,4,256]{2,1,0:T(4,128)S(1)}, f32[64,4,256]{2,1,0:T(4,128)S(1)}, u32[]{:S(2)}, u32[]{:S(2)}) %collective-permute-start.10) | collective-permute-done | bytes 262176 | tf_op jit(solution)/shard_map/ppermute | solution.py:372
  90.6 3.9 %shard_map.115 = (f32[64,16,256]{2,1,0:T(8,128)}, f32[64,16,256]{2,1,0:T(8,128)S(1)}, f32[64,4,256]{2,1,0:T(4,128)}) custom-call(s32[1]{0:T(128)} %bitcast.1.tile_ref, f32[64,16,256]{2,1,0:T(8,128)S(1)} %get-tuple-element.62.cur_ref, f32[64,16,256]{2,1,0:T(8,128)S(1)} %get-tuple-element.56.cur_ref.prev_ref, ...), custom_call_target="tpu_custom_call", output_to_operand_aliasing={{1}: (7, {}), {0}: (8, {})} | custom-call | flops 7864320 | bytes 3670016 | tf_op jit(solution)/shard_map/pallas_call | solution.py:254
  94.5 0.7 gather_fusion
  95.2 0.2 select_select_fusion
  95.4 23.9 %all_to_all.10 = f32[8,10,16,256]{3,2,1,0:T(8,128)S(1)} all-to-all(f32[8,10,16,256]{3,2,1,0:T(8,128)S(1)} %select_select_fusion), channel_id=1, replica_groups=mesh['shot'=8,'space'=16] {'shot'}, dimensions={0} | all-to-all | bytes 2621440 | tf_op jit(solution)/shard_map/all_to_all | solution.py:388
  119.3 0.8 reduce_sum.19
  (16 shorter events, 0.1 us)
Async XLA Ops:
  0.6 2.3 %copy-start = (bf16[1,256,1536]{2,1,0:T(8,128)(2,1)S(1)}, bf16[1,256,1536]{2,1,0:T(8,128)(2,1)}, u32[]{:S(2)}) copy-start(bf16[1,256,1536]{2,1,0:T(8,128)(2,1)} %param.9) | copy-start | bytes 2359300
  0.6 10.8 %copy-start.2 = (f32[1,64,16,256]{3,2,1,0:T(8,128)S(1)}, f32[1,64,16,256]{3,2,1,0:T(8,128)}, u32[]{:S(2)}) copy-start(f32[1,64,16,256]{3,2,1,0:T(8,128)} %param.16) | copy-start | bytes 3145732
  5.6 10.2 %all-to-all-start = ((f32[16,1,336]{2,1,0:T(1,128)}), f32[16,1,336]{2,1,0:T(1,128)S(1)}, u32[]{:S(2)}, u32[]{:S(2)}) async-start(f32[16,1,336]{2,1,0:T(1,128)} %reshape.102), calls=%async_computation | async-start | bytes 49152 | tf_op jit(solution)/shard_map/all_to_all | solution.py:344
  12.3 6.4 %collective-permute-start.1 = (f32[64,4,256]{2,1,0:T(4,128)S(1)}, f32[64,4,256]{2,1,0:T(4,128)S(1)}, u32[]{:S(2)}, u32[]{:S(2)}) collective-permute-start(f32[64,4,256]{2,1,0:T(4,128)S(1)} %get-tuple-element.70), channel_id=1, source_target_pairs={{0,1},{1,0},{2,3},{3,2},{4,5},{5,4},{6,7},{7,6},{8,9},{9,8},{10,11... | collective-permute-start | bytes 786440 | tf_op jit(solution)/shard_map/ppermute | solution.py:371
  12.7 12.5 %collective-permute-start = (f32[64,4,256]{2,1,0:T(4,128)}, f32[64,4,256]{2,1,0:T(4,128)}, u32[]{:S(2)}, u32[]{:S(2)}) collective-permute-start(f32[64,4,256]{2,1,0:T(4,128)} %get-tuple-element.71), channel_id=1, source_target_pairs={{1,2},{2,1},{3,4},{4,3},{5,6},{6,5},{7,8},{8,7},{9,10},{10,9},{11,... | collective-permute-start | bytes 786440 | tf_op jit(solution)/shard_map/ppermute | solution.py:372
  18.7 0.7 copy-start.4
  19.5 1.2 %copy-start.3 = (f32[1,64,16,256]{3,2,1,0:T(8,128)S(1)}, f32[1,64,16,256]{3,2,1,0:T(8,128)}, u32[]{:S(2)}) copy-start(f32[1,64,16,256]{3,2,1,0:T(8,128)} %param.15) | copy-start | bytes 3145732
  20.7 0.9 copy-start.5
  24.9 8.0 %collective-permute-start.3 = (f32[64,4,256]{2,1,0:T(4,128)S(1)}, f32[64,4,256]{2,1,0:T(4,128)S(1)}, u32[]{:S(2)}, u32[]{:S(2)}) collective-permute-start(f32[64,4,256]{2,1,0:T(4,128)S(1)} %get-tuple-element.40), channel_id=1, source_target_pairs={{0,1},{1,0},{2,3},{3,2},{4,5},{5,4},{6,7},{7,6},{8,9},{9,8},{10,11... | collective-permute-start | bytes 786440 | tf_op jit(solution)/shard_map/ppermute | solution.py:371
  28.5 9.8 %collective-permute-start.2 = (f32[64,4,256]{2,1,0:T(4,128)S(1)}, f32[64,4,256]{2,1,0:T(4,128)S(1)}, u32[]{:S(2)}, u32[]{:S(2)}) collective-permute-start(f32[64,4,256]{2,1,0:T(4,128)S(1)} %get-tuple-element.39), channel_id=1, source_target_pairs={{1,2},{2,1},{3,4},{4,3},{5,6},{6,5},{7,8},{8,7},{9,10},{10,9},{11,... | collective-permute-start | bytes 786440 | tf_op jit(solution)/shard_map/ppermute | solution.py:372
  36.2 9.8 %collective-permute-start.5 = (f32[64,4,256]{2,1,0:T(4,128)S(1)}, f32[64,4,256]{2,1,0:T(4,128)S(1)}, u32[]{:S(2)}, u32[]{:S(2)}) collective-permute-start(f32[64,4,256]{2,1,0:T(4,128)S(1)} %get-tuple-element.46), channel_id=1, source_target_pairs={{0,1},{1,0},{2,3},{3,2},{4,5},{5,4},{6,7},{7,6},{8,9},{9,8},{10,11... | collective-permute-start | bytes 786440 | tf_op jit(solution)/shard_map/ppermute | solution.py:371
  41.6 9.8 %collective-permute-start.4 = (f32[64,4,256]{2,1,0:T(4,128)S(1)}, f32[64,4,256]{2,1,0:T(4,128)S(1)}, u32[]{:S(2)}, u32[]{:S(2)}) collective-permute-start(f32[64,4,256]{2,1,0:T(4,128)S(1)} %get-tuple-element.45), channel_id=1, source_target_pairs={{1,2},{2,1},{3,4},{4,3},{5,6},{6,5},{7,8},{8,7},{9,10},{10,9},{11,... | collective-permute-start | bytes 786440 | tf_op jit(solution)/shard_map/ppermute | solution.py:372
  49.3 9.8 %collective-permute-start.7 = (f32[64,4,256]{2,1,0:T(4,128)S(1)}, f32[64,4,256]{2,1,0:T(4,128)S(1)}, u32[]{:S(2)}, u32[]{:S(2)}) collective-permute-start(f32[64,4,256]{2,1,0:T(4,128)S(1)} %get-tuple-element.52), channel_id=1, source_target_pairs={{0,1},{1,0},{2,3},{3,2},{4,5},{5,4},{6,7},{7,6},{8,9},{9,8},{10,11... | collective-permute-start | bytes 786440 | tf_op jit(solution)/shard_map/ppermute | solution.py:371
  54.6 9.8 %collective-permute-start.6 = (f32[64,4,256]{2,1,0:T(4,128)S(1)}, f32[64,4,256]{2,1,0:T(4,128)S(1)}, u32[]{:S(2)}, u32[]{:S(2)}) collective-permute-start(f32[64,4,256]{2,1,0:T(4,128)S(1)} %get-tuple-element.51), channel_id=1, source_target_pairs={{1,2},{2,1},{3,4},{4,3},{5,6},{6,5},{7,8},{8,7},{9,10},{10,9},{11,... | collective-permute-start | bytes 786440 | tf_op jit(solution)/shard_map/ppermute | solution.py:372
  62.3 10.4 %collective-permute-start.9 = (f32[64,4,256]{2,1,0:T(4,128)S(1)}, f32[64,4,256]{2,1,0:T(4,128)S(1)}, u32[]{:S(2)}, u32[]{:S(2)}) collective-permute-start(f32[64,4,256]{2,1,0:T(4,128)S(1)} %get-tuple-element.58), channel_id=1, source_target_pairs={{0,1},{1,0},{2,3},{3,2},{4,5},{5,4},{6,7},{7,6},{8,9},{9,8},{10,11... | collective-permute-start | bytes 786440 | tf_op jit(solution)/shard_map/ppermute | solution.py:371
  67.7 9.8 %collective-permute-start.8 = (f32[64,4,256]{2,1,0:T(4,128)S(1)}, f32[64,4,256]{2,1,0:T(4,128)S(1)}, u32[]{:S(2)}, u32[]{:S(2)}) collective-permute-start(f32[64,4,256]{2,1,0:T(4,128)S(1)} %get-tuple-element.57), channel_id=1, source_target_pairs={{1,2},{2,1},{3,4},{4,3},{5,6},{6,5},{7,8},{8,7},{9,10},{10,9},{11,... | collective-permute-start | bytes 786440 | tf_op jit(solution)/shard_map/ppermute | solution.py:372
  76.0 9.3 %collective-permute-start.11 = (f32[64,4,256]{2,1,0:T(4,128)S(1)}, f32[64,4,256]{2,1,0:T(4,128)S(1)}, u32[]{:S(2)}, u32[]{:S(2)}) collective-permute-start(f32[64,4,256]{2,1,0:T(4,128)S(1)} %get-tuple-element.64), channel_id=1, source_target_pairs={{0,1},{1,0},{2,3},{3,2},{4,5},{5,4},{6,7},{7,6},{8,9},{9,8},{10,11... | collective-permute-start | bytes 786440 | tf_op jit(solution)/shard_map/ppermute | solution.py:371
  77.5 7.8 %copy-start.1 = (f32[1,64,16,256]{3,2,1,0:T(8,128)S(1)}, f32[1,64,16,256]{3,2,1,0:T(8,128)}, u32[]{:S(2)}) copy-start(f32[1,64,16,256]{3,2,1,0:T(8,128)} %param.14) | copy-start | bytes 3145732
  80.8 9.8 %collective-permute-start.10 = (f32[64,4,256]{2,1,0:T(4,128)S(1)}, f32[64,4,256]{2,1,0:T(4,128)S(1)}, u32[]{:S(2)}, u32[]{:S(2)}) collective-permute-start(f32[64,4,256]{2,1,0:T(4,128)S(1)} %get-tuple-element.63), channel_id=1, source_target_pairs={{1,2},{2,1},{3,4},{4,3},{5,6},{6,5},{7,8},{8,7},{9,10},{10,9},{11,... | collective-permute-start | bytes 786440 | tf_op jit(solution)/shard_map/ppermute | solution.py:372

commit v13 on v12

--- a/solution.py
+++ b/solution.py
@@ -362,11 +362,11 @@
     devices = lax.axis_size("space")
     within = [(i, i ^ 1) for i in range(devices)]
     across = [(i, i + 1 - 2 * ((i + 1) % 2)) for i in range(1, devices - 1)]
-    zero = jnp.zeros((), jnp.int32)
-    near_start = (1 - odd) * (cells_x - width)
-    near_edge = lax.dynamic_slice(current, (zero, near_start, zero), (cells_y, width, cells_z))
-    far_start = odd * (cells_x - width)
-    far_edge = lax.dynamic_slice(current, (zero, far_start, zero), (cells_y, width, cells_z))
+    first = current[:, :width]
+    last = current[:, cells_x - width :]
+    even = odd == 0
+    near_edge = jnp.where(even, last, first)
+    far_edge = jnp.where(even, first, last)
     for moment in range(step_count):
         near_halo = lax.ppermute(near_edge, "space", within)
         far_halo = lax.ppermute(far_edge, "space", across)

time: 121 us -> 121 us (level)
  no operation moved by 1% of the time
where the time goes in v13:
time: 121 us; the launch traced here: 120 us
  Pallas kernels  40.4 us (33%)
  starting transfers between devices  31.9 us (26%)
  blocking collectives  23.8 us (20%)
  waiting for transfers between devices  8.98 us (7%)
  local copies, waits for them, and re-layouts  5.45 us (5%)
  other arithmetic  4.86 us (4%)
  matrix products  2.95 us (2%)
  between operations  1.66 us (1%)
    pallas_call x12, Pallas kernels, tile_call(): pl.pallas_call(functools.partial(tile_kernel, moment, chained), grid_spec...  40.4 us
    ppermute x6, starting transfers between devices, local(): far_halo = lax.ppermute(far_edge, 'space', across)  25 us
    all_to_all x1, blocking collectives, local(): lax.all_to_all(placed, 'shot', split_axis=0, concat_axis=0, tiled=True)  23.8 us
    ppermute x6, waiting for transfers between devices, local(): far_halo = lax.ppermute(far_edge, 'space', across)  8.96 us
    all_to_all x1, starting transfers between devices, local(): lax.all_to_all(buffer, 'space', split_axis=0, concat_axis=0, tiled=True)  5.82 us
    unnamed x14, local copies, waits for them, and re-layouts  3.68 us
  transfers between devices with their start and end apart: 13, of which 5 were waited for; matrix products, arithmetic and copies ran while one was open for 3% of the time, Pallas kernels for 30%

profile of v13, /device:TPU:97, one launch (start us, length us, event | category | flops | bytes accessed | tf_op | source)
XLA Modules:
  0.0 120.0 jit_solution(16148449218629625850)
XLA Ops:
  0.6 0.0 copy-start
  0.7 0.9 convert_reduce_fusion
  1.6 0.7 multiply_add_fusion
  2.3 0.7 convert_bitcast_fusion
  3.0 1.0 fusion.11
  4.0 0.3 fusion.13
  4.3 0.3 convolution_add_fusion.1
  4.5 0.3 convolution_add_fusion
  4.8 0.1 reshape.87
  4.9 0.7 reshape.100
  5.6 5.8 %all-to-all-start = ((f32[16,1,336]{2,1,0:T(1,128)}), f32[16,1,336]{2,1,0:T(1,128)S(1)}, u32[]{:S(2)}, u32[]{:S(2)}) async-start(f32[16,1,336]{2,1,0:T(1,128)} %reshape.100), calls=%async_computation | async-start | bytes 49152 | tf_op jit(solution)/shard_map/all_to_all | solution.py:344
  11.5 0.8 slice_select_fusion
  12.3 0.4 collective-permute-start.1
  12.6 3.1 %collective-permute-start = (f32[64,4,256]{2,1,0:T(4,128)}, f32[64,4,256]{2,1,0:T(4,128)}, u32[]{:S(2)}, u32[]{:S(2)}) collective-permute-start(f32[64,4,256]{2,1,0:T(4,128)} %get-tuple-element.71), channel_id=1, source_target_pairs={{1,2},{2,1},{3,4},{4,3},{5,6},{6,5},{7,8},{8,7},{9,10},{10,9},{11,... | collective-permute-start | bytes 786440 | tf_op jit(solution)/shard_map/ppermute | solution.py:372
  15.8 0.5 broadcast.101
  16.3 0.7 reduce.2
  17.0 0.1 reshape.101
  17.1 0.1 reshape.88
  17.2 0.4 fusion
  17.6 0.4 fusion.1
  18.0 0.4 fusion.10
  18.4 0.2 copy.37
  18.6 0.0 collective-permute-done.1.halo_ref
  18.6 0.7 copy-done.4
  19.3 0.1 broadcast_in_dim.38.img_ref
  19.4 0.0 copy-start.3
  19.5 1.2 %copy-done.3 = f32[1,64,16,256]{3,2,1,0:T(8,128)S(1)} copy-done((f32[1,64,16,256]{3,2,1,0:T(8,128)S(1)}, f32[1,64,16,256]{3,2,1,0:T(8,128)}, u32[]{:S(2)}) %copy-start.3) | copy-done | bytes 1048600
  20.7 0.9 copy-done.5
  21.6 3.2 %shard_map.104 = (f32[64,16,256]{2,1,0:T(8,128)S(1)}, f32[64,16,256]{2,1,0:T(8,128)S(1)}, f32[64,4,256]{2,1,0:T(4,128)S(1)}) custom-call(s32[1]{0:T(128)} %bitcast.10.tile_ref, f32[64,16,256]{2,1,0:T(8,128)S(1)} %bitcast.54, f32[64,16,256]{2,1,0:T(8,128)S(1)} %bitcast.58, f32[64,4,256]{2,1,0:T(4,128)S(1)} %copy-done.5, ...), custom_call_target="tpu_custom_call", output_to_operand_aliasing={{1}: (7, {})} | custom-call | flops 7864320 | bytes 3670016 | tf_op jit(solution)/shard_map/pallas_call | solution.py:254
  24.9 0.3 collective-permute-start.3
  25.2 0.0 collective-permute-done.halo_ref
  25.2 3.3 %shard_map.105 = (f32[64,16,256]{2,1,0:T(8,128)S(1)}, f32[64,16,256]{2,1,0:T(8,128)S(1)}, f32[64,4,256]{2,1,0:T(4,128)S(1)}) custom-call(s32[1]{0:T(128)} %bitcast.1.tile_ref, f32[64,16,256]{2,1,0:T(8,128)S(1)} %bitcast.55, f32[64,16,256]{2,1,0:T(8,128)S(1)} %bitcast.59, ...), custom_call_target="tpu_custom_call", output_to_operand_aliasing={{1}: (7, {}), {0}: (8, {})} | custom-call | flops 7864320 | bytes 3670016 | tf_op jit(solution)/shard_map/pallas_call | solution.py:254
  28.5 4.4 %collective-permute-start.2 = (f32[64,4,256]{2,1,0:T(4,128)S(1)}, f32[64,4,256]{2,1,0:T(4,128)S(1)}, u32[]{:S(2)}, u32[]{:S(2)}) collective-permute-start(f32[64,4,256]{2,1,0:T(4,128)S(1)} %get-tuple-element.39), channel_id=1, source_target_pairs={{1,2},{2,1},{3,4},{4,3},{5,6},{6,5},{7,8},{8,7},{9,10},{10,9},{11,... | collective-permute-start | bytes 786440 | tf_op jit(solution)/shard_map/ppermute | solution.py:372
  32.9 0.0 collective-permute-done.3.halo_ref
  32.9 3.3 %shard_map.106 = (f32[64,16,256]{2,1,0:T(8,128)S(1)}, f32[64,16,256]{2,1,0:T(8,128)S(1)}, f32[64,4,256]{2,1,0:T(4,128)S(1)}) custom-call(s32[1]{0:T(128)} %bitcast.10.tile_ref, f32[64,16,256]{2,1,0:T(8,128)S(1)} %get-tuple-element.38.cur_ref.prev_ref, f32[64,16,256]{2,1,0:T(8,128)S(1)} %bitcast.56, ...), custom_call_target="tpu_custom_call", output_to_operand_aliasing={{1}: (7, {})} | custom-call | flops 7864320 | bytes 3670016 | tf_op jit(solution)/shard_map/pallas_call | solution.py:254
  36.2 0.1 collective-permute-start.5
  36.3 2.1 %collective-permute-done.2.halo_ref = f32[64,4,256]{2,1,0:T(4,128)S(1)} collective-permute-done((f32[64,4,256]{2,1,0:T(4,128)S(1)}, f32[64,4,256]{2,1,0:T(4,128)S(1)}, u32[]{:S(2)}, u32[]{:S(2)}) %collective-permute-start.2) | collective-permute-done | bytes 262176 | tf_op jit(solution)/shard_map/ppermute | solution.py:372
  38.3 3.2 %shard_map.107 = (f32[64,16,256]{2,1,0:T(8,128)S(1)}, f32[64,16,256]{2,1,0:T(8,128)S(1)}, f32[64,4,256]{2,1,0:T(4,128)S(1)}) custom-call(s32[1]{0:T(128)} %bitcast.1.tile_ref, f32[64,16,256]{2,1,0:T(8,128)S(1)} %get-tuple-element.38.cur_ref.prev_ref, f32[64,16,256]{2,1,0:T(8,128)S(1)} %bitcast.57, ...), custom_call_target="tpu_custom_call", output_to_operand_aliasing={{1}: (7, {}), {0}: (8, {})} | custom-call | flops 7864320 | bytes 3670016 | tf_op jit(solution)/shard_map/pallas_call | solution.py:254
  41.6 4.4 %collective-permute-start.4 = (f32[64,4,256]{2,1,0:T(4,128)S(1)}, f32[64,4,256]{2,1,0:T(4,128)S(1)}, u32[]{:S(2)}, u32[]{:S(2)}) collective-permute-start(f32[64,4,256]{2,1,0:T(4,128)S(1)} %get-tuple-element.45), channel_id=1, source_target_pairs={{1,2},{2,1},{3,4},{4,3},{5,6},{6,5},{7,8},{8,7},{9,10},{10,9},{11,... | collective-permute-start | bytes 786440 | tf_op jit(solution)/shard_map/ppermute | solution.py:372
  46.0 3.3 %shard_map.108 = (f32[64,16,256]{2,1,0:T(8,128)S(1)}, f32[64,16,256]{2,1,0:T(8,128)S(1)}, f32[64,4,256]{2,1,0:T(4,128)S(1)}) custom-call(s32[1]{0:T(128)} %bitcast.10.tile_ref, f32[64,16,256]{2,1,0:T(8,128)S(1)} %get-tuple-element.44.cur_ref.prev_ref, f32[64,16,256]{2,1,0:T(8,128)S(1)} %get-tuple-element.38.cur_ref.prev_ref, ...), custom_call_target="tpu_custom_call", output_to_operand_aliasing={{1}: (7, {})} | custom-call | flops 7864320 | bytes 3670016 | tf_op jit(solution)/shard_map/pallas_call | solution.py:254
  49.2 0.1 collective-permute-start.7
  49.3 2.0 %collective-permute-done.4.halo_ref = f32[64,4,256]{2,1,0:T(4,128)S(1)} collective-permute-done((f32[64,4,256]{2,1,0:T(4,128)S(1)}, f32[64,4,256]{2,1,0:T(4,128)S(1)}, u32[]{:S(2)}, u32[]{:S(2)}) %collective-permute-start.4) | collective-permute-done | bytes 262176 | tf_op jit(solution)/shard_map/ppermute | solution.py:372
  51.4 3.2 %shard_map.109 = (f32[64,16,256]{2,1,0:T(8,128)S(1)}, f32[64,16,256]{2,1,0:T(8,128)S(1)}, f32[64,4,256]{2,1,0:T(4,128)S(1)}) custom-call(s32[1]{0:T(128)} %bitcast.1.tile_ref, f32[64,16,256]{2,1,0:T(8,128)S(1)} %get-tuple-element.44.cur_ref.prev_ref, ...), custom_call_target="tpu_custom_call", output_to_operand_aliasing={{1}: (7, {}), {0}: (8, {})} | custom-call | flops 7864320 | bytes 3670016 | tf_op jit(solution)/shard_map/pallas_call | solution.py:254
  54.6 4.4 %collective-permute-start.6 = (f32[64,4,256]{2,1,0:T(4,128)S(1)}, f32[64,4,256]{2,1,0:T(4,128)S(1)}, u32[]{:S(2)}, u32[]{:S(2)}) collective-permute-start(f32[64,4,256]{2,1,0:T(4,128)S(1)} %get-tuple-element.51), channel_id=1, source_target_pairs={{1,2},{2,1},{3,4},{4,3},{5,6},{6,5},{7,8},{8,7},{9,10},{10,9},{11,... | collective-permute-start | bytes 786440 | tf_op jit(solution)/shard_map/ppermute | solution.py:372
  59.0 0.0 collective-permute-done.7.halo_ref
  59.0 3.3 %shard_map.110 = (f32[64,16,256]{2,1,0:T(8,128)S(1)}, f32[64,16,256]{2,1,0:T(8,128)S(1)}, f32[64,4,256]{2,1,0:T(4,128)S(1)}) custom-call(s32[1]{0:T(128)} %bitcast.10.tile_ref, f32[64,16,256]{2,1,0:T(8,128)S(1)} %get-tuple-element.50.cur_ref.prev_ref, f32[64,16,256]{2,1,0:T(8,128)S(1)} %get-tuple-element.44.cur_ref.prev_ref, ...), custom_call_target="tpu_custom_call", output_to_operand_aliasing={{1}: (7, {})} | custom-call | flops 7864320 | bytes 3670016 | tf_op jit(solution)/shard_map/pallas_call | solution.py:254
  62.3 0.1 collective-permute-start.9
  62.4 2.0 %collective-permute-done.6.halo_ref = f32[64,4,256]{2,1,0:T(4,128)S(1)} collective-permute-done((f32[64,4,256]{2,1,0:T(4,128)S(1)}, f32[64,4,256]{2,1,0:T(4,128)S(1)}, u32[]{:S(2)}, u32[]{:S(2)}) %collective-permute-start.6) | collective-permute-done | bytes 262176 | tf_op jit(solution)/shard_map/ppermute | solution.py:372
  64.4 3.2 %shard_map.111 = (f32[64,16,256]{2,1,0:T(8,128)S(1)}, f32[64,16,256]{2,1,0:T(8,128)S(1)}, f32[64,4,256]{2,1,0:T(4,128)S(1)}) custom-call(s32[1]{0:T(128)} %bitcast.1.tile_ref, f32[64,16,256]{2,1,0:T(8,128)S(1)} %get-tuple-element.50.cur_ref.prev_ref, ...), custom_call_target="tpu_custom_call", output_to_operand_aliasing={{1}: (7, {}), {0}: (8, {})} | custom-call | flops 7864320 | bytes 3670016 | tf_op jit(solution)/shard_map/pallas_call | solution.py:254
  67.7 4.4 %collective-permute-start.8 = (f32[64,4,256]{2,1,0:T(4,128)S(1)}, f32[64,4,256]{2,1,0:T(4,128)S(1)}, u32[]{:S(2)}, u32[]{:S(2)}) collective-permute-start(f32[64,4,256]{2,1,0:T(4,128)S(1)} %get-tuple-element.57), channel_id=1, source_target_pairs={{1,2},{2,1},{3,4},{4,3},{5,6},{6,5},{7,8},{8,7},{9,10},{10,9},{11,... | collective-permute-start | bytes 786440 | tf_op jit(solution)/shard_map/ppermute | solution.py:372
  72.7 0.0 collective-permute-done.9.halo_ref
  72.7 3.3 %shard_map.112 = (f32[64,16,256]{2,1,0:T(8,128)S(1)}, f32[64,16,256]{2,1,0:T(8,128)S(1)}, f32[64,4,256]{2,1,0:T(4,128)S(1)}) custom-call(s32[1]{0:T(128)} %bitcast.10.tile_ref, f32[64,16,256]{2,1,0:T(8,128)S(1)} %get-tuple-element.56.cur_ref.prev_ref, f32[64,16,256]{2,1,0:T(8,128)S(1)} %get-tuple-element.50.cur_ref.prev_ref, ...), custom_call_target="tpu_custom_call", output_to_operand_aliasing={{1}: (7, {})} | custom-call | flops 7864320 | bytes 3670016 | tf_op jit(solution)/shard_map/pallas_call | solution.py:254
  76.0 0.1 collective-permute-start.11
  76.1 1.4 %collective-permute-done.8.halo_ref = f32[64,4,256]{2,1,0:T(4,128)S(1)} collective-permute-done((f32[64,4,256]{2,1,0:T(4,128)S(1)}, f32[64,4,256]{2,1,0:T(4,128)S(1)}, u32[]{:S(2)}, u32[]{:S(2)}) %collective-permute-start.8) | collective-permute-done | bytes 262176 | tf_op jit(solution)/shard_map/ppermute | solution.py:372
  77.5 3.3 %shard_map.113 = (f32[64,16,256]{2,1,0:T(8,128)S(1)}, f32[64,16,256]{2,1,0:T(8,128)S(1)}, f32[64,4,256]{2,1,0:T(4,128)S(1)}) custom-call(s32[1]{0:T(128)} %bitcast.1.tile_ref, f32[64,16,256]{2,1,0:T(8,128)S(1)} %get-tuple-element.56.cur_ref.prev_ref, ...), custom_call_target="tpu_custom_call", output_to_operand_aliasing={{1}: (7, {}), {0}: (8, {})} | custom-call | flops 7864320 | bytes 3670016 | tf_op jit(solution)/shard_map/pallas_call | solution.py:254
  80.8 4.4 %collective-permute-start.10 = (f32[64,4,256]{2,1,0:T(4,128)S(1)}, f32[64,4,256]{2,1,0:T(4,128)S(1)}, u32[]{:S(2)}, u32[]{:S(2)}) collective-permute-start(f32[64,4,256]{2,1,0:T(4,128)S(1)} %get-tuple-element.63), channel_id=1, source_target_pairs={{1,2},{2,1},{3,4},{4,3},{5,6},{6,5},{7,8},{8,7},{9,10},{10,9},{11,... | collective-permute-start | bytes 786440 | tf_op jit(solution)/shard_map/ppermute | solution.py:372
  85.3 0.0 collective-permute-done.11.halo_ref
  85.3 3.9 %shard_map.114 = (f32[64,16,256]{2,1,0:T(8,128)}, f32[64,16,256]{2,1,0:T(8,128)S(1)}, f32[64,4,256]{2,1,0:T(4,128)}) custom-call(s32[1]{0:T(128)} %bitcast.10.tile_ref, f32[64,16,256]{2,1,0:T(8,128)S(1)} %get-tuple-element.62.cur_ref, f32[64,16,256]{2,1,0:T(8,128)S(1)} %get-tuple-element.56.cur_ref.prev_ref, ...), custom_call_target="tpu_custom_call", output_to_operand_aliasing={{1}: (7, {})} | custom-call | flops 7864320 | bytes 3670016 | tf_op jit(solution)/shard_map/pallas_call | solution.py:254
  89.2 1.4 %collective-permute-done.10.halo_ref = f32[64,4,256]{2,1,0:T(4,128)S(1)} collective-permute-done((f32[64,4,256]{2,1,0:T(4,128)S(1)}, f32[64,4,256]{2,1,0:T(4,128)S(1)}, u32[]{:S(2)}, u32[]{:S(2)}) %collective-permute-start.10) | collective-permute-done | bytes 262176 | tf_op jit(solution)/shard_map/ppermute | solution.py:372
  90.6 3.9 %shard_map.115 = (f32[64,16,256]{2,1,0:T(8,128)}, f32[64,16,256]{2,1,0:T(8,128)S(1)}, f32[64,4,256]{2,1,0:T(4,128)}) custom-call(s32[1]{0:T(128)} %bitcast.1.tile_ref, f32[64,16,256]{2,1,0:T(8,128)S(1)} %get-tuple-element.62.cur_ref, f32[64,16,256]{2,1,0:T(8,128)S(1)} %get-tuple-element.56.cur_ref.prev_ref, ...), custom_call_target="tpu_custom_call", output_to_operand_aliasing={{1}: (7, {}), {0}: (8, {})} | custom-call | flops 7864320 | bytes 3670016 | tf_op jit(solution)/shard_map/pallas_call | solution.py:254
  94.5 0.7 gather_fusion
  95.2 0.2 select_select_fusion
  95.4 23.8 %all_to_all.10 = f32[8,10,16,256]{3,2,1,0:T(8,128)S(1)} all-to-all(f32[8,10,16,256]{3,2,1,0:T(8,128)S(1)} %select_select_fusion), channel_id=1, replica_groups=mesh['shot'=8,'space'=16] {'shot'}, dimensions={0} | all-to-all | bytes 2621440 | tf_op jit(solution)/shard_map/all_to_all | solution.py:388
  119.3 0.8 reduce_sum.19
  (16 shorter events, 0.1 us)
Async XLA Ops:
  0.6 2.3 %copy-start = (bf16[1,256,1536]{2,1,0:T(8,128)(2,1)S(1)}, bf16[1,256,1536]{2,1,0:T(8,128)(2,1)}, u32[]{:S(2)}) copy-start(bf16[1,256,1536]{2,1,0:T(8,128)(2,1)} %param.9) | copy-start | bytes 2359300
  0.6 10.8 %copy-start.2 = (f32[1,64,16,256]{3,2,1,0:T(8,128)S(1)}, f32[1,64,16,256]{3,2,1,0:T(8,128)}, u32[]{:S(2)}) copy-start(f32[1,64,16,256]{3,2,1,0:T(8,128)} %param.16) | copy-start | bytes 3145732
  5.6 10.1 %all-to-all-start = ((f32[16,1,336]{2,1,0:T(1,128)}), f32[16,1,336]{2,1,0:T(1,128)S(1)}, u32[]{:S(2)}, u32[]{:S(2)}) async-start(f32[16,1,336]{2,1,0:T(1,128)} %reshape.100), calls=%async_computation | async-start | bytes 49152 | tf_op jit(solution)/shard_map/all_to_all | solution.py:344
  12.3 6.4 %collective-permute-start.1 = (f32[64,4,256]{2,1,0:T(4,128)S(1)}, f32[64,4,256]{2,1,0:T(4,128)S(1)}, u32[]{:S(2)}, u32[]{:S(2)}) collective-permute-start(f32[64,4,256]{2,1,0:T(4,128)S(1)} %get-tuple-element.70), channel_id=1, source_target_pairs={{0,1},{1,0},{2,3},{3,2},{4,5},{5,4},{6,7},{7,6},{8,9},{9,8},{10,11... | collective-permute-start | bytes 786440 | tf_op jit(solution)/shard_map/ppermute | solution.py:371
  12.6 12.6 %collective-permute-start = (f32[64,4,256]{2,1,0:T(4,128)}, f32[64,4,256]{2,1,0:T(4,128)}, u32[]{:S(2)}, u32[]{:S(2)}) collective-permute-start(f32[64,4,256]{2,1,0:T(4,128)} %get-tuple-element.71), channel_id=1, source_target_pairs={{1,2},{2,1},{3,4},{4,3},{5,6},{6,5},{7,8},{8,7},{9,10},{10,9},{11,... | collective-permute-start | bytes 786440 | tf_op jit(solution)/shard_map/ppermute | solution.py:372
  18.6 0.7 copy-start.4
  19.4 1.2 %copy-start.3 = (f32[1,64,16,256]{3,2,1,0:T(8,128)S(1)}, f32[1,64,16,256]{3,2,1,0:T(8,128)}, u32[]{:S(2)}) copy-start(f32[1,64,16,256]{3,2,1,0:T(8,128)} %param.15) | copy-start | bytes 3145732
  20.7 0.9 copy-start.5
  24.9 8.0 %collective-permute-start.3 = (f32[64,4,256]{2,1,0:T(4,128)S(1)}, f32[64,4,256]{2,1,0:T(4,128)S(1)}, u32[]{:S(2)}, u32[]{:S(2)}) collective-permute-start(f32[64,4,256]{2,1,0:T(4,128)S(1)} %get-tuple-element.40), channel_id=1, source_target_pairs={{0,1},{1,0},{2,3},{3,2},{4,5},{5,4},{6,7},{7,6},{8,9},{9,8},{10,11... | collective-permute-start | bytes 786440 | tf_op jit(solution)/shard_map/ppermute | solution.py:371
  28.5 9.8 %collective-permute-start.2 = (f32[64,4,256]{2,1,0:T(4,128)S(1)}, f32[64,4,256]{2,1,0:T(4,128)S(1)}, u32[]{:S(2)}, u32[]{:S(2)}) collective-permute-start(f32[64,4,256]{2,1,0:T(4,128)S(1)} %get-tuple-element.39), channel_id=1, source_target_pairs={{1,2},{2,1},{3,4},{4,3},{5,6},{6,5},{7,8},{8,7},{9,10},{10,9},{11,... | collective-permute-start | bytes 786440 | tf_op jit(solution)/shard_map/ppermute | solution.py:372
  36.2 9.8 %collective-permute-start.5 = (f32[64,4,256]{2,1,0:T(4,128)S(1)}, f32[64,4,256]{2,1,0:T(4,128)S(1)}, u32[]{:S(2)}, u32[]{:S(2)}) collective-permute-start(f32[64,4,256]{2,1,0:T(4,128)S(1)} %get-tuple-element.46), channel_id=1, source_target_pairs={{0,1},{1,0},{2,3},{3,2},{4,5},{5,4},{6,7},{7,6},{8,9},{9,8},{10,11... | collective-permute-start | bytes 786440 | tf_op jit(solution)/shard_map/ppermute | solution.py:371
  41.6 9.8 %collective-permute-start.4 = (f32[64,4,256]{2,1,0:T(4,128)S(1)}, f32[64,4,256]{2,1,0:T(4,128)S(1)}, u32[]{:S(2)}, u32[]{:S(2)}) collective-permute-start(f32[64,4,256]{2,1,0:T(4,128)S(1)} %get-tuple-element.45), channel_id=1, source_target_pairs={{1,2},{2,1},{3,4},{4,3},{5,6},{6,5},{7,8},{8,7},{9,10},{10,9},{11,... | collective-permute-start | bytes 786440 | tf_op jit(solution)/shard_map/ppermute | solution.py:372
  49.2 9.8 %collective-permute-start.7 = (f32[64,4,256]{2,1,0:T(4,128)S(1)}, f32[64,4,256]{2,1,0:T(4,128)S(1)}, u32[]{:S(2)}, u32[]{:S(2)}) collective-permute-start(f32[64,4,256]{2,1,0:T(4,128)S(1)} %get-tuple-element.52), channel_id=1, source_target_pairs={{0,1},{1,0},{2,3},{3,2},{4,5},{5,4},{6,7},{7,6},{8,9},{9,8},{10,11... | collective-permute-start | bytes 786440 | tf_op jit(solution)/shard_map/ppermute | solution.py:371
  54.6 9.8 %collective-permute-start.6 = (f32[64,4,256]{2,1,0:T(4,128)S(1)}, f32[64,4,256]{2,1,0:T(4,128)S(1)}, u32[]{:S(2)}, u32[]{:S(2)}) collective-permute-start(f32[64,4,256]{2,1,0:T(4,128)S(1)} %get-tuple-element.51), channel_id=1, source_target_pairs={{1,2},{2,1},{3,4},{4,3},{5,6},{6,5},{7,8},{8,7},{9,10},{10,9},{11,... | collective-permute-start | bytes 786440 | tf_op jit(solution)/shard_map/ppermute | solution.py:372
  62.3 10.4 %collective-permute-start.9 = (f32[64,4,256]{2,1,0:T(4,128)S(1)}, f32[64,4,256]{2,1,0:T(4,128)S(1)}, u32[]{:S(2)}, u32[]{:S(2)}) collective-permute-start(f32[64,4,256]{2,1,0:T(4,128)S(1)} %get-tuple-element.58), channel_id=1, source_target_pairs={{0,1},{1,0},{2,3},{3,2},{4,5},{5,4},{6,7},{7,6},{8,9},{9,8},{10,11... | collective-permute-start | bytes 786440 | tf_op jit(solution)/shard_map/ppermute | solution.py:371
  67.7 9.8 %collective-permute-start.8 = (f32[64,4,256]{2,1,0:T(4,128)S(1)}, f32[64,4,256]{2,1,0:T(4,128)S(1)}, u32[]{:S(2)}, u32[]{:S(2)}) collective-permute-start(f32[64,4,256]{2,1,0:T(4,128)S(1)} %get-tuple-element.57), channel_id=1, source_target_pairs={{1,2},{2,1},{3,4},{4,3},{5,6},{6,5},{7,8},{8,7},{9,10},{10,9},{11,... | collective-permute-start | bytes 786440 | tf_op jit(solution)/shard_map/ppermute | solution.py:372
  76.0 9.3 %collective-permute-start.11 = (f32[64,4,256]{2,1,0:T(4,128)S(1)}, f32[64,4,256]{2,1,0:T(4,128)S(1)}, u32[]{:S(2)}, u32[]{:S(2)}) collective-permute-start(f32[64,4,256]{2,1,0:T(4,128)S(1)} %get-tuple-element.64), channel_id=1, source_target_pairs={{0,1},{1,0},{2,3},{3,2},{4,5},{5,4},{6,7},{7,6},{8,9},{9,8},{10,11... | collective-permute-start | bytes 786440 | tf_op jit(solution)/shard_map/ppermute | solution.py:371
  77.5 7.8 %copy-start.1 = (f32[1,64,16,256]{3,2,1,0:T(8,128)S(1)}, f32[1,64,16,256]{3,2,1,0:T(8,128)}, u32[]{:S(2)}) copy-start(f32[1,64,16,256]{3,2,1,0:T(8,128)} %param.14) | copy-start | bytes 3145732
  80.8 9.8 %collective-permute-start.10 = (f32[64,4,256]{2,1,0:T(4,128)S(1)}, f32[64,4,256]{2,1,0:T(4,128)S(1)}, u32[]{:S(2)}, u32[]{:S(2)}) collective-permute-start(f32[64,4,256]{2,1,0:T(4,128)S(1)} %get-tuple-element.63), channel_id=1, source_target_pairs={{1,2},{2,1},{3,4},{4,3},{5,6},{6,5},{7,8},{8,7},{9,10},{10,9},{11,... | collective-permute-start | bytes 786440 | tf_op jit(solution)/shard_map/ppermute | solution.py:372

commit v14 on v12

--- a/solution.py
+++ b/solution.py
@@ -269,7 +269,7 @@
         cost_estimate=pl.CostEstimate(
             flops=60 * cells, bytes_accessed=28 * cells, transcendentals=0
         ),
-        compiler_params=pltpu.CompilerParams(vmem_limit_bytes=48 * 1024 * 1024),
+        compiler_params=pltpu.CompilerParams(vmem_limit_bytes=16 * 1024 * 1024),
     )(*operands)
 
 

time: 121 us -> 116 us (0.959)
  Pallas kernels: 40.4 us -> 28.4 us
  waiting for transfers between devices: 8.78 us -> 13.9 us
  local copies, waits for them, and re-layouts: 6.29 us -> 9.5 us
    pallas_call x12, Pallas kernels: 40.4 us -> 28.4 us  [tile_call(): pl.pallas_call(functools.partial(tile_kernel, moment, chained), grid_spec...]
    ppermute x6, waiting for transfers between devices: 8.76 us -> 13.9 us  [local(): far_halo = lax.ppermute(far_edge, 'space', across)]
    unnamed x14 -> x22, local copies, waits for them, and re-layouts: 3.68 us -> 6.8 us
  transfers between devices with their start and end apart: 13 -> 13, of which waited for: 5 -> 5; matrix products, arithmetic and copies ran while one was open for 3% -> 3% of each run, Pallas kernels for 30% -> 22%
where the time goes in v14:
time: 116 us
  starting transfers between devices  32.2 us (28%)
  Pallas kernels  28.4 us (24%)
  blocking collectives  22.8 us (20%)
  waiting for transfers between devices  13.9 us (12%)
  local copies, waits for them, and re-layouts  9.5 us (8%)
  other arithmetic  4.07 us (4%)
  matrix products  2.95 us (3%)
  between operations  1.66 us (1%)
    pallas_call x12, Pallas kernels, tile_call(): pl.pallas_call(functools.partial(tile_kernel, moment, chained), grid_spec...  28.4 us
    ppermute x6, starting transfers between devices, local(): far_halo = lax.ppermute(far_edge, 'space', across)  25.5 us
    all_to_all x1, blocking collectives, local(): lax.all_to_all(placed, 'shot', split_axis=0, concat_axis=0, tiled=True)  22.8 us
    ppermute x6, waiting for transfers between devices, local(): far_halo = lax.ppermute(far_edge, 'space', across)  13.9 us
    unnamed x22, local copies, waits for them, and re-layouts  6.8 us
    all_to_all x1, starting transfers between devices, local(): lax.all_to_all(buffer, 'space', split_axis=0, concat_axis=0, tiled=True)  5.82 us
  transfers between devices with their start and end apart: 13, of which 5 were waited for; matrix products, arithmetic and copies ran while one was open for 3% of the time, Pallas kernels for 22%

profile of v14, /device:TPU:97, one launch (start us, length us, event | category | flops | bytes accessed | tf_op | source)
XLA Modules:
  0.0 115.5 jit_solution(10250287944909473043)
XLA Ops:
  0.6 0.0 copy-start
  0.6 0.0 copy-start.4
  0.7 0.9 convert_reduce_fusion
  1.6 0.7 multiply_add_fusion
  2.3 0.7 convert_bitcast_fusion
  3.0 1.0 fusion.11
  4.0 0.3 fusion.13
  4.3 0.3 convolution_add_fusion.1
  4.5 0.3 convolution_add_fusion
  4.8 0.1 reshape.89
  4.9 0.7 reshape.102
  5.6 5.8 %all-to-all-start = ((f32[16,1,336]{2,1,0:T(1,128)}), f32[16,1,336]{2,1,0:T(1,128)S(1)}, u32[]{:S(2)}, u32[]{:S(2)}) async-start(f32[16,1,336]{2,1,0:T(1,128)} %reshape.102), calls=%async_computation | async-start | bytes 49152 | tf_op jit(solution)/shard_map/all_to_all | solution.py:344
  11.5 0.9 dynamic-slice_bitcast_fusion
  12.4 0.4 collective-permute-start.1
  12.8 3.1 %collective-permute-start = (f32[64,4,256]{2,1,0:T(4,128)}, f32[64,4,256]{2,1,0:T(4,128)}, u32[]{:S(2)}, u32[]{:S(2)}) collective-permute-start(f32[64,4,256]{2,1,0:T(4,128)} %get-tuple-element.71), channel_id=1, source_target_pairs={{1,2},{2,1},{3,4},{4,3},{5,6},{6,5},{7,8},{8,7},{9,10},{10,9},{11,... | collective-permute-start | bytes 786440 | tf_op jit(solution)/shard_map/ppermute | solution.py:372
  15.9 0.5 broadcast.101
  16.4 0.7 reduce.2
  17.1 0.1 reshape.103
  17.2 0.1 reshape.90
  17.3 0.4 fusion
  17.7 0.4 fusion.1
  18.1 0.4 fusion.10
  18.5 0.2 copy.37
  18.7 0.0 collective-permute-done.1.halo_ref
  18.7 0.0 copy-start.8
  18.8 0.7 copy-done.8
  19.5 0.1 broadcast_in_dim.38.img_ref
  19.6 0.0 copy-start.1
  19.6 1.9 %copy-done.1 = bf16[1,6,64,16,256]{4,3,2,1,0:T(8,128)(2,1)S(1)} copy-done((bf16[1,6,64,16,256]{4,3,2,1,0:T(8,128)(2,1)S(1)}, bf16[1,6,64,16,256]{4,3,2,1,0:T(8,128)(2,1)}, u32[]{:S(2)}) %copy-start.1) | copy-done | bytes 3145752
  21.5 1.2 %copy-done.5 = f32[1,64,16,256]{3,2,1,0:T(8,128)S(1)} copy-done((f32[1,64,16,256]{3,2,1,0:T(8,128)S(1)}, f32[1,64,16,256]{3,2,1,0:T(8,128)}, u32[]{:S(2)}) %copy-start.5) | copy-done | bytes 1048600
  22.7 1.2 %copy-done.7 = f32[1,64,16,256]{3,2,1,0:T(8,128)S(1)} copy-done((f32[1,64,16,256]{3,2,1,0:T(8,128)S(1)}, f32[1,64,16,256]{3,2,1,0:T(8,128)}, u32[]{:S(2)}) %copy-start.7) | copy-done | bytes 1048600
  23.9 0.9 copy-done.9
  24.9 2.1 %shard_map.104 = (f32[64,16,256]{2,1,0:T(8,128)S(1)}, f32[64,16,256]{2,1,0:T(8,128)S(1)}, f32[64,4,256]{2,1,0:T(4,128)S(1)}) custom-call(s32[1]{0:T(128)} %bitcast.11.tile_ref, f32[64,16,256]{2,1,0:T(8,128)S(1)} %bitcast.69, f32[64,16,256]{2,1,0:T(8,128)S(1)} %bitcast.73, f32[64,4,256]{2,1,0:T(4,128)S(1)} %copy-done.9, ...), custom_call_target="tpu_custom_call", output_to_operand_aliasing={{1}: (7, {})} | custom-call | flops 7864320 | bytes 3670016 | tf_op jit(solution)/shard_map/pallas_call | solution.py:254
  27.0 0.2 collective-permute-start.3
  27.3 3.0 %shard_map.105 = (f32[64,16,256]{2,1,0:T(8,128)S(1)}, f32[64,16,256]{2,1,0:T(8,128)S(1)}, f32[64,4,256]{2,1,0:T(4,128)S(1)}) custom-call(s32[1]{0:T(128)} %bitcast.1.tile_ref, f32[64,16,256]{2,1,0:T(8,128)S(1)} %bitcast.70, f32[64,16,256]{2,1,0:T(8,128)S(1)} %bitcast.74, ...), custom_call_target="tpu_custom_call", output_to_operand_aliasing={{1}: (7, {}), {0}: (8, {})} | custom-call | flops 7864320 | bytes 3670016 | tf_op jit(solution)/shard_map/pallas_call | solution.py:254
  30.3 4.5 %collective-permute-start.2 = (f32[64,4,256]{2,1,0:T(4,128)S(1)}, f32[64,4,256]{2,1,0:T(4,128)S(1)}, u32[]{:S(2)}, u32[]{:S(2)}) collective-permute-start(f32[64,4,256]{2,1,0:T(4,128)S(1)} %get-tuple-element.39), channel_id=1, source_target_pairs={{1,2},{2,1},{3,4},{4,3},{5,6},{6,5},{7,8},{8,7},{9,10},{10,9},{11,... | collective-permute-start | bytes 786440 | tf_op jit(solution)/shard_map/ppermute | solution.py:372
  34.8 0.0 collective-permute-done.3.halo_ref
  34.8 2.2 %shard_map.106 = (f32[64,16,256]{2,1,0:T(8,128)S(1)}, f32[64,16,256]{2,1,0:T(8,128)S(1)}, f32[64,4,256]{2,1,0:T(4,128)S(1)}) custom-call(s32[1]{0:T(128)} %bitcast.11.tile_ref, f32[64,16,256]{2,1,0:T(8,128)S(1)} %get-tuple-element.38.cur_ref.prev_ref, f32[64,16,256]{2,1,0:T(8,128)S(1)} %bitcast.71, ...), custom_call_target="tpu_custom_call", output_to_operand_aliasing={{1}: (7, {})} | custom-call | flops 7864320 | bytes 3670016 | tf_op jit(solution)/shard_map/pallas_call | solution.py:254
  36.9 0.1 collective-permute-start.5
  37.0 3.0 %collective-permute-done.2.halo_ref = f32[64,4,256]{2,1,0:T(4,128)S(1)} collective-permute-done((f32[64,4,256]{2,1,0:T(4,128)S(1)}, f32[64,4,256]{2,1,0:T(4,128)S(1)}, u32[]{:S(2)}, u32[]{:S(2)}) %collective-permute-start.2) | collective-permute-done | bytes 262176 | tf_op jit(solution)/shard_map/ppermute | solution.py:372
  40.1 2.1 %shard_map.107 = (f32[64,16,256]{2,1,0:T(8,128)S(1)}, f32[64,16,256]{2,1,0:T(8,128)S(1)}, f32[64,4,256]{2,1,0:T(4,128)S(1)}) custom-call(s32[1]{0:T(128)} %bitcast.1.tile_ref, f32[64,16,256]{2,1,0:T(8,128)S(1)} %get-tuple-element.38.cur_ref.prev_ref, f32[64,16,256]{2,1,0:T(8,128)S(1)} %bitcast.72, ...), custom_call_target="tpu_custom_call", output_to_operand_aliasing={{1}: (7, {}), {0}: (8, {})} | custom-call | flops 7864320 | bytes 3670016 | tf_op jit(solution)/shard_map/pallas_call | solution.py:254
  42.2 4.5 %collective-permute-start.4 = (f32[64,4,256]{2,1,0:T(4,128)S(1)}, f32[64,4,256]{2,1,0:T(4,128)S(1)}, u32[]{:S(2)}, u32[]{:S(2)}) collective-permute-start(f32[64,4,256]{2,1,0:T(4,128)S(1)} %get-tuple-element.45), channel_id=1, source_target_pairs={{1,2},{2,1},{3,4},{4,3},{5,6},{6,5},{7,8},{8,7},{9,10},{10,9},{11,... | collective-permute-start | bytes 786440 | tf_op jit(solution)/shard_map/ppermute | solution.py:372
  46.7 2.2 %shard_map.108 = (f32[64,16,256]{2,1,0:T(8,128)S(1)}, f32[64,16,256]{2,1,0:T(8,128)S(1)}, f32[64,4,256]{2,1,0:T(4,128)S(1)}) custom-call(s32[1]{0:T(128)} %bitcast.11.tile_ref, f32[64,16,256]{2,1,0:T(8,128)S(1)} %get-tuple-element.44.cur_ref.prev_ref, f32[64,16,256]{2,1,0:T(8,128)S(1)} %get-tuple-element.38.cur_ref.prev_ref, ...), custom_call_target="tpu_custom_call", output_to_operand_aliasing={{1}: (7, {})} | custom-call | flops 7864320 | bytes 3670016 | tf_op jit(solution)/shard_map/pallas_call | solution.py:254
  48.9 0.1 collective-permute-start.7
  49.0 3.0 %collective-permute-done.4.halo_ref = f32[64,4,256]{2,1,0:T(4,128)S(1)} collective-permute-done((f32[64,4,256]{2,1,0:T(4,128)S(1)}, f32[64,4,256]{2,1,0:T(4,128)S(1)}, u32[]{:S(2)}, u32[]{:S(2)}) %collective-permute-start.4) | collective-permute-done | bytes 262176 | tf_op jit(solution)/shard_map/ppermute | solution.py:372
  52.0 2.1 %shard_map.109 = (f32[64,16,256]{2,1,0:T(8,128)S(1)}, f32[64,16,256]{2,1,0:T(8,128)S(1)}, f32[64,4,256]{2,1,0:T(4,128)S(1)}) custom-call(s32[1]{0:T(128)} %bitcast.1.tile_ref, f32[64,16,256]{2,1,0:T(8,128)S(1)} %get-tuple-element.44.cur_ref.prev_ref, ...), custom_call_target="tpu_custom_call", output_to_operand_aliasing={{1}: (7, {}), {0}: (8, {})} | custom-call | flops 7864320 | bytes 3670016 | tf_op jit(solution)/shard_map/pallas_call | solution.py:254
  54.2 4.5 %collective-permute-start.6 = (f32[64,4,256]{2,1,0:T(4,128)S(1)}, f32[64,4,256]{2,1,0:T(4,128)S(1)}, u32[]{:S(2)}, u32[]{:S(2)}) collective-permute-start(f32[64,4,256]{2,1,0:T(4,128)S(1)} %get-tuple-element.51), channel_id=1, source_target_pairs={{1,2},{2,1},{3,4},{4,3},{5,6},{6,5},{7,8},{8,7},{9,10},{10,9},{11,... | collective-permute-start | bytes 786440 | tf_op jit(solution)/shard_map/ppermute | solution.py:372
  58.7 2.2 %shard_map.110 = (f32[64,16,256]{2,1,0:T(8,128)S(1)}, f32[64,16,256]{2,1,0:T(8,128)S(1)}, f32[64,4,256]{2,1,0:T(4,128)S(1)}) custom-call(s32[1]{0:T(128)} %bitcast.11.tile_ref, f32[64,16,256]{2,1,0:T(8,128)S(1)} %get-tuple-element.50.cur_ref.prev_ref, f32[64,16,256]{2,1,0:T(8,128)S(1)} %get-tuple-element.44.cur_ref.prev_ref, ...), custom_call_target="tpu_custom_call", output_to_operand_aliasing={{1}: (7, {})} | custom-call | flops 7864320 | bytes 3670016 | tf_op jit(solution)/shard_map/pallas_call | solution.py:254
  60.8 0.1 collective-permute-start.9
  60.9 3.1 %collective-permute-done.6.halo_ref = f32[64,4,256]{2,1,0:T(4,128)S(1)} collective-permute-done((f32[64,4,256]{2,1,0:T(4,128)S(1)}, f32[64,4,256]{2,1,0:T(4,128)S(1)}, u32[]{:S(2)}, u32[]{:S(2)}) %collective-permute-start.6) | collective-permute-done | bytes 262176 | tf_op jit(solution)/shard_map/ppermute | solution.py:372
  64.0 2.1 %shard_map.111 = (f32[64,16,256]{2,1,0:T(8,128)S(1)}, f32[64,16,256]{2,1,0:T(8,128)S(1)}, f32[64,4,256]{2,1,0:T(4,128)S(1)}) custom-call(s32[1]{0:T(128)} %bitcast.1.tile_ref, f32[64,16,256]{2,1,0:T(8,128)S(1)} %get-tuple-element.50.cur_ref.prev_ref, ...), custom_call_target="tpu_custom_call", output_to_operand_aliasing={{1}: (7, {}), {0}: (8, {})} | custom-call | flops 7864320 | bytes 3670016 | tf_op jit(solution)/shard_map/pallas_call | solution.py:254
  66.1 4.5 %collective-permute-start.8 = (f32[64,4,256]{2,1,0:T(4,128)S(1)}, f32[64,4,256]{2,1,0:T(4,128)S(1)}, u32[]{:S(2)}, u32[]{:S(2)}) collective-permute-start(f32[64,4,256]{2,1,0:T(4,128)S(1)} %get-tuple-element.57), channel_id=1, source_target_pairs={{1,2},{2,1},{3,4},{4,3},{5,6},{6,5},{7,8},{8,7},{9,10},{10,9},{11,... | collective-permute-start | bytes 786440 | tf_op jit(solution)/shard_map/ppermute | solution.py:372
  71.3 2.2 %shard_map.112 = (f32[64,16,256]{2,1,0:T(8,128)S(1)}, f32[64,16,256]{2,1,0:T(8,128)S(1)}, f32[64,4,256]{2,1,0:T(4,128)S(1)}) custom-call(s32[1]{0:T(128)} %bitcast.11.tile_ref, f32[64,16,256]{2,1,0:T(8,128)S(1)} %get-tuple-element.56.cur_ref.prev_ref, f32[64,16,256]{2,1,0:T(8,128)S(1)} %get-tuple-element.50.cur_ref.prev_ref, ...), custom_call_target="tpu_custom_call", output_to_operand_aliasing={{1}: (7, {})} | custom-call | flops 7864320 | bytes 3670016 | tf_op jit(solution)/shard_map/pallas_call | solution.py:254
  73.4 0.1 collective-permute-start.11
  73.5 2.4 %collective-permute-done.8.halo_ref = f32[64,4,256]{2,1,0:T(4,128)S(1)} collective-permute-done((f32[64,4,256]{2,1,0:T(4,128)S(1)}, f32[64,4,256]{2,1,0:T(4,128)S(1)}, u32[]{:S(2)}, u32[]{:S(2)}) %collective-permute-start.8) | collective-permute-done | bytes 262176 | tf_op jit(solution)/shard_map/ppermute | solution.py:372
  75.9 2.3 %shard_map.113 = (f32[64,16,256]{2,1,0:T(8,128)S(1)}, f32[64,16,256]{2,1,0:T(8,128)S(1)}, f32[64,4,256]{2,1,0:T(4,128)S(1)}) custom-call(s32[1]{0:T(128)} %bitcast.1.tile_ref, f32[64,16,256]{2,1,0:T(8,128)S(1)} %get-tuple-element.56.cur_ref.prev_ref, ...), custom_call_target="tpu_custom_call", output_to_operand_aliasing={{1}: (7, {}), {0}: (8, {})} | custom-call | flops 7864320 | bytes 3670016 | tf_op jit(solution)/shard_map/pallas_call | solution.py:254
  78.3 4.5 %collective-permute-start.10 = (f32[64,4,256]{2,1,0:T(4,128)S(1)}, f32[64,4,256]{2,1,0:T(4,128)S(1)}, u32[]{:S(2)}, u32[]{:S(2)}) collective-permute-start(f32[64,4,256]{2,1,0:T(4,128)S(1)} %get-tuple-element.63), channel_id=1, source_target_pairs={{1,2},{2,1},{3,4},{4,3},{5,6},{6,5},{7,8},{8,7},{9,10},{10,9},{11,... | collective-permute-start | bytes 786440 | tf_op jit(solution)/shard_map/ppermute | solution.py:372
  82.8 3.0 %shard_map.114 = (f32[64,16,256]{2,1,0:T(8,128)}, f32[64,16,256]{2,1,0:T(8,128)S(1)}, f32[64,4,256]{2,1,0:T(4,128)}) custom-call(s32[1]{0:T(128)} %bitcast.11.tile_ref, f32[64,16,256]{2,1,0:T(8,128)S(1)} %get-tuple-element.62.cur_ref, f32[64,16,256]{2,1,0:T(8,128)S(1)} %get-tuple-element.56.cur_ref.prev_ref, ...), custom_call_target="tpu_custom_call", output_to_operand_aliasing={{1}: (7, {})} | custom-call | flops 7864320 | bytes 3670016 | tf_op jit(solution)/shard_map/pallas_call | solution.py:254
  85.8 2.3 %collective-permute-done.10.halo_ref = f32[64,4,256]{2,1,0:T(4,128)S(1)} collective-permute-done((f32[64,4,256]{2,1,0:T(4,128)S(1)}, f32[64,4,256]{2,1,0:T(4,128)S(1)}, u32[]{:S(2)}, u32[]{:S(2)}) %collective-permute-start.10) | collective-permute-done | bytes 262176 | tf_op jit(solution)/shard_map/ppermute | solution.py:372
  88.1 3.0 %shard_map.115 = (f32[64,16,256]{2,1,0:T(8,128)}, f32[64,16,256]{2,1,0:T(8,128)S(1)}, f32[64,4,256]{2,1,0:T(4,128)}) custom-call(s32[1]{0:T(128)} %bitcast.1.tile_ref, f32[64,16,256]{2,1,0:T(8,128)S(1)} %get-tuple-element.62.cur_ref, f32[64,16,256]{2,1,0:T(8,128)S(1)} %get-tuple-element.56.cur_ref.prev_ref, ...), custom_call_target="tpu_custom_call", output_to_operand_aliasing={{1}: (7, {}), {0}: (8, {})} | custom-call | flops 7864320 | bytes 3670016 | tf_op jit(solution)/shard_map/pallas_call | solution.py:254
  91.0 0.7 gather_fusion
  91.7 0.2 select_select_fusion
  92.0 22.8 %all_to_all.10 = f32[8,10,16,256]{3,2,1,0:T(8,128)S(1)} all-to-all(f32[8,10,16,256]{3,2,1,0:T(8,128)S(1)} %select_select_fusion), channel_id=1, replica_groups=mesh['shot'=8,'space'=16] {'shot'}, dimensions={0} | all-to-all | bytes 2621440 | tf_op jit(solution)/shard_map/all_to_all | solution.py:388
  114.8 0.8 reduce_sum.19
  (24 shorter events, 0.1 us)
Async XLA Ops:
  0.6 2.3 %copy-start = (bf16[1,256,1536]{2,1,0:T(8,128)(2,1)S(1)}, bf16[1,256,1536]{2,1,0:T(8,128)(2,1)}, u32[]{:S(2)}) copy-start(bf16[1,256,1536]{2,1,0:T(8,128)(2,1)} %param.9) | copy-start | bytes 2359300
  0.6 10.8 %copy-start.4 = (f32[1,64,16,256]{3,2,1,0:T(8,128)S(1)}, f32[1,64,16,256]{3,2,1,0:T(8,128)}, u32[]{:S(2)}) copy-start(f32[1,64,16,256]{3,2,1,0:T(8,128)} %param.16) | copy-start | bytes 3145732
  5.6 10.3 %all-to-all-start = ((f32[16,1,336]{2,1,0:T(1,128)}), f32[16,1,336]{2,1,0:T(1,128)S(1)}, u32[]{:S(2)}, u32[]{:S(2)}) async-start(f32[16,1,336]{2,1,0:T(1,128)} %reshape.102), calls=%async_computation | async-start | bytes 49152 | tf_op jit(solution)/shard_map/all_to_all | solution.py:344
  12.4 6.4 %collective-permute-start.1 = (f32[64,4,256]{2,1,0:T(4,128)}, f32[64,4,256]{2,1,0:T(4,128)S(1)}, u32[]{:S(2)}, u32[]{:S(2)}) collective-permute-start(f32[64,4,256]{2,1,0:T(4,128)} %get-tuple-element.70), channel_id=1, source_target_pairs={{0,1},{1,0},{2,3},{3,2},{4,5},{5,4},{6,7},{7,6},{8,9},{9,8},{10,11... | collective-permute-start | bytes 786440 | tf_op jit(solution)/shard_map/ppermute | solution.py:371
  12.8 14.5 %collective-permute-start = (f32[64,4,256]{2,1,0:T(4,128)}, f32[64,4,256]{2,1,0:T(4,128)}, u32[]{:S(2)}, u32[]{:S(2)}) collective-permute-start(f32[64,4,256]{2,1,0:T(4,128)} %get-tuple-element.71), channel_id=1, source_target_pairs={{1,2},{2,1},{3,4},{4,3},{5,6},{6,5},{7,8},{8,7},{9,10},{10,9},{11,... | collective-permute-start | bytes 786440 | tf_op jit(solution)/shard_map/ppermute | solution.py:372
  18.1 1.5 %copy-start.3 = (f32[1,64,16,256]{3,2,1,0:T(8,128)S(1)}, f32[1,64,16,256]{3,2,1,0:T(8,128)}, u32[]{:S(2)}) copy-start(f32[1,64,16,256]{3,2,1,0:T(8,128)} %param.14) | copy-start | bytes 3145732
  18.7 0.7 copy-start.8
  19.6 1.9 %copy-start.1 = (bf16[1,6,64,16,256]{4,3,2,1,0:T(8,128)(2,1)S(1)}, bf16[1,6,64,16,256]{4,3,2,1,0:T(8,128)(2,1)}, u32[]{:S(2)}) copy-start(bf16[1,6,64,16,256]{4,3,2,1,0:T(8,128)(2,1)} %param.17) | copy-start | bytes 9437188
  21.5 1.2 %copy-start.5 = (f32[1,64,16,256]{3,2,1,0:T(8,128)S(1)}, f32[1,64,16,256]{3,2,1,0:T(8,128)}, u32[]{:S(2)}) copy-start(f32[1,64,16,256]{3,2,1,0:T(8,128)} %param.16) | copy-start | bytes 3145732
  22.7 1.2 %copy-start.7 = (f32[1,64,16,256]{3,2,1,0:T(8,128)S(1)}, f32[1,64,16,256]{3,2,1,0:T(8,128)}, u32[]{:S(2)}) copy-start(f32[1,64,16,256]{3,2,1,0:T(8,128)} %param.15) | copy-start | bytes 3145732
  23.9 0.9 copy-start.9
  24.9 2.4 %copy-start.2 = (bf16[1,6,64,16,256]{4,3,2,1,0:T(8,128)(2,1)S(1)}, bf16[1,6,64,16,256]{4,3,2,1,0:T(8,128)(2,1)}, u32[]{:S(2)}) copy-start(bf16[1,6,64,16,256]{4,3,2,1,0:T(8,128)(2,1)} %param.17) | copy-start | bytes 9437188
  24.9 2.4 %copy-start.6 = (f32[1,64,16,256]{3,2,1,0:T(8,128)S(1)}, f32[1,64,16,256]{3,2,1,0:T(8,128)}, u32[]{:S(2)}) copy-start(f32[1,64,16,256]{3,2,1,0:T(8,128)} %param.16) | copy-start | bytes 3145732
  27.0 7.7 %collective-permute-start.3 = (f32[64,4,256]{2,1,0:T(4,128)S(1)}, f32[64,4,256]{2,1,0:T(4,128)S(1)}, u32[]{:S(2)}, u32[]{:S(2)}) collective-permute-start(f32[64,4,256]{2,1,0:T(4,128)S(1)} %get-tuple-element.40), channel_id=1, source_target_pairs={{0,1},{1,0},{2,3},{3,2},{4,5},{5,4},{6,7},{7,6},{8,9},{9,8},{10,11... | collective-permute-start | bytes 786440 | tf_op jit(solution)/shard_map/ppermute | solution.py:371
  30.3 9.8 %collective-permute-start.2 = (f32[64,4,256]{2,1,0:T(4,128)S(1)}, f32[64,4,256]{2,1,0:T(4,128)S(1)}, u32[]{:S(2)}, u32[]{:S(2)}) collective-permute-start(f32[64,4,256]{2,1,0:T(4,128)S(1)} %get-tuple-element.39), channel_id=1, source_target_pairs={{1,2},{2,1},{3,4},{4,3},{5,6},{6,5},{7,8},{8,7},{9,10},{10,9},{11,... | collective-permute-start | bytes 786440 | tf_op jit(solution)/shard_map/ppermute | solution.py:372
  36.9 9.8 %collective-permute-start.5 = (f32[64,4,256]{2,1,0:T(4,128)S(1)}, f32[64,4,256]{2,1,0:T(4,128)S(1)}, u32[]{:S(2)}, u32[]{:S(2)}) collective-permute-start(f32[64,4,256]{2,1,0:T(4,128)S(1)} %get-tuple-element.46), channel_id=1, source_target_pairs={{0,1},{1,0},{2,3},{3,2},{4,5},{5,4},{6,7},{7,6},{8,9},{9,8},{10,11... | collective-permute-start | bytes 786440 | tf_op jit(solution)/shard_map/ppermute | solution.py:371
  42.2 9.8 %collective-permute-start.4 = (f32[64,4,256]{2,1,0:T(4,128)S(1)}, f32[64,4,256]{2,1,0:T(4,128)S(1)}, u32[]{:S(2)}, u32[]{:S(2)}) collective-permute-start(f32[64,4,256]{2,1,0:T(4,128)S(1)} %get-tuple-element.45), channel_id=1, source_target_pairs={{1,2},{2,1},{3,4},{4,3},{5,6},{6,5},{7,8},{8,7},{9,10},{10,9},{11,... | collective-permute-start | bytes 786440 | tf_op jit(solution)/shard_map/ppermute | solution.py:372
  48.9 9.8 %collective-permute-start.7 = (f32[64,4,256]{2,1,0:T(4,128)S(1)}, f32[64,4,256]{2,1,0:T(4,128)S(1)}, u32[]{:S(2)}, u32[]{:S(2)}) collective-permute-start(f32[64,4,256]{2,1,0:T(4,128)S(1)} %get-tuple-element.52), channel_id=1, source_target_pairs={{0,1},{1,0},{2,3},{3,2},{4,5},{5,4},{6,7},{7,6},{8,9},{9,8},{10,11... | collective-permute-start | bytes 786440 | tf_op jit(solution)/shard_map/ppermute | solution.py:371
  54.2 9.8 %collective-permute-start.6 = (f32[64,4,256]{2,1,0:T(4,128)S(1)}, f32[64,4,256]{2,1,0:T(4,128)S(1)}, u32[]{:S(2)}, u32[]{:S(2)}) collective-permute-start(f32[64,4,256]{2,1,0:T(4,128)S(1)} %get-tuple-element.51), channel_id=1, source_target_pairs={{1,2},{2,1},{3,4},{4,3},{5,6},{6,5},{7,8},{8,7},{9,10},{10,9},{11,... | collective-permute-start | bytes 786440 | tf_op jit(solution)/shard_map/ppermute | solution.py:372
  60.8 10.4 %collective-permute-start.9 = (f32[64,4,256]{2,1,0:T(4,128)S(1)}, f32[64,4,256]{2,1,0:T(4,128)S(1)}, u32[]{:S(2)}, u32[]{:S(2)}) collective-permute-start(f32[64,4,256]{2,1,0:T(4,128)S(1)} %get-tuple-element.58), channel_id=1, source_target_pairs={{0,1},{1,0},{2,3},{3,2},{4,5},{5,4},{6,7},{7,6},{8,9},{9,8},{10,11... | collective-permute-start | bytes 786440 | tf_op jit(solution)/shard_map/ppermute | solution.py:371
  66.1 9.8 %collective-permute-start.8 = (f32[64,4,256]{2,1,0:T(4,128)S(1)}, f32[64,4,256]{2,1,0:T(4,128)S(1)}, u32[]{:S(2)}, u32[]{:S(2)}) collective-permute-start(f32[64,4,256]{2,1,0:T(4,128)S(1)} %get-tuple-element.57), channel_id=1, source_target_pairs={{1,2},{2,1},{3,4},{4,3},{5,6},{6,5},{7,8},{8,7},{9,10},{10,9},{11,... | collective-permute-start | bytes 786440 | tf_op jit(solution)/shard_map/ppermute | solution.py:372
  73.4 9.4 %collective-permute-start.11 = (f32[64,4,256]{2,1,0:T(4,128)S(1)}, f32[64,4,256]{2,1,0:T(4,128)S(1)}, u32[]{:S(2)}, u32[]{:S(2)}) collective-permute-start(f32[64,4,256]{2,1,0:T(4,128)S(1)} %get-tuple-element.64), channel_id=1, source_target_pairs={{0,1},{1,0},{2,3},{3,2},{4,5},{5,4},{6,7},{7,6},{8,9},{9,8},{10,11... | collective-permute-start | bytes 786440 | tf_op jit(solution)/shard_map/ppermute | solution.py:371
  78.3 9.8 %collective-permute-start.10 = (f32[64,4,256]{2,1,0:T(4,128)S(1)}, f32[64,4,256]{2,1,0:T(4,128)S(1)}, u32[]{:S(2)}, u32[]{:S(2)}) collective-permute-start(f32[64,4,256]{2,1,0:T(4,128)S(1)} %get-tuple-element.63), channel_id=1, source_target_pairs={{1,2},{2,1},{3,4},{4,3},{5,6},{6,5},{7,8},{8,7},{9,10},{10,9},{11,... | collective-permute-start | bytes 786440 | tf_op jit(solution)/shard_map/ppermute | solution.py:372

commit v15 on v14

--- a/solution.py
+++ b/solution.py
@@ -269,7 +269,7 @@
         cost_estimate=pl.CostEstimate(
             flops=60 * cells, bytes_accessed=28 * cells, transcendentals=0
         ),
-        compiler_params=pltpu.CompilerParams(vmem_limit_bytes=16 * 1024 * 1024),
+        compiler_params=pltpu.CompilerParams(vmem_limit_bytes=12 * 1024 * 1024),
     )(*operands)
 
 

time: 116 us -> 116 us (level)
  no operation moved by 1% of the time
where the time goes in v15:
time: 116 us
  starting transfers between devices  32.2 us (28%)
  Pallas kernels  28.4 us (24%)
  blocking collectives  22.8 us (20%)
  waiting for transfers between devices  13.9 us (12%)
  local copies, waits for them, and re-layouts  9.5 us (8%)
  other arithmetic  4.07 us (4%)
  matrix products  2.95 us (3%)
  between operations  1.66 us (1%)
    pallas_call x12, Pallas kernels, tile_call(): pl.pallas_call(functools.partial(tile_kernel, moment, chained), grid_spec...  28.4 us
    ppermute x6, starting transfers between devices, local(): far_halo = lax.ppermute(far_edge, 'space', across)  25.5 us
    all_to_all x1, blocking collectives, local(): lax.all_to_all(placed, 'shot', split_axis=0, concat_axis=0, tiled=True)  22.8 us
    ppermute x6, waiting for transfers between devices, local(): far_halo = lax.ppermute(far_edge, 'space', across)  13.9 us
    unnamed x22, local copies, waits for them, and re-layouts  6.8 us
    all_to_all x1, starting transfers between devices, local(): lax.all_to_all(buffer, 'space', split_axis=0, concat_axis=0, tiled=True)  5.82 us
  transfers between devices with their start and end apart: 13, of which 5 were waited for; matrix products, arithmetic and copies ran while one was open for 3% of the time, Pallas kernels for 22%

profile of v15, /device:TPU:97, one launch (start us, length us, event | category | flops | bytes accessed | tf_op | source)
XLA Modules:
  0.0 115.5 jit_solution(3742185751553844042)
XLA Ops:
  0.6 0.0 copy-start
  0.6 0.0 copy-start.4
  0.7 0.9 convert_reduce_fusion
  1.6 0.7 multiply_add_fusion
  2.3 0.7 convert_bitcast_fusion
  3.0 1.0 fusion.11
  4.0 0.3 fusion.13
  4.3 0.3 convolution_add_fusion.1
  4.5 0.3 convolution_add_fusion
  4.8 0.1 reshape.89
  4.9 0.7 reshape.102
  5.6 5.8 %all-to-all-start = ((f32[16,1,336]{2,1,0:T(1,128)}), f32[16,1,336]{2,1,0:T(1,128)S(1)}, u32[]{:S(2)}, u32[]{:S(2)}) async-start(f32[16,1,336]{2,1,0:T(1,128)} %reshape.102), calls=%async_computation | async-start | bytes 49152 | tf_op jit(solution)/shard_map/all_to_all | solution.py:344
  11.5 0.9 dynamic-slice_bitcast_fusion
  12.4 0.4 collective-permute-start.1
  12.8 3.1 %collective-permute-start = (f32[64,4,256]{2,1,0:T(4,128)}, f32[64,4,256]{2,1,0:T(4,128)}, u32[]{:S(2)}, u32[]{:S(2)}) collective-permute-start(f32[64,4,256]{2,1,0:T(4,128)} %get-tuple-element.71), channel_id=1, source_target_pairs={{1,2},{2,1},{3,4},{4,3},{5,6},{6,5},{7,8},{8,7},{9,10},{10,9},{11,... | collective-permute-start | bytes 786440 | tf_op jit(solution)/shard_map/ppermute | solution.py:372
  15.9 0.5 broadcast.101
  16.4 0.7 reduce.2
  17.1 0.1 reshape.103
  17.2 0.1 reshape.90
  17.3 0.4 fusion
  17.7 0.4 fusion.1
  18.1 0.4 fusion.10
  18.5 0.2 copy.37
  18.7 0.0 collective-permute-done.1.halo_ref
  18.7 0.0 copy-start.8
  18.8 0.7 copy-done.8
  19.5 0.1 broadcast_in_dim.38.img_ref
  19.6 0.0 copy-start.1
  19.6 1.9 %copy-done.1 = bf16[1,6,64,16,256]{4,3,2,1,0:T(8,128)(2,1)S(1)} copy-done((bf16[1,6,64,16,256]{4,3,2,1,0:T(8,128)(2,1)S(1)}, bf16[1,6,64,16,256]{4,3,2,1,0:T(8,128)(2,1)}, u32[]{:S(2)}) %copy-start.1) | copy-done | bytes 3145752
  21.5 1.2 %copy-done.5 = f32[1,64,16,256]{3,2,1,0:T(8,128)S(1)} copy-done((f32[1,64,16,256]{3,2,1,0:T(8,128)S(1)}, f32[1,64,16,256]{3,2,1,0:T(8,128)}, u32[]{:S(2)}) %copy-start.5) | copy-done | bytes 1048600
  22.7 1.2 %copy-done.7 = f32[1,64,16,256]{3,2,1,0:T(8,128)S(1)} copy-done((f32[1,64,16,256]{3,2,1,0:T(8,128)S(1)}, f32[1,64,16,256]{3,2,1,0:T(8,128)}, u32[]{:S(2)}) %copy-start.7) | copy-done | bytes 1048600
  23.9 0.9 copy-done.9
  24.9 2.1 %shard_map.104 = (f32[64,16,256]{2,1,0:T(8,128)S(1)}, f32[64,16,256]{2,1,0:T(8,128)S(1)}, f32[64,4,256]{2,1,0:T(4,128)S(1)}) custom-call(s32[1]{0:T(128)} %bitcast.11.tile_ref, f32[64,16,256]{2,1,0:T(8,128)S(1)} %bitcast.69, f32[64,16,256]{2,1,0:T(8,128)S(1)} %bitcast.73, f32[64,4,256]{2,1,0:T(4,128)S(1)} %copy-done.9, ...), custom_call_target="tpu_custom_call", output_to_operand_aliasing={{1}: (7, {})} | custom-call | flops 7864320 | bytes 3670016 | tf_op jit(solution)/shard_map/pallas_call | solution.py:254
  27.0 0.2 collective-permute-start.3
  27.3 3.0 %shard_map.105 = (f32[64,16,256]{2,1,0:T(8,128)S(1)}, f32[64,16,256]{2,1,0:T(8,128)S(1)}, f32[64,4,256]{2,1,0:T(4,128)S(1)}) custom-call(s32[1]{0:T(128)} %bitcast.1.tile_ref, f32[64,16,256]{2,1,0:T(8,128)S(1)} %bitcast.70, f32[64,16,256]{2,1,0:T(8,128)S(1)} %bitcast.74, ...), custom_call_target="tpu_custom_call", output_to_operand_aliasing={{1}: (7, {}), {0}: (8, {})} | custom-call | flops 7864320 | bytes 3670016 | tf_op jit(solution)/shard_map/pallas_call | solution.py:254
  30.3 4.5 %collective-permute-start.2 = (f32[64,4,256]{2,1,0:T(4,128)S(1)}, f32[64,4,256]{2,1,0:T(4,128)S(1)}, u32[]{:S(2)}, u32[]{:S(2)}) collective-permute-start(f32[64,4,256]{2,1,0:T(4,128)S(1)} %get-tuple-element.39), channel_id=1, source_target_pairs={{1,2},{2,1},{3,4},{4,3},{5,6},{6,5},{7,8},{8,7},{9,10},{10,9},{11,... | collective-permute-start | bytes 786440 | tf_op jit(solution)/shard_map/ppermute | solution.py:372
  34.8 0.0 collective-permute-done.3.halo_ref
  34.8 2.2 %shard_map.106 = (f32[64,16,256]{2,1,0:T(8,128)S(1)}, f32[64,16,256]{2,1,0:T(8,128)S(1)}, f32[64,4,256]{2,1,0:T(4,128)S(1)}) custom-call(s32[1]{0:T(128)} %bitcast.11.tile_ref, f32[64,16,256]{2,1,0:T(8,128)S(1)} %get-tuple-element.38.cur_ref.prev_ref, f32[64,16,256]{2,1,0:T(8,128)S(1)} %bitcast.71, ...), custom_call_target="tpu_custom_call", output_to_operand_aliasing={{1}: (7, {})} | custom-call | flops 7864320 | bytes 3670016 | tf_op jit(solution)/shard_map/pallas_call | solution.py:254
  36.9 0.1 collective-permute-start.5
  37.0 3.0 %collective-permute-done.2.halo_ref = f32[64,4,256]{2,1,0:T(4,128)S(1)} collective-permute-done((f32[64,4,256]{2,1,0:T(4,128)S(1)}, f32[64,4,256]{2,1,0:T(4,128)S(1)}, u32[]{:S(2)}, u32[]{:S(2)}) %collective-permute-start.2) | collective-permute-done | bytes 262176 | tf_op jit(solution)/shard_map/ppermute | solution.py:372
  40.1 2.1 %shard_map.107 = (f32[64,16,256]{2,1,0:T(8,128)S(1)}, f32[64,16,256]{2,1,0:T(8,128)S(1)}, f32[64,4,256]{2,1,0:T(4,128)S(1)}) custom-call(s32[1]{0:T(128)} %bitcast.1.tile_ref, f32[64,16,256]{2,1,0:T(8,128)S(1)} %get-tuple-element.38.cur_ref.prev_ref, f32[64,16,256]{2,1,0:T(8,128)S(1)} %bitcast.72, ...), custom_call_target="tpu_custom_call", output_to_operand_aliasing={{1}: (7, {}), {0}: (8, {})} | custom-call | flops 7864320 | bytes 3670016 | tf_op jit(solution)/shard_map/pallas_call | solution.py:254
  42.2 4.5 %collective-permute-start.4 = (f32[64,4,256]{2,1,0:T(4,128)S(1)}, f32[64,4,256]{2,1,0:T(4,128)S(1)}, u32[]{:S(2)}, u32[]{:S(2)}) collective-permute-start(f32[64,4,256]{2,1,0:T(4,128)S(1)} %get-tuple-element.45), channel_id=1, source_target_pairs={{1,2},{2,1},{3,4},{4,3},{5,6},{6,5},{7,8},{8,7},{9,10},{10,9},{11,... | collective-permute-start | bytes 786440 | tf_op jit(solution)/shard_map/ppermute | solution.py:372
  46.7 2.2 %shard_map.108 = (f32[64,16,256]{2,1,0:T(8,128)S(1)}, f32[64,16,256]{2,1,0:T(8,128)S(1)}, f32[64,4,256]{2,1,0:T(4,128)S(1)}) custom-call(s32[1]{0:T(128)} %bitcast.11.tile_ref, f32[64,16,256]{2,1,0:T(8,128)S(1)} %get-tuple-element.44.cur_ref.prev_ref, f32[64,16,256]{2,1,0:T(8,128)S(1)} %get-tuple-element.38.cur_ref.prev_ref, ...), custom_call_target="tpu_custom_call", output_to_operand_aliasing={{1}: (7, {})} | custom-call | flops 7864320 | bytes 3670016 | tf_op jit(solution)/shard_map/pallas_call | solution.py:254
  48.9 0.1 collective-permute-start.7
  49.0 3.0 %collective-permute-done.4.halo_ref = f32[64,4,256]{2,1,0:T(4,128)S(1)} collective-permute-done((f32[64,4,256]{2,1,0:T(4,128)S(1)}, f32[64,4,256]{2,1,0:T(4,128)S(1)}, u32[]{:S(2)}, u32[]{:S(2)}) %collective-permute-start.4) | collective-permute-done | bytes 262176 | tf_op jit(solution)/shard_map/ppermute | solution.py:372
  52.0 2.1 %shard_map.109 = (f32[64,16,256]{2,1,0:T(8,128)S(1)}, f32[64,16,256]{2,1,0:T(8,128)S(1)}, f32[64,4,256]{2,1,0:T(4,128)S(1)}) custom-call(s32[1]{0:T(128)} %bitcast.1.tile_ref, f32[64,16,256]{2,1,0:T(8,128)S(1)} %get-tuple-element.44.cur_ref.prev_ref, ...), custom_call_target="tpu_custom_call", output_to_operand_aliasing={{1}: (7, {}), {0}: (8, {})} | custom-call | flops 7864320 | bytes 3670016 | tf_op jit(solution)/shard_map/pallas_call | solution.py:254
  54.2 4.5 %collective-permute-start.6 = (f32[64,4,256]{2,1,0:T(4,128)S(1)}, f32[64,4,256]{2,1,0:T(4,128)S(1)}, u32[]{:S(2)}, u32[]{:S(2)}) collective-permute-start(f32[64,4,256]{2,1,0:T(4,128)S(1)} %get-tuple-element.51), channel_id=1, source_target_pairs={{1,2},{2,1},{3,4},{4,3},{5,6},{6,5},{7,8},{8,7},{9,10},{10,9},{11,... | collective-permute-start | bytes 786440 | tf_op jit(solution)/shard_map/ppermute | solution.py:372
  58.7 2.2 %shard_map.110 = (f32[64,16,256]{2,1,0:T(8,128)S(1)}, f32[64,16,256]{2,1,0:T(8,128)S(1)}, f32[64,4,256]{2,1,0:T(4,128)S(1)}) custom-call(s32[1]{0:T(128)} %bitcast.11.tile_ref, f32[64,16,256]{2,1,0:T(8,128)S(1)} %get-tuple-element.50.cur_ref.prev_ref, f32[64,16,256]{2,1,0:T(8,128)S(1)} %get-tuple-element.44.cur_ref.prev_ref, ...), custom_call_target="tpu_custom_call", output_to_operand_aliasing={{1}: (7, {})} | custom-call | flops 7864320 | bytes 3670016 | tf_op jit(solution)/shard_map/pallas_call | solution.py:254
  60.8 0.1 collective-permute-start.9
  60.9 3.1 %collective-permute-done.6.halo_ref = f32[64,4,256]{2,1,0:T(4,128)S(1)} collective-permute-done((f32[64,4,256]{2,1,0:T(4,128)S(1)}, f32[64,4,256]{2,1,0:T(4,128)S(1)}, u32[]{:S(2)}, u32[]{:S(2)}) %collective-permute-start.6) | collective-permute-done | bytes 262176 | tf_op jit(solution)/shard_map/ppermute | solution.py:372
  64.0 2.1 %shard_map.111 = (f32[64,16,256]{2,1,0:T(8,128)S(1)}, f32[64,16,256]{2,1,0:T(8,128)S(1)}, f32[64,4,256]{2,1,0:T(4,128)S(1)}) custom-call(s32[1]{0:T(128)} %bitcast.1.tile_ref, f32[64,16,256]{2,1,0:T(8,128)S(1)} %get-tuple-element.50.cur_ref.prev_ref, ...), custom_call_target="tpu_custom_call", output_to_operand_aliasing={{1}: (7, {}), {0}: (8, {})} | custom-call | flops 7864320 | bytes 3670016 | tf_op jit(solution)/shard_map/pallas_call | solution.py:254
  66.1 4.5 %collective-permute-start.8 = (f32[64,4,256]{2,1,0:T(4,128)S(1)}, f32[64,4,256]{2,1,0:T(4,128)S(1)}, u32[]{:S(2)}, u32[]{:S(2)}) collective-permute-start(f32[64,4,256]{2,1,0:T(4,128)S(1)} %get-tuple-element.57), channel_id=1, source_target_pairs={{1,2},{2,1},{3,4},{4,3},{5,6},{6,5},{7,8},{8,7},{9,10},{10,9},{11,... | collective-permute-start | bytes 786440 | tf_op jit(solution)/shard_map/ppermute | solution.py:372
  71.3 2.2 %shard_map.112 = (f32[64,16,256]{2,1,0:T(8,128)S(1)}, f32[64,16,256]{2,1,0:T(8,128)S(1)}, f32[64,4,256]{2,1,0:T(4,128)S(1)}) custom-call(s32[1]{0:T(128)} %bitcast.11.tile_ref, f32[64,16,256]{2,1,0:T(8,128)S(1)} %get-tuple-element.56.cur_ref.prev_ref, f32[64,16,256]{2,1,0:T(8,128)S(1)} %get-tuple-element.50.cur_ref.prev_ref, ...), custom_call_target="tpu_custom_call", output_to_operand_aliasing={{1}: (7, {})} | custom-call | flops 7864320 | bytes 3670016 | tf_op jit(solution)/shard_map/pallas_call | solution.py:254
  73.4 0.1 collective-permute-start.11
  73.5 2.4 %collective-permute-done.8.halo_ref = f32[64,4,256]{2,1,0:T(4,128)S(1)} collective-permute-done((f32[64,4,256]{2,1,0:T(4,128)S(1)}, f32[64,4,256]{2,1,0:T(4,128)S(1)}, u32[]{:S(2)}, u32[]{:S(2)}) %collective-permute-start.8) | collective-permute-done | bytes 262176 | tf_op jit(solution)/shard_map/ppermute | solution.py:372
  75.9 2.3 %shard_map.113 = (f32[64,16,256]{2,1,0:T(8,128)S(1)}, f32[64,16,256]{2,1,0:T(8,128)S(1)}, f32[64,4,256]{2,1,0:T(4,128)S(1)}) custom-call(s32[1]{0:T(128)} %bitcast.1.tile_ref, f32[64,16,256]{2,1,0:T(8,128)S(1)} %get-tuple-element.56.cur_ref.prev_ref, ...), custom_call_target="tpu_custom_call", output_to_operand_aliasing={{1}: (7, {}), {0}: (8, {})} | custom-call | flops 7864320 | bytes 3670016 | tf_op jit(solution)/shard_map/pallas_call | solution.py:254
  78.3 4.5 %collective-permute-start.10 = (f32[64,4,256]{2,1,0:T(4,128)S(1)}, f32[64,4,256]{2,1,0:T(4,128)S(1)}, u32[]{:S(2)}, u32[]{:S(2)}) collective-permute-start(f32[64,4,256]{2,1,0:T(4,128)S(1)} %get-tuple-element.63), channel_id=1, source_target_pairs={{1,2},{2,1},{3,4},{4,3},{5,6},{6,5},{7,8},{8,7},{9,10},{10,9},{11,... | collective-permute-start | bytes 786440 | tf_op jit(solution)/shard_map/ppermute | solution.py:372
  82.8 3.0 %shard_map.114 = (f32[64,16,256]{2,1,0:T(8,128)}, f32[64,16,256]{2,1,0:T(8,128)S(1)}, f32[64,4,256]{2,1,0:T(4,128)}) custom-call(s32[1]{0:T(128)} %bitcast.11.tile_ref, f32[64,16,256]{2,1,0:T(8,128)S(1)} %get-tuple-element.62.cur_ref, f32[64,16,256]{2,1,0:T(8,128)S(1)} %get-tuple-element.56.cur_ref.prev_ref, ...), custom_call_target="tpu_custom_call", output_to_operand_aliasing={{1}: (7, {})} | custom-call | flops 7864320 | bytes 3670016 | tf_op jit(solution)/shard_map/pallas_call | solution.py:254
  85.8 2.3 %collective-permute-done.10.halo_ref = f32[64,4,256]{2,1,0:T(4,128)S(1)} collective-permute-done((f32[64,4,256]{2,1,0:T(4,128)S(1)}, f32[64,4,256]{2,1,0:T(4,128)S(1)}, u32[]{:S(2)}, u32[]{:S(2)}) %collective-permute-start.10) | collective-permute-done | bytes 262176 | tf_op jit(solution)/shard_map/ppermute | solution.py:372
  88.1 3.0 %shard_map.115 = (f32[64,16,256]{2,1,0:T(8,128)}, f32[64,16,256]{2,1,0:T(8,128)S(1)}, f32[64,4,256]{2,1,0:T(4,128)}) custom-call(s32[1]{0:T(128)} %bitcast.1.tile_ref, f32[64,16,256]{2,1,0:T(8,128)S(1)} %get-tuple-element.62.cur_ref, f32[64,16,256]{2,1,0:T(8,128)S(1)} %get-tuple-element.56.cur_ref.prev_ref, ...), custom_call_target="tpu_custom_call", output_to_operand_aliasing={{1}: (7, {}), {0}: (8, {})} | custom-call | flops 7864320 | bytes 3670016 | tf_op jit(solution)/shard_map/pallas_call | solution.py:254
  91.0 0.7 gather_fusion
  91.7 0.2 select_select_fusion
  92.0 22.8 %all_to_all.10 = f32[8,10,16,256]{3,2,1,0:T(8,128)S(1)} all-to-all(f32[8,10,16,256]{3,2,1,0:T(8,128)S(1)} %select_select_fusion), channel_id=1, replica_groups=mesh['shot'=8,'space'=16] {'shot'}, dimensions={0} | all-to-all | bytes 2621440 | tf_op jit(solution)/shard_map/all_to_all | solution.py:388
  114.8 0.8 reduce_sum.19
  (24 shorter events, 0.1 us)
Async XLA Ops:
  0.6 2.3 %copy-start = (bf16[1,256,1536]{2,1,0:T(8,128)(2,1)S(1)}, bf16[1,256,1536]{2,1,0:T(8,128)(2,1)}, u32[]{:S(2)}) copy-start(bf16[1,256,1536]{2,1,0:T(8,128)(2,1)} %param.9) | copy-start | bytes 2359300
  0.6 10.8 %copy-start.4 = (f32[1,64,16,256]{3,2,1,0:T(8,128)S(1)}, f32[1,64,16,256]{3,2,1,0:T(8,128)}, u32[]{:S(2)}) copy-start(f32[1,64,16,256]{3,2,1,0:T(8,128)} %param.16) | copy-start | bytes 3145732
  5.6 10.3 %all-to-all-start = ((f32[16,1,336]{2,1,0:T(1,128)}), f32[16,1,336]{2,1,0:T(1,128)S(1)}, u32[]{:S(2)}, u32[]{:S(2)}) async-start(f32[16,1,336]{2,1,0:T(1,128)} %reshape.102), calls=%async_computation | async-start | bytes 49152 | tf_op jit(solution)/shard_map/all_to_all | solution.py:344
  12.4 6.4 %collective-permute-start.1 = (f32[64,4,256]{2,1,0:T(4,128)}, f32[64,4,256]{2,1,0:T(4,128)S(1)}, u32[]{:S(2)}, u32[]{:S(2)}) collective-permute-start(f32[64,4,256]{2,1,0:T(4,128)} %get-tuple-element.70), channel_id=1, source_target_pairs={{0,1},{1,0},{2,3},{3,2},{4,5},{5,4},{6,7},{7,6},{8,9},{9,8},{10,11... | collective-permute-start | bytes 786440 | tf_op jit(solution)/shard_map/ppermute | solution.py:371
  12.8 14.5 %collective-permute-start = (f32[64,4,256]{2,1,0:T(4,128)}, f32[64,4,256]{2,1,0:T(4,128)}, u32[]{:S(2)}, u32[]{:S(2)}) collective-permute-start(f32[64,4,256]{2,1,0:T(4,128)} %get-tuple-element.71), channel_id=1, source_target_pairs={{1,2},{2,1},{3,4},{4,3},{5,6},{6,5},{7,8},{8,7},{9,10},{10,9},{11,... | collective-permute-start | bytes 786440 | tf_op jit(solution)/shard_map/ppermute | solution.py:372
  18.1 1.5 %copy-start.3 = (f32[1,64,16,256]{3,2,1,0:T(8,128)S(1)}, f32[1,64,16,256]{3,2,1,0:T(8,128)}, u32[]{:S(2)}) copy-start(f32[1,64,16,256]{3,2,1,0:T(8,128)} %param.14) | copy-start | bytes 3145732
  18.7 0.7 copy-start.8
  19.6 1.9 %copy-start.1 = (bf16[1,6,64,16,256]{4,3,2,1,0:T(8,128)(2,1)S(1)}, bf16[1,6,64,16,256]{4,3,2,1,0:T(8,128)(2,1)}, u32[]{:S(2)}) copy-start(bf16[1,6,64,16,256]{4,3,2,1,0:T(8,128)(2,1)} %param.17) | copy-start | bytes 9437188
  21.5 1.2 %copy-start.5 = (f32[1,64,16,256]{3,2,1,0:T(8,128)S(1)}, f32[1,64,16,256]{3,2,1,0:T(8,128)}, u32[]{:S(2)}) copy-start(f32[1,64,16,256]{3,2,1,0:T(8,128)} %param.16) | copy-start | bytes 3145732
  22.7 1.2 %copy-start.7 = (f32[1,64,16,256]{3,2,1,0:T(8,128)S(1)}, f32[1,64,16,256]{3,2,1,0:T(8,128)}, u32[]{:S(2)}) copy-start(f32[1,64,16,256]{3,2,1,0:T(8,128)} %param.15) | copy-start | bytes 3145732
  23.9 0.9 copy-start.9
  24.9 2.4 %copy-start.2 = (bf16[1,6,64,16,256]{4,3,2,1,0:T(8,128)(2,1)S(1)}, bf16[1,6,64,16,256]{4,3,2,1,0:T(8,128)(2,1)}, u32[]{:S(2)}) copy-start(bf16[1,6,64,16,256]{4,3,2,1,0:T(8,128)(2,1)} %param.17) | copy-start | bytes 9437188
  24.9 2.4 %copy-start.6 = (f32[1,64,16,256]{3,2,1,0:T(8,128)S(1)}, f32[1,64,16,256]{3,2,1,0:T(8,128)}, u32[]{:S(2)}) copy-start(f32[1,64,16,256]{3,2,1,0:T(8,128)} %param.16) | copy-start | bytes 3145732
  27.0 7.7 %collective-permute-start.3 = (f32[64,4,256]{2,1,0:T(4,128)S(1)}, f32[64,4,256]{2,1,0:T(4,128)S(1)}, u32[]{:S(2)}, u32[]{:S(2)}) collective-permute-start(f32[64,4,256]{2,1,0:T(4,128)S(1)} %get-tuple-element.40), channel_id=1, source_target_pairs={{0,1},{1,0},{2,3},{3,2},{4,5},{5,4},{6,7},{7,6},{8,9},{9,8},{10,11... | collective-permute-start | bytes 786440 | tf_op jit(solution)/shard_map/ppermute | solution.py:371
  30.3 9.8 %collective-permute-start.2 = (f32[64,4,256]{2,1,0:T(4,128)S(1)}, f32[64,4,256]{2,1,0:T(4,128)S(1)}, u32[]{:S(2)}, u32[]{:S(2)}) collective-permute-start(f32[64,4,256]{2,1,0:T(4,128)S(1)} %get-tuple-element.39), channel_id=1, source_target_pairs={{1,2},{2,1},{3,4},{4,3},{5,6},{6,5},{7,8},{8,7},{9,10},{10,9},{11,... | collective-permute-start | bytes 786440 | tf_op jit(solution)/shard_map/ppermute | solution.py:372
  36.9 9.8 %collective-permute-start.5 = (f32[64,4,256]{2,1,0:T(4,128)S(1)}, f32[64,4,256]{2,1,0:T(4,128)S(1)}, u32[]{:S(2)}, u32[]{:S(2)}) collective-permute-start(f32[64,4,256]{2,1,0:T(4,128)S(1)} %get-tuple-element.46), channel_id=1, source_target_pairs={{0,1},{1,0},{2,3},{3,2},{4,5},{5,4},{6,7},{7,6},{8,9},{9,8},{10,11... | collective-permute-start | bytes 786440 | tf_op jit(solution)/shard_map/ppermute | solution.py:371
  42.2 9.8 %collective-permute-start.4 = (f32[64,4,256]{2,1,0:T(4,128)S(1)}, f32[64,4,256]{2,1,0:T(4,128)S(1)}, u32[]{:S(2)}, u32[]{:S(2)}) collective-permute-start(f32[64,4,256]{2,1,0:T(4,128)S(1)} %get-tuple-element.45), channel_id=1, source_target_pairs={{1,2},{2,1},{3,4},{4,3},{5,6},{6,5},{7,8},{8,7},{9,10},{10,9},{11,... | collective-permute-start | bytes 786440 | tf_op jit(solution)/shard_map/ppermute | solution.py:372
  48.9 9.8 %collective-permute-start.7 = (f32[64,4,256]{2,1,0:T(4,128)S(1)}, f32[64,4,256]{2,1,0:T(4,128)S(1)}, u32[]{:S(2)}, u32[]{:S(2)}) collective-permute-start(f32[64,4,256]{2,1,0:T(4,128)S(1)} %get-tuple-element.52), channel_id=1, source_target_pairs={{0,1},{1,0},{2,3},{3,2},{4,5},{5,4},{6,7},{7,6},{8,9},{9,8},{10,11... | collective-permute-start | bytes 786440 | tf_op jit(solution)/shard_map/ppermute | solution.py:371
  54.2 9.8 %collective-permute-start.6 = (f32[64,4,256]{2,1,0:T(4,128)S(1)}, f32[64,4,256]{2,1,0:T(4,128)S(1)}, u32[]{:S(2)}, u32[]{:S(2)}) collective-permute-start(f32[64,4,256]{2,1,0:T(4,128)S(1)} %get-tuple-element.51), channel_id=1, source_target_pairs={{1,2},{2,1},{3,4},{4,3},{5,6},{6,5},{7,8},{8,7},{9,10},{10,9},{11,... | collective-permute-start | bytes 786440 | tf_op jit(solution)/shard_map/ppermute | solution.py:372
  60.8 10.4 %collective-permute-start.9 = (f32[64,4,256]{2,1,0:T(4,128)S(1)}, f32[64,4,256]{2,1,0:T(4,128)S(1)}, u32[]{:S(2)}, u32[]{:S(2)}) collective-permute-start(f32[64,4,256]{2,1,0:T(4,128)S(1)} %get-tuple-element.58), channel_id=1, source_target_pairs={{0,1},{1,0},{2,3},{3,2},{4,5},{5,4},{6,7},{7,6},{8,9},{9,8},{10,11... | collective-permute-start | bytes 786440 | tf_op jit(solution)/shard_map/ppermute | solution.py:371
  66.1 9.8 %collective-permute-start.8 = (f32[64,4,256]{2,1,0:T(4,128)S(1)}, f32[64,4,256]{2,1,0:T(4,128)S(1)}, u32[]{:S(2)}, u32[]{:S(2)}) collective-permute-start(f32[64,4,256]{2,1,0:T(4,128)S(1)} %get-tuple-element.57), channel_id=1, source_target_pairs={{1,2},{2,1},{3,4},{4,3},{5,6},{6,5},{7,8},{8,7},{9,10},{10,9},{11,... | collective-permute-start | bytes 786440 | tf_op jit(solution)/shard_map/ppermute | solution.py:372
  73.4 9.4 %collective-permute-start.11 = (f32[64,4,256]{2,1,0:T(4,128)S(1)}, f32[64,4,256]{2,1,0:T(4,128)S(1)}, u32[]{:S(2)}, u32[]{:S(2)}) collective-permute-start(f32[64,4,256]{2,1,0:T(4,128)S(1)} %get-tuple-element.64), channel_id=1, source_target_pairs={{0,1},{1,0},{2,3},{3,2},{4,5},{5,4},{6,7},{7,6},{8,9},{9,8},{10,11... | collective-permute-start | bytes 786440 | tf_op jit(solution)/shard_map/ppermute | solution.py:371
  78.3 9.8 %collective-permute-start.10 = (f32[64,4,256]{2,1,0:T(4,128)S(1)}, f32[64,4,256]{2,1,0:T(4,128)S(1)}, u32[]{:S(2)}, u32[]{:S(2)}) collective-permute-start(f32[64,4,256]{2,1,0:T(4,128)S(1)} %get-tuple-element.63), channel_id=1, source_target_pairs={{1,2},{2,1},{3,4},{4,3},{5,6},{6,5},{7,8},{8,7},{9,10},{10,9},{11,... | collective-permute-start | bytes 786440 | tf_op jit(solution)/shard_map/ppermute | solution.py:372

commit v16 on v15

--- a/solution.py
+++ b/solution.py
@@ -269,7 +269,7 @@
         cost_estimate=pl.CostEstimate(
             flops=60 * cells, bytes_accessed=28 * cells, transcendentals=0
         ),
-        compiler_params=pltpu.CompilerParams(vmem_limit_bytes=12 * 1024 * 1024),
+        compiler_params=pltpu.CompilerParams(vmem_limit_bytes=10 * 1024 * 1024),
     )(*operands)
 
 

time: 116 us -> 116 us (level)
  no operation moved by 1% of the time
where the time goes in v16:
time: 116 us
  starting transfers between devices  32.2 us (28%)
  Pallas kernels  28.4 us (24%)
  blocking collectives  22.8 us (20%)
  waiting for transfers between devices  13.9 us (12%)
  local copies, waits for them, and re-layouts  9.5 us (8%)
  other arithmetic  4.07 us (4%)
  matrix products  2.95 us (3%)
  between operations  1.66 us (1%)
    pallas_call x12, Pallas kernels, tile_call(): pl.pallas_call(functools.partial(tile_kernel, moment, chained), grid_spec...  28.4 us
    ppermute x6, starting transfers between devices, local(): far_halo = lax.ppermute(far_edge, 'space', across)  25.5 us
    all_to_all x1, blocking collectives, local(): lax.all_to_all(placed, 'shot', split_axis=0, concat_axis=0, tiled=True)  22.8 us
    ppermute x6, waiting for transfers between devices, local(): far_halo = lax.ppermute(far_edge, 'space', across)  13.9 us
    unnamed x22, local copies, waits for them, and re-layouts  6.8 us
    all_to_all x1, starting transfers between devices, local(): lax.all_to_all(buffer, 'space', split_axis=0, concat_axis=0, tiled=True)  5.82 us
  transfers between devices with their start and end apart: 13, of which 5 were waited for; matrix products, arithmetic and copies ran while one was open for 3% of the time, Pallas kernels for 22%

profile of v16, /device:TPU:97, one launch (start us, length us, event | category | flops | bytes accessed | tf_op | source)
XLA Modules:
  0.0 115.5 jit_solution(12303322628254912774)
XLA Ops:
  0.6 0.0 copy-start
  0.6 0.0 copy-start.4
  0.7 0.9 convert_reduce_fusion
  1.6 0.7 multiply_add_fusion
  2.3 0.7 convert_bitcast_fusion
  3.0 1.0 fusion.11
  4.0 0.3 fusion.13
  4.3 0.3 convolution_add_fusion.1
  4.5 0.3 convolution_add_fusion
  4.8 0.1 reshape.89
  4.9 0.7 reshape.102
  5.6 5.8 %all-to-all-start = ((f32[16,1,336]{2,1,0:T(1,128)}), f32[16,1,336]{2,1,0:T(1,128)S(1)}, u32[]{:S(2)}, u32[]{:S(2)}) async-start(f32[16,1,336]{2,1,0:T(1,128)} %reshape.102), calls=%async_computation | async-start | bytes 49152 | tf_op jit(solution)/shard_map/all_to_all | solution.py:344
  11.5 0.9 dynamic-slice_bitcast_fusion
  12.4 0.4 collective-permute-start.1
  12.8 3.1 %collective-permute-start = (f32[64,4,256]{2,1,0:T(4,128)}, f32[64,4,256]{2,1,0:T(4,128)}, u32[]{:S(2)}, u32[]{:S(2)}) collective-permute-start(f32[64,4,256]{2,1,0:T(4,128)} %get-tuple-element.71), channel_id=1, source_target_pairs={{1,2},{2,1},{3,4},{4,3},{5,6},{6,5},{7,8},{8,7},{9,10},{10,9},{11,... | collective-permute-start | bytes 786440 | tf_op jit(solution)/shard_map/ppermute | solution.py:372
  15.9 0.5 broadcast.101
  16.4 0.7 reduce.2
  17.1 0.1 reshape.103
  17.2 0.1 reshape.90
  17.3 0.4 fusion
  17.7 0.4 fusion.1
  18.1 0.4 fusion.10
  18.5 0.2 copy.37
  18.7 0.0 collective-permute-done.1.halo_ref
  18.7 0.0 copy-start.8
  18.8 0.7 copy-done.8
  19.5 0.1 broadcast_in_dim.38.img_ref
  19.6 0.0 copy-start.1
  19.6 1.9 %copy-done.1 = bf16[1,6,64,16,256]{4,3,2,1,0:T(8,128)(2,1)S(1)} copy-done((bf16[1,6,64,16,256]{4,3,2,1,0:T(8,128)(2,1)S(1)}, bf16[1,6,64,16,256]{4,3,2,1,0:T(8,128)(2,1)}, u32[]{:S(2)}) %copy-start.1) | copy-done | bytes 3145752
  21.5 1.2 %copy-done.5 = f32[1,64,16,256]{3,2,1,0:T(8,128)S(1)} copy-done((f32[1,64,16,256]{3,2,1,0:T(8,128)S(1)}, f32[1,64,16,256]{3,2,1,0:T(8,128)}, u32[]{:S(2)}) %copy-start.5) | copy-done | bytes 1048600
  22.7 1.2 %copy-done.7 = f32[1,64,16,256]{3,2,1,0:T(8,128)S(1)} copy-done((f32[1,64,16,256]{3,2,1,0:T(8,128)S(1)}, f32[1,64,16,256]{3,2,1,0:T(8,128)}, u32[]{:S(2)}) %copy-start.7) | copy-done | bytes 1048600
  23.9 0.9 copy-done.9
  24.9 2.1 %shard_map.104 = (f32[64,16,256]{2,1,0:T(8,128)S(1)}, f32[64,16,256]{2,1,0:T(8,128)S(1)}, f32[64,4,256]{2,1,0:T(4,128)S(1)}) custom-call(s32[1]{0:T(128)} %bitcast.11.tile_ref, f32[64,16,256]{2,1,0:T(8,128)S(1)} %bitcast.69, f32[64,16,256]{2,1,0:T(8,128)S(1)} %bitcast.73, f32[64,4,256]{2,1,0:T(4,128)S(1)} %copy-done.9, ...), custom_call_target="tpu_custom_call", output_to_operand_aliasing={{1}: (7, {})} | custom-call | flops 7864320 | bytes 3670016 | tf_op jit(solution)/shard_map/pallas_call | solution.py:254
  27.0 0.2 collective-permute-start.3
  27.3 3.0 %shard_map.105 = (f32[64,16,256]{2,1,0:T(8,128)S(1)}, f32[64,16,256]{2,1,0:T(8,128)S(1)}, f32[64,4,256]{2,1,0:T(4,128)S(1)}) custom-call(s32[1]{0:T(128)} %bitcast.1.tile_ref, f32[64,16,256]{2,1,0:T(8,128)S(1)} %bitcast.70, f32[64,16,256]{2,1,0:T(8,128)S(1)} %bitcast.74, ...), custom_call_target="tpu_custom_call", output_to_operand_aliasing={{1}: (7, {}), {0}: (8, {})} | custom-call | flops 7864320 | bytes 3670016 | tf_op jit(solution)/shard_map/pallas_call | solution.py:254
  30.3 4.5 %collective-permute-start.2 = (f32[64,4,256]{2,1,0:T(4,128)S(1)}, f32[64,4,256]{2,1,0:T(4,128)S(1)}, u32[]{:S(2)}, u32[]{:S(2)}) collective-permute-start(f32[64,4,256]{2,1,0:T(4,128)S(1)} %get-tuple-element.39), channel_id=1, source_target_pairs={{1,2},{2,1},{3,4},{4,3},{5,6},{6,5},{7,8},{8,7},{9,10},{10,9},{11,... | collective-permute-start | bytes 786440 | tf_op jit(solution)/shard_map/ppermute | solution.py:372
  34.8 0.0 collective-permute-done.3.halo_ref
  34.8 2.2 %shard_map.106 = (f32[64,16,256]{2,1,0:T(8,128)S(1)}, f32[64,16,256]{2,1,0:T(8,128)S(1)}, f32[64,4,256]{2,1,0:T(4,128)S(1)}) custom-call(s32[1]{0:T(128)} %bitcast.11.tile_ref, f32[64,16,256]{2,1,0:T(8,128)S(1)} %get-tuple-element.38.cur_ref.prev_ref, f32[64,16,256]{2,1,0:T(8,128)S(1)} %bitcast.71, ...), custom_call_target="tpu_custom_call", output_to_operand_aliasing={{1}: (7, {})} | custom-call | flops 7864320 | bytes 3670016 | tf_op jit(solution)/shard_map/pallas_call | solution.py:254
  36.9 0.1 collective-permute-start.5
  37.0 3.0 %collective-permute-done.2.halo_ref = f32[64,4,256]{2,1,0:T(4,128)S(1)} collective-permute-done((f32[64,4,256]{2,1,0:T(4,128)S(1)}, f32[64,4,256]{2,1,0:T(4,128)S(1)}, u32[]{:S(2)}, u32[]{:S(2)}) %collective-permute-start.2) | collective-permute-done | bytes 262176 | tf_op jit(solution)/shard_map/ppermute | solution.py:372
  40.1 2.1 %shard_map.107 = (f32[64,16,256]{2,1,0:T(8,128)S(1)}, f32[64,16,256]{2,1,0:T(8,128)S(1)}, f32[64,4,256]{2,1,0:T(4,128)S(1)}) custom-call(s32[1]{0:T(128)} %bitcast.1.tile_ref, f32[64,16,256]{2,1,0:T(8,128)S(1)} %get-tuple-element.38.cur_ref.prev_ref, f32[64,16,256]{2,1,0:T(8,128)S(1)} %bitcast.72, ...), custom_call_target="tpu_custom_call", output_to_operand_aliasing={{1}: (7, {}), {0}: (8, {})} | custom-call | flops 7864320 | bytes 3670016 | tf_op jit(solution)/shard_map/pallas_call | solution.py:254
  42.2 4.5 %collective-permute-start.4 = (f32[64,4,256]{2,1,0:T(4,128)S(1)}, f32[64,4,256]{2,1,0:T(4,128)S(1)}, u32[]{:S(2)}, u32[]{:S(2)}) collective-permute-start(f32[64,4,256]{2,1,0:T(4,128)S(1)} %get-tuple-element.45), channel_id=1, source_target_pairs={{1,2},{2,1},{3,4},{4,3},{5,6},{6,5},{7,8},{8,7},{9,10},{10,9},{11,... | collective-permute-start | bytes 786440 | tf_op jit(solution)/shard_map/ppermute | solution.py:372
  46.7 2.2 %shard_map.108 = (f32[64,16,256]{2,1,0:T(8,128)S(1)}, f32[64,16,256]{2,1,0:T(8,128)S(1)}, f32[64,4,256]{2,1,0:T(4,128)S(1)}) custom-call(s32[1]{0:T(128)} %bitcast.11.tile_ref, f32[64,16,256]{2,1,0:T(8,128)S(1)} %get-tuple-element.44.cur_ref.prev_ref, f32[64,16,256]{2,1,0:T(8,128)S(1)} %get-tuple-element.38.cur_ref.prev_ref, ...), custom_call_target="tpu_custom_call", output_to_operand_aliasing={{1}: (7, {})} | custom-call | flops 7864320 | bytes 3670016 | tf_op jit(solution)/shard_map/pallas_call | solution.py:254
  48.9 0.1 collective-permute-start.7
  49.0 3.0 %collective-permute-done.4.halo_ref = f32[64,4,256]{2,1,0:T(4,128)S(1)} collective-permute-done((f32[64,4,256]{2,1,0:T(4,128)S(1)}, f32[64,4,256]{2,1,0:T(4,128)S(1)}, u32[]{:S(2)}, u32[]{:S(2)}) %collective-permute-start.4) | collective-permute-done | bytes 262176 | tf_op jit(solution)/shard_map/ppermute | solution.py:372
  52.0 2.1 %shard_map.109 = (f32[64,16,256]{2,1,0:T(8,128)S(1)}, f32[64,16,256]{2,1,0:T(8,128)S(1)}, f32[64,4,256]{2,1,0:T(4,128)S(1)}) custom-call(s32[1]{0:T(128)} %bitcast.1.tile_ref, f32[64,16,256]{2,1,0:T(8,128)S(1)} %get-tuple-element.44.cur_ref.prev_ref, ...), custom_call_target="tpu_custom_call", output_to_operand_aliasing={{1}: (7, {}), {0}: (8, {})} | custom-call | flops 7864320 | bytes 3670016 | tf_op jit(solution)/shard_map/pallas_call | solution.py:254
  54.2 4.5 %collective-permute-start.6 = (f32[64,4,256]{2,1,0:T(4,128)S(1)}, f32[64,4,256]{2,1,0:T(4,128)S(1)}, u32[]{:S(2)}, u32[]{:S(2)}) collective-permute-start(f32[64,4,256]{2,1,0:T(4,128)S(1)} %get-tuple-element.51), channel_id=1, source_target_pairs={{1,2},{2,1},{3,4},{4,3},{5,6},{6,5},{7,8},{8,7},{9,10},{10,9},{11,... | collective-permute-start | bytes 786440 | tf_op jit(solution)/shard_map/ppermute | solution.py:372
  58.7 2.2 %shard_map.110 = (f32[64,16,256]{2,1,0:T(8,128)S(1)}, f32[64,16,256]{2,1,0:T(8,128)S(1)}, f32[64,4,256]{2,1,0:T(4,128)S(1)}) custom-call(s32[1]{0:T(128)} %bitcast.11.tile_ref, f32[64,16,256]{2,1,0:T(8,128)S(1)} %get-tuple-element.50.cur_ref.prev_ref, f32[64,16,256]{2,1,0:T(8,128)S(1)} %get-tuple-element.44.cur_ref.prev_ref, ...), custom_call_target="tpu_custom_call", output_to_operand_aliasing={{1}: (7, {})} | custom-call | flops 7864320 | bytes 3670016 | tf_op jit(solution)/shard_map/pallas_call | solution.py:254
  60.8 0.1 collective-permute-start.9
  60.9 3.1 %collective-permute-done.6.halo_ref = f32[64,4,256]{2,1,0:T(4,128)S(1)} collective-permute-done((f32[64,4,256]{2,1,0:T(4,128)S(1)}, f32[64,4,256]{2,1,0:T(4,128)S(1)}, u32[]{:S(2)}, u32[]{:S(2)}) %collective-permute-start.6) | collective-permute-done | bytes 262176 | tf_op jit(solution)/shard_map/ppermute | solution.py:372
  64.0 2.1 %shard_map.111 = (f32[64,16,256]{2,1,0:T(8,128)S(1)}, f32[64,16,256]{2,1,0:T(8,128)S(1)}, f32[64,4,256]{2,1,0:T(4,128)S(1)}) custom-call(s32[1]{0:T(128)} %bitcast.1.tile_ref, f32[64,16,256]{2,1,0:T(8,128)S(1)} %get-tuple-element.50.cur_ref.prev_ref, ...), custom_call_target="tpu_custom_call", output_to_operand_aliasing={{1}: (7, {}), {0}: (8, {})} | custom-call | flops 7864320 | bytes 3670016 | tf_op jit(solution)/shard_map/pallas_call | solution.py:254
  66.1 4.5 %collective-permute-start.8 = (f32[64,4,256]{2,1,0:T(4,128)S(1)}, f32[64,4,256]{2,1,0:T(4,128)S(1)}, u32[]{:S(2)}, u32[]{:S(2)}) collective-permute-start(f32[64,4,256]{2,1,0:T(4,128)S(1)} %get-tuple-element.57), channel_id=1, source_target_pairs={{1,2},{2,1},{3,4},{4,3},{5,6},{6,5},{7,8},{8,7},{9,10},{10,9},{11,... | collective-permute-start | bytes 786440 | tf_op jit(solution)/shard_map/ppermute | solution.py:372
  71.3 2.2 %shard_map.112 = (f32[64,16,256]{2,1,0:T(8,128)S(1)}, f32[64,16,256]{2,1,0:T(8,128)S(1)}, f32[64,4,256]{2,1,0:T(4,128)S(1)}) custom-call(s32[1]{0:T(128)} %bitcast.11.tile_ref, f32[64,16,256]{2,1,0:T(8,128)S(1)} %get-tuple-element.56.cur_ref.prev_ref, f32[64,16,256]{2,1,0:T(8,128)S(1)} %get-tuple-element.50.cur_ref.prev_ref, ...), custom_call_target="tpu_custom_call", output_to_operand_aliasing={{1}: (7, {})} | custom-call | flops 7864320 | bytes 3670016 | tf_op jit(solution)/shard_map/pallas_call | solution.py:254
  73.4 0.1 collective-permute-start.11
  73.5 2.4 %collective-permute-done.8.halo_ref = f32[64,4,256]{2,1,0:T(4,128)S(1)} collective-permute-done((f32[64,4,256]{2,1,0:T(4,128)S(1)}, f32[64,4,256]{2,1,0:T(4,128)S(1)}, u32[]{:S(2)}, u32[]{:S(2)}) %collective-permute-start.8) | collective-permute-done | bytes 262176 | tf_op jit(solution)/shard_map/ppermute | solution.py:372
  75.9 2.3 %shard_map.113 = (f32[64,16,256]{2,1,0:T(8,128)S(1)}, f32[64,16,256]{2,1,0:T(8,128)S(1)}, f32[64,4,256]{2,1,0:T(4,128)S(1)}) custom-call(s32[1]{0:T(128)} %bitcast.1.tile_ref, f32[64,16,256]{2,1,0:T(8,128)S(1)} %get-tuple-element.56.cur_ref.prev_ref, ...), custom_call_target="tpu_custom_call", output_to_operand_aliasing={{1}: (7, {}), {0}: (8, {})} | custom-call | flops 7864320 | bytes 3670016 | tf_op jit(solution)/shard_map/pallas_call | solution.py:254
  78.3 4.5 %collective-permute-start.10 = (f32[64,4,256]{2,1,0:T(4,128)S(1)}, f32[64,4,256]{2,1,0:T(4,128)S(1)}, u32[]{:S(2)}, u32[]{:S(2)}) collective-permute-start(f32[64,4,256]{2,1,0:T(4,128)S(1)} %get-tuple-element.63), channel_id=1, source_target_pairs={{1,2},{2,1},{3,4},{4,3},{5,6},{6,5},{7,8},{8,7},{9,10},{10,9},{11,... | collective-permute-start | bytes 786440 | tf_op jit(solution)/shard_map/ppermute | solution.py:372
  82.8 3.0 %shard_map.114 = (f32[64,16,256]{2,1,0:T(8,128)}, f32[64,16,256]{2,1,0:T(8,128)S(1)}, f32[64,4,256]{2,1,0:T(4,128)}) custom-call(s32[1]{0:T(128)} %bitcast.11.tile_ref, f32[64,16,256]{2,1,0:T(8,128)S(1)} %get-tuple-element.62.cur_ref, f32[64,16,256]{2,1,0:T(8,128)S(1)} %get-tuple-element.56.cur_ref.prev_ref, ...), custom_call_target="tpu_custom_call", output_to_operand_aliasing={{1}: (7, {})} | custom-call | flops 7864320 | bytes 3670016 | tf_op jit(solution)/shard_map/pallas_call | solution.py:254
  85.8 2.3 %collective-permute-done.10.halo_ref = f32[64,4,256]{2,1,0:T(4,128)S(1)} collective-permute-done((f32[64,4,256]{2,1,0:T(4,128)S(1)}, f32[64,4,256]{2,1,0:T(4,128)S(1)}, u32[]{:S(2)}, u32[]{:S(2)}) %collective-permute-start.10) | collective-permute-done | bytes 262176 | tf_op jit(solution)/shard_map/ppermute | solution.py:372
  88.1 3.0 %shard_map.115 = (f32[64,16,256]{2,1,0:T(8,128)}, f32[64,16,256]{2,1,0:T(8,128)S(1)}, f32[64,4,256]{2,1,0:T(4,128)}) custom-call(s32[1]{0:T(128)} %bitcast.1.tile_ref, f32[64,16,256]{2,1,0:T(8,128)S(1)} %get-tuple-element.62.cur_ref, f32[64,16,256]{2,1,0:T(8,128)S(1)} %get-tuple-element.56.cur_ref.prev_ref, ...), custom_call_target="tpu_custom_call", output_to_operand_aliasing={{1}: (7, {}), {0}: (8, {})} | custom-call | flops 7864320 | bytes 3670016 | tf_op jit(solution)/shard_map/pallas_call | solution.py:254
  91.0 0.7 gather_fusion
  91.7 0.2 select_select_fusion
  92.0 22.8 %all_to_all.10 = f32[8,10,16,256]{3,2,1,0:T(8,128)S(1)} all-to-all(f32[8,10,16,256]{3,2,1,0:T(8,128)S(1)} %select_select_fusion), channel_id=1, replica_groups=mesh['shot'=8,'space'=16] {'shot'}, dimensions={0} | all-to-all | bytes 2621440 | tf_op jit(solution)/shard_map/all_to_all | solution.py:388
  114.8 0.8 reduce_sum.19
  (24 shorter events, 0.1 us)
Async XLA Ops:
  0.6 2.3 %copy-start = (bf16[1,256,1536]{2,1,0:T(8,128)(2,1)S(1)}, bf16[1,256,1536]{2,1,0:T(8,128)(2,1)}, u32[]{:S(2)}) copy-start(bf16[1,256,1536]{2,1,0:T(8,128)(2,1)} %param.9) | copy-start | bytes 2359300
  0.6 10.8 %copy-start.4 = (f32[1,64,16,256]{3,2,1,0:T(8,128)S(1)}, f32[1,64,16,256]{3,2,1,0:T(8,128)}, u32[]{:S(2)}) copy-start(f32[1,64,16,256]{3,2,1,0:T(8,128)} %param.16) | copy-start | bytes 3145732
  5.6 10.3 %all-to-all-start = ((f32[16,1,336]{2,1,0:T(1,128)}), f32[16,1,336]{2,1,0:T(1,128)S(1)}, u32[]{:S(2)}, u32[]{:S(2)}) async-start(f32[16,1,336]{2,1,0:T(1,128)} %reshape.102), calls=%async_computation | async-start | bytes 49152 | tf_op jit(solution)/shard_map/all_to_all | solution.py:344
  12.4 6.4 %collective-permute-start.1 = (f32[64,4,256]{2,1,0:T(4,128)}, f32[64,4,256]{2,1,0:T(4,128)S(1)}, u32[]{:S(2)}, u32[]{:S(2)}) collective-permute-start(f32[64,4,256]{2,1,0:T(4,128)} %get-tuple-element.70), channel_id=1, source_target_pairs={{0,1},{1,0},{2,3},{3,2},{4,5},{5,4},{6,7},{7,6},{8,9},{9,8},{10,11... | collective-permute-start | bytes 786440 | tf_op jit(solution)/shard_map/ppermute | solution.py:371
  12.8 14.5 %collective-permute-start = (f32[64,4,256]{2,1,0:T(4,128)}, f32[64,4,256]{2,1,0:T(4,128)}, u32[]{:S(2)}, u32[]{:S(2)}) collective-permute-start(f32[64,4,256]{2,1,0:T(4,128)} %get-tuple-element.71), channel_id=1, source_target_pairs={{1,2},{2,1},{3,4},{4,3},{5,6},{6,5},{7,8},{8,7},{9,10},{10,9},{11,... | collective-permute-start | bytes 786440 | tf_op jit(solution)/shard_map/ppermute | solution.py:372
  18.1 1.5 %copy-start.3 = (f32[1,64,16,256]{3,2,1,0:T(8,128)S(1)}, f32[1,64,16,256]{3,2,1,0:T(8,128)}, u32[]{:S(2)}) copy-start(f32[1,64,16,256]{3,2,1,0:T(8,128)} %param.14) | copy-start | bytes 3145732
  18.7 0.7 copy-start.8
  19.6 1.9 %copy-start.1 = (bf16[1,6,64,16,256]{4,3,2,1,0:T(8,128)(2,1)S(1)}, bf16[1,6,64,16,256]{4,3,2,1,0:T(8,128)(2,1)}, u32[]{:S(2)}) copy-start(bf16[1,6,64,16,256]{4,3,2,1,0:T(8,128)(2,1)} %param.17) | copy-start | bytes 9437188
  21.5 1.2 %copy-start.5 = (f32[1,64,16,256]{3,2,1,0:T(8,128)S(1)}, f32[1,64,16,256]{3,2,1,0:T(8,128)}, u32[]{:S(2)}) copy-start(f32[1,64,16,256]{3,2,1,0:T(8,128)} %param.16) | copy-start | bytes 3145732
  22.7 1.2 %copy-start.7 = (f32[1,64,16,256]{3,2,1,0:T(8,128)S(1)}, f32[1,64,16,256]{3,2,1,0:T(8,128)}, u32[]{:S(2)}) copy-start(f32[1,64,16,256]{3,2,1,0:T(8,128)} %param.15) | copy-start | bytes 3145732
  23.9 0.9 copy-start.9
  24.9 2.4 %copy-start.2 = (bf16[1,6,64,16,256]{4,3,2,1,0:T(8,128)(2,1)S(1)}, bf16[1,6,64,16,256]{4,3,2,1,0:T(8,128)(2,1)}, u32[]{:S(2)}) copy-start(bf16[1,6,64,16,256]{4,3,2,1,0:T(8,128)(2,1)} %param.17) | copy-start | bytes 9437188
  24.9 2.4 %copy-start.6 = (f32[1,64,16,256]{3,2,1,0:T(8,128)S(1)}, f32[1,64,16,256]{3,2,1,0:T(8,128)}, u32[]{:S(2)}) copy-start(f32[1,64,16,256]{3,2,1,0:T(8,128)} %param.16) | copy-start | bytes 3145732
  27.0 7.7 %collective-permute-start.3 = (f32[64,4,256]{2,1,0:T(4,128)S(1)}, f32[64,4,256]{2,1,0:T(4,128)S(1)}, u32[]{:S(2)}, u32[]{:S(2)}) collective-permute-start(f32[64,4,256]{2,1,0:T(4,128)S(1)} %get-tuple-element.40), channel_id=1, source_target_pairs={{0,1},{1,0},{2,3},{3,2},{4,5},{5,4},{6,7},{7,6},{8,9},{9,8},{10,11... | collective-permute-start | bytes 786440 | tf_op jit(solution)/shard_map/ppermute | solution.py:371
  30.3 9.8 %collective-permute-start.2 = (f32[64,4,256]{2,1,0:T(4,128)S(1)}, f32[64,4,256]{2,1,0:T(4,128)S(1)}, u32[]{:S(2)}, u32[]{:S(2)}) collective-permute-start(f32[64,4,256]{2,1,0:T(4,128)S(1)} %get-tuple-element.39), channel_id=1, source_target_pairs={{1,2},{2,1},{3,4},{4,3},{5,6},{6,5},{7,8},{8,7},{9,10},{10,9},{11,... | collective-permute-start | bytes 786440 | tf_op jit(solution)/shard_map/ppermute | solution.py:372
  36.9 9.8 %collective-permute-start.5 = (f32[64,4,256]{2,1,0:T(4,128)S(1)}, f32[64,4,256]{2,1,0:T(4,128)S(1)}, u32[]{:S(2)}, u32[]{:S(2)}) collective-permute-start(f32[64,4,256]{2,1,0:T(4,128)S(1)} %get-tuple-element.46), channel_id=1, source_target_pairs={{0,1},{1,0},{2,3},{3,2},{4,5},{5,4},{6,7},{7,6},{8,9},{9,8},{10,11... | collective-permute-start | bytes 786440 | tf_op jit(solution)/shard_map/ppermute | solution.py:371
  42.2 9.8 %collective-permute-start.4 = (f32[64,4,256]{2,1,0:T(4,128)S(1)}, f32[64,4,256]{2,1,0:T(4,128)S(1)}, u32[]{:S(2)}, u32[]{:S(2)}) collective-permute-start(f32[64,4,256]{2,1,0:T(4,128)S(1)} %get-tuple-element.45), channel_id=1, source_target_pairs={{1,2},{2,1},{3,4},{4,3},{5,6},{6,5},{7,8},{8,7},{9,10},{10,9},{11,... | collective-permute-start | bytes 786440 | tf_op jit(solution)/shard_map/ppermute | solution.py:372
  48.9 9.8 %collective-permute-start.7 = (f32[64,4,256]{2,1,0:T(4,128)S(1)}, f32[64,4,256]{2,1,0:T(4,128)S(1)}, u32[]{:S(2)}, u32[]{:S(2)}) collective-permute-start(f32[64,4,256]{2,1,0:T(4,128)S(1)} %get-tuple-element.52), channel_id=1, source_target_pairs={{0,1},{1,0},{2,3},{3,2},{4,5},{5,4},{6,7},{7,6},{8,9},{9,8},{10,11... | collective-permute-start | bytes 786440 | tf_op jit(solution)/shard_map/ppermute | solution.py:371
  54.2 9.8 %collective-permute-start.6 = (f32[64,4,256]{2,1,0:T(4,128)S(1)}, f32[64,4,256]{2,1,0:T(4,128)S(1)}, u32[]{:S(2)}, u32[]{:S(2)}) collective-permute-start(f32[64,4,256]{2,1,0:T(4,128)S(1)} %get-tuple-element.51), channel_id=1, source_target_pairs={{1,2},{2,1},{3,4},{4,3},{5,6},{6,5},{7,8},{8,7},{9,10},{10,9},{11,... | collective-permute-start | bytes 786440 | tf_op jit(solution)/shard_map/ppermute | solution.py:372
  60.8 10.4 %collective-permute-start.9 = (f32[64,4,256]{2,1,0:T(4,128)S(1)}, f32[64,4,256]{2,1,0:T(4,128)S(1)}, u32[]{:S(2)}, u32[]{:S(2)}) collective-permute-start(f32[64,4,256]{2,1,0:T(4,128)S(1)} %get-tuple-element.58), channel_id=1, source_target_pairs={{0,1},{1,0},{2,3},{3,2},{4,5},{5,4},{6,7},{7,6},{8,9},{9,8},{10,11... | collective-permute-start | bytes 786440 | tf_op jit(solution)/shard_map/ppermute | solution.py:371
  66.1 9.8 %collective-permute-start.8 = (f32[64,4,256]{2,1,0:T(4,128)S(1)}, f32[64,4,256]{2,1,0:T(4,128)S(1)}, u32[]{:S(2)}, u32[]{:S(2)}) collective-permute-start(f32[64,4,256]{2,1,0:T(4,128)S(1)} %get-tuple-element.57), channel_id=1, source_target_pairs={{1,2},{2,1},{3,4},{4,3},{5,6},{6,5},{7,8},{8,7},{9,10},{10,9},{11,... | collective-permute-start | bytes 786440 | tf_op jit(solution)/shard_map/ppermute | solution.py:372
  73.4 9.4 %collective-permute-start.11 = (f32[64,4,256]{2,1,0:T(4,128)S(1)}, f32[64,4,256]{2,1,0:T(4,128)S(1)}, u32[]{:S(2)}, u32[]{:S(2)}) collective-permute-start(f32[64,4,256]{2,1,0:T(4,128)S(1)} %get-tuple-element.64), channel_id=1, source_target_pairs={{0,1},{1,0},{2,3},{3,2},{4,5},{5,4},{6,7},{7,6},{8,9},{9,8},{10,11... | collective-permute-start | bytes 786440 | tf_op jit(solution)/shard_map/ppermute | solution.py:371
  78.3 9.8 %collective-permute-start.10 = (f32[64,4,256]{2,1,0:T(4,128)S(1)}, f32[64,4,256]{2,1,0:T(4,128)S(1)}, u32[]{:S(2)}, u32[]{:S(2)}) collective-permute-start(f32[64,4,256]{2,1,0:T(4,128)S(1)} %get-tuple-element.63), channel_id=1, source_target_pairs={{1,2},{2,1},{3,4},{4,3},{5,6},{6,5},{7,8},{8,7},{9,10},{10,9},{11,... | collective-permute-start | bytes 786440 | tf_op jit(solution)/shard_map/ppermute | solution.py:372
